TPU v7x, 32 devices: a whole 2x2x4 slice. The times are simulated.
32 devices in a mesh: src: 8 (over z, core), rcv: 4 (over y, x).
Axes of the slice: x: 2, y: 2, z: 4, core: 2. Of those that a mesh axis runs over, the one named last changes fastest.
Arguments:
- spectra: bfloat16 [128, 4, 2, 2048], P(('src', 'rcv')), may hold values from -50 to 50
- valid: int32 [128, 4], P(('src', 'rcv')), may hold values 0 or 1
Outputs:
- correlations: bfloat16 [128, 128, 512], P('src', 'rcv')
All inputs are finite; a program needn't handle non-finite values. No bound on the sum of `valid` on one device may be relied on, other than what follows from the above.
Results may differ from a plain program's by a relative error of at most 0.0065.
Values may be sent and summed in bfloat16 or wider, within the bound.
No kernel may reach another device: no remote copies, remote signals or barrier semaphores. Data moves between devices by JAX's collectives and lax.ppermute only.
A program may use at most 64 MiB of HBM per device.

v0:
```python
import math

import jax
import jax.numpy as jnp
from jax import lax
from jax.sharding import PartitionSpec as P

LAGS = 512
BAND = 32
NSAMP = 7500


epsilon = 1e-06


def whiten_spectra(spectra):
    values = spectra.astype(jnp.float32)
    squares = values[:, :, 0] ** 2 + values[:, :, 1] ** 2
    banded = squares.reshape(squares.shape[0], squares.shape[1], squares.shape[2] // BAND, BAND)
    power = jnp.sum(banded, axis=3) / (2.0 * BAND)
    factor = jnp.repeat(1.0 / jnp.sqrt(power + epsilon), BAND, axis=2)
    return (values * factor[:, :, None, :]).astype(jnp.bfloat16)


def lag_table(freq_count, lag_count):
    bins_index = jnp.arange(freq_count, dtype=jnp.int32)
    shifts = jnp.arange(lag_count, dtype=jnp.int32) - lag_count // 2
    phase = jnp.mod(bins_index[:, None] * shifts[None, :], NSAMP)
    angle = phase.astype(jnp.float32) * (2.0 * math.pi / NSAMP)
    factor = 1.0 / math.sqrt(2.0 * freq_count)
    cosines = (jnp.cos(angle) * factor).astype(jnp.bfloat16)
    sines = (-jnp.sin(angle) * factor).astype(jnp.bfloat16)
    return jnp.concatenate([cosines, sines], axis=0)


def weighted_cross(rec_spec, rec_mask, src_spec, src_mask):
    counts = jnp.dot(rec_mask, src_mask.T, preferred_element_type=jnp.float32)
    inverse = 1.0 / jnp.maximum(counts, 1.0)
    real_part = jnp.zeros((rec_spec.shape[0], src_spec.shape[0], rec_spec.shape[-1]), jnp.float32)
    imag_part = jnp.zeros_like(real_part)
    for window in range(rec_spec.shape[1]):
        rec_a = rec_spec[:, window, 0].astype(jnp.float32)[:, None, :]
        rec_b = rec_spec[:, window, 1].astype(jnp.float32)[:, None, :]
        src_a = src_spec[:, window, 0].astype(jnp.float32)[None, :, :]
        src_b = src_spec[:, window, 1].astype(jnp.float32)[None, :, :]
        pair_weight = (rec_mask[:, window][:, None] * src_mask[:, window][None, :] * inverse)[
            :, :, None
        ]
        real_part = real_part + pair_weight * (src_a * rec_a + src_b * rec_b)
        imag_part = imag_part + pair_weight * (src_b * rec_a - src_a * rec_b)
    return (real_part, imag_part)


def correlate_block(rec_spec, rec_mask, src_spec, src_mask, table):
    real_part, imag_part = weighted_cross(rec_spec, rec_mask, src_spec, src_mask)
    stacked = jnp.concatenate(
        [real_part.astype(jnp.bfloat16), imag_part.astype(jnp.bfloat16)], axis=2
    )
    return jnp.einsum("iqk,kl->iql", stacked, table, preferred_element_type=jnp.float32)


def group_rows(rec_spec, rec_mask, src_spec, src_mask, table):
    receiver_count = rec_spec.shape[0]
    group_count = receiver_count // 8
    source_masks = src_mask.astype(jnp.float32)

    def one_group(group):
        return correlate_block(
            group[0], group[1].astype(jnp.float32), src_spec, source_masks, table
        ).astype(jnp.bfloat16)

    grouped = (
        rec_spec.reshape((group_count, 8) + rec_spec.shape[1:]),
        rec_mask.reshape(group_count, 8, rec_mask.shape[1]),
    )
    result = lax.map(one_group, grouped)
    return result.reshape(receiver_count, src_spec.shape[0], table.shape[1])


def local(spectra, valid):
    table = lag_table(spectra.shape[-1], LAGS)
    mask_wire = valid.astype(jnp.bfloat16)
    whitened = whiten_spectra(spectra)
    rec_spec, rec_mask = (
        lax.all_gather(whitened, "rcv", axis=0, tiled=True),
        lax.all_gather(mask_wire, "rcv", axis=0, tiled=True),
    )
    portion = lax.all_gather((whitened, mask_wire), "src", axis=0, tiled=True)
    return group_rows(rec_spec, rec_mask, portion[0], portion[1], table)


def solution(mesh):
    return jax.shard_map(
        local,
        mesh=mesh,
        in_specs=(P(("src", "rcv"), None, None, None), P(("src", "rcv"), None)),
        out_specs=P("src", "rcv", None),
        check_vma=False,
    )
```

profile of v0, /device:TPU:0, one launch (start us, length us, event | category | flops | bytes accessed | tf_op | source)
XLA Modules:
  0.0 84.7 jit_solution(15054777667643042789)
XLA Ops:
  6.5 0.0 copy-start.1
  6.5 0.0 copy-start.2
  6.5 0.0 all-gather.4.cloned.1.call-start
  6.5 1.0 %copy_convert_fusion = f32[4,4,2,2048]{3,1,2,0:T(4,128)S(1)} fusion(bf16[4,4,2,2048]{3,2,1,0:T(2,128)(2,1)} %param.4), kind=kLoop, calls=%fused_computation.68 | loop fusion | flops 65536 | bytes 393216 | tf_op jit(solution)/shard_map/convert_element_type | solution.py:17
  7.6 0.2 add.64
  7.8 0.2 reduce_sum.9
  8.0 0.2 broadcast_in_dim.8
  8.3 0.3 mul.164
  8.5 0.0 copy-done.1
  8.5 0.7 multiply_convert_fusion.2
  9.3 0.0 all-gather.4.cloned.1.call-update
  9.3 0.0 copy-done.2
  9.3 9.5 %all-gather = bf16[4,4,4]{2,1,0:T(4,128)(2,1)S(1)} all-gather(bf16[1,4,4]{2,1,0:T(4,128)(2,1)S(1)} %convert_bitcast_fusion), channel_id=1, replica_groups=mesh['src'=8,'rcv'=4] {'rcv'}, dimensions={0}, use_global_device_ids=true | all-gather | bytes 160 | tf_op jit(solution)/shard_map/all_gather | solution.py:86
  18.8 12.0 %all-gather.1 = bf16[8,4,4]{2,1,0:T(4,128)(2,1)S(1)} all-gather(bf16[1,4,4]{2,1,0:T(4,128)(2,1)S(1)} %convert_bitcast_fusion), channel_id=1, replica_groups=mesh['src'=8,'rcv'=4] {'src'}, dimensions={0}, use_global_device_ids=true | all-gather | bytes 288 | tf_op jit(solution)/shard_map/all_gather | solution.py:88
  30.9 0.1 copy.22
  31.0 0.1 copy.23
  31.1 0.1 reshape.163
  31.2 0.1 copy.26
  31.3 10.3 %all_gather.15 = bf16[16,4,2,2048]{3,1,2,0:T(4,128)(2,1)S(1)} all-gather(bf16[4,4,2,2048]{3,1,2,0:T(4,128)(2,1)} %multiply_convert_fusion.2), channel_id=1, replica_groups=mesh['src'=8,'rcv'=4] {'rcv'}, dimensions={0}, use_global_device_ids=true | all-gather | bytes 655360 | tf_op jit(solution)/shard_map/all_gather | solution.py:85
  41.5 17.7 %multiply_convert_fusion.1 = (bf16[2048,512]{1,0:T(8,128)(2,1)S(1)}, bf16[2048,512]{1,0:T(8,128)(2,1)S(1)}) fusion(s32[512]{0:T(512)S(1)} %iota_add_fusion), kind=kLoop, calls=%fused_computation.59 | loop fusion | flops 14680064 | bytes 4196352 | tf_op jit(solution)/shard_map/convert_element_type | solution.py:31
  59.2 2.2 %pad_maximum_fusion = bf16[4096,512]{1,0:T(8,128)(2,1)} fusion(bf16[2048,512]{1,0:T(8,128)(2,1)S(1)} %get-tuple-element.114, bf16[2048,512]{1,0:T(8,128)(2,1)S(1)} %get-tuple-element.113), kind=kLoop, calls=%fused_computation.57 | loop fusion | flops 8388608 | bytes 8388608 | tf_op jit(solution)/shard_map/concatenate | solution.py:33
  61.4 0.0 all-gather.4.cloned.1.call-done
  61.4 1.8 %copy.27 = bf16[32,4,2,2048]{3,0,2,1:T(8,128)(2,1)S(1)} copy(bf16[32,4,2,2048]{3,1,2,0:T(4,128)(2,1)} %all-gather.4.cloned.1.call-done) | data formatting | bytes 2097152 | tf_op jit(solution)/shard_map/while | solution.py:76
  63.2 13.8 %while.10 = (s32[]{:T(128)}, bf16[2,8,32,512]{3,2,1,0:T(8,128)(2,1)S(1)}, bf16[2,8,4]{1,2,0:T(4,128)(2,1)S(1)}, f32[32,4]{0,1:T(4,128)S(1)}, bf16[32,4,2,2048]{3...) while((s32[]{:T(128)}, ...), condition=%wide.region_2.3_spmd, body=%wide.region_1.2_spmd.sunk | while | flops 1099698688 | bytes 35672640 | solution.py:76
  63.3 0.2 multiply_multiply_fusion.5
  63.5 0.1 constant_dynamic-slice_fusion.4
  63.6 0.2 copy.40
  63.8 0.2 bitcast_convert_fusion.11
  64.1 0.0 copy-start
  64.1 2.3 %add_convert_fusion.5 = bf16[8,32,2048]{2,1,0:T(8,128)(2,1)S(1)} fusion(f32[8,2048]{1,0:T(8,128)S(1)} %get-tuple-element.186, f32[32,2048]{1,0:T(8,128)S(1)} %get-tuple-element.187, f32[8,2048]{1,0:T(8,128)S(1)} %get-tuple-element.188, f32[32,2048]{1,0:T(8,128)S(1)} %get-tuple-element.189, f32[8,32]{1,0:T(8,128)S(1)} %get-tuple-element.198, ...), kind=kLoop, calls=%fused_computation.6.clone.1 | loop fusion | flops 10485760 | bytes 3674112 | tf_op jit(solution)/shard_map/while/body/eval_jaxpr/convert_element_type | solution.py:57
  66.4 2.5 %add_convert_fusion.4 = bf16[8,32,2048]{2,1,0:T(8,128)(2,1)S(1)} fusion(f32[8,2048]{1,0:T(8,128)S(1)} %get-tuple-element.186, f32[32,2048]{1,0:T(8,128)S(1)} %get-tuple-element.187, f32[8,2048]{1,0:T(8,128)S(1)} %get-tuple-element.188, f32[32,2048]{1,0:T(8,128)S(1)} %get-tuple-element.189, f32[8,32]{1,0:T(8,128)S(1)} %get-tuple-element.198, ...), kind=kLoop, calls=%fused_computation.5.clone.1 | loop fusion | flops 10485760 | bytes 3674112 | tf_op jit(solution)/shard_map/while/body/eval_jaxpr/convert_element_type | solution.py:57
  68.9 0.0 copy-done
  68.9 1.2 %fusion.47 = bf16[2,8,32,512]{3,2,1,0:T(8,128)(2,1)S(1)} fusion(bf16[2,8,32,512]{3,2,1,0:T(8,128)(2,1)S(1)} %get-tuple-element.223, s32[]{:T(128)} %get-tuple-element.222, bf16[4096,512]{1,0:T(8,128)(2,1)S(1)} %copy-done, bf16[8,32,2048]{2,1,0:T(8,128)(2,1)S(1)} %add_convert_fusion.4, bf16[8,32,2048]{2,1,0:T(8,128)(2,1)S(1)} %add_convert_fusion.5), kind=kOutput, calls=%fused_computation.9.clone.1 | convolution fusion | flops 1078067200 | bytes 6553604 | tf_op jit(solution)/shard_map/while/body/eval_jaxpr/iqk,kl->iql/dot_general | solution.py:59
  70.2 0.2 multiply_multiply_fusion.5
  70.4 0.1 constant_dynamic-slice_fusion.4
  70.5 0.2 copy.40
  70.7 0.2 bitcast_convert_fusion.11
  70.9 0.0 copy-start
  71.0 2.3 %add_convert_fusion.5 = bf16[8,32,2048]{2,1,0:T(8,128)(2,1)S(1)} fusion(f32[8,2048]{1,0:T(8,128)S(1)} %get-tuple-element.186, f32[32,2048]{1,0:T(8,128)S(1)} %get-tuple-element.187, f32[8,2048]{1,0:T(8,128)S(1)} %get-tuple-element.188, f32[32,2048]{1,0:T(8,128)S(1)} %get-tuple-element.189, f32[8,32]{1,0:T(8,128)S(1)} %get-tuple-element.198, ...), kind=kLoop, calls=%fused_computation.6.clone.1 | loop fusion | flops 10485760 | bytes 3674112 | tf_op jit(solution)/shard_map/while/body/eval_jaxpr/convert_element_type | solution.py:57
  73.3 2.5 %add_convert_fusion.4 = bf16[8,32,2048]{2,1,0:T(8,128)(2,1)S(1)} fusion(f32[8,2048]{1,0:T(8,128)S(1)} %get-tuple-element.186, f32[32,2048]{1,0:T(8,128)S(1)} %get-tuple-element.187, f32[8,2048]{1,0:T(8,128)S(1)} %get-tuple-element.188, f32[32,2048]{1,0:T(8,128)S(1)} %get-tuple-element.189, f32[8,32]{1,0:T(8,128)S(1)} %get-tuple-element.198, ...), kind=kLoop, calls=%fused_computation.5.clone.1 | loop fusion | flops 10485760 | bytes 3674112 | tf_op jit(solution)/shard_map/while/body/eval_jaxpr/convert_element_type | solution.py:57
  75.8 0.0 copy-done
  75.8 1.2 %fusion.47 = bf16[2,8,32,512]{3,2,1,0:T(8,128)(2,1)S(1)} fusion(bf16[2,8,32,512]{3,2,1,0:T(8,128)(2,1)S(1)} %get-tuple-element.223, s32[]{:T(128)} %get-tuple-element.222, bf16[4096,512]{1,0:T(8,128)(2,1)S(1)} %copy-done, bf16[8,32,2048]{2,1,0:T(8,128)(2,1)S(1)} %add_convert_fusion.4, bf16[8,32,2048]{2,1,0:T(8,128)(2,1)S(1)} %add_convert_fusion.5), kind=kOutput, calls=%fused_computation.9.clone.1 | convolution fusion | flops 1078067200 | bytes 6553604 | tf_op jit(solution)/shard_map/while/body/eval_jaxpr/iqk,kl->iql/dot_general | solution.py:59
  77.0 0.0 copy-start.3
  77.0 0.8 copy-done.3
  (13 shorter events, 0.2 us)
Async XLA Ops:
  6.5 2.0 %copy-start.1 = (bf16[4,4,2,2048]{3,2,1,0:T(2,128)(2,1)S(1)}, bf16[4,4,2,2048]{3,2,1,0:T(2,128)(2,1)}, u32[]{:S(2)}) copy-start(bf16[4,4,2,2048]{3,2,1,0:T(2,128)(2,1)} %param.4) | copy-start | bytes 393220
  6.5 2.8 %copy-start.2 = (s32[4,4]{1,0:T(4,128)S(1)}, s32[4,4]{1,0:T(4,128)}, u32[]{:S(2)}) copy-start(s32[4,4]{1,0:T(4,128)} %param.5) | copy-start | bytes 196
  6.5 54.9 %all-gather.4.cloned.1.call-start = ((), (), s32[]{:S(2)}) async-start(), calls=%async_computation | async-start | bytes 1179648 | tf_op jit(solution)/shard_map/all_gather | solution.py:88
  64.1 4.8 %copy-start = (bf16[4096,512]{1,0:T(8,128)(2,1)S(1)}, bf16[4096,512]{1,0:T(8,128)(2,1)}, u32[]{:S(2)}) copy-start(bf16[4096,512]{1,0:T(8,128)(2,1)} %get-tuple-element.236) | copy-start | bytes 12582916 | tf_op jit(solution)/shard_map/while
  70.9 4.8 %copy-start = (bf16[4096,512]{1,0:T(8,128)(2,1)S(1)}, bf16[4096,512]{1,0:T(8,128)(2,1)}, u32[]{:S(2)}) copy-start(bf16[4096,512]{1,0:T(8,128)(2,1)} %get-tuple-element.236) | copy-start | bytes 12582916 | tf_op jit(solution)/shard_map/while
  77.0 0.8 copy-start.3
Sparse Core Ops, SparseCore 0:
  9.4 24.8 all-gather.3
where the time goes:
time: 84.9 us; the launch traced here: 84.7 us
  other arithmetic  32.1 us (38%)
  blocking collectives  31.8 us (37%)
  between operations  13.5 us (16%)
  local copies, waits for them, and re-layouts  4.24 us (5%)
  matrix products  2.84 us (3%)
    convert_element_type x1, other arithmetic, lag_table(): cosines = (jnp.cos(angle) * factor).astype(jnp.bfloat16)  17.7 us
    all_gather x1, blocking collectives, local(): portion = lax.all_gather((whitened, mask_wire), 'src', axis=0, tiled=True)  12 us
    all_gather x1, blocking collectives, local(): lax.all_gather(whitened, 'rcv', axis=0, tiled=True)  10.3 us
    all_gather x1, blocking collectives, local(): lax.all_gather(mask_wire, 'rcv', axis=0, tiled=True)  9.52 us
    convert_element_type x2, other arithmetic, correlate_block(): imag_part.astype(jnp.bfloat16)  4.96 us
    convert_element_type x2, other arithmetic, correlate_block(): real_part.astype(jnp.bfloat16)  4.61 us
    dot_general x2, matrix products, correlate_block(): jnp.einsum('iqk,kl->iql', stacked, table, preferred_element_type=jnp.floa...  2.49 us
    concatenate x1, other arithmetic, lag_table(): return jnp.concatenate([cosines, sines], axis=0)  2.23 us
  transfers between devices with their start and end apart: 1, of which 0 were waited for; matrix products, arithmetic and copies ran while one was open for 24% of the time, Pallas kernels for 0%

commit v1 on v0

v1 whole, which is shorter than its diff:
```python
import math

import jax
import jax.numpy as jnp
from jax import lax
from jax.sharding import PartitionSpec as P

LAGS = 512
BAND = 32
NSAMP = 7500
PAD = 128

epsilon = 1e-06


def whiten_spectra(spectra):
    values = spectra.astype(jnp.float32)
    squares = values[:, :, 0] ** 2 + values[:, :, 1] ** 2
    banded = squares.reshape(squares.shape[0], squares.shape[1], squares.shape[2] // BAND, BAND)
    power = jnp.sum(banded, axis=3) / (2.0 * BAND)
    factor = jnp.repeat(1.0 / jnp.sqrt(power + epsilon), BAND, axis=2)
    return (values * factor[:, :, None, :]).astype(jnp.bfloat16)


def lag_table(freq_count, lag_count):
    step = 64
    shifts = jnp.arange(lag_count, dtype=jnp.int32) - lag_count // 2
    hi = jnp.arange(freq_count // step, dtype=jnp.int32) * step
    lo = jnp.arange(step, dtype=jnp.int32)
    scale = 2.0 * math.pi / NSAMP
    angle_hi = jnp.mod(hi[:, None] * shifts[None, :], NSAMP).astype(jnp.float32) * scale
    angle_lo = jnp.mod(lo[:, None] * shifts[None, :], NSAMP).astype(jnp.float32) * scale
    cos_hi, sin_hi = jnp.cos(angle_hi)[:, None, :], jnp.sin(angle_hi)[:, None, :]
    cos_lo, sin_lo = jnp.cos(angle_lo)[None, :, :], jnp.sin(angle_lo)[None, :, :]
    factor = 1.0 / math.sqrt(2.0 * freq_count)
    cosines = (cos_hi * cos_lo - sin_hi * sin_lo) * factor
    sines = (sin_hi * cos_lo + cos_hi * sin_lo) * (-factor)
    cosines = cosines.reshape(freq_count, lag_count).astype(jnp.bfloat16)
    sines = sines.reshape(freq_count, lag_count).astype(jnp.bfloat16)
    return jnp.stack([cosines, sines], axis=0)


def pack(whitened, mask):
    channels = whitened.shape[0]
    flat = whitened.reshape(channels, -1)
    tail = jnp.zeros((channels, PAD), jnp.bfloat16).at[:, : mask.shape[1]].set(mask)
    return jnp.concatenate([flat, tail], axis=1)


def unpack(packed, windows, freqs):
    channels = packed.shape[0]
    body = packed[:, : windows * 2 * freqs].reshape(channels, windows, 2, freqs)
    mask = packed[:, windows * 2 * freqs : windows * 2 * freqs + windows].astype(jnp.float32)
    return body, mask


def local(spectra, valid):
    channels, windows, _, freqs = spectra.shape
    table = lag_table(freqs, LAGS)
    mask_wire = valid.astype(jnp.bfloat16)
    whitened = whiten_spectra(spectra)
    packed = pack(whitened, mask_wire)
    rec_packed = lax.all_gather(packed, "rcv", axis=0, tiled=True)
    src_packed = lax.all_gather(packed, "src", axis=0, tiled=True)
    rec_spec, rec_mask = unpack(rec_packed, windows, freqs)
    src_spec, src_mask = unpack(src_packed, windows, freqs)

    counts = jnp.dot(rec_mask, src_mask.T, preferred_element_type=jnp.float32)
    inverse = 1.0 / jnp.maximum(counts, 1.0)
    rec = rec_spec.astype(jnp.float32) * rec_mask[:, :, None, None]
    src = src_spec.astype(jnp.float32) * src_mask[:, :, None, None]
    ra, rb = rec[:, :, 0][:, None], rec[:, :, 1][:, None]
    sa, sb = src[:, :, 0][None], src[:, :, 1][None]
    real_part = jnp.sum(sa * ra + sb * rb, axis=2) * inverse[:, :, None]
    imag_part = jnp.sum(sb * ra - sa * rb, axis=2) * inverse[:, :, None]
    stacked = jnp.stack(
        [real_part.astype(jnp.bfloat16), imag_part.astype(jnp.bfloat16)], axis=2
    )
    out = jnp.einsum("iqpf,pfl->iql", stacked, table, preferred_element_type=jnp.float32)
    return out.astype(jnp.bfloat16)


def solution(mesh):
    return jax.shard_map(
        local,
        mesh=mesh,
        in_specs=(P(("src", "rcv"), None, None, None), P(("src", "rcv"), None)),
        out_specs=P("src", "rcv", None),
        check_vma=False,
    )
```

time: 84.9 us -> 67.3 us (0.79)
  blocking collectives: 31.8 us -> 11.9 us
  other arithmetic: 32.1 us -> 20.3 us
  local copies, waits for them, and re-layouts: 4.24 us -> 11.4 us
  waiting for transfers between devices: 0.02 us -> 5.86 us
  matrix products: 2.84 us -> 3.93 us
    convert_element_type x11 -> x6, other arithmetic: 27.8 us -> 5.01 us  [the longest x1 3.48 us: lag_table(): cosines = cosines.reshape(freq_count, lag_count).astype(jnp.bfloat16)]
    all_gather x3 -> x1, blocking collectives: 31.8 us -> 11.9 us  [local(): rec_packed = lax.all_gather(packed, 'rcv', axis=0, tiled=True)]
    reduce_sum x0 -> x1, other arithmetic: none -> 5.87 us  [local(): real_part = jnp.sum(sa * ra + sb * rb, axis=2) * inverse[:, :, None]]
    all_gather x1, waiting for transfers between devices: 0.01 us -> 5.84 us  [local(): src_packed = lax.all_gather(packed, 'src', axis=0, tiled=True)]
    convert_element_type x2, local copies, waits for them, and re-layouts: 0.19 us -> 3.69 us  [the longest x1 2.8 us: local(): src = src_spec.astype(jnp.float32) * src_mask[:, :, None, None]]
    mul x0 -> x3, other arithmetic: none -> 3.08 us  [the longest x1 2.39 us: local(): src = src_spec.astype(jnp.float32) * src_mask[:, :, None, None]]
    slice x0 -> x1, local copies, waits for them, and re-layouts: none -> 2.33 us  [local(): sa, sb = (src[:, :, 0][None], src[:, :, 1][None])]
    mul x4 -> x2, local copies, waits for them, and re-layouts: 0.02 us -> 2.31 us  [local(): real_part = jnp.sum(sa * ra + sb * rb, axis=2) * inverse[:, :, None]]
  transfers between devices with their start and end apart: 1 -> 1, of which waited for: 0 -> 1; matrix products, arithmetic and copies ran while one was open for 24% -> 11% of each run, Pallas kernels for 0% -> 0%
where the time goes in v1:
time: 67.3 us; the launch traced here: 67 us
  other arithmetic  20.3 us (30%)
  between operations  13.6 us (20%)
  blocking collectives  11.9 us (18%)
  local copies, waits for them, and re-layouts  11.4 us (17%)
  waiting for transfers between devices  5.86 us (9%)
  matrix products  3.93 us (6%)
    all_gather x1, blocking collectives, local(): rec_packed = lax.all_gather(packed, 'rcv', axis=0, tiled=True)  11.9 us
    reduce_sum x1, other arithmetic, local(): real_part = jnp.sum(sa * ra + sb * rb, axis=2) * inverse[:, :, None]  5.87 us
    all_gather x1, waiting for transfers between devices, local(): src_packed = lax.all_gather(packed, 'src', axis=0, tiled=True)  5.84 us
    convert_element_type x1, other arithmetic, lag_table(): cosines = cosines.reshape(freq_count, lag_count).astype(jnp.bfloat16)  3.48 us
    dot_general x1, matrix products, local(): jnp.einsum('iqpf,pfl->iql', stacked, table, preferred_element_type=jnp.fl...  3.12 us
    convert_element_type x1, local copies, waits for them, and re-layouts, local(): src = src_spec.astype(jnp.float32) * src_mask[:, :, None, None]  2.8 us
    mul x1, other arithmetic, local(): src = src_spec.astype(jnp.float32) * src_mask[:, :, None, None]  2.39 us
    unnamed x12, local copies, waits for them, and re-layouts  2.37 us
  transfers between devices with their start and end apart: 1, of which 1 were waited for; matrix products, arithmetic and copies ran while one was open for 11% of the time, Pallas kernels for 0%

profile of v1, /device:TPU:0, one launch (start us, length us, event | category | flops | bytes accessed | tf_op | source)
XLA Modules:
  0.0 67.0 jit_solution(18312585500879750957)
XLA Ops:
  6.5 0.0 all-gather.4.cloned.1.call-start
  6.5 0.6 compare_reduce_fusion
  7.2 1.0 %convert_element_type.100 = f32[4,4,2,2048]{3,2,1,0:T(2,128)S(1)} convert(bf16[4,4,2,2048]{3,2,1,0:T(2,128)(2,1)} %param.4) | non-fusion elementwise | flops 65536 | bytes 393216 | tf_op jit(solution)/shard_map/convert_element_type | solution.py:17
  8.2 0.5 fusion.25
  8.7 0.2 add.72
  8.9 0.2 reduce_sum.31
  9.1 0.2 broadcast_in_dim.2
  9.3 0.3 mul.318
  9.6 1.0 %multiply_convert_fusion.2 = bf16[4,4,2,2048]{3,2,1,0:T(2,128)(2,1)S(1)} fusion(f32[4,4,2048]{2,1,0:T(4,128)S(1)} %mul.318, bf16[4,4,2,2048]{3,2,1,0:T(2,128)(2,1)} %param.4), kind=kLoop, calls=%fused_computation.29 | loop fusion | flops 196608 | bytes 393216 | tf_op jit(solution)/shard_map/convert_element_type | solution.py:22
  10.6 0.1 reshape.288
  10.7 1.3 %convert_select_fusion = bf16[4,4]{1,0:T(4,128)(2,1)S(1)} fusion(s32[4,4]{1,0:T(4,128)} %param.5, pred[]{:T(512)} %compare_reduce_fusion), kind=kLoop, calls=%fused_computation.61 | loop fusion | flops 32 | bytes 97 | tf_op jit(solution)/shard_map/select.1
  12.0 0.7 %fusion.17 = bf16[1,4,16512]{2,1,0:T(4,128)(2,1)} fusion(bf16[4,4]{1,0:T(4,128)(2,1)S(1)} %convert_select_fusion, bf16[4,16384]{1,0:T(4,128)(2,1)S(1)} %reshape.288), kind=kLoop, calls=%fused_computation.32 | loop fusion | flops 396288 | bytes 263200
  12.8 0.0 all-gather.4.cloned.1.call-update
  12.8 11.9 %all-gather.1 = bf16[4,4,16512]{2,1,0:T(4,128)(2,1)S(1)} all-gather(bf16[1,4,16512]{2,1,0:T(4,128)(2,1)} %fusion.17), channel_id=1, replica_groups=mesh['src'=8,'rcv'=4] {'rcv'}, dimensions={0}, use_global_device_ids=true | all-gather | bytes 660480 | tf_op jit(solution)/shard_map/all_gather | solution.py:63
  24.7 0.1 reshape.294
  24.8 0.0 copy-start
  24.8 0.1 slice_convert_fusion.1
  24.9 0.9 %reshape.290 = f32[16,4,2,2048]{3,2,1,0:T(2,128)S(1)} reshape(f32[16,16384]{1,0:T(8,128)S(1)} %slice_convert_fusion.1) | data formatting | bytes 2097152 | tf_op jit(solution)/shard_map/convert_element_type | solution.py:70
  25.8 0.3 fusion.32
  26.2 0.5 fusion.24
  26.7 3.5 %multiply_convert_fusion.1 = (bf16[32,64,512]{2,1,0:T(8,128)(2,1)}, bf16[32,64,512]{2,1,0:T(8,128)(2,1)}) fusion(f32[64,512]{1,0:T(8,128)S(1)} %get-tuple-element.30, f32[32,512]{1,0:T(8,128)S(1)} %get-tuple-element.28, f32[64,512]{1,0:T(8,128)S(1)} %get-tuple-element.29, f32[32,512]{1,0:T(8,128)S(1)} %get-tuple-element.27), kind=kLoop, calls=%fused_computation.14 | loop fusion | flops 10485760 | bytes 4587520 | tf_op jit(solution)/shard_map/convert_element_type | solution.py:38
  30.2 0.0 copy-done
  30.2 0.7 %copy_multiply_fusion = f32[16,4,2,2048]{3,1,0,2:T(4,128)S(1)} fusion(f32[16,4,2,2048]{3,2,1,0:T(2,128)S(1)} %reshape.290, f32[16,4]{1,0:T(8,128)S(1)} %slice_convert_fusion.3), kind=kLoop, calls=%fused_computation.22 | loop fusion | flops 262144 | bytes 2097408 | tf_op jit(solution)/shard_map/mul | solution.py:70
  30.9 1.1 %slice_bitcast_fusion.1 = (f32[16,4,2048]{2,1,0:T(4,128)}, f32[16,4,2048]{2,1,0:T(4,128)}) fusion(f32[16,4,2,2048]{3,1,0,2:T(4,128)S(1)} %copy_multiply_fusion), kind=kLoop, calls=%fused_computation.25 | loop fusion | bytes 2097152 | tf_op jit(solution)/shard_map/mul | solution.py:74
  32.0 5.8 %all-gather.4.cloned.1.call-done = bf16[8,4,16512]{2,1,0:T(4,128)(2,1)} async-done(((bf16[1,4,16512]{2,1,0:T(4,128)(2,1)}), bf16[8,4,16512]{2,1,0:T(4,128)(2,1)}) %all-gather.4.cloned.1.call-update) | async-done | bytes 1056784 | tf_op jit(solution)/shard_map/all_gather | solution.py:64
  37.8 1.3 %reshape.292 = bf16[32,16512]{1,0:T(8,128)(2,1)S(1)} reshape(bf16[8,4,16512]{2,1,0:T(4,128)(2,1)} %all-gather.4.cloned.1.call-done) | data formatting | bytes 2113536
  39.2 0.1 slice_convert_fusion
  39.3 0.8 %fusion.14 = f32[16,32]{1,0:T(8,128)S(1)} fusion(bf16[32,16512]{1,0:T(8,128)(2,1)S(1)} %reshape.292, bf16[16,16512]{1,0:T(8,128)(2,1)} %copy-done), kind=kOutput, calls=%fused_computation.18 | convolution fusion | flops 5120 | bytes 14336 | tf_op jit(solution)/shard_map/dot_general | solution.py:68
  40.1 2.8 %reshape.289 = f32[32,4,2,2048]{3,2,1,0:T(2,128)} reshape(f32[32,16384]{1,0:T(8,128)S(1)} %slice_convert_fusion) | data formatting | bytes 4194304 | tf_op jit(solution)/shard_map/convert_element_type | solution.py:71
  42.9 2.4 %broadcast_multiply_fusion = f32[32,4,2,2048]{3,2,1,0:T(2,128)S(1)} fusion(f32[32,4,2,2048]{3,2,1,0:T(2,128)} %reshape.289, f32[32,4]{1,0:T(8,128)S(1)} %slice_convert_fusion.2), kind=kLoop, calls=%fused_computation.23 | loop fusion | flops 524288 | bytes 4194816 | tf_op jit(solution)/shard_map/mul | solution.py:71
  45.3 0.0 copy-start.3
  45.3 0.0 copy-start.4
  45.4 2.3 %fusion.37 = (f32[32,4,1,2048]{3,2,1,0:T(1,128)S(1)}, f32[32,4,1,2048]{3,2,1,0:T(1,128)S(1)}) fusion(f32[32,4,2,2048]{3,2,1,0:T(2,128)S(1)} %broadcast_multiply_fusion), kind=kLoop, calls=%fused_computation.64 | loop fusion | bytes 4194304 | tf_op jit(solution)/shard_map/slice | solution.py:73
  47.7 1.2 %copy_bitcast_fusion = (f32[32,4,2048]{2,0,1:T(8,128)S(1)}, f32[32,4,2048]{2,0,1:T(8,128)S(1)}) fusion(f32[32,4,1,2048]{3,2,1,0:T(1,128)S(1)} %get-tuple-element.20, f32[32,4,1,2048]{3,2,1,0:T(1,128)S(1)} %get-tuple-element.19), kind=kLoop, calls=%fused_computation.20 | loop fusion | bytes 4194304 | tf_op jit(solution)/shard_map/mul | solution.py:74
  48.9 0.0 copy-done.3
  48.9 0.0 copy-done.4
  48.9 5.9 %add_reduce_fusion = (f32[16,32,2048]{2,1,0:T(8,128)S(1)}, f32[16,32,2048]{2,1,0:T(8,128)S(1)}) fusion(f32[16,4,2048]{2,1,0:T(4,128)S(1)} %copy-done.4, f32[32,4,2048]{2,0,1:T(8,128)S(1)} %get-tuple-element.31, f32[16,4,2048]{2,1,0:T(4,128)S(1)} %copy-done.3, f32[32,4,2048]{2,0,1:T(8,128)S(1)} %get-tuple-element.32), kind=kLoop, calls=%fused_computation.1 | loop fusion | flops 31457280 | bytes 11534336 | tf_op jit(solution)/shard_map/reduce_sum | solution.py:74
  54.8 0.0 copy-start.1
  54.8 0.0 copy-start.2
  54.8 1.3 %fusion.7 = (bf16[16,32,1,2048]{3,1,2,0:T(8,128)(2,1)S(1)}, bf16[16,32,1,2048]{3,1,2,0:T(8,128)(2,1)S(1)}) fusion(f32[16,32,2048]{2,1,0:T(8,128)S(1)} %get-tuple-element.17, f32[16,32]{1,0:T(8,128)S(1)} %fusion.14, f32[16,32,2048]{2,1,0:T(8,128)S(1)} %get-tuple-element.18), kind=kLoop, calls=%fused_computation.12 | loop fusion | flops 4194304 | bytes 12584960 | tf_op jit(solution)/shard_map/convert_element_type | solution.py:77
  56.2 0.2 copy-done.1
  56.4 0.6 copy-done.2
  57.0 3.1 %fusion.11 = bf16[16,32,512]{2,1,0:T(8,128)(2,1)} fusion(bf16[1,2048,512]{2,1,0:T(8,128)(2,1)S(1)} %bitcast.35, bf16[1,2048,512]{2,1,0:T(8,128)(2,1)S(1)} %bitcast.34, bf16[16,32,1,2048]{3,1,2,0:T(8,128)(2,1)S(1)} %get-tuple-element.26, bf16[16,32,1,2048]{3,1,2,0:T(8,128)(2,1)S(1)} %get-tuple-element.25), kind=kOutput, calls=%fused_computation.16 | convolution fusion | flops 2151940096 | bytes 8912896 | tf_op jit(solution)/shard_map/iqpf,pfl->iql/dot_general | solution.py:79
  (5 shorter events, 0.0 us)
Async XLA Ops:
  6.5 31.3 %all-gather.4.cloned.1.call-start = ((), (), s32[]{:S(2)}) async-start(), calls=%async_computation | async-start | bytes 1188864 | tf_op jit(solution)/shard_map/all_gather | solution.py:64
  24.8 5.4 %copy-start = (bf16[16,16512]{1,0:T(8,128)(2,1)}, bf16[16,16512]{1,0:T(8,128)(2,1)S(1)}, u32[]{:S(2)}) copy-start(bf16[16,16512]{1,0:T(8,128)(2,1)S(1)} %reshape.294) | copy-start | bytes 1585156
  45.3 3.6 %copy-start.3 = (f32[16,4,2048]{2,1,0:T(4,128)S(1)}, f32[16,4,2048]{2,1,0:T(4,128)}, u32[]{:S(2)}) copy-start(f32[16,4,2048]{2,1,0:T(4,128)} %get-tuple-element.21) | copy-start | bytes 1572868
  45.3 3.6 %copy-start.4 = (f32[16,4,2048]{2,1,0:T(4,128)S(1)}, f32[16,4,2048]{2,1,0:T(4,128)}, u32[]{:S(2)}) copy-start(f32[16,4,2048]{2,1,0:T(4,128)} %get-tuple-element.22) | copy-start | bytes 1572868
  54.8 1.6 %copy-start.1 = (bf16[32,64,512]{2,1,0:T(8,128)(2,1)S(1)}, bf16[32,64,512]{2,1,0:T(8,128)(2,1)}, u32[]{:S(2)}) copy-start(bf16[32,64,512]{2,1,0:T(8,128)(2,1)} %get-tuple-element.23) | copy-start | bytes 6291460
  54.8 2.2 %copy-start.2 = (bf16[32,64,512]{2,1,0:T(8,128)(2,1)S(1)}, bf16[32,64,512]{2,1,0:T(8,128)(2,1)}, u32[]{:S(2)}) copy-start(bf16[32,64,512]{2,1,0:T(8,128)(2,1)} %get-tuple-element.24) | copy-start | bytes 6291460
Sparse Core Ops, SparseCore 0:
  12.9 24.8 all-gather.3

commit v2 on v1

--- a/solution.py
+++ b/solution.py
@@ -1,8 +1,11 @@
+import functools
 import math
 
 import jax
 import jax.numpy as jnp
 from jax import lax
+from jax.experimental import pallas as pl
+from jax.experimental.pallas import tpu as pltpu
 from jax.sharding import PartitionSpec as P
 
 LAGS = 512
@@ -47,37 +50,92 @@
     return jnp.concatenate([flat, tail], axis=1)
 
 
-def unpack(packed, windows, freqs):
-    channels = packed.shape[0]
-    body = packed[:, : windows * 2 * freqs].reshape(channels, windows, 2, freqs)
-    mask = packed[:, windows * 2 * freqs : windows * 2 * freqs + windows].astype(jnp.float32)
-    return body, mask
+def cross_kernel(rec_ref, src_ref, tab_ref, out_ref, srcf, recf, rtails, cross, *, windows, freqs, group, chunk):
+    step = pl.program_id(0)
+    nsrc = src_ref.shape[0]
+    body = windows * 2 * freqs
+    width = 2 * freqs
+
+    @pl.when(step == 0)
+    def _():
+        smask = src_ref[:, body : body + PAD].astype(jnp.float32)
+        rmask = rec_ref[:, body : body + PAD].astype(jnp.float32)
+        rtails[...] = rmask
+        for w in range(windows):
+            cols = slice(w * width, (w + 1) * width)
+            srcf[:, cols] = src_ref[:, cols].astype(jnp.float32) * smask[:, w : w + 1]
+            recf[:, cols] = rec_ref[:, cols].astype(jnp.float32) * rmask[:, w : w + 1]
+
+    smask = src_ref[:, body : body + PAD].astype(jnp.float32)
+
+    def per_receiver(j, carry):
+        i = step * group + j
+        rtail = rtails[pl.ds(i, 1), :]
+        count = jnp.sum(smask * rtail, axis=1, keepdims=True)
+        inverse = 1.0 / jnp.maximum(count, 1.0)
+        rows = pl.ds(pl.multiple_of(j * nsrc, nsrc), nsrc)
+        for c in range(freqs // chunk):
+            real = jnp.zeros((nsrc, chunk), jnp.float32)
+            imag = jnp.zeros((nsrc, chunk), jnp.float32)
+            for w in range(windows):
+                a0 = w * width + c * chunk
+                b0 = a0 + freqs
+                sa = srcf[:, a0 : a0 + chunk]
+                sb = srcf[:, b0 : b0 + chunk]
+                ra = recf[pl.ds(i, 1), a0 : a0 + chunk]
+                rb = recf[pl.ds(i, 1), b0 : b0 + chunk]
+                real = real + (sa * ra + sb * rb)
+                imag = imag + (sb * ra - sa * rb)
+            cross[rows, c * chunk : (c + 1) * chunk] = (real * inverse).astype(jnp.bfloat16)
+            cross[rows, freqs + c * chunk : freqs + (c + 1) * chunk] = (imag * inverse).astype(
+                jnp.bfloat16
+            )
+        return carry
+
+    lax.fori_loop(0, group, per_receiver, 0)
+    out_ref[...] = jnp.dot(
+        cross[...], tab_ref[...], preferred_element_type=jnp.float32
+    ).astype(jnp.bfloat16)
+
+
+def correlate(rec_packed, src_packed, table, windows, freqs):
+    nrec, width = rec_packed.shape
+    nsrc = src_packed.shape[0]
+    lags = table.shape[1]
+    group = 8
+    kernel = functools.partial(
+        cross_kernel, windows=windows, freqs=freqs, group=group, chunk=256
+    )
+    out = pl.pallas_call(
+        kernel,
+        grid=(nrec // group,),
+        in_specs=[
+            pl.BlockSpec((nrec, width), lambda g: (0, 0)),
+            pl.BlockSpec((nsrc, width), lambda g: (0, 0)),
+            pl.BlockSpec(table.shape, lambda g: (0, 0)),
+        ],
+        out_specs=pl.BlockSpec((group * nsrc, lags), lambda g: (g, 0)),
+        out_shape=jax.ShapeDtypeStruct((nrec * nsrc, lags), jnp.bfloat16),
+        scratch_shapes=[
+            pltpu.VMEM((nsrc, windows * 2 * freqs), jnp.float32),
+            pltpu.VMEM((nrec, windows * 2 * freqs), jnp.float32),
+            pltpu.VMEM((nrec, PAD), jnp.float32),
+            pltpu.VMEM((group * nsrc, 2 * freqs), jnp.bfloat16),
+        ],
+        compiler_params=pltpu.CompilerParams(dimension_semantics=("arbitrary",)),
+    )(rec_packed, src_packed, table)
+    return out.reshape(nrec, nsrc, lags)
 
 
 def local(spectra, valid):
     channels, windows, _, freqs = spectra.shape
-    table = lag_table(freqs, LAGS)
+    table = lag_table(freqs, LAGS).reshape(2 * freqs, LAGS)
     mask_wire = valid.astype(jnp.bfloat16)
     whitened = whiten_spectra(spectra)
     packed = pack(whitened, mask_wire)
     rec_packed = lax.all_gather(packed, "rcv", axis=0, tiled=True)
     src_packed = lax.all_gather(packed, "src", axis=0, tiled=True)
-    rec_spec, rec_mask = unpack(rec_packed, windows, freqs)
-    src_spec, src_mask = unpack(src_packed, windows, freqs)
-
-    counts = jnp.dot(rec_mask, src_mask.T, preferred_element_type=jnp.float32)
-    inverse = 1.0 / jnp.maximum(counts, 1.0)
-    rec = rec_spec.astype(jnp.float32) * rec_mask[:, :, None, None]
-    src = src_spec.astype(jnp.float32) * src_mask[:, :, None, None]
-    ra, rb = rec[:, :, 0][:, None], rec[:, :, 1][:, None]
-    sa, sb = src[:, :, 0][None], src[:, :, 1][None]
-    real_part = jnp.sum(sa * ra + sb * rb, axis=2) * inverse[:, :, None]
-    imag_part = jnp.sum(sb * ra - sa * rb, axis=2) * inverse[:, :, None]
-    stacked = jnp.stack(
-        [real_part.astype(jnp.bfloat16), imag_part.astype(jnp.bfloat16)], axis=2
-    )
-    out = jnp.einsum("iqpf,pfl->iql", stacked, table, preferred_element_type=jnp.float32)
-    return out.astype(jnp.bfloat16)
+    return correlate(rec_packed, src_packed, table, windows, freqs)
 
 
 def solution(mesh):

time: 67.3 us -> 58.2 us (0.86)
  Pallas kernels: 0 us -> 11.1 us
  other arithmetic: 20.3 us -> 10.2 us
  local copies, waits for them, and re-layouts: 11.4 us -> 3.84 us
  matrix products: 3.93 us -> 0 us
  waiting for transfers between devices: 5.86 us -> 7.49 us
    pallas_call x0 -> x1, Pallas kernels: none -> 11.1 us  [correlate(): pl.pallas_call(kernel, grid=(nrec // group,), in_specs=[pl.BlockSpec((nre...]
    reduce_sum x1 -> x0, other arithmetic: 5.87 us -> none  [local(): real_part = jnp.sum(sa * ra + sb * rb, axis=2) * inverse[:, :, None]]
    dot_general x2 -> x0, matrix products: 3.93 us -> none  [the longest x1 3.12 us: local(): jnp.einsum('iqpf,pfl->iql', stacked, table, preferred_element_type=jnp.fl...]
    convert_element_type x2 -> x0, local copies, waits for them, and re-layouts: 3.69 us -> none  [the longest x1 2.8 us: local(): src = src_spec.astype(jnp.float32) * src_mask[:, :, None, None]]
    mul x2 -> x0, other arithmetic: 3.08 us -> none  [the longest x1 2.39 us: local(): src = src_spec.astype(jnp.float32) * src_mask[:, :, None, None]]
    slice x1 -> x0, local copies, waits for them, and re-layouts: 2.33 us -> none  [local(): sa, sb = (src[:, :, 0][None], src[:, :, 1][None])]
    mul x2 -> x0, local copies, waits for them, and re-layouts: 2.31 us -> none  [local(): real_part = jnp.sum(sa * ra + sb * rb, axis=2) * inverse[:, :, None]]
    another operation x2 -> x3, other arithmetic: 1.97 us -> 4.26 us  [the longest x1 2.29 us: lag_table(): return jnp.stack([cosines, sines], axis=0)]
  transfers between devices with their start and end apart: 1 -> 1, of which waited for: 1 -> 1; matrix products, arithmetic and copies ran while one was open for 11% -> 10% of each run, Pallas kernels for 0% -> 0%
where the time goes in v2:
time: 58.2 us; the launch traced here: 57.9 us
  between operations  13.4 us (23%)
  blocking collectives  11.9 us (20%)
  Pallas kernels  11.1 us (19%)
  other arithmetic  10.2 us (18%)
  waiting for transfers between devices  7.49 us (13%)
  local copies, waits for them, and re-layouts  3.84 us (7%)
    all_gather x1, blocking collectives, local(): rec_packed = lax.all_gather(packed, 'rcv', axis=0, tiled=True)  11.9 us
    pallas_call x1, Pallas kernels, correlate(): pl.pallas_call(kernel, grid=(nrec // group,), in_specs=[pl.BlockSpec((nre...  11.1 us
    all_gather x1, waiting for transfers between devices, local(): src_packed = lax.all_gather(packed, 'src', axis=0, tiled=True)  7.47 us
    unnamed x2, local copies, waits for them, and re-layouts  3.11 us
    another operation x1, other arithmetic, lag_table(): return jnp.stack([cosines, sines], axis=0)  2.29 us
    another operation x2, other arithmetic  1.97 us
    convert_element_type x1, other arithmetic, lag_table(): cosines = cosines.reshape(freq_count, lag_count).astype(jnp.bfloat16)  1.55 us
  transfers between devices with their start and end apart: 1, of which 1 were waited for; matrix products, arithmetic and copies ran while one was open for 10% of the time, Pallas kernels for 0%

profile of v2, /device:TPU:0, one launch (start us, length us, event | category | flops | bytes accessed | tf_op | source)
XLA Modules:
  0.0 57.9 jit_solution(8911937955784651479)
XLA Ops:
  6.5 0.0 all-gather.4.cloned.1.call-start
  6.5 0.6 %compare_reduce_fusion = pred[]{:T(512)} fusion(), kind=kLoop, calls=%fused_computation.32 | loop fusion | flops 5 | bytes 1 | tf_op jit(solution)/shard_map/reduce.1
  7.2 1.0 %convert_element_type.59 = f32[4,4,2,2048]{3,2,1,0:T(2,128)S(1)} convert(bf16[4,4,2,2048]{3,2,1,0:T(2,128)(2,1)} %param.4) | non-fusion elementwise | flops 65536 | bytes 393216 | tf_op jit(solution)/shard_map/convert_element_type | solution.py:20
  8.2 0.5 fusion.10
  8.7 0.2 add.69
  8.9 0.2 reduce_sum.9
  9.1 0.2 broadcast_in_dim.2
  9.3 0.3 mul.222
  9.6 1.0 %multiply_convert_fusion.2 = bf16[4,4,2,2048]{3,2,1,0:T(2,128)(2,1)S(1)} fusion(f32[4,4,2048]{2,1,0:T(4,128)S(1)} %mul.222, bf16[4,4,2,2048]{3,2,1,0:T(2,128)(2,1)} %param.4), kind=kLoop, calls=%fused_computation.5 | loop fusion | flops 196608 | bytes 393216 | tf_op jit(solution)/shard_map/convert_element_type | solution.py:25
  10.6 0.1 reshape.261
  10.7 1.3 %convert_select_fusion = bf16[4,4]{1,0:T(4,128)(2,1)S(1)} fusion(s32[4,4]{1,0:T(4,128)} %param.5, pred[]{:T(512)} %compare_reduce_fusion), kind=kLoop, calls=%fused_computation.33 | loop fusion | flops 32 | bytes 97 | tf_op jit(solution)/shard_map/select.1
  12.0 0.7 %fusion.2 = bf16[1,4,16512]{2,1,0:T(4,128)(2,1)} fusion(bf16[4,4]{1,0:T(4,128)(2,1)S(1)} %convert_select_fusion, bf16[4,16384]{1,0:T(4,128)(2,1)S(1)} %reshape.261), kind=kLoop, calls=%fused_computation.8 | loop fusion | flops 396288 | bytes 263200
  12.8 0.0 all-gather.4.cloned.1.call-update
  12.8 11.9 %all-gather = bf16[4,4,16512]{2,1,0:T(4,128)(2,1)S(1)} all-gather(bf16[1,4,16512]{2,1,0:T(4,128)(2,1)} %fusion.2), channel_id=1, replica_groups=mesh['src'=8,'rcv'=4] {'rcv'}, dimensions={0}, use_global_device_ids=true | all-gather | bytes 660480 | tf_op jit(solution)/shard_map/all_gather | solution.py:136
  24.7 0.9 %reshape.265.rec_ref = bf16[16,16512]{1,0:T(8,128)(2,1)} reshape(bf16[4,4,16512]{2,1,0:T(4,128)(2,1)S(1)} %all-gather) | data formatting | bytes 1056768
  25.6 0.4 fusion.17
  26.0 0.5 fusion.9
  26.5 1.5 %multiply_convert_fusion.1 = (bf16[32,64,512]{2,1,0:T(8,128)(2,1)S(1)}, bf16[32,64,512]{2,1,0:T(8,128)(2,1)S(1)}) fusion(f32[64,512]{1,0:T(8,128)S(1)} %get-tuple-element.22, f32[32,512]{1,0:T(8,128)S(1)} %get-tuple-element.20, f32[64,512]{1,0:T(8,128)S(1)} %get-tuple-element.21, f32[32,512]{1,0:T(8,128)S(1)} %get-tuple-element.19), kind=kLoop, calls=%fused_computation.2 | loop fusion | flops 10485760 | bytes 4587520 | tf_op jit(solution)/shard_map/convert_element_type | solution.py:41
  28.1 2.3 %pad_maximum_fusion = bf16[2,2048,512]{2,1,0:T(8,128)(2,1)} fusion(bf16[1,2048,512]{2,1,0:T(8,128)(2,1)S(1)} %bitcast.10, bf16[1,2048,512]{2,1,0:T(8,128)(2,1)S(1)} %bitcast.9), kind=kLoop, calls=%fused_computation | loop fusion | flops 2097152 | bytes 8388608 | tf_op jit(solution)/shard_map/stack | solution.py:43
  30.3 7.5 %all-gather.4.cloned.1.call-done = bf16[8,4,16512]{2,1,0:T(4,128)(2,1)} async-done(((bf16[1,4,16512]{2,1,0:T(4,128)(2,1)}), bf16[8,4,16512]{2,1,0:T(4,128)(2,1)}) %all-gather.4.cloned.1.call-update) | async-done | bytes 1056784 | tf_op jit(solution)/shard_map/all_gather | solution.py:137
  37.8 2.2 %reshape.267.src_ref = bf16[32,16512]{1,0:T(8,128)(2,1)} reshape(bf16[8,4,16512]{2,1,0:T(4,128)(2,1)} %all-gather.4.cloned.1.call-done) | data formatting | bytes 2113536
  40.0 11.1 %shard_map.28 = bf16[512,512]{1,0:T(8,128)(2,1)} custom-call(bf16[16,16512]{1,0:T(8,128)(2,1)} %reshape.265.rec_ref, bf16[32,16512]{1,0:T(8,128)(2,1)} %reshape.267.src_ref, bf16[4096,512]{1,0:T(8,128)(2,1)} %bitcast.8), custom_call_target="tpu_custom_call" | custom-call | tf_op jit(solution)/shard_map/pallas_call | solution.py:109
  (3 shorter events, 0.0 us)
Async XLA Ops:
  6.5 31.3 %all-gather.4.cloned.1.call-start = ((), (), s32[]{:S(2)}) async-start(), calls=%async_computation | async-start | bytes 1188864 | tf_op jit(solution)/shard_map/all_gather | solution.py:137
Sparse Core Ops, SparseCore 0:
  12.9 24.8 all-gather.3

commit v3 on v2

--- a/solution.py
+++ b/solution.py
@@ -127,20 +127,32 @@
     return out.reshape(nrec, nsrc, lags)
 
 
-def local(spectra, valid):
+def permute_gather(x, axis, count):
+    index = lax.axis_index(axis)
+    parts = [x]
+    for shift in range(1, count):
+        pairs = [(j, (j + shift) % count) for j in range(count)]
+        parts.append(lax.ppermute(x, axis, perm=pairs))
+    backward = jnp.stack(parts[::-1])
+    doubled = jnp.concatenate([backward, backward], axis=0)
+    ordered = lax.dynamic_slice_in_dim(doubled, count - 1 - index, count, axis=0)
+    return ordered.reshape((count * x.shape[0],) + x.shape[1:])
+
+
+def local(spectra, valid, rcv_count):
     channels, windows, _, freqs = spectra.shape
     table = lag_table(freqs, LAGS).reshape(2 * freqs, LAGS)
     mask_wire = valid.astype(jnp.bfloat16)
     whitened = whiten_spectra(spectra)
     packed = pack(whitened, mask_wire)
-    rec_packed = lax.all_gather(packed, "rcv", axis=0, tiled=True)
+    rec_packed = permute_gather(packed, "rcv", rcv_count)
     src_packed = lax.all_gather(packed, "src", axis=0, tiled=True)
     return correlate(rec_packed, src_packed, table, windows, freqs)
 
 
 def solution(mesh):
     return jax.shard_map(
-        local,
+        functools.partial(local, rcv_count=mesh.shape["rcv"]),
         mesh=mesh,
         in_specs=(P(("src", "rcv"), None, None, None), P(("src", "rcv"), None)),
         out_specs=P("src", "rcv", None),

time: 58.2 us -> 60.2 us (1.034)
  blocking collectives: 11.9 us -> 0 us
  waiting for transfers between devices: 7.49 us -> 17.1 us
  starting transfers between devices: 0.01 us -> 5.05 us
  other arithmetic: 10.2 us -> 8.84 us
    all_gather x1 -> x0, blocking collectives: 11.9 us -> none  [local(): rec_packed = lax.all_gather(packed, 'rcv', axis=0, tiled=True)]
    all_gather x1, waiting for transfers between devices: 7.47 us -> 15.9 us  [local(): src_packed = lax.all_gather(packed, 'src', axis=0, tiled=True)]
    ppermute x0 -> x3, starting transfers between devices: none -> 5.04 us  [permute_gather(): parts.append(lax.ppermute(x, axis, perm=pairs))]
    ppermute x0 -> x3, waiting for transfers between devices: none -> 1.15 us  [permute_gather(): parts.append(lax.ppermute(x, axis, perm=pairs))]
    reshape x0 -> x1, local copies, waits for them, and re-layouts: none -> 0.94 us  [permute_gather(): return ordered.reshape((count * x.shape[0],) + x.shape[1:])]
    convert_element_type x1, other arithmetic: 1.04 us -> 0.14 us  [whiten_spectra(): return (values * factor[:, :, None, :]).astype(jnp.bfloat16)]
    unnamed x1, other arithmetic: 0.72 us -> 0.09 us
    unnamed x2 -> x11, local copies, waits for them, and re-layouts: 3.11 us -> 2.56 us
  transfers between devices with their start and end apart: 1 -> 4, of which waited for: 1 -> 2; matrix products, arithmetic and copies ran while one was open for 10% -> 12% of each run, Pallas kernels for 0% -> 0%
where the time goes in v3:
time: 60.2 us; the launch traced here: 60 us
  waiting for transfers between devices  17.1 us (28%)
  between operations  13.5 us (22%)
  Pallas kernels  11.1 us (18%)
  other arithmetic  8.84 us (15%)
  starting transfers between devices  5.05 us (8%)
  local copies, waits for them, and re-layouts  4.41 us (7%)
    all_gather x1, waiting for transfers between devices, local(): src_packed = lax.all_gather(packed, 'src', axis=0, tiled=True)  15.9 us
    pallas_call x1, Pallas kernels, correlate(): pl.pallas_call(kernel, grid=(nrec // group,), in_specs=[pl.BlockSpec((nre...  11.1 us
    ppermute x3, starting transfers between devices, permute_gather(): parts.append(lax.ppermute(x, axis, perm=pairs))  5.04 us
    unnamed x11, local copies, waits for them, and re-layouts  2.56 us
    another operation x1, other arithmetic, lag_table(): return jnp.stack([cosines, sines], axis=0)  2.3 us
    convert_element_type x1, other arithmetic, lag_table(): cosines = cosines.reshape(freq_count, lag_count).astype(jnp.bfloat16)  1.55 us
    another operation x2, other arithmetic  1.29 us
  transfers between devices with their start and end apart: 4, of which 2 were waited for; matrix products, arithmetic and copies ran while one was open for 12% of the time, Pallas kernels for 0%

profile of v3, /device:TPU:0, one launch (start us, length us, event | category | flops | bytes accessed | tf_op | source)
XLA Modules:
  0.0 60.0 jit_solution(14426163843493565439)
XLA Ops:
  6.5 0.0 all-gather.3.cloned.1.call-start
  6.5 0.6 %compare_reduce_fusion = pred[]{:T(512)} fusion(), kind=kLoop, calls=%fused_computation.39 | loop fusion | flops 5 | bytes 1 | tf_op jit(solution)/shard_map/reduce.1
  7.2 1.0 %convert_element_type.59 = f32[4,4,2,2048]{3,2,1,0:T(2,128)S(1)} convert(bf16[4,4,2,2048]{3,2,1,0:T(2,128)(2,1)} %param.4) | non-fusion elementwise | flops 65536 | bytes 393216 | tf_op jit(solution)/shard_map/convert_element_type | solution.py:20
  8.2 0.5 fusion.9
  8.7 0.0 copy-start
  8.7 0.2 add.73
  8.9 0.2 reduce_sum.9
  9.1 0.0 copy-start.1
  9.1 0.2 broadcast_in_dim.2
  9.3 0.3 mul.222
  9.6 0.0 copy-done
  9.6 0.1 multiply_convert_fusion.2
  9.7 0.1 reshape.264
  9.8 0.0 copy-done.1
  9.8 0.7 %convert_select_fusion = bf16[4,4]{1,0:T(4,128)(2,1)S(1)} fusion(s32[4,4]{1,0:T(4,128)S(1)} %copy-done.1, pred[]{:T(512)} %compare_reduce_fusion), kind=kLoop, calls=%fused_computation.40 | loop fusion | flops 32 | bytes 97 | tf_op jit(solution)/shard_map/select.1
  10.5 0.1 fusion.1
  10.6 3.9 %collective-permute-start = (bf16[4,16512]{1,0:T(4,128)(2,1)S(1)}, bf16[4,16512]{1,0:T(4,128)(2,1)S(1)}, u32[]{:S(2)}, u32[]{:S(2)}) collective-permute-start(bf16[4,16512]{1,0:T(4,128)(2,1)S(1)} %fusion.1), channel_id=1, source_target_pairs={{0,3},{1,0},{2,1},{3,2},{4,7},{5,4},{6,5},{7,6},{8,11},{9,8},{10,9... | collective-permute-start | bytes 396296 | tf_op jit(solution)/shard_map/ppermute | solution.py:135
  14.5 0.5 collective-permute-start.1
  15.0 0.6 collective-permute-start.2
  15.6 0.7 %fusion.18 = bf16[1,4,16512]{2,1,0:T(4,128)(2,1)} fusion(bf16[4,4]{1,0:T(4,128)(2,1)S(1)} %convert_select_fusion, bf16[4,16384]{1,0:T(4,128)(2,1)S(1)} %reshape.264), kind=kLoop, calls=%fused_computation.43 | loop fusion | flops 396288 | bytes 263200 | tf_op jit(solution)/shard_map/stack | solution.py:136
  16.3 0.0 all-gather.3.cloned.1.call-update
  16.4 0.5 fusion.8
  16.9 0.3 fusion.16
  17.3 1.5 %multiply_convert_fusion.1 = (bf16[32,64,512]{2,1,0:T(8,128)(2,1)S(1)}, bf16[32,64,512]{2,1,0:T(8,128)(2,1)S(1)}) fusion(f32[64,512]{1,0:T(8,128)S(1)} %get-tuple-element.22, f32[32,512]{1,0:T(8,128)S(1)} %get-tuple-element.20, f32[64,512]{1,0:T(8,128)S(1)} %get-tuple-element.21, f32[32,512]{1,0:T(8,128)S(1)} %get-tuple-element.19), kind=kLoop, calls=%fused_computation.2 | loop fusion | flops 10485760 | bytes 4587520 | tf_op jit(solution)/shard_map/convert_element_type | solution.py:41
  18.8 2.3 %pad_maximum_fusion = bf16[2,2048,512]{2,1,0:T(8,128)(2,1)} fusion(bf16[1,2048,512]{2,1,0:T(8,128)(2,1)S(1)} %bitcast.21, bf16[1,2048,512]{2,1,0:T(8,128)(2,1)S(1)} %bitcast.20), kind=kLoop, calls=%fused_computation | loop fusion | flops 2097152 | bytes 8388608 | tf_op jit(solution)/shard_map/stack | solution.py:43
  21.1 0.0 collective-permute-done
  21.2 1.1 %collective-permute-done.1 = bf16[4,16512]{1,0:T(4,128)(2,1)S(1)} collective-permute-done((bf16[4,16512]{1,0:T(4,128)(2,1)S(1)}, bf16[4,16512]{1,0:T(4,128)(2,1)S(1)}, u32[]{:S(2)}, u32[]{:S(2)}) %collective-permute-start.1) | collective-permute-done | bytes 132128 | tf_op jit(solution)/shard_map/ppermute | solution.py:135
  22.3 0.1 bitcast_dynamic-update-slice_fusion.2
  22.4 0.0 collective-permute-done.2
  22.4 0.1 bitcast_dynamic-update-slice_fusion
  22.5 0.1 constant_dynamic-update-slice_fusion.1
  22.6 0.1 bitcast_dynamic-update-slice_fusion.5
  22.6 0.1 bitcast_dynamic-update-slice_fusion.3
  22.7 0.1 bitcast_dynamic-update-slice_fusion.1
  22.8 0.1 constant_dynamic-update-slice_fusion
  22.8 0.2 constant_dynamic-slice_fusion
  23.0 0.9 %reshape.265.rec_ref = bf16[16,16512]{1,0:T(8,128)(2,1)} reshape(bf16[4,4,16512]{2,1,0:T(4,128)(2,1)S(1)} %constant_dynamic-slice_fusion) | data formatting | bytes 1056768 | tf_op jit(solution)/shard_map/reshape | solution.py:139
  24.0 15.9 %all-gather.3.cloned.1.call-done = bf16[8,4,16512]{2,1,0:T(4,128)(2,1)} async-done(((bf16[1,4,16512]{2,1,0:T(4,128)(2,1)}), bf16[8,4,16512]{2,1,0:T(4,128)(2,1)}) %all-gather.3.cloned.1.call-update) | async-done | bytes 1056784 | tf_op jit(solution)/shard_map/all_gather | solution.py:149
  39.9 2.2 %reshape.269.src_ref = bf16[32,16512]{1,0:T(8,128)(2,1)} reshape(bf16[8,4,16512]{2,1,0:T(4,128)(2,1)} %all-gather.3.cloned.1.call-done) | data formatting | bytes 2113536
  42.1 11.1 %shard_map.28 = bf16[512,512]{1,0:T(8,128)(2,1)} custom-call(bf16[16,16512]{1,0:T(8,128)(2,1)} %reshape.265.rec_ref, bf16[32,16512]{1,0:T(8,128)(2,1)} %reshape.269.src_ref, bf16[4096,512]{1,0:T(8,128)(2,1)} %bitcast.19), custom_call_target="tpu_custom_call" | custom-call | tf_op jit(solution)/shard_map/pallas_call | solution.py:109
  (4 shorter events, 0.1 us)
Async XLA Ops:
  6.5 33.3 %all-gather.3.cloned.1.call-start = ((), (), s32[]{:S(2)}) async-start(), calls=%async_computation | async-start | bytes 1188864 | tf_op jit(solution)/shard_map/all_gather | solution.py:149
  8.7 0.9 %copy-start = (bf16[4,4,2,2048]{3,2,1,0:T(2,128)(2,1)S(1)}, bf16[4,4,2,2048]{3,2,1,0:T(2,128)(2,1)}, u32[]{:S(2)}) copy-start(bf16[4,4,2,2048]{3,2,1,0:T(2,128)(2,1)} %param.4) | copy-start | bytes 393220
  9.1 0.7 %copy-start.1 = (s32[4,4]{1,0:T(4,128)S(1)}, s32[4,4]{1,0:T(4,128)}, u32[]{:S(2)}) copy-start(s32[4,4]{1,0:T(4,128)} %param.5) | copy-start | bytes 196
  10.6 10.6 %collective-permute-start = (bf16[4,16512]{1,0:T(4,128)(2,1)S(1)}, bf16[4,16512]{1,0:T(4,128)(2,1)S(1)}, u32[]{:S(2)}, u32[]{:S(2)}) collective-permute-start(bf16[4,16512]{1,0:T(4,128)(2,1)S(1)} %fusion.1), channel_id=1, source_target_pairs={{0,3},{1,0},{2,1},{3,2},{4,7},{5,4},{6,5},{7,6},{8,11},{9,8},{10,9... | collective-permute-start | bytes 396296 | tf_op jit(solution)/shard_map/ppermute | solution.py:135
  14.5 7.8 %collective-permute-start.1 = (bf16[4,16512]{1,0:T(4,128)(2,1)S(1)}, bf16[4,16512]{1,0:T(4,128)(2,1)S(1)}, u32[]{:S(2)}, u32[]{:S(2)}) collective-permute-start(bf16[4,16512]{1,0:T(4,128)(2,1)S(1)} %fusion.1), channel_id=1, source_target_pairs={{0,2},{1,3},{2,0},{3,1},{4,6},{5,7},{6,4},{7,5},{8,10},{9,11},{10,... | collective-permute-start | bytes 396296 | tf_op jit(solution)/shard_map/ppermute | solution.py:135
  15.0 7.4 %collective-permute-start.2 = (bf16[4,16512]{1,0:T(4,128)(2,1)S(1)}, bf16[4,16512]{1,0:T(4,128)(2,1)S(1)}, u32[]{:S(2)}, u32[]{:S(2)}) collective-permute-start(bf16[4,16512]{1,0:T(4,128)(2,1)S(1)} %fusion.1), channel_id=1, source_target_pairs={{0,1},{1,2},{2,3},{3,0},{4,5},{5,6},{6,7},{7,4},{8,9},{9,10},{10,1... | collective-permute-start | bytes 396296 | tf_op jit(solution)/shard_map/ppermute | solution.py:135
Sparse Core Ops, SparseCore 0:
  16.5 23.3 all-gather.2

commit v4 on v3

--- a/solution.py
+++ b/solution.py
@@ -139,20 +139,36 @@
     return ordered.reshape((count * x.shape[0],) + x.shape[1:])
 
 
-def local(spectra, valid, rcv_count):
+def chip_gather(x, axis, count):
+    index = lax.axis_index(axis)
+    chips = count // 2
+    parts = [x]
+    for shift in range(1, chips):
+        pairs = [(j, (j + 2 * shift) % count) for j in range(count)]
+        parts.append(lax.ppermute(x, axis, perm=pairs))
+    backward = jnp.stack(parts[::-1])
+    doubled = jnp.concatenate([backward, backward], axis=0)
+    mine = lax.dynamic_slice_in_dim(doubled, chips - 1 - index // 2, chips, axis=0)
+    sibling = lax.ppermute(mine, axis, perm=[(j, j ^ 1) for j in range(count)])
+    low = index % 2 == 0
+    full = jnp.stack([jnp.where(low, mine, sibling), jnp.where(low, sibling, mine)], axis=1)
+    return full.reshape((count * x.shape[0],) + x.shape[1:])
+
+
+def local(spectra, valid, rcv_count, src_count):
     channels, windows, _, freqs = spectra.shape
     table = lag_table(freqs, LAGS).reshape(2 * freqs, LAGS)
     mask_wire = valid.astype(jnp.bfloat16)
     whitened = whiten_spectra(spectra)
     packed = pack(whitened, mask_wire)
     rec_packed = permute_gather(packed, "rcv", rcv_count)
-    src_packed = lax.all_gather(packed, "src", axis=0, tiled=True)
+    src_packed = chip_gather(packed, "src", src_count)
     return correlate(rec_packed, src_packed, table, windows, freqs)
 
 
 def solution(mesh):
     return jax.shard_map(
-        functools.partial(local, rcv_count=mesh.shape["rcv"]),
+        functools.partial(local, rcv_count=mesh.shape["rcv"], src_count=mesh.shape["src"]),
         mesh=mesh,
         in_specs=(P(("src", "rcv"), None, None, None), P(("src", "rcv"), None)),
         out_specs=P("src", "rcv", None),

time: 60.2 us -> 40 us (0.66)
  between operations: 13.5 us -> 0.21 us
  waiting for transfers between devices: 17.1 us -> 5.14 us
  starting transfers between devices: 5.05 us -> 10.1 us
    all_gather x1 -> x0, waiting for transfers between devices: 15.9 us -> none  [local(): src_packed = lax.all_gather(packed, 'src', axis=0, tiled=True)]
    ppermute x0 -> x4, starting transfers between devices: none -> 6.2 us  [the longest x3 6.13 us: chip_gather(): parts.append(lax.ppermute(x, axis, perm=pairs))]
    ppermute x3, waiting for transfers between devices: 1.15 us -> 4.39 us  [permute_gather(): parts.append(lax.ppermute(x, axis, perm=pairs))]
    unnamed x11 -> x15, local copies, waits for them, and re-layouts: 2.56 us -> 0.74 us
    ppermute x3, starting transfers between devices: 5.04 us -> 3.92 us  [permute_gather(): parts.append(lax.ppermute(x, axis, perm=pairs))]
    reshape x0 -> x1, local copies, waits for them, and re-layouts: none -> 1.11 us  [chip_gather(): return full.reshape((count * x.shape[0],) + x.shape[1:])]
    ppermute x0 -> x4, waiting for transfers between devices: none -> 0.75 us  [the longest x1 0.75 us: chip_gather(): sibling = lax.ppermute(mine, axis, perm=[(j, j ^ 1) for j in range(count)])]
    another operation x3 -> x4, other arithmetic: 2.01 us -> 2.48 us
  transfers between devices with their start and end apart: 4 -> 7, of which waited for: 2 -> 3; matrix products, arithmetic and copies ran while one was open for 12% -> 16% of each run, Pallas kernels for 0% -> 0%
where the time goes in v4:
time: 40 us; the launch traced here: 39.8 us
  Pallas kernels  11.1 us (28%)
  starting transfers between devices  10.1 us (25%)
  other arithmetic  9.36 us (23%)
  waiting for transfers between devices  5.14 us (13%)
  local copies, waits for them, and re-layouts  3.92 us (10%)
    pallas_call x1, Pallas kernels, correlate(): pl.pallas_call(kernel, grid=(nrec // group,), in_specs=[pl.BlockSpec((nre...  11.1 us
    ppermute x3, starting transfers between devices, chip_gather(): parts.append(lax.ppermute(x, axis, perm=pairs))  6.13 us
    ppermute x3, waiting for transfers between devices, permute_gather(): parts.append(lax.ppermute(x, axis, perm=pairs))  4.39 us
    ppermute x3, starting transfers between devices, permute_gather(): parts.append(lax.ppermute(x, axis, perm=pairs))  3.92 us
    another operation x1, other arithmetic, lag_table(): return jnp.stack([cosines, sines], axis=0)  2.3 us
    convert_element_type x1, other arithmetic, lag_table(): cosines = cosines.reshape(freq_count, lag_count).astype(jnp.bfloat16)  1.54 us
    another operation x2, other arithmetic  1.29 us
    another operation x2, other arithmetic, chip_gather(): jnp.stack([jnp.where(low, mine, sibling), jnp.where(low, sibling, mine)],...  1.19 us
  transfers between devices with their start and end apart: 7, of which 3 were waited for; matrix products, arithmetic and copies ran while one was open for 16% of the time, Pallas kernels for 0%

profile of v4, /device:TPU:0, one launch (start us, length us, event | category | flops | bytes accessed | tf_op | source)
XLA Modules:
  0.0 39.8 jit_solution(5246213417255209163)
XLA Ops:
  0.0 0.6 %compare_reduce_fusion = pred[]{:T(512)} fusion(), kind=kLoop, calls=%fused_computation.50 | loop fusion | flops 5 | bytes 1 | tf_op jit(solution)/shard_map/reduce.1
  0.6 1.0 %convert_element_type.59 = f32[4,4,2,2048]{3,2,1,0:T(2,128)S(1)} convert(bf16[4,4,2,2048]{3,2,1,0:T(2,128)(2,1)} %param.4) | non-fusion elementwise | flops 65536 | bytes 393216 | tf_op jit(solution)/shard_map/convert_element_type | solution.py:20
  1.7 0.5 %fusion.9 = f32[4,4,2048]{2,1,0:T(4,128)S(1)} fusion(f32[4,4,2,2048]{3,2,1,0:T(2,128)S(1)} %convert_element_type.59), kind=kLoop, calls=%fused_computation.37 | loop fusion | flops 98304 | bytes 393216 | tf_op jit(solution)/shard_map/add | solution.py:21
  2.1 0.0 copy-start
  2.1 0.2 add.82
  2.3 0.2 reduce_sum.9
  2.6 0.2 broadcast_in_dim.2
  2.8 0.3 mul.222
  3.1 0.1 multiply_convert_fusion.2
  3.2 0.1 reshape.267
  3.3 0.7 %convert_select_fusion = bf16[4,4]{1,0:T(4,128)(2,1)S(1)} fusion(s32[4,4]{1,0:T(4,128)S(1)} %copy-done.1, pred[]{:T(512)} %compare_reduce_fusion), kind=kLoop, calls=%fused_computation.51 | loop fusion | flops 32 | bytes 97 | tf_op jit(solution)/shard_map/select.1
  4.0 0.1 fusion.1
  4.0 4.1 %collective-permute-start.4 = (bf16[4,16512]{1,0:T(4,128)(2,1)S(1)}, bf16[4,16512]{1,0:T(4,128)(2,1)S(1)}, u32[]{:S(2)}, u32[]{:S(2)}) collective-permute-start(bf16[4,16512]{1,0:T(4,128)(2,1)S(1)} %fusion.1), channel_id=1, source_target_pairs={{0,16},{4,20},{8,24},{12,28},{16,0},{20,4},{24,8},{28,12},{1,17},{... | collective-permute-start | bytes 396296 | tf_op jit(solution)/shard_map/ppermute | solution.py:148
  8.1 1.3 %collective-permute-start.3 = (bf16[4,16512]{1,0:T(4,128)(2,1)S(1)}, bf16[4,16512]{1,0:T(4,128)(2,1)S(1)}, u32[]{:S(2)}, u32[]{:S(2)}) collective-permute-start(bf16[4,16512]{1,0:T(4,128)(2,1)S(1)} %fusion.1), channel_id=1, source_target_pairs={{0,24},{4,28},{8,0},{12,4},{16,8},{20,12},{24,16},{28,20},{1,25},{... | collective-permute-start | bytes 396296 | tf_op jit(solution)/shard_map/ppermute | solution.py:148
  9.5 0.7 %collective-permute-start.5 = (bf16[4,16512]{1,0:T(4,128)(2,1)S(1)}, bf16[4,16512]{1,0:T(4,128)(2,1)S(1)}, u32[]{:S(2)}, u32[]{:S(2)}) collective-permute-start(bf16[4,16512]{1,0:T(4,128)(2,1)S(1)} %fusion.1), channel_id=1, source_target_pairs={{0,8},{4,12},{8,16},{12,20},{16,24},{20,28},{24,0},{28,4},{1,9},{5... | collective-permute-start | bytes 396296 | tf_op jit(solution)/shard_map/ppermute | solution.py:148
  10.2 1.5 %collective-permute-start.2 = (bf16[4,16512]{1,0:T(4,128)(2,1)S(1)}, bf16[4,16512]{1,0:T(4,128)(2,1)S(1)}, u32[]{:S(2)}, u32[]{:S(2)}) collective-permute-start(bf16[4,16512]{1,0:T(4,128)(2,1)S(1)} %fusion.1), channel_id=1, source_target_pairs={{0,1},{1,2},{2,3},{3,0},{4,5},{5,6},{6,7},{7,4},{8,9},{9,10},{10,1... | collective-permute-start | bytes 396296 | tf_op jit(solution)/shard_map/ppermute | solution.py:135
  11.7 1.4 %collective-permute-start = (bf16[4,16512]{1,0:T(4,128)(2,1)S(1)}, bf16[4,16512]{1,0:T(4,128)(2,1)S(1)}, u32[]{:S(2)}, u32[]{:S(2)}) collective-permute-start(bf16[4,16512]{1,0:T(4,128)(2,1)S(1)} %fusion.1), channel_id=1, source_target_pairs={{0,3},{1,0},{2,1},{3,2},{4,7},{5,4},{6,5},{7,6},{8,11},{9,8},{10,9... | collective-permute-start | bytes 396296 | tf_op jit(solution)/shard_map/ppermute | solution.py:135
  13.1 0.5 %fusion.8 = (f32[64,512]{1,0:T(8,128)S(1)}, f32[64,512]{1,0:T(8,128)S(1)}) fusion(s32[512]{0:T(512)S(1)} %iota_add_fusion), kind=kLoop, calls=%fused_computation.36 | loop fusion | flops 294912 | bytes 264192 | tf_op jit(solution)/shard_map/cos | solution.py:37
  13.6 0.3 fusion.16
  14.0 1.5 %multiply_convert_fusion.1 = (bf16[32,64,512]{2,1,0:T(8,128)(2,1)S(1)}, bf16[32,64,512]{2,1,0:T(8,128)(2,1)S(1)}) fusion(f32[64,512]{1,0:T(8,128)S(1)} %get-tuple-element.28, f32[32,512]{1,0:T(8,128)S(1)} %get-tuple-element.26, f32[64,512]{1,0:T(8,128)S(1)} %get-tuple-element.27, f32[32,512]{1,0:T(8,128)S(1)} %get-tuple-element.25), kind=kLoop, calls=%fused_computation.2 | loop fusion | flops 10485760 | bytes 4587520 | tf_op jit(solution)/shard_map/convert_element_type | solution.py:41
  15.5 2.3 %pad_maximum_fusion = bf16[2,2048,512]{2,1,0:T(8,128)(2,1)} fusion(bf16[1,2048,512]{2,1,0:T(8,128)(2,1)S(1)} %bitcast.37, bf16[1,2048,512]{2,1,0:T(8,128)(2,1)S(1)} %bitcast.36), kind=kLoop, calls=%fused_computation | loop fusion | flops 2097152 | bytes 8388608 | tf_op jit(solution)/shard_map/stack | solution.py:43
  17.9 0.5 %collective-permute-done = bf16[4,16512]{1,0:T(4,128)(2,1)S(1)} collective-permute-done((bf16[4,16512]{1,0:T(4,128)(2,1)S(1)}, bf16[4,16512]{1,0:T(4,128)(2,1)S(1)}, u32[]{:S(2)}, u32[]{:S(2)}) %collective-permute-start) | collective-permute-done | bytes 132128 | tf_op jit(solution)/shard_map/ppermute | solution.py:135
  18.4 1.0 %collective-permute-start.1 = (bf16[4,16512]{1,0:T(4,128)(2,1)S(1)}, bf16[4,16512]{1,0:T(4,128)(2,1)S(1)}, u32[]{:S(2)}, u32[]{:S(2)}) collective-permute-start(bf16[4,16512]{1,0:T(4,128)(2,1)S(1)} %fusion.1), channel_id=1, source_target_pairs={{0,2},{1,3},{2,0},{3,1},{4,6},{5,7},{6,4},{7,5},{8,10},{9,11},{10,... | collective-permute-start | bytes 396296 | tf_op jit(solution)/shard_map/ppermute | solution.py:135
  19.4 0.0 collective-permute-done.3
  19.5 3.9 %collective-permute-done.1 = bf16[4,16512]{1,0:T(4,128)(2,1)S(1)} collective-permute-done((bf16[4,16512]{1,0:T(4,128)(2,1)S(1)}, bf16[4,16512]{1,0:T(4,128)(2,1)S(1)}, u32[]{:S(2)}, u32[]{:S(2)}) %collective-permute-start.1) | collective-permute-done | bytes 132128 | tf_op jit(solution)/shard_map/ppermute | solution.py:135
  23.4 0.1 bitcast_dynamic-update-slice_fusion.12
  23.4 0.0 collective-permute-done.2
  23.4 0.1 bitcast_dynamic-update-slice_fusion.10
  23.5 0.0 collective-permute-done.4
  23.5 0.1 bitcast_dynamic-update-slice_fusion.2
  23.6 0.0 collective-permute-done.5
  23.6 0.1 bitcast_dynamic-update-slice_fusion
  23.6 0.1 bitcast_dynamic-update-slice_fusion.7
  23.8 0.1 bitcast_dynamic-update-slice_fusion.5
  23.9 0.1 bitcast_dynamic-update-slice_fusion.3
  23.9 0.1 bitcast_dynamic-update-slice_fusion.1
  24.0 0.1 bitcast_dynamic-update-slice_fusion.13
  24.1 0.1 bitcast_dynamic-update-slice_fusion.11
  24.1 0.1 bitcast_dynamic-update-slice_fusion.8
  24.3 0.2 constant_dynamic-slice_fusion
  24.5 0.1 collective-permute-start.6
  24.5 0.2 constant_dynamic-slice_fusion.1
  24.7 1.0 %reshape.268.rec_ref = bf16[16,16512]{1,0:T(8,128)(2,1)} reshape(bf16[4,4,16512]{2,1,0:T(4,128)(2,1)S(1)} %constant_dynamic-slice_fusion.1) | data formatting | bytes 1056768 | tf_op jit(solution)/shard_map/reshape | solution.py:139
  25.7 0.7 %collective-permute-done.6 = bf16[4,4,16512]{2,1,0:T(4,128)(2,1)S(1)} collective-permute-done((bf16[4,4,16512]{2,1,0:T(4,128)(2,1)S(1)}, bf16[4,4,16512]{2,1,0:T(4,128)(2,1)S(1)}, u32[]{:S(2)}, u32[]{:S(2)}) %collective-permute-start.6) | collective-permute-done | bytes 528416 | tf_op jit(solution)/shard_map/ppermute | solution.py:152
  26.4 0.4 %select_bitcast_fusion.1 = (bf16[4,1,4,16512]{3,2,1,0:T(4,128)(2,1)S(1)}, bf16[4,1,4,16512]{3,2,1,0:T(4,128)(2,1)S(1)}) fusion(bf16[4,4,16512]{2,1,0:T(4,128)(2,1)S(1)} %collective-permute-done.6, pred[]{:T(512)S(6)} %eq.9, bf16[8,4,16512]{2,1,0:T(4,128)(2,1)S(1)} %get-tuple-element.21, s32[]{:T(128)S(6)} %select_n.63), kind=kLoop, calls=%fused_computation.5 | loop fusion | flops 528384 | bytes 2113541 | tf_op jit(solution)/shard_map/stack | solution.py:154
  26.9 0.7 %pad_maximum_fusion.1 = bf16[4,2,4,16512]{3,2,1,0:T(4,128)(2,1)S(1)} fusion(bf16[4,1,4,16512]{3,2,1,0:T(4,128)(2,1)S(1)} %get-tuple-element.18, bf16[4,1,4,16512]{3,2,1,0:T(4,128)(2,1)S(1)} %get-tuple-element.17), kind=kLoop, calls=%fused_computation.3 | loop fusion | flops 528384 | bytes 2113536 | tf_op jit(solution)/shard_map/stack | solution.py:154
  27.6 1.1 %reshape.269.src_ref = bf16[32,16512]{1,0:T(8,128)(2,1)} reshape(bf16[4,2,4,16512]{3,2,1,0:T(4,128)(2,1)S(1)} %pad_maximum_fusion.1) | data formatting | bytes 2113536 | tf_op jit(solution)/shard_map/reshape | solution.py:155
  28.7 11.1 %shard_map.28 = bf16[512,512]{1,0:T(8,128)(2,1)} custom-call(bf16[16,16512]{1,0:T(8,128)(2,1)} %reshape.268.rec_ref, bf16[32,16512]{1,0:T(8,128)(2,1)} %reshape.269.src_ref, bf16[4096,512]{1,0:T(8,128)(2,1)} %bitcast.35), custom_call_target="tpu_custom_call" | custom-call | tf_op jit(solution)/shard_map/pallas_call | solution.py:109
  (8 shorter events, 0.1 us)
Async XLA Ops:
  2.1 0.9 %copy-start = (bf16[4,4,2,2048]{3,2,1,0:T(2,128)(2,1)S(1)}, bf16[4,4,2,2048]{3,2,1,0:T(2,128)(2,1)}, u32[]{:S(2)}) copy-start(bf16[4,4,2,2048]{3,2,1,0:T(2,128)(2,1)} %param.4) | copy-start | bytes 393220
  2.6 0.7 %copy-start.1 = (s32[4,4]{1,0:T(4,128)S(1)}, s32[4,4]{1,0:T(4,128)}, u32[]{:S(2)}) copy-start(s32[4,4]{1,0:T(4,128)} %param.5) | copy-start | bytes 196
  4.0 19.5 %collective-permute-start.4 = (bf16[4,16512]{1,0:T(4,128)(2,1)S(1)}, bf16[4,16512]{1,0:T(4,128)(2,1)S(1)}, u32[]{:S(2)}, u32[]{:S(2)}) collective-permute-start(bf16[4,16512]{1,0:T(4,128)(2,1)S(1)} %fusion.1), channel_id=1, source_target_pairs={{0,16},{4,20},{8,24},{12,28},{16,0},{20,4},{24,8},{28,12},{1,17},{... | collective-permute-start | bytes 396296 | tf_op jit(solution)/shard_map/ppermute | solution.py:148
  8.1 11.3 %collective-permute-start.3 = (bf16[4,16512]{1,0:T(4,128)(2,1)S(1)}, bf16[4,16512]{1,0:T(4,128)(2,1)S(1)}, u32[]{:S(2)}, u32[]{:S(2)}) collective-permute-start(bf16[4,16512]{1,0:T(4,128)(2,1)S(1)} %fusion.1), channel_id=1, source_target_pairs={{0,24},{4,28},{8,0},{12,4},{16,8},{20,12},{24,16},{28,20},{1,25},{... | collective-permute-start | bytes 396296 | tf_op jit(solution)/shard_map/ppermute | solution.py:148
  9.5 14.1 %collective-permute-start.5 = (bf16[4,16512]{1,0:T(4,128)(2,1)S(1)}, bf16[4,16512]{1,0:T(4,128)(2,1)S(1)}, u32[]{:S(2)}, u32[]{:S(2)}) collective-permute-start(bf16[4,16512]{1,0:T(4,128)(2,1)S(1)} %fusion.1), channel_id=1, source_target_pairs={{0,8},{4,12},{8,16},{12,20},{16,24},{20,28},{24,0},{28,4},{1,9},{5... | collective-permute-start | bytes 396296 | tf_op jit(solution)/shard_map/ppermute | solution.py:148
  10.2 13.3 %collective-permute-start.2 = (bf16[4,16512]{1,0:T(4,128)(2,1)S(1)}, bf16[4,16512]{1,0:T(4,128)(2,1)S(1)}, u32[]{:S(2)}, u32[]{:S(2)}) collective-permute-start(bf16[4,16512]{1,0:T(4,128)(2,1)S(1)} %fusion.1), channel_id=1, source_target_pairs={{0,1},{1,2},{2,3},{3,0},{4,5},{5,6},{6,7},{7,4},{8,9},{9,10},{10,1... | collective-permute-start | bytes 396296 | tf_op jit(solution)/shard_map/ppermute | solution.py:135
  11.7 6.7 %collective-permute-start = (bf16[4,16512]{1,0:T(4,128)(2,1)S(1)}, bf16[4,16512]{1,0:T(4,128)(2,1)S(1)}, u32[]{:S(2)}, u32[]{:S(2)}) collective-permute-start(bf16[4,16512]{1,0:T(4,128)(2,1)S(1)} %fusion.1), channel_id=1, source_target_pairs={{0,3},{1,0},{2,1},{3,2},{4,7},{5,4},{6,5},{7,6},{8,11},{9,8},{10,9... | collective-permute-start | bytes 396296 | tf_op jit(solution)/shard_map/ppermute | solution.py:135
  18.4 5.0 %collective-permute-start.1 = (bf16[4,16512]{1,0:T(4,128)(2,1)S(1)}, bf16[4,16512]{1,0:T(4,128)(2,1)S(1)}, u32[]{:S(2)}, u32[]{:S(2)}) collective-permute-start(bf16[4,16512]{1,0:T(4,128)(2,1)S(1)} %fusion.1), channel_id=1, source_target_pairs={{0,2},{1,3},{2,0},{3,1},{4,6},{5,7},{6,4},{7,5},{8,10},{9,11},{10,... | collective-permute-start | bytes 396296 | tf_op jit(solution)/shard_map/ppermute | solution.py:135
  24.5 2.0 %collective-permute-start.6 = (bf16[4,4,16512]{2,1,0:T(4,128)(2,1)S(1)}, bf16[4,4,16512]{2,1,0:T(4,128)(2,1)S(1)}, u32[]{:S(2)}, u32[]{:S(2)}) collective-permute-start(bf16[4,4,16512]{2,1,0:T(4,128)(2,1)S(1)} %constant_dynamic-slice_fusion), channel_id=1, source_target_pairs={{0,4},{4,0},{8,12},{12,8},{16,20},{20,16},{24,28},{28,24},{1,5},{5... | collective-permute-start | bytes 1585160 | tf_op jit(solution)/shard_map/ppermute | solution.py:152

commit v5 on v2

--- a/solution.py
+++ b/solution.py
@@ -46,27 +46,45 @@
 def pack(whitened, mask):
     channels = whitened.shape[0]
     flat = whitened.reshape(channels, -1)
-    tail = jnp.zeros((channels, PAD), jnp.bfloat16).at[:, : mask.shape[1]].set(mask)
+    tail = jnp.pad(mask, ((0, 0), (0, PAD - mask.shape[1])))
     return jnp.concatenate([flat, tail], axis=1)
 
 
-def cross_kernel(rec_ref, src_ref, tab_ref, out_ref, srcf, recf, rtails, cross, *, windows, freqs, group, chunk):
+def cross_kernel(
+    place_ref, rec_ref, own_ref, sib_ref, tab_ref, out_ref, srcf, recf, rtails, stails, cross,
+    *, windows, freqs, group, chunk
+):
     step = pl.program_id(0)
-    nsrc = src_ref.shape[0]
+    rcv_count, per = rec_ref.shape[0], rec_ref.shape[1]
+    chips = own_ref.shape[0]
+    nsrc = 2 * chips * per
     body = windows * 2 * freqs
     width = 2 * freqs
 
+    def place(block, dst, values, tails):
+        rows = slice(dst * per, (dst + 1) * per)
+        mask = block[:, body : body + PAD].astype(jnp.float32)
+        tails[rows, :] = mask
+        for w in range(windows):
+            cols = slice(w * width, (w + 1) * width)
+            values[rows, cols] = block[:, cols].astype(jnp.float32) * mask[:, w : w + 1]
+
     @pl.when(step == 0)
     def _():
-        smask = src_ref[:, body : body + PAD].astype(jnp.float32)
-        rmask = rec_ref[:, body : body + PAD].astype(jnp.float32)
-        rtails[...] = rmask
-        for w in range(windows):
-            cols = slice(w * width, (w + 1) * width)
-            srcf[:, cols] = src_ref[:, cols].astype(jnp.float32) * smask[:, w : w + 1]
-            recf[:, cols] = rec_ref[:, cols].astype(jnp.float32) * rmask[:, w : w + 1]
+        rcv_index, chip, core = place_ref[0], place_ref[1], place_ref[2]
+        for dst in range(rcv_count):
+            k = (rcv_index - dst + rcv_count) % rcv_count
+            place(rec_ref[k], dst, recf, rtails)
+        for zz in range(chips):
+            k = (chip - zz + chips) % chips
+            own_block = own_ref[k]
+            sib_block = sib_ref[k]
+            for cc in range(2):
+                same = core == cc
+                block = jnp.where(same, own_block, sib_block)
+                place(block, zz * 2 + cc, srcf, stails)
 
-    smask = src_ref[:, body : body + PAD].astype(jnp.float32)
+    smask = stails[...]
 
     def per_receiver(j, carry):
         i = step * group + j
@@ -98,49 +116,70 @@
     ).astype(jnp.bfloat16)
 
 
-def correlate(rec_packed, src_packed, table, windows, freqs):
-    nrec, width = rec_packed.shape
-    nsrc = src_packed.shape[0]
+def correlate(place, rec_stack, own_stack, sib_stack, table, windows, freqs):
+    rcv_count, per, width = rec_stack.shape
+    chips = own_stack.shape[0]
+    nrec = rcv_count * per
+    nsrc = 2 * chips * per
     lags = table.shape[1]
     group = 8
     kernel = functools.partial(
         cross_kernel, windows=windows, freqs=freqs, group=group, chunk=256
     )
+    full3 = lambda g, p: (0, 0, 0)
     out = pl.pallas_call(
         kernel,
-        grid=(nrec // group,),
-        in_specs=[
-            pl.BlockSpec((nrec, width), lambda g: (0, 0)),
-            pl.BlockSpec((nsrc, width), lambda g: (0, 0)),
-            pl.BlockSpec(table.shape, lambda g: (0, 0)),
-        ],
-        out_specs=pl.BlockSpec((group * nsrc, lags), lambda g: (g, 0)),
+        grid_spec=pltpu.PrefetchScalarGridSpec(
+            num_scalar_prefetch=1,
+            grid=(nrec // group,),
+            in_specs=[
+                pl.BlockSpec(rec_stack.shape, full3),
+                pl.BlockSpec(own_stack.shape, full3),
+                pl.BlockSpec(sib_stack.shape, full3),
+                pl.BlockSpec(table.shape, lambda g, p: (0, 0)),
+            ],
+            out_specs=pl.BlockSpec((group * nsrc, lags), lambda g, p: (g, 0)),
+            scratch_shapes=[
+                pltpu.VMEM((nsrc, windows * 2 * freqs), jnp.float32),
+                pltpu.VMEM((nrec, windows * 2 * freqs), jnp.float32),
+                pltpu.VMEM((nrec, PAD), jnp.float32),
+                pltpu.VMEM((nsrc, PAD), jnp.float32),
+                pltpu.VMEM((group * nsrc, 2 * freqs), jnp.bfloat16),
+            ],
+        ),
         out_shape=jax.ShapeDtypeStruct((nrec * nsrc, lags), jnp.bfloat16),
-        scratch_shapes=[
-            pltpu.VMEM((nsrc, windows * 2 * freqs), jnp.float32),
-            pltpu.VMEM((nrec, windows * 2 * freqs), jnp.float32),
-            pltpu.VMEM((nrec, PAD), jnp.float32),
-            pltpu.VMEM((group * nsrc, 2 * freqs), jnp.bfloat16),
-        ],
         compiler_params=pltpu.CompilerParams(dimension_semantics=("arbitrary",)),
-    )(rec_packed, src_packed, table)
+    )(place, rec_stack, own_stack, sib_stack, table)
     return out.reshape(nrec, nsrc, lags)
 
 
-def local(spectra, valid):
+def shifted(x, axis, count, stride):
+    parts = [x]
+    for shift in range(1, count // stride):
+        pairs = [(j, (j + stride * shift) % count) for j in range(count)]
+        parts.append(lax.ppermute(x, axis, perm=pairs))
+    return jnp.stack(parts)
+
+
+def local(spectra, valid, rcv_count, src_count):
     channels, windows, _, freqs = spectra.shape
     table = lag_table(freqs, LAGS).reshape(2 * freqs, LAGS)
     mask_wire = valid.astype(jnp.bfloat16)
     whitened = whiten_spectra(spectra)
     packed = pack(whitened, mask_wire)
-    rec_packed = lax.all_gather(packed, "rcv", axis=0, tiled=True)
-    src_packed = lax.all_gather(packed, "src", axis=0, tiled=True)
-    return correlate(rec_packed, src_packed, table, windows, freqs)
+    rec_stack = shifted(packed, "rcv", rcv_count, 1)
+    own_stack = shifted(packed, "src", src_count, 2)
+    sib_stack = lax.ppermute(own_stack, "src", perm=[(j, j ^ 1) for j in range(src_count)])
+    src_index = lax.axis_index("src")
+    place = jnp.stack(
+        [lax.axis_index("rcv"), src_index // 2, src_index % 2]
+    ).astype(jnp.int32)
+    return correlate(place, rec_stack, own_stack, sib_stack, table, windows, freqs)
 
 
 def solution(mesh):
     return jax.shard_map(
-        local,
+        functools.partial(local, rcv_count=mesh.shape["rcv"], src_count=mesh.shape["src"]),
         mesh=mesh,
         in_specs=(P(("src", "rcv"), None, None, None), P(("src", "rcv"), None)),
         out_specs=P("src", "rcv", None),

time: 58.2 us -> 44.9 us (0.77)
  between operations: 13.4 us -> 0.1 us
  blocking collectives: 11.9 us -> 0 us
  starting transfers between devices: 0.01 us -> 10 us
  other arithmetic: 10.2 us -> 13.6 us
  local copies, waits for them, and re-layouts: 3.84 us -> 1.55 us
  Pallas kernels: 11.1 us -> 12.1 us
    all_gather x1 -> x0, blocking collectives: 11.9 us -> none  [local(): rec_packed = lax.all_gather(packed, 'rcv', axis=0, tiled=True)]
    ppermute x0 -> x7, starting transfers between devices: none -> 10 us  [the longest x6 10 us: shifted(): parts.append(lax.ppermute(x, axis, perm=pairs))]
    all_gather x1 -> x0, waiting for transfers between devices: 7.47 us -> none  [local(): src_packed = lax.all_gather(packed, 'src', axis=0, tiled=True)]
    ppermute x0 -> x7, waiting for transfers between devices: none -> 7.24 us  [the longest x6 7.24 us: shifted(): parts.append(lax.ppermute(x, axis, perm=pairs))]
    unnamed x2 -> x4, local copies, waits for them, and re-layouts: 3.11 us -> 0.82 us
    another operation x1, other arithmetic: 2.29 us -> 3.91 us  [lag_table(): return jnp.stack([cosines, sines], axis=0)]
    convert_element_type x1, other arithmetic: 1.55 us -> 2.82 us  [lag_table(): cosines = cosines.reshape(freq_count, lag_count).astype(jnp.bfloat16)]
    pallas_call x1, Pallas kernels: 11.1 us -> 12.1 us  [correlate(): pl.pallas_call(kernel, grid_spec=pltpu.PrefetchScalarGridSpec(num_scalar_...]
  transfers between devices with their start and end apart: 1 -> 7, of which waited for: 1 -> 3; matrix products, arithmetic and copies ran while one was open for 10% -> 19% of each run, Pallas kernels for 0% -> 0%
where the time goes in v5:
time: 44.9 us; the launch traced here: 44.6 us
  other arithmetic  13.6 us (30%)
  Pallas kernels  12.1 us (27%)
  starting transfers between devices  10 us (22%)
  waiting for transfers between devices  7.24 us (16%)
  local copies, waits for them, and re-layouts  1.55 us (3%)
    pallas_call x1, Pallas kernels, correlate(): pl.pallas_call(kernel, grid_spec=pltpu.PrefetchScalarGridSpec(num_scalar_...  12.1 us
    ppermute x6, starting transfers between devices, shifted(): parts.append(lax.ppermute(x, axis, perm=pairs))  10 us
    ppermute x6, waiting for transfers between devices, shifted(): parts.append(lax.ppermute(x, axis, perm=pairs))  7.24 us
    another operation x1, other arithmetic, lag_table(): return jnp.stack([cosines, sines], axis=0)  3.91 us
    convert_element_type x1, other arithmetic, lag_table(): cosines = cosines.reshape(freq_count, lag_count).astype(jnp.bfloat16)  2.82 us
    another operation x2, other arithmetic, shifted(): return jnp.stack(parts)  1.78 us
    convert_element_type x1, other arithmetic, whiten_spectra(): return (values * factor[:, :, None, :]).astype(jnp.bfloat16)  1.04 us
    convert_element_type x1, other arithmetic, whiten_spectra(): values = spectra.astype(jnp.float32)  1.02 us
  transfers between devices with their start and end apart: 7, of which 3 were waited for; matrix products, arithmetic and copies ran while one was open for 19% of the time, Pallas kernels for 0%

profile of v5, /device:TPU:0, one launch (start us, length us, event | category | flops | bytes accessed | tf_op | source)
XLA Modules:
  0.0 44.6 jit_solution(13579633867644881709)
XLA Ops:
  0.0 0.7 %convert_element_type.63 = bf16[4,4]{1,0:T(4,128)(2,1)S(1)} convert(s32[4,4]{1,0:T(4,128)} %param.3) | non-fusion elementwise | flops 16 | bytes 96 | tf_op jit(solution)/shard_map/convert_element_type | solution.py:167
  0.7 1.0 %convert_element_type.61 = f32[4,4,2,2048]{3,2,1,0:T(2,128)S(1)} convert(bf16[4,4,2,2048]{3,2,1,0:T(2,128)(2,1)} %param.2) | non-fusion elementwise | flops 65536 | bytes 393216 | tf_op jit(solution)/shard_map/convert_element_type | solution.py:20
  1.7 0.5 %fusion.13 = f32[4,4,2048]{2,1,0:T(4,128)S(1)} fusion(f32[4,4,2,2048]{3,2,1,0:T(2,128)S(1)} %convert_element_type.61), kind=kLoop, calls=%fused_computation.24 | loop fusion | flops 98304 | bytes 393216 | tf_op jit(solution)/shard_map/add | solution.py:21
  2.2 0.2 add.73
  2.4 0.2 reduce_sum.9
  2.6 0.2 broadcast_in_dim.2
  2.8 0.3 mul.222
  3.1 1.0 %multiply_convert_fusion.2 = bf16[4,4,2,2048]{3,2,1,0:T(2,128)(2,1)S(1)} fusion(f32[4,4,2048]{2,1,0:T(4,128)S(1)} %mul.222, bf16[4,4,2,2048]{3,2,1,0:T(2,128)(2,1)} %param.2), kind=kLoop, calls=%fused_computation.11 | loop fusion | flops 196608 | bytes 393216 | tf_op jit(solution)/shard_map/convert_element_type | solution.py:25
  4.1 0.1 reshape.235
  4.2 0.1 fusion.5
  4.3 4.1 %collective-permute-start.4 = (bf16[4,16512]{1,0:T(4,128)(2,1)S(1)}, bf16[4,16512]{1,0:T(4,128)(2,1)S(1)}, u32[]{:S(2)}, u32[]{:S(2)}) collective-permute-start(bf16[4,16512]{1,0:T(4,128)(2,1)S(1)} %fusion.5), channel_id=1, source_target_pairs={{0,16},{4,20},{8,24},{12,28},{16,0},{20,4},{24,8},{28,12},{1,17},{... | collective-permute-start | bytes 396296 | tf_op jit(solution)/shard_map/ppermute | solution.py:160
  8.4 1.6 %collective-permute-start.3 = (bf16[4,16512]{1,0:T(4,128)(2,1)S(1)}, bf16[4,16512]{1,0:T(4,128)(2,1)S(1)}, u32[]{:S(2)}, u32[]{:S(2)}) collective-permute-start(bf16[4,16512]{1,0:T(4,128)(2,1)S(1)} %fusion.5), channel_id=1, source_target_pairs={{0,8},{4,12},{8,16},{12,20},{16,24},{20,28},{24,0},{28,4},{1,9},{5... | collective-permute-start | bytes 396296 | tf_op jit(solution)/shard_map/ppermute | solution.py:160
  10.0 2.4 %collective-permute-start.2 = (bf16[4,16512]{1,0:T(4,128)(2,1)S(1)}, bf16[4,16512]{1,0:T(4,128)(2,1)S(1)}, u32[]{:S(2)}, u32[]{:S(2)}) collective-permute-start(bf16[4,16512]{1,0:T(4,128)(2,1)S(1)} %fusion.5), channel_id=1, source_target_pairs={{0,3},{1,0},{2,1},{3,2},{4,7},{5,4},{6,5},{7,6},{8,11},{9,8},{10,9... | collective-permute-start | bytes 396296 | tf_op jit(solution)/shard_map/ppermute | solution.py:160
  12.4 0.5 %collective-permute-start.1 = (bf16[4,16512]{1,0:T(4,128)(2,1)S(1)}, bf16[4,16512]{1,0:T(4,128)(2,1)S(1)}, u32[]{:S(2)}, u32[]{:S(2)}) collective-permute-start(bf16[4,16512]{1,0:T(4,128)(2,1)S(1)} %fusion.5), channel_id=1, source_target_pairs={{0,2},{1,3},{2,0},{3,1},{4,6},{5,7},{6,4},{7,5},{8,10},{9,11},{10,... | collective-permute-start | bytes 396296 | tf_op jit(solution)/shard_map/ppermute | solution.py:160
  12.9 0.6 %collective-permute-start = (bf16[4,16512]{1,0:T(4,128)(2,1)S(1)}, bf16[4,16512]{1,0:T(4,128)(2,1)S(1)}, u32[]{:S(2)}, u32[]{:S(2)}) collective-permute-start(bf16[4,16512]{1,0:T(4,128)(2,1)S(1)} %fusion.5), channel_id=1, source_target_pairs={{0,1},{1,2},{2,3},{3,0},{4,5},{5,6},{6,7},{7,4},{8,9},{9,10},{10,1... | collective-permute-start | bytes 396296 | tf_op jit(solution)/shard_map/ppermute | solution.py:160
  13.5 0.1 fusion.22
  13.6 0.5 %fusion.12 = (f32[64,512]{1,0:T(8,128)S(1)}, f32[64,512]{1,0:T(8,128)S(1)}) fusion(s32[512]{0:T(512)S(1)} %iota_add_fusion), kind=kLoop, calls=%fused_computation.23 | loop fusion | flops 294912 | bytes 264192 | tf_op jit(solution)/shard_map/cos | solution.py:37
  14.1 3.4 %collective-permute-done.4 = bf16[4,16512]{1,0:T(4,128)(2,1)S(1)} collective-permute-done((bf16[4,16512]{1,0:T(4,128)(2,1)S(1)}, bf16[4,16512]{1,0:T(4,128)(2,1)S(1)}, u32[]{:S(2)}, u32[]{:S(2)}) %collective-permute-start.4) | collective-permute-done | bytes 132128 | tf_op jit(solution)/shard_map/ppermute | solution.py:160
  17.6 0.8 %collective-permute-start.5 = (bf16[4,16512]{1,0:T(4,128)(2,1)S(1)}, bf16[4,16512]{1,0:T(4,128)(2,1)S(1)}, u32[]{:S(2)}, u32[]{:S(2)}) collective-permute-start(bf16[4,16512]{1,0:T(4,128)(2,1)S(1)} %fusion.5), channel_id=1, source_target_pairs={{0,24},{4,28},{8,0},{12,4},{16,8},{20,12},{24,16},{28,20},{1,25},{... | collective-permute-start | bytes 396296 | tf_op jit(solution)/shard_map/ppermute | solution.py:160
  18.4 0.3 fusion.20
  18.7 0.0 collective-permute-done.3
  18.7 0.0 collective-permute-done.2
  18.7 1.0 %collective-permute-done.1 = bf16[4,16512]{1,0:T(4,128)(2,1)S(1)} collective-permute-done((bf16[4,16512]{1,0:T(4,128)(2,1)S(1)}, bf16[4,16512]{1,0:T(4,128)(2,1)S(1)}, u32[]{:S(2)}, u32[]{:S(2)}) %collective-permute-start.1) | collective-permute-done | bytes 132128 | tf_op jit(solution)/shard_map/ppermute | solution.py:160
  19.8 0.0 collective-permute-done
  19.8 2.8 %collective-permute-done.5 = bf16[4,16512]{1,0:T(4,128)(2,1)S(1)} collective-permute-done((bf16[4,16512]{1,0:T(4,128)(2,1)S(1)}, bf16[4,16512]{1,0:T(4,128)(2,1)S(1)}, u32[]{:S(2)}, u32[]{:S(2)}) %collective-permute-start.5) | collective-permute-done | bytes 132128 | tf_op jit(solution)/shard_map/ppermute | solution.py:160
  22.6 1.7 %fusion.3 = (bf16[4,4,16512]{2,1,0:T(4,128)(2,1)S(1)}, bf16[4,4,16512]{2,1,0:T(4,128)(2,1)}) fusion(bf16[1,4,16512]{2,1,0:T(4,128)(2,1)S(1)} %fusion.22, bf16[1,4,16512]{2,1,0:T(4,128)(2,1)S(1)} %bitcast.25, bf16[1,4,16512]{2,1,0:T(4,128)(2,1)S(1)} %bitcast.20, bf16[1,4,16512]{2,1,0:T(4,128)(2,1)S(1)} %bitcast.21, bf16[1,4,16512]{2,1,0:T(4,128)(2,1)S(1)} %bitcast.22, ...), kind=kLoop, calls=%fused_computation.8 | loop fusion | flops 1585152 | bytes 1981440 | tf_op jit(solution)/shard_map/stack | solution.py:161
  24.3 0.0 copy-start
  24.3 0.0 collective-permute-start.6
  24.3 2.8 %multiply_convert_fusion.1 = (bf16[32,64,512]{2,1,0:T(8,128)(2,1)S(1)}, bf16[32,64,512]{2,1,0:T(8,128)(2,1)}) fusion(f32[64,512]{1,0:T(8,128)S(1)} %get-tuple-element.12, f32[32,512]{1,0:T(8,128)S(1)} %get-tuple-element.10, f32[64,512]{1,0:T(8,128)S(1)} %get-tuple-element.11, f32[32,512]{1,0:T(8,128)S(1)} %get-tuple-element.9), kind=kLoop, calls=%fused_computation.2 | loop fusion | flops 10485760 | bytes 4587520 | tf_op jit(solution)/shard_map/convert_element_type | solution.py:41
  27.1 0.7 %pad_add_fusion.place_ref = s32[3]{0:T(128)} fusion(s32[1]{0:T(128)} %bitcast.2, s32[1]{0:T(128)} %bitcast.1, s32[1]{0:T(128)} %bitcast), kind=kLoop, calls=%fused_computation.37 | loop fusion | flops 6 | bytes 24 | tf_op jit(solution)/shard_map/stack | solution.py:174
  27.8 3.9 %pad_maximum_fusion = bf16[2,2048,512]{2,1,0:T(8,128)(2,1)} fusion(bf16[1,2048,512]{2,1,0:T(8,128)(2,1)} %bitcast.19, bf16[1,2048,512]{2,1,0:T(8,128)(2,1)S(1)} %bitcast.18), kind=kLoop, calls=%fused_computation | loop fusion | flops 2097152 | bytes 8388608 | tf_op jit(solution)/shard_map/stack | solution.py:43
  31.7 0.0 copy-done
  31.7 0.0 collective-permute-done.6.sib_ref
  31.7 0.0 copy-start.1
  31.7 0.8 %copy-done.1 = bf16[4,4,16512]{2,1,0:T(4,128)(2,1)} copy-done((bf16[4,4,16512]{2,1,0:T(4,128)(2,1)}, bf16[4,4,16512]{2,1,0:T(4,128)(2,1)S(1)}, u32[]{:S(2)}) %copy-start.1) | copy-done | bytes 528408
  32.5 12.1 %shard_map.28 = bf16[512,512]{1,0:T(8,128)(2,1)} custom-call(s32[3]{0:T(128)} %pad_add_fusion.place_ref, bf16[4,4,16512]{2,1,0:T(4,128)(2,1)} %get-tuple-element.8.rec_ref, bf16[4,4,16512]{2,1,0:T(4,128)(2,1)} %copy-done, bf16[4,4,16512]{2,1,0:T(4,128)(2,1)} %copy-done.1, bf16[4096,512]{1,0:T(8,128)(2,1)} %bitcast.17), custom_call_target="tpu_custom_call" | custom-call | tf_op jit(solution)/shard_map/pallas_call | solution.py:130
  (3 shorter events, 0.0 us)
Async XLA Ops:
  4.3 13.3 %collective-permute-start.4 = (bf16[4,16512]{1,0:T(4,128)(2,1)S(1)}, bf16[4,16512]{1,0:T(4,128)(2,1)S(1)}, u32[]{:S(2)}, u32[]{:S(2)}) collective-permute-start(bf16[4,16512]{1,0:T(4,128)(2,1)S(1)} %fusion.5), channel_id=1, source_target_pairs={{0,16},{4,20},{8,24},{12,28},{16,0},{20,4},{24,8},{28,12},{1,17},{... | collective-permute-start | bytes 396296 | tf_op jit(solution)/shard_map/ppermute | solution.py:160
  8.4 10.3 %collective-permute-start.3 = (bf16[4,16512]{1,0:T(4,128)(2,1)S(1)}, bf16[4,16512]{1,0:T(4,128)(2,1)S(1)}, u32[]{:S(2)}, u32[]{:S(2)}) collective-permute-start(bf16[4,16512]{1,0:T(4,128)(2,1)S(1)} %fusion.5), channel_id=1, source_target_pairs={{0,8},{4,12},{8,16},{12,20},{16,24},{20,28},{24,0},{28,4},{1,9},{5... | collective-permute-start | bytes 396296 | tf_op jit(solution)/shard_map/ppermute | solution.py:160
  10.0 8.8 %collective-permute-start.2 = (bf16[4,16512]{1,0:T(4,128)(2,1)S(1)}, bf16[4,16512]{1,0:T(4,128)(2,1)S(1)}, u32[]{:S(2)}, u32[]{:S(2)}) collective-permute-start(bf16[4,16512]{1,0:T(4,128)(2,1)S(1)} %fusion.5), channel_id=1, source_target_pairs={{0,3},{1,0},{2,1},{3,2},{4,7},{5,4},{6,5},{7,6},{8,11},{9,8},{10,9... | collective-permute-start | bytes 396296 | tf_op jit(solution)/shard_map/ppermute | solution.py:160
  12.4 7.4 %collective-permute-start.1 = (bf16[4,16512]{1,0:T(4,128)(2,1)S(1)}, bf16[4,16512]{1,0:T(4,128)(2,1)S(1)}, u32[]{:S(2)}, u32[]{:S(2)}) collective-permute-start(bf16[4,16512]{1,0:T(4,128)(2,1)S(1)} %fusion.5), channel_id=1, source_target_pairs={{0,2},{1,3},{2,0},{3,1},{4,6},{5,7},{6,4},{7,5},{8,10},{9,11},{10,... | collective-permute-start | bytes 396296 | tf_op jit(solution)/shard_map/ppermute | solution.py:160
  12.9 6.9 %collective-permute-start = (bf16[4,16512]{1,0:T(4,128)(2,1)S(1)}, bf16[4,16512]{1,0:T(4,128)(2,1)S(1)}, u32[]{:S(2)}, u32[]{:S(2)}) collective-permute-start(bf16[4,16512]{1,0:T(4,128)(2,1)S(1)} %fusion.5), channel_id=1, source_target_pairs={{0,1},{1,2},{2,3},{3,0},{4,5},{5,6},{6,7},{7,4},{8,9},{9,10},{10,1... | collective-permute-start | bytes 396296 | tf_op jit(solution)/shard_map/ppermute | solution.py:160
  17.6 5.0 %collective-permute-start.5 = (bf16[4,16512]{1,0:T(4,128)(2,1)S(1)}, bf16[4,16512]{1,0:T(4,128)(2,1)S(1)}, u32[]{:S(2)}, u32[]{:S(2)}) collective-permute-start(bf16[4,16512]{1,0:T(4,128)(2,1)S(1)} %fusion.5), channel_id=1, source_target_pairs={{0,24},{4,28},{8,0},{12,4},{16,8},{20,12},{24,16},{28,20},{1,25},{... | collective-permute-start | bytes 396296 | tf_op jit(solution)/shard_map/ppermute | solution.py:160
  24.3 7.4 %copy-start = (bf16[4,4,16512]{2,1,0:T(4,128)(2,1)}, bf16[4,4,16512]{2,1,0:T(4,128)(2,1)S(1)}, u32[]{:S(2)}) copy-start(bf16[4,4,16512]{2,1,0:T(4,128)(2,1)S(1)} %get-tuple-element.7.own_ref) | copy-start | bytes 1585156
  24.3 7.4 %collective-permute-start.6 = (bf16[4,4,16512]{2,1,0:T(4,128)(2,1)S(1)}, bf16[4,4,16512]{2,1,0:T(4,128)(2,1)S(1)}, u32[]{:S(2)}, u32[]{:S(2)}) collective-permute-start(bf16[4,4,16512]{2,1,0:T(4,128)(2,1)S(1)} %get-tuple-element.7.own_ref), channel_id=1, source_target_pairs={{0,4},{4,0},{8,12},{12,8},{16,20},{20,16},{24,28},{28,24},{1,5},{5... | collective-permute-start | bytes 1585160 | tf_op jit(solution)/shard_map/ppermute | solution.py:172
  31.7 0.8 %copy-start.1 = (bf16[4,4,16512]{2,1,0:T(4,128)(2,1)}, bf16[4,4,16512]{2,1,0:T(4,128)(2,1)S(1)}, u32[]{:S(2)}) copy-start(bf16[4,4,16512]{2,1,0:T(4,128)(2,1)S(1)} %collective-permute-done.6.sib_ref) | copy-start | bytes 1585156

commit v6 on v5

--- a/solution.py
+++ b/solution.py
@@ -16,13 +16,75 @@
 epsilon = 1e-06
 
 
-def whiten_spectra(spectra):
-    values = spectra.astype(jnp.float32)
-    squares = values[:, :, 0] ** 2 + values[:, :, 1] ** 2
-    banded = squares.reshape(squares.shape[0], squares.shape[1], squares.shape[2] // BAND, BAND)
-    power = jnp.sum(banded, axis=3) / (2.0 * BAND)
-    factor = jnp.repeat(1.0 / jnp.sqrt(power + epsilon), BAND, axis=2)
-    return (values * factor[:, :, None, :]).astype(jnp.bfloat16)
+def split3(x):
+    hi = x.astype(jnp.bfloat16)
+    rest = x - hi.astype(jnp.float32)
+    mid = rest.astype(jnp.bfloat16)
+    lo = (rest - mid.astype(jnp.float32)).astype(jnp.bfloat16)
+    return hi, mid, lo
+
+
+def exact_dot(x, ones):
+    return sum(jnp.dot(part, ones, preferred_element_type=jnp.float32) for part in split3(x))
+
+
+def whiten_kernel(x_ref, v_ref, out_ref, sq_ref, *, channels, windows, freqs):
+    bands = freqs // BAND
+    band_of = lax.broadcasted_iota(jnp.int32, (freqs, bands), 0) // BAND
+    to_band = (band_of == lax.broadcasted_iota(jnp.int32, (freqs, bands), 1)).astype(jnp.bfloat16)
+    band_row = lax.broadcasted_iota(jnp.int32, (bands, freqs), 1) // BAND
+    from_band = (band_row == lax.broadcasted_iota(jnp.int32, (bands, freqs), 0)).astype(
+        jnp.bfloat16
+    )
+    for c in range(channels):
+        for w in range(windows):
+            x = x_ref[c, w].astype(jnp.float32)
+            row = c * windows + w
+            sq_ref[row : row + 1, :] = x[0:1] ** 2 + x[1:2] ** 2
+    power = exact_dot(sq_ref[...], to_band) / (2.0 * BAND)
+    factor = exact_dot(1.0 / jnp.sqrt(power + epsilon), from_band)
+    width = 2 * freqs
+    for c in range(channels):
+        for w in range(windows):
+            x = x_ref[c, w].astype(jnp.float32)
+            row = c * windows + w
+            scale = factor[row : row + 1, :]
+            out_ref[c : c + 1, w * width : w * width + freqs] = (x[0:1] * scale).astype(
+                jnp.bfloat16
+            )
+            out_ref[c : c + 1, w * width + freqs : (w + 1) * width] = (x[1:2] * scale).astype(
+                jnp.bfloat16
+            )
+    body = windows * width
+    out_ref[:, body : body + PAD] = v_ref[...].astype(jnp.float32).astype(jnp.bfloat16)
+
+
+def whiten_pack(spectra, valid):
+    channels, windows, _, freqs = spectra.shape
+    tail = jnp.pad(valid, ((0, 0), (0, PAD - windows)))
+    kernel = functools.partial(whiten_kernel, channels=channels, windows=windows, freqs=freqs)
+    return pl.pallas_call(
+        kernel,
+        out_shape=jax.ShapeDtypeStruct((channels, windows * 2 * freqs + PAD), jnp.bfloat16),
+        scratch_shapes=[pltpu.VMEM((channels * windows, freqs), jnp.float32)],
+    )(spectra, tail)
+
+
+def table_kernel(chi_ref, shi_ref, clo_ref, slo_ref, out_ref, *, freqs, factor):
+    step = clo_ref.shape[0]
+    clo = clo_ref[...]
+    slo = slo_ref[...]
+
+    def body(h, carry):
+        ch = chi_ref[pl.ds(h, 1), :]
+        sh = shi_ref[pl.ds(h, 1), :]
+        rows = pl.ds(pl.multiple_of(h * step, step), step)
+        out_ref[rows, :] = ((ch * clo - sh * slo) * factor).astype(jnp.bfloat16)
+        rows = pl.ds(pl.multiple_of(freqs + h * step, step), step)
+        out_ref[rows, :] = ((sh * clo + ch * slo) * (-factor)).astype(jnp.bfloat16)
+        return carry
+
+    lax.fori_loop(0, chi_ref.shape[0], body, 0)
 
 
 def lag_table(freq_count, lag_count):
@@ -33,21 +95,12 @@
     scale = 2.0 * math.pi / NSAMP
     angle_hi = jnp.mod(hi[:, None] * shifts[None, :], NSAMP).astype(jnp.float32) * scale
     angle_lo = jnp.mod(lo[:, None] * shifts[None, :], NSAMP).astype(jnp.float32) * scale
-    cos_hi, sin_hi = jnp.cos(angle_hi)[:, None, :], jnp.sin(angle_hi)[:, None, :]
-    cos_lo, sin_lo = jnp.cos(angle_lo)[None, :, :], jnp.sin(angle_lo)[None, :, :]
     factor = 1.0 / math.sqrt(2.0 * freq_count)
-    cosines = (cos_hi * cos_lo - sin_hi * sin_lo) * factor
-    sines = (sin_hi * cos_lo + cos_hi * sin_lo) * (-factor)
-    cosines = cosines.reshape(freq_count, lag_count).astype(jnp.bfloat16)
-    sines = sines.reshape(freq_count, lag_count).astype(jnp.bfloat16)
-    return jnp.stack([cosines, sines], axis=0)
-
-
-def pack(whitened, mask):
-    channels = whitened.shape[0]
-    flat = whitened.reshape(channels, -1)
-    tail = jnp.pad(mask, ((0, 0), (0, PAD - mask.shape[1])))
-    return jnp.concatenate([flat, tail], axis=1)
+    kernel = functools.partial(table_kernel, freqs=freq_count, factor=factor)
+    return pl.pallas_call(
+        kernel,
+        out_shape=jax.ShapeDtypeStruct((2 * freq_count, lag_count), jnp.bfloat16),
+    )(jnp.cos(angle_hi), jnp.sin(angle_hi), jnp.cos(angle_lo), jnp.sin(angle_lo))
 
 
 def cross_kernel(
@@ -163,10 +216,8 @@
 
 def local(spectra, valid, rcv_count, src_count):
     channels, windows, _, freqs = spectra.shape
-    table = lag_table(freqs, LAGS).reshape(2 * freqs, LAGS)
-    mask_wire = valid.astype(jnp.bfloat16)
-    whitened = whiten_spectra(spectra)
-    packed = pack(whitened, mask_wire)
+    table = lag_table(freqs, LAGS)
+    packed = whiten_pack(spectra, valid)
     rec_stack = shifted(packed, "rcv", rcv_count, 1)
     own_stack = shifted(packed, "src", src_count, 2)
     sib_stack = lax.ppermute(own_stack, "src", perm=[(j, j ^ 1) for j in range(src_count)])

time: 44.9 us -> 43.4 us (0.967)
  other arithmetic: 13.6 us -> 5.48 us
  Pallas kernels: 12.1 us -> 19 us
  waiting for transfers between devices: 7.24 us -> 6.03 us
  local copies, waits for them, and re-layouts: 1.55 us -> 2.1 us
  starting transfers between devices: 10 us -> 10.5 us
    pallas_call x0 -> x2, Pallas kernels: none -> 6.89 us  [the longest x1 4.42 us: lag_table(): pl.pallas_call(kernel, out_shape=jax.ShapeDtypeStruct((2 * freq_count, la...]
    convert_element_type x4 -> x0, other arithmetic: 5.57 us -> none  [the longest x1 2.82 us: lag_table(): cosines = cosines.reshape(freq_count, lag_count).astype(jnp.bfloat16)]
    another operation x1 -> x0, other arithmetic: 3.91 us -> none  [lag_table(): return jnp.stack([cosines, sines], axis=0)]
    sin x0 -> x2, other arithmetic: none -> 2.24 us  [the longest x1 1.25 us: lag_table(): jnp.sin(angle_lo)]
    pad x0 -> x1, local copies, waits for them, and re-layouts: none -> 1.26 us  [whiten_pack(): tail = jnp.pad(valid, ((0, 0), (0, PAD - windows)))]
    ppermute x6, waiting for transfers between devices: 7.24 us -> 6.03 us  [shifted(): parts.append(lax.ppermute(x, axis, perm=pairs))]
    cos x2 -> x0, other arithmetic: 0.89 us -> none  [the longest x1 0.54 us: lag_table(): jnp.cos(angle_lo)[None, :, :]]
    another operation x2 -> x1, other arithmetic: 1.78 us -> 2.61 us  [shifted(): return jnp.stack(parts)]
  transfers between devices with their start and end apart: 7 -> 7, of which waited for: 3 -> 2; matrix products, arithmetic and copies ran while one was open for 19% -> 7% of each run, Pallas kernels for 0% -> 10%
where the time goes in v6:
time: 43.4 us; the launch traced here: 43.1 us
  Pallas kernels  19 us (44%)
  starting transfers between devices  10.5 us (24%)
  waiting for transfers between devices  6.03 us (14%)
  other arithmetic  5.48 us (13%)
  local copies, waits for them, and re-layouts  2.1 us (5%)
    pallas_call x1, Pallas kernels, correlate(): pl.pallas_call(kernel, grid_spec=pltpu.PrefetchScalarGridSpec(num_scalar_...  12.1 us
    ppermute x6, starting transfers between devices, shifted(): parts.append(lax.ppermute(x, axis, perm=pairs))  10.5 us
    ppermute x6, waiting for transfers between devices, shifted(): parts.append(lax.ppermute(x, axis, perm=pairs))  6.03 us
    pallas_call x1, Pallas kernels, lag_table(): pl.pallas_call(kernel, out_shape=jax.ShapeDtypeStruct((2 * freq_count, la...  4.42 us
    another operation x1, other arithmetic, shifted(): return jnp.stack(parts)  2.61 us
    pallas_call x1, Pallas kernels, whiten_pack(): pl.pallas_call(kernel, out_shape=jax.ShapeDtypeStruct((channels, windows...  2.47 us
    pad x1, local copies, waits for them, and re-layouts, whiten_pack(): tail = jnp.pad(valid, ((0, 0), (0, PAD - windows)))  1.26 us
    sin x1, other arithmetic, lag_table(): jnp.sin(angle_lo)  1.25 us
  transfers between devices with their start and end apart: 7, of which 2 were waited for; matrix products, arithmetic and copies ran while one was open for 7% of the time, Pallas kernels for 10%

profile of v6, /device:TPU:0, one launch (start us, length us, event | category | flops | bytes accessed | tf_op | source)
XLA Modules:
  0.0 43.1 jit_solution(991378663011927164)
XLA Ops:
  0.0 1.3 %pad.4.v_ref = s32[4,128]{1,0:T(4,128)} pad(s32[4,4]{1,0:T(4,128)} %param.3, s32[]{:T(128)} %constant.52.clone.1), padding=0_0x0_124 | pad | bytes 2116 | tf_op jit(solution)/shard_map/jit(_pad)/pad | solution.py:64
  1.3 2.5 %shard_map.28 = bf16[4,16512]{1,0:T(4,128)(2,1)} custom-call(bf16[4,4,2,2048]{3,2,1,0:T(2,128)(2,1)} %x_ref.1, s32[4,128]{1,0:T(4,128)} %pad.4.v_ref), custom_call_target="tpu_custom_call" | custom-call | tf_op jit(solution)/shard_map/pallas_call | solution.py:66
  3.7 5.0 %collective-permute-start.5 = (bf16[4,16512]{1,0:T(4,128)(2,1)}, bf16[4,16512]{1,0:T(4,128)(2,1)S(1)}, u32[]{:S(2)}, u32[]{:S(2)}) collective-permute-start(bf16[4,16512]{1,0:T(4,128)(2,1)} %shard_map.28), channel_id=1, source_target_pairs={{0,24},{4,28},{8,0},{12,4},{16,8},{20,12},{24,16},{28,20},{1,25},{... | collective-permute-start | bytes 396296 | tf_op jit(solution)/shard_map/ppermute | solution.py:213
  8.8 0.0 collective-permute-start.4
  8.8 1.0 %collective-permute-start.3 = (bf16[4,16512]{1,0:T(4,128)(2,1)}, bf16[4,16512]{1,0:T(4,128)(2,1)S(1)}, u32[]{:S(2)}, u32[]{:S(2)}) collective-permute-start(bf16[4,16512]{1,0:T(4,128)(2,1)} %shard_map.28), channel_id=1, source_target_pairs={{0,8},{4,12},{8,16},{12,20},{16,24},{20,28},{24,0},{28,4},{1,9},{5... | collective-permute-start | bytes 396296 | tf_op jit(solution)/shard_map/ppermute | solution.py:213
  9.8 2.4 %collective-permute-start.2 = (bf16[4,16512]{1,0:T(4,128)(2,1)}, bf16[4,16512]{1,0:T(4,128)(2,1)S(1)}, u32[]{:S(2)}, u32[]{:S(2)}) collective-permute-start(bf16[4,16512]{1,0:T(4,128)(2,1)} %shard_map.28), channel_id=1, source_target_pairs={{0,3},{1,0},{2,1},{3,2},{4,7},{5,4},{6,5},{7,6},{8,11},{9,8},{10,9... | collective-permute-start | bytes 396296 | tf_op jit(solution)/shard_map/ppermute | solution.py:213
  12.2 0.5 %collective-permute-start.1 = (bf16[4,16512]{1,0:T(4,128)(2,1)}, bf16[4,16512]{1,0:T(4,128)(2,1)S(1)}, u32[]{:S(2)}, u32[]{:S(2)}) collective-permute-start(bf16[4,16512]{1,0:T(4,128)(2,1)} %shard_map.28), channel_id=1, source_target_pairs={{0,2},{1,3},{2,0},{3,1},{4,6},{5,7},{6,4},{7,5},{8,10},{9,11},{10,... | collective-permute-start | bytes 396296 | tf_op jit(solution)/shard_map/ppermute | solution.py:213
  12.7 0.3 collective-permute-done.5
  13.0 1.5 %collective-permute-start = (bf16[4,16512]{1,0:T(4,128)(2,1)}, bf16[4,16512]{1,0:T(4,128)(2,1)S(1)}, u32[]{:S(2)}, u32[]{:S(2)}) collective-permute-start(bf16[4,16512]{1,0:T(4,128)(2,1)} %shard_map.28), channel_id=1, source_target_pairs={{0,1},{1,2},{2,3},{3,0},{4,5},{5,6},{6,7},{7,4},{8,9},{9,10},{10,1... | collective-permute-start | bytes 396296 | tf_op jit(solution)/shard_map/ppermute | solution.py:213
  14.5 5.7 %collective-permute-done.4 = bf16[4,16512]{1,0:T(4,128)(2,1)S(1)} collective-permute-done((bf16[4,16512]{1,0:T(4,128)(2,1)}, bf16[4,16512]{1,0:T(4,128)(2,1)S(1)}, u32[]{:S(2)}, u32[]{:S(2)}) %collective-permute-start.4) | collective-permute-done | bytes 132128 | tf_op jit(solution)/shard_map/ppermute | solution.py:213
  20.3 0.0 collective-permute-done.3
  20.3 0.0 collective-permute-done.2
  20.3 0.0 collective-permute-done.1
  20.3 0.0 collective-permute-done
  20.3 2.6 %fusion.3 = (bf16[4,4,16512]{2,1,0:T(4,128)(2,1)S(1)}, bf16[4,4,16512]{2,1,0:T(4,128)(2,1)}) fusion(bf16[1,4,16512]{2,1,0:T(4,128)(2,1)} %bitcast.11, bf16[1,4,16512]{2,1,0:T(4,128)(2,1)S(1)} %bitcast.12, bf16[1,4,16512]{2,1,0:T(4,128)(2,1)S(1)} %bitcast.13, bf16[1,4,16512]{2,1,0:T(4,128)(2,1)S(1)} %bitcast.14, bf16[1,4,16512]{2,1,0:T(4,128)(2,1)S(1)} %bitcast.15, ...), kind=kLoop, calls=%fused_computation.5 | loop fusion | flops 1585152 | bytes 1981440 | tf_op jit(solution)/shard_map/stack | solution.py:214
  22.9 0.0 copy-start
  22.9 0.0 collective-permute-start.6
  22.9 1.0 %fusion.15 = (f32[32,512]{1,0:T(8,128)}, f32[32,512]{1,0:T(8,128)}) fusion(s32[512]{0:T(512)S(1)} %iota_add_fusion, s32[32]{0:T(128)S(1)} %iota_multiply_fusion), kind=kLoop, calls=%fused_computation.21 | loop fusion | flops 147456 | bytes 133248 | tf_op jit(solution)/shard_map/sin | solution.py:103
  23.9 1.2 %fusion.8 = (f32[64,512]{1,0:T(8,128)}, f32[64,512]{1,0:T(8,128)}) fusion(s32[512]{0:T(512)S(1)} %iota_add_fusion), kind=kLoop, calls=%fused_computation.12 | loop fusion | flops 294912 | bytes 264192 | tf_op jit(solution)/shard_map/sin | solution.py:103
  25.2 4.4 %shard_map.29.tab_ref = bf16[4096,512]{1,0:T(8,128)(2,1)} custom-call(f32[32,512]{1,0:T(8,128)} %get-tuple-element.8.chi_ref, f32[32,512]{1,0:T(8,128)} %get-tuple-element.7.shi_ref, f32[64,512]{1,0:T(8,128)} %get-tuple-element.10.clo_ref, f32[64,512]{1,0:T(8,128)} %get-tuple-element.9.slo_ref), custom_call_target="tpu_custom_call" | custom-call | tf_op jit(solution)/shard_map/pallas_call | solution.py:100
  29.6 0.6 %pad_add_fusion.place_ref = s32[3]{0:T(128)} fusion(s32[1]{0:T(128)} %bitcast.2, s32[1]{0:T(128)} %bitcast.1, s32[1]{0:T(128)} %bitcast), kind=kLoop, calls=%fused_computation.25 | loop fusion | flops 6 | bytes 24 | tf_op jit(solution)/shard_map/stack | solution.py:225
  30.2 0.0 collective-permute-done.6.sib_ref
  30.2 0.0 copy-start.1
  30.2 0.0 copy-done
  30.2 0.8 %copy-done.1 = bf16[4,4,16512]{2,1,0:T(4,128)(2,1)} copy-done((bf16[4,4,16512]{2,1,0:T(4,128)(2,1)}, bf16[4,4,16512]{2,1,0:T(4,128)(2,1)S(1)}, u32[]{:S(2)}) %copy-start.1) | copy-done | bytes 528408
  31.0 12.1 %shard_map.30 = bf16[512,512]{1,0:T(8,128)(2,1)} custom-call(s32[3]{0:T(128)} %pad_add_fusion.place_ref, bf16[4,4,16512]{2,1,0:T(4,128)(2,1)} %get-tuple-element.6.rec_ref, bf16[4,4,16512]{2,1,0:T(4,128)(2,1)} %copy-done, bf16[4,4,16512]{2,1,0:T(4,128)(2,1)} %copy-done.1, bf16[4096,512]{1,0:T(8,128)(2,1)} %shard_map.29.tab_ref), custom_call_target="tpu_custom_call" | custom-call | tf_op jit(solution)/shard_map/pallas_call | solution.py:183
  (2 shorter events, 0.0 us)
Async XLA Ops:
  3.7 9.3 %collective-permute-start.5 = (bf16[4,16512]{1,0:T(4,128)(2,1)}, bf16[4,16512]{1,0:T(4,128)(2,1)S(1)}, u32[]{:S(2)}, u32[]{:S(2)}) collective-permute-start(bf16[4,16512]{1,0:T(4,128)(2,1)} %shard_map.28), channel_id=1, source_target_pairs={{0,24},{4,28},{8,0},{12,4},{16,8},{20,12},{24,16},{28,20},{1,25},{... | collective-permute-start | bytes 396296 | tf_op jit(solution)/shard_map/ppermute | solution.py:213
  8.8 11.5 %collective-permute-start.4 = (bf16[4,16512]{1,0:T(4,128)(2,1)}, bf16[4,16512]{1,0:T(4,128)(2,1)S(1)}, u32[]{:S(2)}, u32[]{:S(2)}) collective-permute-start(bf16[4,16512]{1,0:T(4,128)(2,1)} %shard_map.28), channel_id=1, source_target_pairs={{0,16},{4,20},{8,24},{12,28},{16,0},{20,4},{24,8},{28,12},{1,17},{... | collective-permute-start | bytes 396296 | tf_op jit(solution)/shard_map/ppermute | solution.py:213
  8.8 11.5 %collective-permute-start.3 = (bf16[4,16512]{1,0:T(4,128)(2,1)}, bf16[4,16512]{1,0:T(4,128)(2,1)S(1)}, u32[]{:S(2)}, u32[]{:S(2)}) collective-permute-start(bf16[4,16512]{1,0:T(4,128)(2,1)} %shard_map.28), channel_id=1, source_target_pairs={{0,8},{4,12},{8,16},{12,20},{16,24},{20,28},{24,0},{28,4},{1,9},{5... | collective-permute-start | bytes 396296 | tf_op jit(solution)/shard_map/ppermute | solution.py:213
  9.8 10.5 %collective-permute-start.2 = (bf16[4,16512]{1,0:T(4,128)(2,1)}, bf16[4,16512]{1,0:T(4,128)(2,1)S(1)}, u32[]{:S(2)}, u32[]{:S(2)}) collective-permute-start(bf16[4,16512]{1,0:T(4,128)(2,1)} %shard_map.28), channel_id=1, source_target_pairs={{0,3},{1,0},{2,1},{3,2},{4,7},{5,4},{6,5},{7,6},{8,11},{9,8},{10,9... | collective-permute-start | bytes 396296 | tf_op jit(solution)/shard_map/ppermute | solution.py:213
  12.2 8.0 %collective-permute-start.1 = (bf16[4,16512]{1,0:T(4,128)(2,1)}, bf16[4,16512]{1,0:T(4,128)(2,1)S(1)}, u32[]{:S(2)}, u32[]{:S(2)}) collective-permute-start(bf16[4,16512]{1,0:T(4,128)(2,1)} %shard_map.28), channel_id=1, source_target_pairs={{0,2},{1,3},{2,0},{3,1},{4,6},{5,7},{6,4},{7,5},{8,10},{9,11},{10,... | collective-permute-start | bytes 396296 | tf_op jit(solution)/shard_map/ppermute | solution.py:213
  13.0 7.3 %collective-permute-start = (bf16[4,16512]{1,0:T(4,128)(2,1)}, bf16[4,16512]{1,0:T(4,128)(2,1)S(1)}, u32[]{:S(2)}, u32[]{:S(2)}) collective-permute-start(bf16[4,16512]{1,0:T(4,128)(2,1)} %shard_map.28), channel_id=1, source_target_pairs={{0,1},{1,2},{2,3},{3,0},{4,5},{5,6},{6,7},{7,4},{8,9},{9,10},{10,1... | collective-permute-start | bytes 396296 | tf_op jit(solution)/shard_map/ppermute | solution.py:213
  22.9 7.3 %copy-start = (bf16[4,4,16512]{2,1,0:T(4,128)(2,1)}, bf16[4,4,16512]{2,1,0:T(4,128)(2,1)S(1)}, u32[]{:S(2)}) copy-start(bf16[4,4,16512]{2,1,0:T(4,128)(2,1)S(1)} %get-tuple-element.5.own_ref) | copy-start | bytes 1585156
  22.9 7.3 %collective-permute-start.6 = (bf16[4,4,16512]{2,1,0:T(4,128)(2,1)S(1)}, bf16[4,4,16512]{2,1,0:T(4,128)(2,1)S(1)}, u32[]{:S(2)}, u32[]{:S(2)}) collective-permute-start(bf16[4,4,16512]{2,1,0:T(4,128)(2,1)S(1)} %get-tuple-element.5.own_ref), channel_id=1, source_target_pairs={{0,4},{4,0},{8,12},{12,8},{16,20},{20,16},{24,28},{28,24},{1,5},{5... | collective-permute-start | bytes 1585160 | tf_op jit(solution)/shard_map/ppermute | solution.py:223
  30.2 0.8 %copy-start.1 = (bf16[4,4,16512]{2,1,0:T(4,128)(2,1)}, bf16[4,4,16512]{2,1,0:T(4,128)(2,1)S(1)}, u32[]{:S(2)}) copy-start(bf16[4,4,16512]{2,1,0:T(4,128)(2,1)S(1)} %collective-permute-done.6.sib_ref) | copy-start | bytes 1585156

commit v7 on v6

--- a/solution.py
+++ b/solution.py
@@ -70,23 +70,6 @@
     )(spectra, tail)
 
 
-def table_kernel(chi_ref, shi_ref, clo_ref, slo_ref, out_ref, *, freqs, factor):
-    step = clo_ref.shape[0]
-    clo = clo_ref[...]
-    slo = slo_ref[...]
-
-    def body(h, carry):
-        ch = chi_ref[pl.ds(h, 1), :]
-        sh = shi_ref[pl.ds(h, 1), :]
-        rows = pl.ds(pl.multiple_of(h * step, step), step)
-        out_ref[rows, :] = ((ch * clo - sh * slo) * factor).astype(jnp.bfloat16)
-        rows = pl.ds(pl.multiple_of(freqs + h * step, step), step)
-        out_ref[rows, :] = ((sh * clo + ch * slo) * (-factor)).astype(jnp.bfloat16)
-        return carry
-
-    lax.fori_loop(0, chi_ref.shape[0], body, 0)
-
-
 def lag_table(freq_count, lag_count):
     step = 64
     shifts = jnp.arange(lag_count, dtype=jnp.int32) - lag_count // 2
@@ -95,12 +78,14 @@
     scale = 2.0 * math.pi / NSAMP
     angle_hi = jnp.mod(hi[:, None] * shifts[None, :], NSAMP).astype(jnp.float32) * scale
     angle_lo = jnp.mod(lo[:, None] * shifts[None, :], NSAMP).astype(jnp.float32) * scale
+    cos_hi, sin_hi = jnp.cos(angle_hi)[:, None, :], jnp.sin(angle_hi)[:, None, :]
+    cos_lo, sin_lo = jnp.cos(angle_lo)[None, :, :], jnp.sin(angle_lo)[None, :, :]
     factor = 1.0 / math.sqrt(2.0 * freq_count)
-    kernel = functools.partial(table_kernel, freqs=freq_count, factor=factor)
-    return pl.pallas_call(
-        kernel,
-        out_shape=jax.ShapeDtypeStruct((2 * freq_count, lag_count), jnp.bfloat16),
-    )(jnp.cos(angle_hi), jnp.sin(angle_hi), jnp.cos(angle_lo), jnp.sin(angle_lo))
+    cosines = (cos_hi * cos_lo - sin_hi * sin_lo) * factor
+    sines = (sin_hi * cos_lo + cos_hi * sin_lo) * (-factor)
+    cosines = cosines.reshape(freq_count, lag_count).astype(jnp.bfloat16)
+    sines = sines.reshape(freq_count, lag_count).astype(jnp.bfloat16)
+    return jnp.stack([cosines, sines], axis=0).reshape(2 * freq_count, lag_count)
 
 
 def cross_kernel(
@@ -220,6 +205,7 @@
     packed = whiten_pack(spectra, valid)
     rec_stack = shifted(packed, "rcv", rcv_count, 1)
     own_stack = shifted(packed, "src", src_count, 2)
+    table, rec_stack, own_stack = lax.optimization_barrier((table, rec_stack, own_stack))
     sib_stack = lax.ppermute(own_stack, "src", perm=[(j, j ^ 1) for j in range(src_count)])
     src_index = lax.axis_index("src")
     place = jnp.stack(

time: 43.4 us -> 38.4 us (0.88)
  Pallas kernels: 19 us -> 15.1 us
  waiting for transfers between devices: 6.03 us -> 4.17 us
  other arithmetic: 5.48 us -> 7.15 us
  starting transfers between devices: 10.5 us -> 9.66 us
    pallas_call x1 -> x0, Pallas kernels: 4.42 us -> none  [lag_table(): pl.pallas_call(kernel, out_shape=jax.ShapeDtypeStruct((2 * freq_count, la...]
    ppermute x6, waiting for transfers between devices: 6.03 us -> 2.98 us  [shifted(): parts.append(lax.ppermute(x, axis, perm=pairs))]
    another operation x0 -> x1, other arithmetic: none -> 2.31 us  [lag_table(): jnp.stack([cosines, sines], axis=0).reshape(2 * freq_count, lag_count)]
    sin x2 -> x0, other arithmetic: 2.24 us -> none  [the longest x1 1.25 us: lag_table(): jnp.sin(angle_lo)]
    convert_element_type x0 -> x1, other arithmetic: none -> 1.54 us  [lag_table(): cosines = cosines.reshape(freq_count, lag_count).astype(jnp.bfloat16)]
    ppermute x1, waiting for transfers between devices: 0.01 us -> 1.2 us  [local(): lax.ppermute(own_stack, 'src', perm=[(j, j ^ 1) for j in range(src_count)])]
    another operation x1, other arithmetic: 2.61 us -> 1.69 us  [shifted(): return jnp.stack(parts)]
    cos x0 -> x2, other arithmetic: none -> 0.89 us  [the longest x1 0.54 us: lag_table(): jnp.cos(angle_lo)[None, :, :]]
  transfers between devices with their start and end apart: 7 -> 7, of which waited for: 2 -> 3; matrix products, arithmetic and copies ran while one was open for 7% -> 14% of each run, Pallas kernels for 10% -> 0%
where the time goes in v7:
time: 38.4 us; the launch traced here: 38.2 us
  Pallas kernels  15.1 us (39%)
  starting transfers between devices  9.66 us (25%)
  other arithmetic  7.15 us (19%)
  waiting for transfers between devices  4.17 us (11%)
  local copies, waits for them, and re-layouts  2.08 us (5%)
    pallas_call x1, Pallas kernels, correlate(): pl.pallas_call(kernel, grid_spec=pltpu.PrefetchScalarGridSpec(num_scalar_...  12.7 us
    ppermute x6, starting transfers between devices, shifted(): parts.append(lax.ppermute(x, axis, perm=pairs))  9.66 us
    ppermute x6, waiting for transfers between devices, shifted(): parts.append(lax.ppermute(x, axis, perm=pairs))  2.98 us
    pallas_call x1, Pallas kernels, whiten_pack(): pl.pallas_call(kernel, out_shape=jax.ShapeDtypeStruct((channels, windows...  2.47 us
    another operation x1, other arithmetic, lag_table(): jnp.stack([cosines, sines], axis=0).reshape(2 * freq_count, lag_count)  2.31 us
    another operation x1, other arithmetic, shifted(): return jnp.stack(parts)  1.69 us
    convert_element_type x1, other arithmetic, lag_table(): cosines = cosines.reshape(freq_count, lag_count).astype(jnp.bfloat16)  1.54 us
    pad x1, local copies, waits for them, and re-layouts, whiten_pack(): tail = jnp.pad(valid, ((0, 0), (0, PAD - windows)))  1.25 us
  transfers between devices with their start and end apart: 7, of which 3 were waited for; matrix products, arithmetic and copies ran while one was open for 14% of the time, Pallas kernels for 0%

profile of v7, /device:TPU:0, one launch (start us, length us, event | category | flops | bytes accessed | tf_op | source)
XLA Modules:
  0.0 38.2 jit_solution(12150845363511350290)
XLA Ops:
  0.0 1.2 %pad.4.v_ref = s32[4,128]{1,0:T(4,128)} pad(s32[4,4]{1,0:T(4,128)} %param.3, s32[]{:T(128)} %constant.54.clone.1), padding=0_0x0_124 | pad | bytes 2116 | tf_op jit(solution)/shard_map/jit(_pad)/pad | solution.py:64
  1.2 2.5 %shard_map.28 = bf16[4,16512]{1,0:T(4,128)(2,1)} custom-call(bf16[4,4,2,2048]{3,2,1,0:T(2,128)(2,1)} %x_ref.1, s32[4,128]{1,0:T(4,128)} %pad.4.v_ref), custom_call_target="tpu_custom_call" | custom-call | tf_op jit(solution)/shard_map/pallas_call | solution.py:66
  3.7 0.0 copy-start.2
  3.7 5.0 %collective-permute-start.5 = (bf16[4,16512]{1,0:T(4,128)(2,1)}, bf16[4,16512]{1,0:T(4,128)(2,1)S(1)}, u32[]{:S(2)}, u32[]{:S(2)}) collective-permute-start(bf16[4,16512]{1,0:T(4,128)(2,1)} %shard_map.28), channel_id=1, source_target_pairs={{0,24},{4,28},{8,0},{12,4},{16,8},{20,12},{24,16},{28,20},{1,25},{... | collective-permute-start | bytes 396296 | tf_op jit(solution)/shard_map/ppermute | solution.py:198
  8.8 0.0 collective-permute-start.4
  8.8 1.0 %collective-permute-start.3 = (bf16[4,16512]{1,0:T(4,128)(2,1)}, bf16[4,16512]{1,0:T(4,128)(2,1)S(1)}, u32[]{:S(2)}, u32[]{:S(2)}) collective-permute-start(bf16[4,16512]{1,0:T(4,128)(2,1)} %shard_map.28), channel_id=1, source_target_pairs={{0,8},{4,12},{8,16},{12,20},{16,24},{20,28},{24,0},{28,4},{1,9},{5... | collective-permute-start | bytes 396296 | tf_op jit(solution)/shard_map/ppermute | solution.py:198
  9.8 2.4 %collective-permute-start.2 = (bf16[4,16512]{1,0:T(4,128)(2,1)}, bf16[4,16512]{1,0:T(4,128)(2,1)S(1)}, u32[]{:S(2)}, u32[]{:S(2)}) collective-permute-start(bf16[4,16512]{1,0:T(4,128)(2,1)} %shard_map.28), channel_id=1, source_target_pairs={{0,3},{1,0},{2,1},{3,2},{4,7},{5,4},{6,5},{7,6},{8,11},{9,8},{10,9... | collective-permute-start | bytes 396296 | tf_op jit(solution)/shard_map/ppermute | solution.py:198
  12.2 0.5 %collective-permute-start.1 = (bf16[4,16512]{1,0:T(4,128)(2,1)}, bf16[4,16512]{1,0:T(4,128)(2,1)S(1)}, u32[]{:S(2)}, u32[]{:S(2)}) collective-permute-start(bf16[4,16512]{1,0:T(4,128)(2,1)} %shard_map.28), channel_id=1, source_target_pairs={{0,2},{1,3},{2,0},{3,1},{4,6},{5,7},{6,4},{7,5},{8,10},{9,11},{10,... | collective-permute-start | bytes 396296 | tf_op jit(solution)/shard_map/ppermute | solution.py:198
  12.7 0.5 %fusion.9 = (f32[64,512]{1,0:T(8,128)S(1)}, f32[64,512]{1,0:T(8,128)S(1)}) fusion(s32[512]{0:T(512)S(1)} %iota_add_fusion), kind=kLoop, calls=%fused_computation.16 | loop fusion | flops 294912 | bytes 264192 | tf_op jit(solution)/shard_map/cos | solution.py:82
  13.3 0.3 fusion.16
  13.6 1.5 %multiply_convert_fusion.1 = (bf16[32,64,512]{2,1,0:T(8,128)(2,1)S(1)}, bf16[32,64,512]{2,1,0:T(8,128)(2,1)S(1)}) fusion(f32[64,512]{1,0:T(8,128)S(1)} %get-tuple-element.18, f32[32,512]{1,0:T(8,128)S(1)} %get-tuple-element.16, f32[64,512]{1,0:T(8,128)S(1)} %get-tuple-element.17, f32[32,512]{1,0:T(8,128)S(1)} %get-tuple-element.15), kind=kLoop, calls=%fused_computation.2 | loop fusion | flops 10485760 | bytes 4587520 | tf_op jit(solution)/shard_map/convert_element_type | solution.py:86
  15.2 0.0 collective-permute-done.5
  15.2 0.0 copy-done.2
  15.2 0.6 %collective-permute-start = (bf16[4,16512]{1,0:T(4,128)(2,1)S(1)}, bf16[4,16512]{1,0:T(4,128)(2,1)S(1)}, u32[]{:S(2)}, u32[]{:S(2)}) collective-permute-start(bf16[4,16512]{1,0:T(4,128)(2,1)S(1)} %copy-done.2), channel_id=1, source_target_pairs={{0,1},{1,2},{2,3},{3,0},{4,5},{5,6},{6,7},{7,4},{8,9},{9,10},{10,1... | collective-permute-start | bytes 396296 | tf_op jit(solution)/shard_map/ppermute | solution.py:198
  15.8 2.3 %pad_maximum_fusion = bf16[2,2048,512]{2,1,0:T(8,128)(2,1)} fusion(bf16[1,2048,512]{2,1,0:T(8,128)(2,1)S(1)} %bitcast.16, bf16[1,2048,512]{2,1,0:T(8,128)(2,1)S(1)} %bitcast.15), kind=kLoop, calls=%fused_computation | loop fusion | flops 2097152 | bytes 8388608 | tf_op jit(solution)/shard_map/stack | solution.py:88
  18.2 2.1 %collective-permute-done.4 = bf16[4,16512]{1,0:T(4,128)(2,1)S(1)} collective-permute-done((bf16[4,16512]{1,0:T(4,128)(2,1)}, bf16[4,16512]{1,0:T(4,128)(2,1)S(1)}, u32[]{:S(2)}, u32[]{:S(2)}) %collective-permute-start.4) | collective-permute-done | bytes 132128 | tf_op jit(solution)/shard_map/ppermute | solution.py:198
  20.3 0.0 collective-permute-done.3
  20.3 0.0 collective-permute-done.2
  20.3 0.0 collective-permute-done.1
  20.3 0.9 %collective-permute-done = bf16[4,16512]{1,0:T(4,128)(2,1)S(1)} collective-permute-done((bf16[4,16512]{1,0:T(4,128)(2,1)S(1)}, bf16[4,16512]{1,0:T(4,128)(2,1)S(1)}, u32[]{:S(2)}, u32[]{:S(2)}) %collective-permute-start) | collective-permute-done | bytes 132128 | tf_op jit(solution)/shard_map/ppermute | solution.py:198
  21.1 1.7 %fusion.3 = (bf16[4,4,16512]{2,1,0:T(4,128)(2,1)S(1)}, bf16[4,4,16512]{2,1,0:T(4,128)(2,1)}) fusion(bf16[1,4,16512]{2,1,0:T(4,128)(2,1)S(1)} %bitcast.17, bf16[1,4,16512]{2,1,0:T(4,128)(2,1)S(1)} %bitcast.18, bf16[1,4,16512]{2,1,0:T(4,128)(2,1)S(1)} %bitcast.19, bf16[1,4,16512]{2,1,0:T(4,128)(2,1)S(1)} %bitcast.20, bf16[1,4,16512]{2,1,0:T(4,128)(2,1)S(1)} %bitcast.21, ...), kind=kLoop, calls=%fused_computation.8 | loop fusion | flops 1585152 | bytes 1981440 | tf_op jit(solution)/shard_map/stack | solution.py:199
  22.8 0.0 copy-start
  22.8 0.0 collective-permute-start.6
  22.8 0.7 %pad_add_fusion.place_ref = s32[3]{0:T(128)} fusion(s32[1]{0:T(128)} %bitcast.2, s32[1]{0:T(128)} %bitcast.1, s32[1]{0:T(128)} %bitcast), kind=kLoop, calls=%fused_computation.28 | loop fusion | flops 6 | bytes 24 | tf_op jit(solution)/shard_map/stack | solution.py:211
  23.5 1.2 %collective-permute-done.6.sib_ref = bf16[4,4,16512]{2,1,0:T(4,128)(2,1)S(1)} collective-permute-done((bf16[4,4,16512]{2,1,0:T(4,128)(2,1)S(1)}, bf16[4,4,16512]{2,1,0:T(4,128)(2,1)S(1)}, u32[]{:S(2)}, u32[]{:S(2)}) %collective-permute-start.6) | collective-permute-done | bytes 528416 | tf_op jit(solution)/shard_map/ppermute | solution.py:209
  24.7 0.0 copy-done
  24.7 0.0 copy-start.1
  24.8 0.8 %copy-done.1 = bf16[4,4,16512]{2,1,0:T(4,128)(2,1)} copy-done((bf16[4,4,16512]{2,1,0:T(4,128)(2,1)}, bf16[4,4,16512]{2,1,0:T(4,128)(2,1)S(1)}, u32[]{:S(2)}) %copy-start.1) | copy-done | bytes 528408
  25.6 12.7 %shard_map.29 = bf16[512,512]{1,0:T(8,128)(2,1)} custom-call(s32[3]{0:T(128)} %pad_add_fusion.place_ref, bf16[4,4,16512]{2,1,0:T(4,128)(2,1)} %get-tuple-element.8.rec_ref, bf16[4,4,16512]{2,1,0:T(4,128)(2,1)} %copy-done, bf16[4,4,16512]{2,1,0:T(4,128)(2,1)} %copy-done.1, bf16[4096,512]{1,0:T(8,128)(2,1)} %bitcast.14), custom_call_target="tpu_custom_call" | custom-call | tf_op jit(solution)/shard_map/pallas_call | solution.py:168
  (2 shorter events, 0.0 us)
Async XLA Ops:
  3.7 11.5 %copy-start.2 = (bf16[4,16512]{1,0:T(4,128)(2,1)S(1)}, bf16[4,16512]{1,0:T(4,128)(2,1)}, u32[]{:S(2)}) copy-start(bf16[4,16512]{1,0:T(4,128)(2,1)} %shard_map.28) | copy-start | bytes 396292
  3.7 11.5 %collective-permute-start.5 = (bf16[4,16512]{1,0:T(4,128)(2,1)}, bf16[4,16512]{1,0:T(4,128)(2,1)S(1)}, u32[]{:S(2)}, u32[]{:S(2)}) collective-permute-start(bf16[4,16512]{1,0:T(4,128)(2,1)} %shard_map.28), channel_id=1, source_target_pairs={{0,24},{4,28},{8,0},{12,4},{16,8},{20,12},{24,16},{28,20},{1,25},{... | collective-permute-start | bytes 396296 | tf_op jit(solution)/shard_map/ppermute | solution.py:198
  8.8 11.5 %collective-permute-start.4 = (bf16[4,16512]{1,0:T(4,128)(2,1)}, bf16[4,16512]{1,0:T(4,128)(2,1)S(1)}, u32[]{:S(2)}, u32[]{:S(2)}) collective-permute-start(bf16[4,16512]{1,0:T(4,128)(2,1)} %shard_map.28), channel_id=1, source_target_pairs={{0,16},{4,20},{8,24},{12,28},{16,0},{20,4},{24,8},{28,12},{1,17},{... | collective-permute-start | bytes 396296 | tf_op jit(solution)/shard_map/ppermute | solution.py:198
  8.8 11.5 %collective-permute-start.3 = (bf16[4,16512]{1,0:T(4,128)(2,1)}, bf16[4,16512]{1,0:T(4,128)(2,1)S(1)}, u32[]{:S(2)}, u32[]{:S(2)}) collective-permute-start(bf16[4,16512]{1,0:T(4,128)(2,1)} %shard_map.28), channel_id=1, source_target_pairs={{0,8},{4,12},{8,16},{12,20},{16,24},{20,28},{24,0},{28,4},{1,9},{5... | collective-permute-start | bytes 396296 | tf_op jit(solution)/shard_map/ppermute | solution.py:198
  9.8 10.5 %collective-permute-start.2 = (bf16[4,16512]{1,0:T(4,128)(2,1)}, bf16[4,16512]{1,0:T(4,128)(2,1)S(1)}, u32[]{:S(2)}, u32[]{:S(2)}) collective-permute-start(bf16[4,16512]{1,0:T(4,128)(2,1)} %shard_map.28), channel_id=1, source_target_pairs={{0,3},{1,0},{2,1},{3,2},{4,7},{5,4},{6,5},{7,6},{8,11},{9,8},{10,9... | collective-permute-start | bytes 396296 | tf_op jit(solution)/shard_map/ppermute | solution.py:198
  12.2 8.0 %collective-permute-start.1 = (bf16[4,16512]{1,0:T(4,128)(2,1)}, bf16[4,16512]{1,0:T(4,128)(2,1)S(1)}, u32[]{:S(2)}, u32[]{:S(2)}) collective-permute-start(bf16[4,16512]{1,0:T(4,128)(2,1)} %shard_map.28), channel_id=1, source_target_pairs={{0,2},{1,3},{2,0},{3,1},{4,6},{5,7},{6,4},{7,5},{8,10},{9,11},{10,... | collective-permute-start | bytes 396296 | tf_op jit(solution)/shard_map/ppermute | solution.py:198
  15.2 5.9 %collective-permute-start = (bf16[4,16512]{1,0:T(4,128)(2,1)S(1)}, bf16[4,16512]{1,0:T(4,128)(2,1)S(1)}, u32[]{:S(2)}, u32[]{:S(2)}) collective-permute-start(bf16[4,16512]{1,0:T(4,128)(2,1)S(1)} %copy-done.2), channel_id=1, source_target_pairs={{0,1},{1,2},{2,3},{3,0},{4,5},{5,6},{6,7},{7,4},{8,9},{9,10},{10,1... | collective-permute-start | bytes 396296 | tf_op jit(solution)/shard_map/ppermute | solution.py:198
  22.8 1.9 %copy-start = (bf16[4,4,16512]{2,1,0:T(4,128)(2,1)}, bf16[4,4,16512]{2,1,0:T(4,128)(2,1)S(1)}, u32[]{:S(2)}) copy-start(bf16[4,4,16512]{2,1,0:T(4,128)(2,1)S(1)} %get-tuple-element.9.own_ref) | copy-start | bytes 1585156
  22.8 1.9 %collective-permute-start.6 = (bf16[4,4,16512]{2,1,0:T(4,128)(2,1)S(1)}, bf16[4,4,16512]{2,1,0:T(4,128)(2,1)S(1)}, u32[]{:S(2)}, u32[]{:S(2)}) collective-permute-start(bf16[4,4,16512]{2,1,0:T(4,128)(2,1)S(1)} %get-tuple-element.9.own_ref), channel_id=1, source_target_pairs={{0,4},{4,0},{8,12},{12,8},{16,20},{20,16},{24,28},{28,24},{1,5},{5... | collective-permute-start | bytes 1585160 | tf_op jit(solution)/shard_map/ppermute | solution.py:209
  24.7 0.8 %copy-start.1 = (bf16[4,4,16512]{2,1,0:T(4,128)(2,1)}, bf16[4,4,16512]{2,1,0:T(4,128)(2,1)S(1)}, u32[]{:S(2)}) copy-start(bf16[4,4,16512]{2,1,0:T(4,128)(2,1)S(1)} %collective-permute-done.6.sib_ref) | copy-start | bytes 1585156

commit v8 on v7

--- a/solution.py
+++ b/solution.py
@@ -99,20 +99,28 @@
     body = windows * 2 * freqs
     width = 2 * freqs
 
-    def place(block, dst, values, tails):
+    def place(block, dst, values, tails, source_side):
         rows = slice(dst * per, (dst + 1) * per)
         mask = block[:, body : body + PAD].astype(jnp.float32)
         tails[rows, :] = mask
         for w in range(windows):
-            cols = slice(w * width, (w + 1) * width)
-            values[rows, cols] = block[:, cols].astype(jnp.float32) * mask[:, w : w + 1]
+            m = mask[:, w : w + 1]
+            a = block[:, w * width : w * width + freqs].astype(jnp.float32) * m
+            b = block[:, w * width + freqs : (w + 1) * width].astype(jnp.float32) * m
+            if source_side:
+                terms = (a, b - a, a + b)
+            else:
+                terms = (a - b, a, b)
+            for t, term in enumerate(terms):
+                start = (3 * w + t) * freqs
+                values[rows, start : start + freqs] = term
 
     @pl.when(step == 0)
     def _():
         rcv_index, chip, core = place_ref[0], place_ref[1], place_ref[2]
         for dst in range(rcv_count):
             k = (rcv_index - dst + rcv_count) % rcv_count
-            place(rec_ref[k], dst, recf, rtails)
+            place(rec_ref[k], dst, recf, rtails, False)
         for zz in range(chips):
             k = (chip - zz + chips) % chips
             own_block = own_ref[k]
@@ -120,7 +128,7 @@
             for cc in range(2):
                 same = core == cc
                 block = jnp.where(same, own_block, sib_block)
-                place(block, zz * 2 + cc, srcf, stails)
+                place(block, zz * 2 + cc, srcf, stails, True)
 
     smask = stails[...]
 
@@ -131,21 +139,24 @@
         inverse = 1.0 / jnp.maximum(count, 1.0)
         rows = pl.ds(pl.multiple_of(j * nsrc, nsrc), nsrc)
         for c in range(freqs // chunk):
-            real = jnp.zeros((nsrc, chunk), jnp.float32)
-            imag = jnp.zeros((nsrc, chunk), jnp.float32)
+            k1 = jnp.zeros((nsrc, chunk), jnp.float32)
+            k2 = jnp.zeros((nsrc, chunk), jnp.float32)
+            k3 = jnp.zeros((nsrc, chunk), jnp.float32)
             for w in range(windows):
-                a0 = w * width + c * chunk
-                b0 = a0 + freqs
-                sa = srcf[:, a0 : a0 + chunk]
-                sb = srcf[:, b0 : b0 + chunk]
-                ra = recf[pl.ds(i, 1), a0 : a0 + chunk]
-                rb = recf[pl.ds(i, 1), b0 : b0 + chunk]
-                real = real + (sa * ra + sb * rb)
-                imag = imag + (sb * ra - sa * rb)
-            cross[rows, c * chunk : (c + 1) * chunk] = (real * inverse).astype(jnp.bfloat16)
-            cross[rows, freqs + c * chunk : freqs + (c + 1) * chunk] = (imag * inverse).astype(
-                jnp.bfloat16
-            )
+                at = [(3 * w + t) * freqs + c * chunk for t in range(3)]
+                sa = srcf[:, at[0] : at[0] + chunk]
+                sd = srcf[:, at[1] : at[1] + chunk]
+                se = srcf[:, at[2] : at[2] + chunk]
+                ru = recf[pl.ds(i, 1), at[0] : at[0] + chunk]
+                ra = recf[pl.ds(i, 1), at[1] : at[1] + chunk]
+                rb = recf[pl.ds(i, 1), at[2] : at[2] + chunk]
+                k1 = k1 + sa * ru
+                k2 = k2 + ra * sd
+                k3 = k3 + rb * se
+            real = (k1 + k3) * inverse
+            imag = (k1 + k2) * inverse
+            cross[rows, c * chunk : (c + 1) * chunk] = real.astype(jnp.bfloat16)
+            cross[rows, freqs + c * chunk : freqs + (c + 1) * chunk] = imag.astype(jnp.bfloat16)
         return carry
 
     lax.fori_loop(0, group, per_receiver, 0)
@@ -178,8 +189,8 @@
             ],
             out_specs=pl.BlockSpec((group * nsrc, lags), lambda g, p: (g, 0)),
             scratch_shapes=[
-                pltpu.VMEM((nsrc, windows * 2 * freqs), jnp.float32),
-                pltpu.VMEM((nrec, windows * 2 * freqs), jnp.float32),
+                pltpu.VMEM((nsrc, windows * 3 * freqs), jnp.float32),
+                pltpu.VMEM((nrec, windows * 3 * freqs), jnp.float32),
                 pltpu.VMEM((nrec, PAD), jnp.float32),
                 pltpu.VMEM((nsrc, PAD), jnp.float32),
                 pltpu.VMEM((group * nsrc, 2 * freqs), jnp.bfloat16),

time: 38.4 us -> 38.4 us (level)
  no operation moved by 1% of the time
where the time goes in v8:
time: 38.4 us; the launch traced here: 38.2 us
  Pallas kernels  15.1 us (39%)
  starting transfers between devices  9.66 us (25%)
  other arithmetic  7.15 us (19%)
  waiting for transfers between devices  4.17 us (11%)
  local copies, waits for them, and re-layouts  2.08 us (5%)
    pallas_call x1, Pallas kernels, correlate(): pl.pallas_call(kernel, grid_spec=pltpu.PrefetchScalarGridSpec(num_scalar_...  12.7 us
    ppermute x6, starting transfers between devices, shifted(): parts.append(lax.ppermute(x, axis, perm=pairs))  9.66 us
    ppermute x6, waiting for transfers between devices, shifted(): parts.append(lax.ppermute(x, axis, perm=pairs))  2.98 us
    pallas_call x1, Pallas kernels, whiten_pack(): pl.pallas_call(kernel, out_shape=jax.ShapeDtypeStruct((channels, windows...  2.47 us
    another operation x1, other arithmetic, lag_table(): jnp.stack([cosines, sines], axis=0).reshape(2 * freq_count, lag_count)  2.31 us
    another operation x1, other arithmetic, shifted(): return jnp.stack(parts)  1.69 us
    convert_element_type x1, other arithmetic, lag_table(): cosines = cosines.reshape(freq_count, lag_count).astype(jnp.bfloat16)  1.54 us
    pad x1, local copies, waits for them, and re-layouts, whiten_pack(): tail = jnp.pad(valid, ((0, 0), (0, PAD - windows)))  1.25 us
  transfers between devices with their start and end apart: 7, of which 3 were waited for; matrix products, arithmetic and copies ran while one was open for 14% of the time, Pallas kernels for 0%

profile of v8, /device:TPU:0, one launch (start us, length us, event | category | flops | bytes accessed | tf_op | source)
XLA Modules:
  0.0 38.2 jit_solution(5386535878770824498)
XLA Ops:
  0.0 1.2 %pad.4.v_ref = s32[4,128]{1,0:T(4,128)} pad(s32[4,4]{1,0:T(4,128)} %param.3, s32[]{:T(128)} %constant.54.clone.1), padding=0_0x0_124 | pad | bytes 2116 | tf_op jit(solution)/shard_map/jit(_pad)/pad | solution.py:64
  1.2 2.5 %shard_map.28 = bf16[4,16512]{1,0:T(4,128)(2,1)} custom-call(bf16[4,4,2,2048]{3,2,1,0:T(2,128)(2,1)} %x_ref.1, s32[4,128]{1,0:T(4,128)} %pad.4.v_ref), custom_call_target="tpu_custom_call" | custom-call | tf_op jit(solution)/shard_map/pallas_call | solution.py:66
  3.7 0.0 copy-start.2
  3.7 5.0 %collective-permute-start.5 = (bf16[4,16512]{1,0:T(4,128)(2,1)}, bf16[4,16512]{1,0:T(4,128)(2,1)S(1)}, u32[]{:S(2)}, u32[]{:S(2)}) collective-permute-start(bf16[4,16512]{1,0:T(4,128)(2,1)} %shard_map.28), channel_id=1, source_target_pairs={{0,24},{4,28},{8,0},{12,4},{16,8},{20,12},{24,16},{28,20},{1,25},{... | collective-permute-start | bytes 396296 | tf_op jit(solution)/shard_map/ppermute | solution.py:209
  8.8 0.0 collective-permute-start.4
  8.8 1.0 %collective-permute-start.3 = (bf16[4,16512]{1,0:T(4,128)(2,1)}, bf16[4,16512]{1,0:T(4,128)(2,1)S(1)}, u32[]{:S(2)}, u32[]{:S(2)}) collective-permute-start(bf16[4,16512]{1,0:T(4,128)(2,1)} %shard_map.28), channel_id=1, source_target_pairs={{0,8},{4,12},{8,16},{12,20},{16,24},{20,28},{24,0},{28,4},{1,9},{5... | collective-permute-start | bytes 396296 | tf_op jit(solution)/shard_map/ppermute | solution.py:209
  9.8 2.4 %collective-permute-start.2 = (bf16[4,16512]{1,0:T(4,128)(2,1)}, bf16[4,16512]{1,0:T(4,128)(2,1)S(1)}, u32[]{:S(2)}, u32[]{:S(2)}) collective-permute-start(bf16[4,16512]{1,0:T(4,128)(2,1)} %shard_map.28), channel_id=1, source_target_pairs={{0,3},{1,0},{2,1},{3,2},{4,7},{5,4},{6,5},{7,6},{8,11},{9,8},{10,9... | collective-permute-start | bytes 396296 | tf_op jit(solution)/shard_map/ppermute | solution.py:209
  12.2 0.5 %collective-permute-start.1 = (bf16[4,16512]{1,0:T(4,128)(2,1)}, bf16[4,16512]{1,0:T(4,128)(2,1)S(1)}, u32[]{:S(2)}, u32[]{:S(2)}) collective-permute-start(bf16[4,16512]{1,0:T(4,128)(2,1)} %shard_map.28), channel_id=1, source_target_pairs={{0,2},{1,3},{2,0},{3,1},{4,6},{5,7},{6,4},{7,5},{8,10},{9,11},{10,... | collective-permute-start | bytes 396296 | tf_op jit(solution)/shard_map/ppermute | solution.py:209
  12.7 0.5 %fusion.9 = (f32[64,512]{1,0:T(8,128)S(1)}, f32[64,512]{1,0:T(8,128)S(1)}) fusion(s32[512]{0:T(512)S(1)} %iota_add_fusion), kind=kLoop, calls=%fused_computation.16 | loop fusion | flops 294912 | bytes 264192 | tf_op jit(solution)/shard_map/cos | solution.py:82
  13.3 0.3 fusion.16
  13.6 1.5 %multiply_convert_fusion.1 = (bf16[32,64,512]{2,1,0:T(8,128)(2,1)S(1)}, bf16[32,64,512]{2,1,0:T(8,128)(2,1)S(1)}) fusion(f32[64,512]{1,0:T(8,128)S(1)} %get-tuple-element.18, f32[32,512]{1,0:T(8,128)S(1)} %get-tuple-element.16, f32[64,512]{1,0:T(8,128)S(1)} %get-tuple-element.17, f32[32,512]{1,0:T(8,128)S(1)} %get-tuple-element.15), kind=kLoop, calls=%fused_computation.2 | loop fusion | flops 10485760 | bytes 4587520 | tf_op jit(solution)/shard_map/convert_element_type | solution.py:86
  15.2 0.0 collective-permute-done.5
  15.2 0.0 copy-done.2
  15.2 0.6 %collective-permute-start = (bf16[4,16512]{1,0:T(4,128)(2,1)S(1)}, bf16[4,16512]{1,0:T(4,128)(2,1)S(1)}, u32[]{:S(2)}, u32[]{:S(2)}) collective-permute-start(bf16[4,16512]{1,0:T(4,128)(2,1)S(1)} %copy-done.2), channel_id=1, source_target_pairs={{0,1},{1,2},{2,3},{3,0},{4,5},{5,6},{6,7},{7,4},{8,9},{9,10},{10,1... | collective-permute-start | bytes 396296 | tf_op jit(solution)/shard_map/ppermute | solution.py:209
  15.8 2.3 %pad_maximum_fusion = bf16[2,2048,512]{2,1,0:T(8,128)(2,1)} fusion(bf16[1,2048,512]{2,1,0:T(8,128)(2,1)S(1)} %bitcast.16, bf16[1,2048,512]{2,1,0:T(8,128)(2,1)S(1)} %bitcast.15), kind=kLoop, calls=%fused_computation | loop fusion | flops 2097152 | bytes 8388608 | tf_op jit(solution)/shard_map/stack | solution.py:88
  18.2 2.1 %collective-permute-done.4 = bf16[4,16512]{1,0:T(4,128)(2,1)S(1)} collective-permute-done((bf16[4,16512]{1,0:T(4,128)(2,1)}, bf16[4,16512]{1,0:T(4,128)(2,1)S(1)}, u32[]{:S(2)}, u32[]{:S(2)}) %collective-permute-start.4) | collective-permute-done | bytes 132128 | tf_op jit(solution)/shard_map/ppermute | solution.py:209
  20.3 0.0 collective-permute-done.3
  20.3 0.0 collective-permute-done.2
  20.3 0.0 collective-permute-done.1
  20.3 0.9 %collective-permute-done = bf16[4,16512]{1,0:T(4,128)(2,1)S(1)} collective-permute-done((bf16[4,16512]{1,0:T(4,128)(2,1)S(1)}, bf16[4,16512]{1,0:T(4,128)(2,1)S(1)}, u32[]{:S(2)}, u32[]{:S(2)}) %collective-permute-start) | collective-permute-done | bytes 132128 | tf_op jit(solution)/shard_map/ppermute | solution.py:209
  21.1 1.7 %fusion.3 = (bf16[4,4,16512]{2,1,0:T(4,128)(2,1)S(1)}, bf16[4,4,16512]{2,1,0:T(4,128)(2,1)}) fusion(bf16[1,4,16512]{2,1,0:T(4,128)(2,1)S(1)} %bitcast.17, bf16[1,4,16512]{2,1,0:T(4,128)(2,1)S(1)} %bitcast.18, bf16[1,4,16512]{2,1,0:T(4,128)(2,1)S(1)} %bitcast.19, bf16[1,4,16512]{2,1,0:T(4,128)(2,1)S(1)} %bitcast.20, bf16[1,4,16512]{2,1,0:T(4,128)(2,1)S(1)} %bitcast.21, ...), kind=kLoop, calls=%fused_computation.8 | loop fusion | flops 1585152 | bytes 1981440 | tf_op jit(solution)/shard_map/stack | solution.py:210
  22.8 0.0 copy-start
  22.8 0.0 collective-permute-start.6
  22.8 0.7 %pad_add_fusion.place_ref = s32[3]{0:T(128)} fusion(s32[1]{0:T(128)} %bitcast.2, s32[1]{0:T(128)} %bitcast.1, s32[1]{0:T(128)} %bitcast), kind=kLoop, calls=%fused_computation.28 | loop fusion | flops 6 | bytes 24 | tf_op jit(solution)/shard_map/stack | solution.py:222
  23.5 1.2 %collective-permute-done.6.sib_ref = bf16[4,4,16512]{2,1,0:T(4,128)(2,1)S(1)} collective-permute-done((bf16[4,4,16512]{2,1,0:T(4,128)(2,1)S(1)}, bf16[4,4,16512]{2,1,0:T(4,128)(2,1)S(1)}, u32[]{:S(2)}, u32[]{:S(2)}) %collective-permute-start.6) | collective-permute-done | bytes 528416 | tf_op jit(solution)/shard_map/ppermute | solution.py:220
  24.7 0.0 copy-done
  24.7 0.0 copy-start.1
  24.8 0.8 %copy-done.1 = bf16[4,4,16512]{2,1,0:T(4,128)(2,1)} copy-done((bf16[4,4,16512]{2,1,0:T(4,128)(2,1)}, bf16[4,4,16512]{2,1,0:T(4,128)(2,1)S(1)}, u32[]{:S(2)}) %copy-start.1) | copy-done | bytes 528408
  25.6 12.7 %shard_map.29 = bf16[512,512]{1,0:T(8,128)(2,1)} custom-call(s32[3]{0:T(128)} %pad_add_fusion.place_ref, bf16[4,4,16512]{2,1,0:T(4,128)(2,1)} %get-tuple-element.8.rec_ref, bf16[4,4,16512]{2,1,0:T(4,128)(2,1)} %copy-done, bf16[4,4,16512]{2,1,0:T(4,128)(2,1)} %copy-done.1, bf16[4096,512]{1,0:T(8,128)(2,1)} %bitcast.14), custom_call_target="tpu_custom_call" | custom-call | tf_op jit(solution)/shard_map/pallas_call | solution.py:179
  (2 shorter events, 0.0 us)
Async XLA Ops:
  3.7 11.5 %copy-start.2 = (bf16[4,16512]{1,0:T(4,128)(2,1)S(1)}, bf16[4,16512]{1,0:T(4,128)(2,1)}, u32[]{:S(2)}) copy-start(bf16[4,16512]{1,0:T(4,128)(2,1)} %shard_map.28) | copy-start | bytes 396292
  3.7 11.5 %collective-permute-start.5 = (bf16[4,16512]{1,0:T(4,128)(2,1)}, bf16[4,16512]{1,0:T(4,128)(2,1)S(1)}, u32[]{:S(2)}, u32[]{:S(2)}) collective-permute-start(bf16[4,16512]{1,0:T(4,128)(2,1)} %shard_map.28), channel_id=1, source_target_pairs={{0,24},{4,28},{8,0},{12,4},{16,8},{20,12},{24,16},{28,20},{1,25},{... | collective-permute-start | bytes 396296 | tf_op jit(solution)/shard_map/ppermute | solution.py:209
  8.8 11.5 %collective-permute-start.4 = (bf16[4,16512]{1,0:T(4,128)(2,1)}, bf16[4,16512]{1,0:T(4,128)(2,1)S(1)}, u32[]{:S(2)}, u32[]{:S(2)}) collective-permute-start(bf16[4,16512]{1,0:T(4,128)(2,1)} %shard_map.28), channel_id=1, source_target_pairs={{0,16},{4,20},{8,24},{12,28},{16,0},{20,4},{24,8},{28,12},{1,17},{... | collective-permute-start | bytes 396296 | tf_op jit(solution)/shard_map/ppermute | solution.py:209
  8.8 11.5 %collective-permute-start.3 = (bf16[4,16512]{1,0:T(4,128)(2,1)}, bf16[4,16512]{1,0:T(4,128)(2,1)S(1)}, u32[]{:S(2)}, u32[]{:S(2)}) collective-permute-start(bf16[4,16512]{1,0:T(4,128)(2,1)} %shard_map.28), channel_id=1, source_target_pairs={{0,8},{4,12},{8,16},{12,20},{16,24},{20,28},{24,0},{28,4},{1,9},{5... | collective-permute-start | bytes 396296 | tf_op jit(solution)/shard_map/ppermute | solution.py:209
  9.8 10.5 %collective-permute-start.2 = (bf16[4,16512]{1,0:T(4,128)(2,1)}, bf16[4,16512]{1,0:T(4,128)(2,1)S(1)}, u32[]{:S(2)}, u32[]{:S(2)}) collective-permute-start(bf16[4,16512]{1,0:T(4,128)(2,1)} %shard_map.28), channel_id=1, source_target_pairs={{0,3},{1,0},{2,1},{3,2},{4,7},{5,4},{6,5},{7,6},{8,11},{9,8},{10,9... | collective-permute-start | bytes 396296 | tf_op jit(solution)/shard_map/ppermute | solution.py:209
  12.2 8.0 %collective-permute-start.1 = (bf16[4,16512]{1,0:T(4,128)(2,1)}, bf16[4,16512]{1,0:T(4,128)(2,1)S(1)}, u32[]{:S(2)}, u32[]{:S(2)}) collective-permute-start(bf16[4,16512]{1,0:T(4,128)(2,1)} %shard_map.28), channel_id=1, source_target_pairs={{0,2},{1,3},{2,0},{3,1},{4,6},{5,7},{6,4},{7,5},{8,10},{9,11},{10,... | collective-permute-start | bytes 396296 | tf_op jit(solution)/shard_map/ppermute | solution.py:209
  15.2 5.9 %collective-permute-start = (bf16[4,16512]{1,0:T(4,128)(2,1)S(1)}, bf16[4,16512]{1,0:T(4,128)(2,1)S(1)}, u32[]{:S(2)}, u32[]{:S(2)}) collective-permute-start(bf16[4,16512]{1,0:T(4,128)(2,1)S(1)} %copy-done.2), channel_id=1, source_target_pairs={{0,1},{1,2},{2,3},{3,0},{4,5},{5,6},{6,7},{7,4},{8,9},{9,10},{10,1... | collective-permute-start | bytes 396296 | tf_op jit(solution)/shard_map/ppermute | solution.py:209
  22.8 1.9 %copy-start = (bf16[4,4,16512]{2,1,0:T(4,128)(2,1)}, bf16[4,4,16512]{2,1,0:T(4,128)(2,1)S(1)}, u32[]{:S(2)}) copy-start(bf16[4,4,16512]{2,1,0:T(4,128)(2,1)S(1)} %get-tuple-element.9.own_ref) | copy-start | bytes 1585156
  22.8 1.9 %collective-permute-start.6 = (bf16[4,4,16512]{2,1,0:T(4,128)(2,1)S(1)}, bf16[4,4,16512]{2,1,0:T(4,128)(2,1)S(1)}, u32[]{:S(2)}, u32[]{:S(2)}) collective-permute-start(bf16[4,4,16512]{2,1,0:T(4,128)(2,1)S(1)} %get-tuple-element.9.own_ref), channel_id=1, source_target_pairs={{0,4},{4,0},{8,12},{12,8},{16,20},{20,16},{24,28},{28,24},{1,5},{5... | collective-permute-start | bytes 1585160 | tf_op jit(solution)/shard_map/ppermute | solution.py:220
  24.7 0.8 %copy-start.1 = (bf16[4,4,16512]{2,1,0:T(4,128)(2,1)}, bf16[4,4,16512]{2,1,0:T(4,128)(2,1)S(1)}, u32[]{:S(2)}) copy-start(bf16[4,4,16512]{2,1,0:T(4,128)(2,1)S(1)} %collective-permute-done.6.sib_ref) | copy-start | bytes 1585156

commit v9 on v8

--- a/solution.py
+++ b/solution.py
@@ -56,18 +56,22 @@
                 jnp.bfloat16
             )
     body = windows * width
-    out_ref[:, body : body + PAD] = v_ref[...].astype(jnp.float32).astype(jnp.bfloat16)
+    valid = v_ref[...].astype(jnp.float32)
+    lane = lax.broadcasted_iota(jnp.int32, (channels, PAD), 1)
+    tail = jnp.zeros((channels, PAD), jnp.float32)
+    for w in range(windows):
+        tail = jnp.where(lane == w, valid[:, w : w + 1], tail)
+    out_ref[:, body : body + PAD] = tail.astype(jnp.bfloat16)
 
 
 def whiten_pack(spectra, valid):
     channels, windows, _, freqs = spectra.shape
-    tail = jnp.pad(valid, ((0, 0), (0, PAD - windows)))
     kernel = functools.partial(whiten_kernel, channels=channels, windows=windows, freqs=freqs)
     return pl.pallas_call(
         kernel,
         out_shape=jax.ShapeDtypeStruct((channels, windows * 2 * freqs + PAD), jnp.bfloat16),
         scratch_shapes=[pltpu.VMEM((channels * windows, freqs), jnp.float32)],
-    )(spectra, tail)
+    )(spectra, valid)
 
 
 def lag_table(freq_count, lag_count):
@@ -89,8 +93,8 @@
 
 
 def cross_kernel(
-    place_ref, rec_ref, own_ref, sib_ref, tab_ref, out_ref, srcf, recf, rtails, stails, cross,
-    *, windows, freqs, group, chunk
+    place_ref, rec_ref, own_ref, sib_ref, tab_hbm, out_ref, srcf, recf, rtails, stails, cross,
+    tab_ref, tab_sem, *, windows, freqs, group, chunk
 ):
     step = pl.program_id(0)
     rcv_count, per = rec_ref.shape[0], rec_ref.shape[1]
@@ -114,6 +118,10 @@
             for t, term in enumerate(terms):
                 start = (3 * w + t) * freqs
                 values[rows, start : start + freqs] = term
+
+    @pl.when(step == 0)
+    def _():
+        pltpu.make_async_copy(tab_hbm, tab_ref, tab_sem).start()
 
     @pl.when(step == 0)
     def _():
@@ -160,6 +168,11 @@
         return carry
 
     lax.fori_loop(0, group, per_receiver, 0)
+
+    @pl.when(step == 0)
+    def _():
+        pltpu.make_async_copy(tab_hbm, tab_ref, tab_sem).wait()
+
     out_ref[...] = jnp.dot(
         cross[...], tab_ref[...], preferred_element_type=jnp.float32
     ).astype(jnp.bfloat16)
@@ -185,7 +198,7 @@
                 pl.BlockSpec(rec_stack.shape, full3),
                 pl.BlockSpec(own_stack.shape, full3),
                 pl.BlockSpec(sib_stack.shape, full3),
-                pl.BlockSpec(table.shape, lambda g, p: (0, 0)),
+                pl.BlockSpec(memory_space=pl.ANY),
             ],
             out_specs=pl.BlockSpec((group * nsrc, lags), lambda g, p: (g, 0)),
             scratch_shapes=[
@@ -194,6 +207,8 @@
                 pltpu.VMEM((nrec, PAD), jnp.float32),
                 pltpu.VMEM((nsrc, PAD), jnp.float32),
                 pltpu.VMEM((group * nsrc, 2 * freqs), jnp.bfloat16),
+                pltpu.VMEM(table.shape, jnp.bfloat16),
+                pltpu.SemaphoreType.DMA(()),
             ],
         ),
         out_shape=jax.ShapeDtypeStruct((nrec * nsrc, lags), jnp.bfloat16),

time: 38.4 us -> 35.8 us (0.932)
  Pallas kernels: 15.1 us -> 13.8 us
  local copies, waits for them, and re-layouts: 2.08 us -> 0.84 us
    pallas_call x1, Pallas kernels: 12.7 us -> 11.3 us  [correlate(): pl.pallas_call(kernel, grid_spec=pltpu.PrefetchScalarGridSpec(num_scalar_...]
    pad x1 -> x0, local copies, waits for them, and re-layouts: 1.25 us -> none  [whiten_pack(): tail = jnp.pad(valid, ((0, 0), (0, PAD - windows)))]
  transfers between devices with their start and end apart: 7 -> 7, of which waited for: 3 -> 3; matrix products, arithmetic and copies ran while one was open for 14% -> 15% of each run, Pallas kernels for 0% -> 0%
where the time goes in v9:
time: 35.8 us; the launch traced here: 35.7 us
  Pallas kernels  13.8 us (39%)
  starting transfers between devices  9.66 us (27%)
  other arithmetic  7.15 us (20%)
  waiting for transfers between devices  4.17 us (12%)
  local copies, waits for them, and re-layouts  0.84 us (2%)
    pallas_call x1, Pallas kernels, correlate(): pl.pallas_call(kernel, grid_spec=pltpu.PrefetchScalarGridSpec(num_scalar_...  11.3 us
    ppermute x6, starting transfers between devices, shifted(): parts.append(lax.ppermute(x, axis, perm=pairs))  9.66 us
    ppermute x6, waiting for transfers between devices, shifted(): parts.append(lax.ppermute(x, axis, perm=pairs))  2.98 us
    pallas_call x1, Pallas kernels, whiten_pack(): pl.pallas_call(kernel, out_shape=jax.ShapeDtypeStruct((channels, windows...  2.47 us
    another operation x1, other arithmetic, lag_table(): jnp.stack([cosines, sines], axis=0).reshape(2 * freq_count, lag_count)  2.31 us
    another operation x1, other arithmetic, shifted(): return jnp.stack(parts)  1.69 us
    convert_element_type x1, other arithmetic, lag_table(): cosines = cosines.reshape(freq_count, lag_count).astype(jnp.bfloat16)  1.54 us
    ppermute x1, waiting for transfers between devices, local(): lax.ppermute(own_stack, 'src', perm=[(j, j ^ 1) for j in range(src_count)])  1.2 us
  transfers between devices with their start and end apart: 7, of which 3 were waited for; matrix products, arithmetic and copies ran while one was open for 15% of the time, Pallas kernels for 0%

profile of v9, /device:TPU:0, one launch (start us, length us, event | category | flops | bytes accessed | tf_op | source)
XLA Modules:
  0.0 35.7 jit_solution(3656460326168879305)
XLA Ops:
  0.0 2.5 %shard_map.28 = bf16[4,16512]{1,0:T(4,128)(2,1)} custom-call(bf16[4,4,2,2048]{3,2,1,0:T(2,128)(2,1)} %x_ref.1, s32[4,4]{1,0:T(4,128)} %v_ref.1), custom_call_target="tpu_custom_call" | custom-call | tf_op jit(solution)/shard_map/pallas_call | solution.py:70
  2.5 0.0 copy-start.2
  2.5 5.0 %collective-permute-start.5 = (bf16[4,16512]{1,0:T(4,128)(2,1)}, bf16[4,16512]{1,0:T(4,128)(2,1)S(1)}, u32[]{:S(2)}, u32[]{:S(2)}) collective-permute-start(bf16[4,16512]{1,0:T(4,128)(2,1)} %shard_map.28), channel_id=1, source_target_pairs={{0,24},{4,28},{8,0},{12,4},{16,8},{20,12},{24,16},{28,20},{1,25},{... | collective-permute-start | bytes 396296 | tf_op jit(solution)/shard_map/ppermute | solution.py:224
  7.5 0.0 collective-permute-start.4
  7.5 1.0 %collective-permute-start.3 = (bf16[4,16512]{1,0:T(4,128)(2,1)}, bf16[4,16512]{1,0:T(4,128)(2,1)S(1)}, u32[]{:S(2)}, u32[]{:S(2)}) collective-permute-start(bf16[4,16512]{1,0:T(4,128)(2,1)} %shard_map.28), channel_id=1, source_target_pairs={{0,8},{4,12},{8,16},{12,20},{16,24},{20,28},{24,0},{28,4},{1,9},{5... | collective-permute-start | bytes 396296 | tf_op jit(solution)/shard_map/ppermute | solution.py:224
  8.5 2.4 %collective-permute-start.2 = (bf16[4,16512]{1,0:T(4,128)(2,1)}, bf16[4,16512]{1,0:T(4,128)(2,1)S(1)}, u32[]{:S(2)}, u32[]{:S(2)}) collective-permute-start(bf16[4,16512]{1,0:T(4,128)(2,1)} %shard_map.28), channel_id=1, source_target_pairs={{0,3},{1,0},{2,1},{3,2},{4,7},{5,4},{6,5},{7,6},{8,11},{9,8},{10,9... | collective-permute-start | bytes 396296 | tf_op jit(solution)/shard_map/ppermute | solution.py:224
  11.0 0.5 %collective-permute-start.1 = (bf16[4,16512]{1,0:T(4,128)(2,1)}, bf16[4,16512]{1,0:T(4,128)(2,1)S(1)}, u32[]{:S(2)}, u32[]{:S(2)}) collective-permute-start(bf16[4,16512]{1,0:T(4,128)(2,1)} %shard_map.28), channel_id=1, source_target_pairs={{0,2},{1,3},{2,0},{3,1},{4,6},{5,7},{6,4},{7,5},{8,10},{9,11},{10,... | collective-permute-start | bytes 396296 | tf_op jit(solution)/shard_map/ppermute | solution.py:224
  11.5 0.5 %fusion.9 = (f32[64,512]{1,0:T(8,128)S(1)}, f32[64,512]{1,0:T(8,128)S(1)}) fusion(s32[512]{0:T(512)S(1)} %iota_add_fusion), kind=kLoop, calls=%fused_computation.16 | loop fusion | flops 294912 | bytes 264192 | tf_op jit(solution)/shard_map/cos | solution.py:86
  12.0 0.3 fusion.16
  12.4 1.5 %multiply_convert_fusion.1 = (bf16[32,64,512]{2,1,0:T(8,128)(2,1)S(1)}, bf16[32,64,512]{2,1,0:T(8,128)(2,1)S(1)}) fusion(f32[64,512]{1,0:T(8,128)S(1)} %get-tuple-element.18, f32[32,512]{1,0:T(8,128)S(1)} %get-tuple-element.16, f32[64,512]{1,0:T(8,128)S(1)} %get-tuple-element.17, f32[32,512]{1,0:T(8,128)S(1)} %get-tuple-element.15), kind=kLoop, calls=%fused_computation.2 | loop fusion | flops 10485760 | bytes 4587520 | tf_op jit(solution)/shard_map/convert_element_type | solution.py:90
  13.9 0.0 collective-permute-done.5
  13.9 0.0 copy-done.2
  14.0 0.6 %collective-permute-start = (bf16[4,16512]{1,0:T(4,128)(2,1)S(1)}, bf16[4,16512]{1,0:T(4,128)(2,1)S(1)}, u32[]{:S(2)}, u32[]{:S(2)}) collective-permute-start(bf16[4,16512]{1,0:T(4,128)(2,1)S(1)} %copy-done.2), channel_id=1, source_target_pairs={{0,1},{1,2},{2,3},{3,0},{4,5},{5,6},{6,7},{7,4},{8,9},{9,10},{10,1... | collective-permute-start | bytes 396296 | tf_op jit(solution)/shard_map/ppermute | solution.py:224
  14.6 2.3 %pad_maximum_fusion = bf16[2,2048,512]{2,1,0:T(8,128)(2,1)} fusion(bf16[1,2048,512]{2,1,0:T(8,128)(2,1)S(1)} %bitcast.16, bf16[1,2048,512]{2,1,0:T(8,128)(2,1)S(1)} %bitcast.15), kind=kLoop, calls=%fused_computation | loop fusion | flops 2097152 | bytes 8388608 | tf_op jit(solution)/shard_map/stack | solution.py:92
  16.9 2.1 %collective-permute-done.4 = bf16[4,16512]{1,0:T(4,128)(2,1)S(1)} collective-permute-done((bf16[4,16512]{1,0:T(4,128)(2,1)}, bf16[4,16512]{1,0:T(4,128)(2,1)S(1)}, u32[]{:S(2)}, u32[]{:S(2)}) %collective-permute-start.4) | collective-permute-done | bytes 132128 | tf_op jit(solution)/shard_map/ppermute | solution.py:224
  19.0 0.0 collective-permute-done.3
  19.0 0.0 collective-permute-done.2
  19.0 0.0 collective-permute-done.1
  19.0 0.9 %collective-permute-done = bf16[4,16512]{1,0:T(4,128)(2,1)S(1)} collective-permute-done((bf16[4,16512]{1,0:T(4,128)(2,1)S(1)}, bf16[4,16512]{1,0:T(4,128)(2,1)S(1)}, u32[]{:S(2)}, u32[]{:S(2)}) %collective-permute-start) | collective-permute-done | bytes 132128 | tf_op jit(solution)/shard_map/ppermute | solution.py:224
  19.9 1.7 %fusion.3 = (bf16[4,4,16512]{2,1,0:T(4,128)(2,1)S(1)}, bf16[4,4,16512]{2,1,0:T(4,128)(2,1)}) fusion(bf16[1,4,16512]{2,1,0:T(4,128)(2,1)S(1)} %bitcast.17, bf16[1,4,16512]{2,1,0:T(4,128)(2,1)S(1)} %bitcast.18, bf16[1,4,16512]{2,1,0:T(4,128)(2,1)S(1)} %bitcast.19, bf16[1,4,16512]{2,1,0:T(4,128)(2,1)S(1)} %bitcast.20, bf16[1,4,16512]{2,1,0:T(4,128)(2,1)S(1)} %bitcast.21, ...), kind=kLoop, calls=%fused_computation.8 | loop fusion | flops 1585152 | bytes 1981440 | tf_op jit(solution)/shard_map/stack | solution.py:225
  21.6 0.0 copy-start
  21.6 0.0 collective-permute-start.6
  21.6 0.7 %pad_add_fusion.place_ref = s32[3]{0:T(128)} fusion(s32[1]{0:T(128)} %bitcast.2, s32[1]{0:T(128)} %bitcast.1, s32[1]{0:T(128)} %bitcast), kind=kLoop, calls=%fused_computation.28 | loop fusion | flops 6 | bytes 24 | tf_op jit(solution)/shard_map/stack | solution.py:237
  22.3 1.2 %collective-permute-done.6.sib_ref = bf16[4,4,16512]{2,1,0:T(4,128)(2,1)S(1)} collective-permute-done((bf16[4,4,16512]{2,1,0:T(4,128)(2,1)S(1)}, bf16[4,4,16512]{2,1,0:T(4,128)(2,1)S(1)}, u32[]{:S(2)}, u32[]{:S(2)}) %collective-permute-start.6) | collective-permute-done | bytes 528416 | tf_op jit(solution)/shard_map/ppermute | solution.py:235
  23.5 0.0 copy-done
  23.5 0.0 copy-start.1
  23.5 0.8 %copy-done.1 = bf16[4,4,16512]{2,1,0:T(4,128)(2,1)} copy-done((bf16[4,4,16512]{2,1,0:T(4,128)(2,1)}, bf16[4,4,16512]{2,1,0:T(4,128)(2,1)S(1)}, u32[]{:S(2)}) %copy-start.1) | copy-done | bytes 528408
  24.3 11.3 %shard_map.29 = bf16[512,512]{1,0:T(8,128)(2,1)} custom-call(s32[3]{0:T(128)} %pad_add_fusion.place_ref, bf16[4,4,16512]{2,1,0:T(4,128)(2,1)} %get-tuple-element.8.rec_ref, bf16[4,4,16512]{2,1,0:T(4,128)(2,1)} %copy-done, bf16[4,4,16512]{2,1,0:T(4,128)(2,1)} %copy-done.1, bf16[4096,512]{1,0:T(8,128)(2,1)} %bitcast.14), custom_call_target="tpu_custom_call" | custom-call | tf_op jit(solution)/shard_map/pallas_call | solution.py:192
  (2 shorter events, 0.0 us)
Async XLA Ops:
  2.5 11.5 %copy-start.2 = (bf16[4,16512]{1,0:T(4,128)(2,1)S(1)}, bf16[4,16512]{1,0:T(4,128)(2,1)}, u32[]{:S(2)}) copy-start(bf16[4,16512]{1,0:T(4,128)(2,1)} %shard_map.28) | copy-start | bytes 396292
  2.5 11.5 %collective-permute-start.5 = (bf16[4,16512]{1,0:T(4,128)(2,1)}, bf16[4,16512]{1,0:T(4,128)(2,1)S(1)}, u32[]{:S(2)}, u32[]{:S(2)}) collective-permute-start(bf16[4,16512]{1,0:T(4,128)(2,1)} %shard_map.28), channel_id=1, source_target_pairs={{0,24},{4,28},{8,0},{12,4},{16,8},{20,12},{24,16},{28,20},{1,25},{... | collective-permute-start | bytes 396296 | tf_op jit(solution)/shard_map/ppermute | solution.py:224
  7.5 11.5 %collective-permute-start.4 = (bf16[4,16512]{1,0:T(4,128)(2,1)}, bf16[4,16512]{1,0:T(4,128)(2,1)S(1)}, u32[]{:S(2)}, u32[]{:S(2)}) collective-permute-start(bf16[4,16512]{1,0:T(4,128)(2,1)} %shard_map.28), channel_id=1, source_target_pairs={{0,16},{4,20},{8,24},{12,28},{16,0},{20,4},{24,8},{28,12},{1,17},{... | collective-permute-start | bytes 396296 | tf_op jit(solution)/shard_map/ppermute | solution.py:224
  7.5 11.5 %collective-permute-start.3 = (bf16[4,16512]{1,0:T(4,128)(2,1)}, bf16[4,16512]{1,0:T(4,128)(2,1)S(1)}, u32[]{:S(2)}, u32[]{:S(2)}) collective-permute-start(bf16[4,16512]{1,0:T(4,128)(2,1)} %shard_map.28), channel_id=1, source_target_pairs={{0,8},{4,12},{8,16},{12,20},{16,24},{20,28},{24,0},{28,4},{1,9},{5... | collective-permute-start | bytes 396296 | tf_op jit(solution)/shard_map/ppermute | solution.py:224
  8.5 10.5 %collective-permute-start.2 = (bf16[4,16512]{1,0:T(4,128)(2,1)}, bf16[4,16512]{1,0:T(4,128)(2,1)S(1)}, u32[]{:S(2)}, u32[]{:S(2)}) collective-permute-start(bf16[4,16512]{1,0:T(4,128)(2,1)} %shard_map.28), channel_id=1, source_target_pairs={{0,3},{1,0},{2,1},{3,2},{4,7},{5,4},{6,5},{7,6},{8,11},{9,8},{10,9... | collective-permute-start | bytes 396296 | tf_op jit(solution)/shard_map/ppermute | solution.py:224
  11.0 8.0 %collective-permute-start.1 = (bf16[4,16512]{1,0:T(4,128)(2,1)}, bf16[4,16512]{1,0:T(4,128)(2,1)S(1)}, u32[]{:S(2)}, u32[]{:S(2)}) collective-permute-start(bf16[4,16512]{1,0:T(4,128)(2,1)} %shard_map.28), channel_id=1, source_target_pairs={{0,2},{1,3},{2,0},{3,1},{4,6},{5,7},{6,4},{7,5},{8,10},{9,11},{10,... | collective-permute-start | bytes 396296 | tf_op jit(solution)/shard_map/ppermute | solution.py:224
  14.0 5.9 %collective-permute-start = (bf16[4,16512]{1,0:T(4,128)(2,1)S(1)}, bf16[4,16512]{1,0:T(4,128)(2,1)S(1)}, u32[]{:S(2)}, u32[]{:S(2)}) collective-permute-start(bf16[4,16512]{1,0:T(4,128)(2,1)S(1)} %copy-done.2), channel_id=1, source_target_pairs={{0,1},{1,2},{2,3},{3,0},{4,5},{5,6},{6,7},{7,4},{8,9},{9,10},{10,1... | collective-permute-start | bytes 396296 | tf_op jit(solution)/shard_map/ppermute | solution.py:224
  21.6 1.9 %copy-start = (bf16[4,4,16512]{2,1,0:T(4,128)(2,1)}, bf16[4,4,16512]{2,1,0:T(4,128)(2,1)S(1)}, u32[]{:S(2)}) copy-start(bf16[4,4,16512]{2,1,0:T(4,128)(2,1)S(1)} %get-tuple-element.9.own_ref) | copy-start | bytes 1585156
  21.6 1.9 %collective-permute-start.6 = (bf16[4,4,16512]{2,1,0:T(4,128)(2,1)S(1)}, bf16[4,4,16512]{2,1,0:T(4,128)(2,1)S(1)}, u32[]{:S(2)}, u32[]{:S(2)}) collective-permute-start(bf16[4,4,16512]{2,1,0:T(4,128)(2,1)S(1)} %get-tuple-element.9.own_ref), channel_id=1, source_target_pairs={{0,4},{4,0},{8,12},{12,8},{16,20},{20,16},{24,28},{28,24},{1,5},{5... | collective-permute-start | bytes 1585160 | tf_op jit(solution)/shard_map/ppermute | solution.py:235
  23.5 0.8 %copy-start.1 = (bf16[4,4,16512]{2,1,0:T(4,128)(2,1)}, bf16[4,4,16512]{2,1,0:T(4,128)(2,1)S(1)}, u32[]{:S(2)}) copy-start(bf16[4,4,16512]{2,1,0:T(4,128)(2,1)S(1)} %collective-permute-done.6.sib_ref) | copy-start | bytes 1585156

commit v10 on v9

--- a/solution.py
+++ b/solution.py
@@ -125,14 +125,12 @@
 
     @pl.when(step == 0)
     def _():
-        rcv_index, chip, core = place_ref[0], place_ref[1], place_ref[2]
+        core = place_ref[0]
         for dst in range(rcv_count):
-            k = (rcv_index - dst + rcv_count) % rcv_count
-            place(rec_ref[k], dst, recf, rtails, False)
+            place(rec_ref[dst], dst, recf, rtails, False)
         for zz in range(chips):
-            k = (chip - zz + chips) % chips
-            own_block = own_ref[k]
-            sib_block = sib_ref[k]
+            own_block = own_ref[zz]
+            sib_block = sib_ref[zz]
             for cc in range(2):
                 same = core == cc
                 block = jnp.where(same, own_block, sib_block)
@@ -217,26 +215,30 @@
     return out.reshape(nrec, nsrc, lags)
 
 
-def shifted(x, axis, count, stride):
-    parts = [x]
-    for shift in range(1, count // stride):
-        pairs = [(j, (j + stride * shift) % count) for j in range(count)]
-        parts.append(lax.ppermute(x, axis, perm=pairs))
-    return jnp.stack(parts)
+def doubling(x, axis, count, first):
+    index = lax.axis_index(axis)
+    blocks = x[None]
+    bit = first
+    while bit < count:
+        other = lax.ppermute(blocks, axis, perm=[(j, j ^ bit) for j in range(count)])
+        low = (index & bit) == 0
+        blocks = jnp.concatenate(
+            [jnp.where(low, blocks, other), jnp.where(low, other, blocks)], axis=0
+        )
+        bit *= 2
+    return blocks
 
 
 def local(spectra, valid, rcv_count, src_count):
     channels, windows, _, freqs = spectra.shape
     table = lag_table(freqs, LAGS)
     packed = whiten_pack(spectra, valid)
-    rec_stack = shifted(packed, "rcv", rcv_count, 1)
-    own_stack = shifted(packed, "src", src_count, 2)
+    rec_stack = doubling(packed, "rcv", rcv_count, 1)
+    own_stack = doubling(packed, "src", src_count, 2)
     table, rec_stack, own_stack = lax.optimization_barrier((table, rec_stack, own_stack))
     sib_stack = lax.ppermute(own_stack, "src", perm=[(j, j ^ 1) for j in range(src_count)])
-    src_index = lax.axis_index("src")
-    place = jnp.stack(
-        [lax.axis_index("rcv"), src_index // 2, src_index % 2]
-    ).astype(jnp.int32)
+    core = lax.axis_index("src") % 2
+    place = jnp.stack([core]).astype(jnp.int32)
     return correlate(place, rec_stack, own_stack, sib_stack, table, windows, freqs)
 
 

time: 35.8 us -> 40 us (1.12)
  waiting for transfers between devices: 4.17 us -> 7.59 us
  other arithmetic: 7.15 us -> 10.4 us
  Pallas kernels: 13.8 us -> 12.1 us
  starting transfers between devices: 9.66 us -> 8.84 us
    ppermute x6 -> x4, waiting for transfers between devices: 2.98 us -> 5.69 us  [doubling(): lax.ppermute(blocks, axis, perm=[(j, j ^ bit) for j in range(count)])]
    another operation x2 -> x0, other arithmetic: 2.41 us -> none  [the longest x1 1.69 us: shifted(): return jnp.stack(parts)]
    concatenate x0 -> x4, other arithmetic: none -> 1.86 us  [doubling(): jnp.concatenate([jnp.where(low, blocks, other), jnp.where(low, other, blo...]
    pallas_call x1, Pallas kernels: 11.3 us -> 9.63 us  [correlate(): pl.pallas_call(kernel, grid_spec=pltpu.PrefetchScalarGridSpec(num_scalar_...]
    another operation x1, other arithmetic: 2.31 us -> 3.92 us  [lag_table(): jnp.stack([cosines, sines], axis=0).reshape(2 * freq_count, lag_count)]
    convert_element_type x1, other arithmetic: 1.54 us -> 2.82 us  [lag_table(): cosines = cosines.reshape(freq_count, lag_count).astype(jnp.bfloat16)]
    ppermute x6 -> x4, starting transfers between devices: 9.66 us -> 8.75 us  [doubling(): lax.ppermute(blocks, axis, perm=[(j, j ^ bit) for j in range(count)])]
    select_n x0 -> x2, other arithmetic: none -> 0.86 us  [doubling(): jnp.where(low, blocks, other)]
  transfers between devices with their start and end apart: 7 -> 5, of which waited for: 3 -> 2; matrix products, arithmetic and copies ran while one was open for 15% -> 20% of each run, Pallas kernels for 0% -> 0%
where the time goes in v10:
time: 40 us; the launch traced here: 39.8 us
  Pallas kernels  12.1 us (30%)
  other arithmetic  10.4 us (26%)
  starting transfers between devices  8.84 us (22%)
  waiting for transfers between devices  7.59 us (19%)
  local copies, waits for them, and re-layouts  0.84 us (2%)
    pallas_call x1, Pallas kernels, correlate(): pl.pallas_call(kernel, grid_spec=pltpu.PrefetchScalarGridSpec(num_scalar_...  9.63 us
    ppermute x4, starting transfers between devices, doubling(): lax.ppermute(blocks, axis, perm=[(j, j ^ bit) for j in range(count)])  8.75 us
    ppermute x4, waiting for transfers between devices, doubling(): lax.ppermute(blocks, axis, perm=[(j, j ^ bit) for j in range(count)])  5.69 us
    another operation x1, other arithmetic, lag_table(): jnp.stack([cosines, sines], axis=0).reshape(2 * freq_count, lag_count)  3.92 us
    convert_element_type x1, other arithmetic, lag_table(): cosines = cosines.reshape(freq_count, lag_count).astype(jnp.bfloat16)  2.82 us
    pallas_call x1, Pallas kernels, whiten_pack(): pl.pallas_call(kernel, out_shape=jax.ShapeDtypeStruct((channels, windows...  2.47 us
    ppermute x1, waiting for transfers between devices, local(): lax.ppermute(own_stack, 'src', perm=[(j, j ^ 1) for j in range(src_count)])  1.89 us
    concatenate x4, other arithmetic, doubling(): jnp.concatenate([jnp.where(low, blocks, other), jnp.where(low, other, blo...  1.86 us
  transfers between devices with their start and end apart: 5, of which 2 were waited for; matrix products, arithmetic and copies ran while one was open for 20% of the time, Pallas kernels for 0%

profile of v10, /device:TPU:0, one launch (start us, length us, event | category | flops | bytes accessed | tf_op | source)
XLA Modules:
  0.0 39.8 jit_solution(8921182304464313967)
XLA Ops:
  0.0 2.5 %shard_map.28 = bf16[4,16512]{1,0:T(4,128)(2,1)} custom-call(bf16[4,4,2,2048]{3,2,1,0:T(2,128)(2,1)} %x_ref.1, s32[4,4]{1,0:T(4,128)} %v_ref.1), custom_call_target="tpu_custom_call" | custom-call | tf_op jit(solution)/shard_map/pallas_call | solution.py:70
  2.5 0.0 copy-start.2
  2.5 3.0 %collective-permute-start.2 = (bf16[1,4,16512]{2,1,0:T(4,128)(2,1)}, bf16[1,4,16512]{2,1,0:T(4,128)(2,1)S(1)}, u32[]{:S(2)}, u32[]{:S(2)}) collective-permute-start(bf16[1,4,16512]{2,1,0:T(4,128)(2,1)} %bitcast.13), channel_id=1, source_target_pairs={{0,8},{4,12},{8,0},{12,4},{16,24},{20,28},{24,16},{28,20},{1,9},{5... | collective-permute-start | bytes 396296 | tf_op jit(solution)/shard_map/ppermute | solution.py:223
  5.5 1.5 %collective-permute-start = (bf16[1,4,16512]{2,1,0:T(4,128)(2,1)}, bf16[1,4,16512]{2,1,0:T(4,128)(2,1)S(1)}, u32[]{:S(2)}, u32[]{:S(2)}) collective-permute-start(bf16[1,4,16512]{2,1,0:T(4,128)(2,1)} %bitcast.14), channel_id=1, source_target_pairs={{0,1},{1,0},{2,3},{3,2},{4,5},{5,4},{6,7},{7,6},{8,9},{9,8},{10,11... | collective-permute-start | bytes 396296 | tf_op jit(solution)/shard_map/ppermute | solution.py:223
  7.0 0.5 %fusion.5 = (f32[64,512]{1,0:T(8,128)S(1)}, f32[64,512]{1,0:T(8,128)S(1)}) fusion(s32[512]{0:T(512)S(1)} %iota_add_fusion), kind=kLoop, calls=%fused_computation.22 | loop fusion | flops 294912 | bytes 264192 | tf_op jit(solution)/shard_map/cos | solution.py:86
  7.5 0.3 fusion.12
  7.9 2.8 %multiply_convert_fusion.1 = (bf16[32,64,512]{2,1,0:T(8,128)(2,1)S(1)}, bf16[32,64,512]{2,1,0:T(8,128)(2,1)}) fusion(f32[64,512]{1,0:T(8,128)S(1)} %get-tuple-element.26, f32[32,512]{1,0:T(8,128)S(1)} %get-tuple-element.24, f32[64,512]{1,0:T(8,128)S(1)} %get-tuple-element.25, f32[32,512]{1,0:T(8,128)S(1)} %get-tuple-element.23), kind=kLoop, calls=%fused_computation.2 | loop fusion | flops 10485760 | bytes 4587520 | tf_op jit(solution)/shard_map/convert_element_type | solution.py:90
  10.7 0.0 collective-permute-done.2
  10.7 0.0 collective-permute-done
  10.7 0.0 copy-done.2
  10.7 0.2 broadcast_select_fusion.5
  10.9 0.2 pad_maximum_fusion.4
  11.1 2.7 %collective-permute-start.3 = (bf16[2,4,16512]{2,1,0:T(4,128)(2,1)S(1)}, bf16[2,4,16512]{2,1,0:T(4,128)(2,1)S(1)}, u32[]{:S(2)}, u32[]{:S(2)}) collective-permute-start(bf16[2,4,16512]{2,1,0:T(4,128)(2,1)S(1)} %pad_maximum_fusion.4), channel_id=1, source_target_pairs={{0,16},{4,20},{8,24},{12,28},{16,0},{20,4},{24,8},{28,12},{1,17},{... | collective-permute-start | bytes 792584 | tf_op jit(solution)/shard_map/ppermute | solution.py:223
  13.8 0.2 pad_maximum_fusion.3
  14.0 1.6 %collective-permute-start.1 = (bf16[2,4,16512]{2,1,0:T(4,128)(2,1)S(1)}, bf16[2,4,16512]{2,1,0:T(4,128)(2,1)S(1)}, u32[]{:S(2)}, u32[]{:S(2)}) collective-permute-start(bf16[2,4,16512]{2,1,0:T(4,128)(2,1)S(1)} %pad_maximum_fusion.3), channel_id=1, source_target_pairs={{0,2},{1,3},{2,0},{3,1},{4,6},{5,7},{6,4},{7,5},{8,10},{9,11},{10,... | collective-permute-start | bytes 792584 | tf_op jit(solution)/shard_map/ppermute | solution.py:223
  15.6 3.9 %pad_maximum_fusion = bf16[2,2048,512]{2,1,0:T(8,128)(2,1)} fusion(bf16[1,2048,512]{2,1,0:T(8,128)(2,1)} %bitcast.12, bf16[1,2048,512]{2,1,0:T(8,128)(2,1)S(1)} %bitcast.11), kind=kLoop, calls=%fused_computation | loop fusion | flops 2097152 | bytes 8388608 | tf_op jit(solution)/shard_map/stack | solution.py:92
  19.5 5.7 %collective-permute-done.3 = bf16[2,4,16512]{2,1,0:T(4,128)(2,1)S(1)} collective-permute-done((bf16[2,4,16512]{2,1,0:T(4,128)(2,1)S(1)}, bf16[2,4,16512]{2,1,0:T(4,128)(2,1)S(1)}, u32[]{:S(2)}, u32[]{:S(2)}) %collective-permute-start.3) | collective-permute-done | bytes 264224 | tf_op jit(solution)/shard_map/ppermute | solution.py:223
  25.2 0.0 collective-permute-done.1
  25.2 0.6 %broadcast_select_fusion.1 = (bf16[2,4,16512]{2,1,0:T(4,128)(2,1)S(1)}, bf16[2,4,16512]{2,1,0:T(4,128)(2,1)S(1)}, bf16[2,4,16512]{2,1,0:T(4,128)(2,1)S(1)}, bf16[2,4,16512]{2,1,0:T(4,128)(2,1)S(1)}) fusion(bf16[2,4,16512]{2,1,0:T(4,128)(2,1)S(1)} %collective-permute-done.3, pred[]{:T(512)S(6)} %eq.20, bf16[1,4,16512]{2,1,0:T(4,128)(2,1)S(1)} %get-tuple-element.18, ...), kind=kLoop, calls=%fused_computation.8 | loop fusion | flops 792576 | bytes 2113538 | tf_op jit(solution)/shard_map/jit(_where)/select_n | solution.py:226
  25.8 1.1 %pad_maximum_fusion.1.rec_ref = bf16[4,4,16512]{2,1,0:T(4,128)(2,1)} fusion(bf16[2,4,16512]{2,1,0:T(4,128)(2,1)S(1)} %get-tuple-element.27, bf16[2,4,16512]{2,1,0:T(4,128)(2,1)S(1)} %get-tuple-element.28), kind=kLoop, calls=%fused_computation.3 | loop fusion | flops 264192 | bytes 1056768 | tf_op jit(solution)/shard_map/concatenate | solution.py:225
  27.0 0.3 pad_maximum_fusion.2.own_ref
  27.3 0.0 copy-start
  27.3 0.1 collective-permute-start.4
  27.4 1.9 %collective-permute-done.4.sib_ref = bf16[4,4,16512]{2,1,0:T(4,128)(2,1)S(1)} collective-permute-done((bf16[4,4,16512]{2,1,0:T(4,128)(2,1)S(1)}, bf16[4,4,16512]{2,1,0:T(4,128)(2,1)S(1)}, u32[]{:S(2)}, u32[]{:S(2)}) %collective-permute-start.4) | collective-permute-done | bytes 528416 | tf_op jit(solution)/shard_map/ppermute | solution.py:239
  29.3 0.0 copy-start.1
  29.3 0.0 copy-done
  29.3 0.8 %copy-done.1 = bf16[4,4,16512]{2,1,0:T(4,128)(2,1)} copy-done((bf16[4,4,16512]{2,1,0:T(4,128)(2,1)}, bf16[4,4,16512]{2,1,0:T(4,128)(2,1)S(1)}, u32[]{:S(2)}) %copy-start.1) | copy-done | bytes 528408
  30.1 9.6 %shard_map.29 = bf16[512,512]{1,0:T(8,128)(2,1)} custom-call(s32[1]{0:T(128)} %bitcast.place_ref, bf16[4,4,16512]{2,1,0:T(4,128)(2,1)} %pad_maximum_fusion.1.rec_ref, bf16[4,4,16512]{2,1,0:T(4,128)(2,1)} %copy-done, bf16[4,4,16512]{2,1,0:T(4,128)(2,1)} %copy-done.1, bf16[4096,512]{1,0:T(8,128)(2,1)} %bitcast.10), custom_call_target="tpu_custom_call" | custom-call | tf_op jit(solution)/shard_map/pallas_call | solution.py:190
  (2 shorter events, 0.0 us)
Async XLA Ops:
  2.5 8.2 %copy-start.2 = (bf16[4,16512]{1,0:T(4,128)(2,1)S(1)}, bf16[4,16512]{1,0:T(4,128)(2,1)}, u32[]{:S(2)}) copy-start(bf16[4,16512]{1,0:T(4,128)(2,1)} %shard_map.28) | copy-start | bytes 396292
  2.5 8.2 %collective-permute-start.2 = (bf16[1,4,16512]{2,1,0:T(4,128)(2,1)}, bf16[1,4,16512]{2,1,0:T(4,128)(2,1)S(1)}, u32[]{:S(2)}, u32[]{:S(2)}) collective-permute-start(bf16[1,4,16512]{2,1,0:T(4,128)(2,1)} %bitcast.13), channel_id=1, source_target_pairs={{0,8},{4,12},{8,0},{12,4},{16,24},{20,28},{24,16},{28,20},{1,9},{5... | collective-permute-start | bytes 396296 | tf_op jit(solution)/shard_map/ppermute | solution.py:223
  5.5 5.2 %collective-permute-start = (bf16[1,4,16512]{2,1,0:T(4,128)(2,1)}, bf16[1,4,16512]{2,1,0:T(4,128)(2,1)S(1)}, u32[]{:S(2)}, u32[]{:S(2)}) collective-permute-start(bf16[1,4,16512]{2,1,0:T(4,128)(2,1)} %bitcast.14), channel_id=1, source_target_pairs={{0,1},{1,0},{2,3},{3,2},{4,5},{5,4},{6,7},{7,6},{8,9},{9,8},{10,11... | collective-permute-start | bytes 396296 | tf_op jit(solution)/shard_map/ppermute | solution.py:223
  11.1 14.0 %collective-permute-start.3 = (bf16[2,4,16512]{2,1,0:T(4,128)(2,1)S(1)}, bf16[2,4,16512]{2,1,0:T(4,128)(2,1)S(1)}, u32[]{:S(2)}, u32[]{:S(2)}) collective-permute-start(bf16[2,4,16512]{2,1,0:T(4,128)(2,1)S(1)} %pad_maximum_fusion.4), channel_id=1, source_target_pairs={{0,16},{4,20},{8,24},{12,28},{16,0},{20,4},{24,8},{28,12},{1,17},{... | collective-permute-start | bytes 792584 | tf_op jit(solution)/shard_map/ppermute | solution.py:223
  14.0 11.2 %collective-permute-start.1 = (bf16[2,4,16512]{2,1,0:T(4,128)(2,1)S(1)}, bf16[2,4,16512]{2,1,0:T(4,128)(2,1)S(1)}, u32[]{:S(2)}, u32[]{:S(2)}) collective-permute-start(bf16[2,4,16512]{2,1,0:T(4,128)(2,1)S(1)} %pad_maximum_fusion.3), channel_id=1, source_target_pairs={{0,2},{1,3},{2,0},{3,1},{4,6},{5,7},{6,4},{7,5},{8,10},{9,11},{10,... | collective-permute-start | bytes 792584 | tf_op jit(solution)/shard_map/ppermute | solution.py:223
  27.3 2.0 %copy-start = (bf16[4,4,16512]{2,1,0:T(4,128)(2,1)}, bf16[4,4,16512]{2,1,0:T(4,128)(2,1)S(1)}, u32[]{:S(2)}) copy-start(bf16[4,4,16512]{2,1,0:T(4,128)(2,1)S(1)} %pad_maximum_fusion.2.own_ref) | copy-start | bytes 1585156
  27.3 2.0 %collective-permute-start.4 = (bf16[4,4,16512]{2,1,0:T(4,128)(2,1)S(1)}, bf16[4,4,16512]{2,1,0:T(4,128)(2,1)S(1)}, u32[]{:S(2)}, u32[]{:S(2)}) collective-permute-start(bf16[4,4,16512]{2,1,0:T(4,128)(2,1)S(1)} %pad_maximum_fusion.2.own_ref), channel_id=1, source_target_pairs={{0,4},{4,0},{8,12},{12,8},{16,20},{20,16},{24,28},{28,24},{1,5},{5... | collective-permute-start | bytes 1585160 | tf_op jit(solution)/shard_map/ppermute | solution.py:239
  29.3 0.8 %copy-start.1 = (bf16[4,4,16512]{2,1,0:T(4,128)(2,1)}, bf16[4,4,16512]{2,1,0:T(4,128)(2,1)S(1)}, u32[]{:S(2)}) copy-start(bf16[4,4,16512]{2,1,0:T(4,128)(2,1)S(1)} %collective-permute-done.4.sib_ref) | copy-start | bytes 1585156

commit v11 on v9

--- a/solution.py
+++ b/solution.py
@@ -126,17 +126,22 @@
     @pl.when(step == 0)
     def _():
         rcv_index, chip, core = place_ref[0], place_ref[1], place_ref[2]
-        for dst in range(rcv_count):
-            k = (rcv_index - dst + rcv_count) % rcv_count
-            place(rec_ref[k], dst, recf, rtails, False)
-        for zz in range(chips):
-            k = (chip - zz + chips) % chips
-            own_block = own_ref[k]
-            sib_block = sib_ref[k]
-            for cc in range(2):
-                same = core == cc
-                block = jnp.where(same, own_block, sib_block)
-                place(block, zz * 2 + cc, srcf, stails, True)
+        for rot in range(rcv_count):
+
+            @pl.when(rcv_index == rot)
+            def _():
+                for dst in range(rcv_count):
+                    place(rec_ref[(rot - dst) % rcv_count], dst, recf, rtails, False)
+
+        for rot in range(chips):
+            for mine in range(2):
+
+                @pl.when((chip == rot) & (core == mine))
+                def _():
+                    for zz in range(chips):
+                        k = (rot - zz) % chips
+                        place(own_ref[k], zz * 2 + mine, srcf, stails, True)
+                        place(sib_ref[k], zz * 2 + 1 - mine, srcf, stails, True)
 
     smask = stails[...]
 

time: 35.8 us -> 35.9 us (level)
  no operation moved by 1% of the time
where the time goes in v11:
time: 35.9 us; the launch traced here: 35.7 us
  Pallas kernels  13.9 us (39%)
  starting transfers between devices  9.66 us (27%)
  other arithmetic  7.15 us (20%)
  waiting for transfers between devices  4.17 us (12%)
  local copies, waits for them, and re-layouts  0.84 us (2%)
    pallas_call x1, Pallas kernels, correlate(): pl.pallas_call(kernel, grid_spec=pltpu.PrefetchScalarGridSpec(num_scalar_...  11.4 us
    ppermute x6, starting transfers between devices, shifted(): parts.append(lax.ppermute(x, axis, perm=pairs))  9.66 us
    ppermute x6, waiting for transfers between devices, shifted(): parts.append(lax.ppermute(x, axis, perm=pairs))  2.98 us
    pallas_call x1, Pallas kernels, whiten_pack(): pl.pallas_call(kernel, out_shape=jax.ShapeDtypeStruct((channels, windows...  2.47 us
    another operation x1, other arithmetic, lag_table(): jnp.stack([cosines, sines], axis=0).reshape(2 * freq_count, lag_count)  2.31 us
    another operation x1, other arithmetic, shifted(): return jnp.stack(parts)  1.69 us
    convert_element_type x1, other arithmetic, lag_table(): cosines = cosines.reshape(freq_count, lag_count).astype(jnp.bfloat16)  1.54 us
    ppermute x1, waiting for transfers between devices, local(): lax.ppermute(own_stack, 'src', perm=[(j, j ^ 1) for j in range(src_count)])  1.2 us
  transfers between devices with their start and end apart: 7, of which 3 were waited for; matrix products, arithmetic and copies ran while one was open for 15% of the time, Pallas kernels for 0%

profile of v11, /device:TPU:0, one launch (start us, length us, event | category | flops | bytes accessed | tf_op | source)
XLA Modules:
  0.0 35.7 jit_solution(7742688254007551604)
XLA Ops:
  0.0 2.5 %shard_map.28 = bf16[4,16512]{1,0:T(4,128)(2,1)} custom-call(bf16[4,4,2,2048]{3,2,1,0:T(2,128)(2,1)} %x_ref.1, s32[4,4]{1,0:T(4,128)} %v_ref.1), custom_call_target="tpu_custom_call" | custom-call | tf_op jit(solution)/shard_map/pallas_call | solution.py:70
  2.5 0.0 copy-start.2
  2.5 5.0 %collective-permute-start.5 = (bf16[4,16512]{1,0:T(4,128)(2,1)}, bf16[4,16512]{1,0:T(4,128)(2,1)S(1)}, u32[]{:S(2)}, u32[]{:S(2)}) collective-permute-start(bf16[4,16512]{1,0:T(4,128)(2,1)} %shard_map.28), channel_id=1, source_target_pairs={{0,24},{4,28},{8,0},{12,4},{16,8},{20,12},{24,16},{28,20},{1,25},{... | collective-permute-start | bytes 396296 | tf_op jit(solution)/shard_map/ppermute | solution.py:229
  7.5 0.0 collective-permute-start.4
  7.5 1.0 %collective-permute-start.3 = (bf16[4,16512]{1,0:T(4,128)(2,1)}, bf16[4,16512]{1,0:T(4,128)(2,1)S(1)}, u32[]{:S(2)}, u32[]{:S(2)}) collective-permute-start(bf16[4,16512]{1,0:T(4,128)(2,1)} %shard_map.28), channel_id=1, source_target_pairs={{0,8},{4,12},{8,16},{12,20},{16,24},{20,28},{24,0},{28,4},{1,9},{5... | collective-permute-start | bytes 396296 | tf_op jit(solution)/shard_map/ppermute | solution.py:229
  8.5 2.4 %collective-permute-start.2 = (bf16[4,16512]{1,0:T(4,128)(2,1)}, bf16[4,16512]{1,0:T(4,128)(2,1)S(1)}, u32[]{:S(2)}, u32[]{:S(2)}) collective-permute-start(bf16[4,16512]{1,0:T(4,128)(2,1)} %shard_map.28), channel_id=1, source_target_pairs={{0,3},{1,0},{2,1},{3,2},{4,7},{5,4},{6,5},{7,6},{8,11},{9,8},{10,9... | collective-permute-start | bytes 396296 | tf_op jit(solution)/shard_map/ppermute | solution.py:229
  11.0 0.5 %collective-permute-start.1 = (bf16[4,16512]{1,0:T(4,128)(2,1)}, bf16[4,16512]{1,0:T(4,128)(2,1)S(1)}, u32[]{:S(2)}, u32[]{:S(2)}) collective-permute-start(bf16[4,16512]{1,0:T(4,128)(2,1)} %shard_map.28), channel_id=1, source_target_pairs={{0,2},{1,3},{2,0},{3,1},{4,6},{5,7},{6,4},{7,5},{8,10},{9,11},{10,... | collective-permute-start | bytes 396296 | tf_op jit(solution)/shard_map/ppermute | solution.py:229
  11.5 0.5 %fusion.9 = (f32[64,512]{1,0:T(8,128)S(1)}, f32[64,512]{1,0:T(8,128)S(1)}) fusion(s32[512]{0:T(512)S(1)} %iota_add_fusion), kind=kLoop, calls=%fused_computation.16 | loop fusion | flops 294912 | bytes 264192 | tf_op jit(solution)/shard_map/cos | solution.py:86
  12.0 0.3 fusion.16
  12.4 1.5 %multiply_convert_fusion.1 = (bf16[32,64,512]{2,1,0:T(8,128)(2,1)S(1)}, bf16[32,64,512]{2,1,0:T(8,128)(2,1)S(1)}) fusion(f32[64,512]{1,0:T(8,128)S(1)} %get-tuple-element.18, f32[32,512]{1,0:T(8,128)S(1)} %get-tuple-element.16, f32[64,512]{1,0:T(8,128)S(1)} %get-tuple-element.17, f32[32,512]{1,0:T(8,128)S(1)} %get-tuple-element.15), kind=kLoop, calls=%fused_computation.2 | loop fusion | flops 10485760 | bytes 4587520 | tf_op jit(solution)/shard_map/convert_element_type | solution.py:90
  13.9 0.0 collective-permute-done.5
  13.9 0.0 copy-done.2
  14.0 0.6 %collective-permute-start = (bf16[4,16512]{1,0:T(4,128)(2,1)S(1)}, bf16[4,16512]{1,0:T(4,128)(2,1)S(1)}, u32[]{:S(2)}, u32[]{:S(2)}) collective-permute-start(bf16[4,16512]{1,0:T(4,128)(2,1)S(1)} %copy-done.2), channel_id=1, source_target_pairs={{0,1},{1,2},{2,3},{3,0},{4,5},{5,6},{6,7},{7,4},{8,9},{9,10},{10,1... | collective-permute-start | bytes 396296 | tf_op jit(solution)/shard_map/ppermute | solution.py:229
  14.6 2.3 %pad_maximum_fusion = bf16[2,2048,512]{2,1,0:T(8,128)(2,1)} fusion(bf16[1,2048,512]{2,1,0:T(8,128)(2,1)S(1)} %bitcast.16, bf16[1,2048,512]{2,1,0:T(8,128)(2,1)S(1)} %bitcast.15), kind=kLoop, calls=%fused_computation | loop fusion | flops 2097152 | bytes 8388608 | tf_op jit(solution)/shard_map/stack | solution.py:92
  16.9 2.1 %collective-permute-done.4 = bf16[4,16512]{1,0:T(4,128)(2,1)S(1)} collective-permute-done((bf16[4,16512]{1,0:T(4,128)(2,1)}, bf16[4,16512]{1,0:T(4,128)(2,1)S(1)}, u32[]{:S(2)}, u32[]{:S(2)}) %collective-permute-start.4) | collective-permute-done | bytes 132128 | tf_op jit(solution)/shard_map/ppermute | solution.py:229
  19.0 0.0 collective-permute-done.3
  19.0 0.0 collective-permute-done.2
  19.0 0.0 collective-permute-done.1
  19.0 0.9 %collective-permute-done = bf16[4,16512]{1,0:T(4,128)(2,1)S(1)} collective-permute-done((bf16[4,16512]{1,0:T(4,128)(2,1)S(1)}, bf16[4,16512]{1,0:T(4,128)(2,1)S(1)}, u32[]{:S(2)}, u32[]{:S(2)}) %collective-permute-start) | collective-permute-done | bytes 132128 | tf_op jit(solution)/shard_map/ppermute | solution.py:229
  19.9 1.7 %fusion.3 = (bf16[4,4,16512]{2,1,0:T(4,128)(2,1)S(1)}, bf16[4,4,16512]{2,1,0:T(4,128)(2,1)}) fusion(bf16[1,4,16512]{2,1,0:T(4,128)(2,1)S(1)} %bitcast.17, bf16[1,4,16512]{2,1,0:T(4,128)(2,1)S(1)} %bitcast.18, bf16[1,4,16512]{2,1,0:T(4,128)(2,1)S(1)} %bitcast.19, bf16[1,4,16512]{2,1,0:T(4,128)(2,1)S(1)} %bitcast.20, bf16[1,4,16512]{2,1,0:T(4,128)(2,1)S(1)} %bitcast.21, ...), kind=kLoop, calls=%fused_computation.8 | loop fusion | flops 1585152 | bytes 1981440 | tf_op jit(solution)/shard_map/stack | solution.py:230
  21.6 0.0 copy-start
  21.6 0.0 collective-permute-start.6
  21.6 0.7 %pad_add_fusion.place_ref = s32[3]{0:T(128)} fusion(s32[1]{0:T(128)} %bitcast.2, s32[1]{0:T(128)} %bitcast.1, s32[1]{0:T(128)} %bitcast), kind=kLoop, calls=%fused_computation.28 | loop fusion | flops 6 | bytes 24 | tf_op jit(solution)/shard_map/stack | solution.py:242
  22.3 1.2 %collective-permute-done.6.sib_ref = bf16[4,4,16512]{2,1,0:T(4,128)(2,1)S(1)} collective-permute-done((bf16[4,4,16512]{2,1,0:T(4,128)(2,1)S(1)}, bf16[4,4,16512]{2,1,0:T(4,128)(2,1)S(1)}, u32[]{:S(2)}, u32[]{:S(2)}) %collective-permute-start.6) | collective-permute-done | bytes 528416 | tf_op jit(solution)/shard_map/ppermute | solution.py:240
  23.5 0.0 copy-done
  23.5 0.0 copy-start.1
  23.5 0.8 %copy-done.1 = bf16[4,4,16512]{2,1,0:T(4,128)(2,1)} copy-done((bf16[4,4,16512]{2,1,0:T(4,128)(2,1)}, bf16[4,4,16512]{2,1,0:T(4,128)(2,1)S(1)}, u32[]{:S(2)}) %copy-start.1) | copy-done | bytes 528408
  24.3 11.4 %shard_map.29 = bf16[512,512]{1,0:T(8,128)(2,1)} custom-call(s32[3]{0:T(128)} %pad_add_fusion.place_ref, bf16[4,4,16512]{2,1,0:T(4,128)(2,1)} %get-tuple-element.8.rec_ref, bf16[4,4,16512]{2,1,0:T(4,128)(2,1)} %copy-done, bf16[4,4,16512]{2,1,0:T(4,128)(2,1)} %copy-done.1, bf16[4096,512]{1,0:T(8,128)(2,1)} %bitcast.14), custom_call_target="tpu_custom_call" | custom-call | tf_op jit(solution)/shard_map/pallas_call | solution.py:197
  (2 shorter events, 0.0 us)
Async XLA Ops:
  2.5 11.5 %copy-start.2 = (bf16[4,16512]{1,0:T(4,128)(2,1)S(1)}, bf16[4,16512]{1,0:T(4,128)(2,1)}, u32[]{:S(2)}) copy-start(bf16[4,16512]{1,0:T(4,128)(2,1)} %shard_map.28) | copy-start | bytes 396292
  2.5 11.5 %collective-permute-start.5 = (bf16[4,16512]{1,0:T(4,128)(2,1)}, bf16[4,16512]{1,0:T(4,128)(2,1)S(1)}, u32[]{:S(2)}, u32[]{:S(2)}) collective-permute-start(bf16[4,16512]{1,0:T(4,128)(2,1)} %shard_map.28), channel_id=1, source_target_pairs={{0,24},{4,28},{8,0},{12,4},{16,8},{20,12},{24,16},{28,20},{1,25},{... | collective-permute-start | bytes 396296 | tf_op jit(solution)/shard_map/ppermute | solution.py:229
  7.5 11.5 %collective-permute-start.4 = (bf16[4,16512]{1,0:T(4,128)(2,1)}, bf16[4,16512]{1,0:T(4,128)(2,1)S(1)}, u32[]{:S(2)}, u32[]{:S(2)}) collective-permute-start(bf16[4,16512]{1,0:T(4,128)(2,1)} %shard_map.28), channel_id=1, source_target_pairs={{0,16},{4,20},{8,24},{12,28},{16,0},{20,4},{24,8},{28,12},{1,17},{... | collective-permute-start | bytes 396296 | tf_op jit(solution)/shard_map/ppermute | solution.py:229
  7.5 11.5 %collective-permute-start.3 = (bf16[4,16512]{1,0:T(4,128)(2,1)}, bf16[4,16512]{1,0:T(4,128)(2,1)S(1)}, u32[]{:S(2)}, u32[]{:S(2)}) collective-permute-start(bf16[4,16512]{1,0:T(4,128)(2,1)} %shard_map.28), channel_id=1, source_target_pairs={{0,8},{4,12},{8,16},{12,20},{16,24},{20,28},{24,0},{28,4},{1,9},{5... | collective-permute-start | bytes 396296 | tf_op jit(solution)/shard_map/ppermute | solution.py:229
  8.5 10.5 %collective-permute-start.2 = (bf16[4,16512]{1,0:T(4,128)(2,1)}, bf16[4,16512]{1,0:T(4,128)(2,1)S(1)}, u32[]{:S(2)}, u32[]{:S(2)}) collective-permute-start(bf16[4,16512]{1,0:T(4,128)(2,1)} %shard_map.28), channel_id=1, source_target_pairs={{0,3},{1,0},{2,1},{3,2},{4,7},{5,4},{6,5},{7,6},{8,11},{9,8},{10,9... | collective-permute-start | bytes 396296 | tf_op jit(solution)/shard_map/ppermute | solution.py:229
  11.0 8.0 %collective-permute-start.1 = (bf16[4,16512]{1,0:T(4,128)(2,1)}, bf16[4,16512]{1,0:T(4,128)(2,1)S(1)}, u32[]{:S(2)}, u32[]{:S(2)}) collective-permute-start(bf16[4,16512]{1,0:T(4,128)(2,1)} %shard_map.28), channel_id=1, source_target_pairs={{0,2},{1,3},{2,0},{3,1},{4,6},{5,7},{6,4},{7,5},{8,10},{9,11},{10,... | collective-permute-start | bytes 396296 | tf_op jit(solution)/shard_map/ppermute | solution.py:229
  14.0 5.9 %collective-permute-start = (bf16[4,16512]{1,0:T(4,128)(2,1)S(1)}, bf16[4,16512]{1,0:T(4,128)(2,1)S(1)}, u32[]{:S(2)}, u32[]{:S(2)}) collective-permute-start(bf16[4,16512]{1,0:T(4,128)(2,1)S(1)} %copy-done.2), channel_id=1, source_target_pairs={{0,1},{1,2},{2,3},{3,0},{4,5},{5,6},{6,7},{7,4},{8,9},{9,10},{10,1... | collective-permute-start | bytes 396296 | tf_op jit(solution)/shard_map/ppermute | solution.py:229
  21.6 1.9 %copy-start = (bf16[4,4,16512]{2,1,0:T(4,128)(2,1)}, bf16[4,4,16512]{2,1,0:T(4,128)(2,1)S(1)}, u32[]{:S(2)}) copy-start(bf16[4,4,16512]{2,1,0:T(4,128)(2,1)S(1)} %get-tuple-element.9.own_ref) | copy-start | bytes 1585156
  21.6 1.9 %collective-permute-start.6 = (bf16[4,4,16512]{2,1,0:T(4,128)(2,1)S(1)}, bf16[4,4,16512]{2,1,0:T(4,128)(2,1)S(1)}, u32[]{:S(2)}, u32[]{:S(2)}) collective-permute-start(bf16[4,4,16512]{2,1,0:T(4,128)(2,1)S(1)} %get-tuple-element.9.own_ref), channel_id=1, source_target_pairs={{0,4},{4,0},{8,12},{12,8},{16,20},{20,16},{24,28},{28,24},{1,5},{5... | collective-permute-start | bytes 1585160 | tf_op jit(solution)/shard_map/ppermute | solution.py:240
  23.5 0.8 %copy-start.1 = (bf16[4,4,16512]{2,1,0:T(4,128)(2,1)}, bf16[4,4,16512]{2,1,0:T(4,128)(2,1)S(1)}, u32[]{:S(2)}) copy-start(bf16[4,4,16512]{2,1,0:T(4,128)(2,1)S(1)} %collective-permute-done.6.sib_ref) | copy-start | bytes 1585156

commit v12 on v11

--- a/solution.py
+++ b/solution.py
@@ -133,15 +133,14 @@
                 for dst in range(rcv_count):
                     place(rec_ref[(rot - dst) % rcv_count], dst, recf, rtails, False)
 
-        for rot in range(chips):
-            for mine in range(2):
-
-                @pl.when((chip == rot) & (core == mine))
+        for mine in range(2):
+            if True:
+
+                @pl.when(core == mine)
                 def _():
                     for zz in range(chips):
-                        k = (rot - zz) % chips
-                        place(own_ref[k], zz * 2 + mine, srcf, stails, True)
-                        place(sib_ref[k], zz * 2 + 1 - mine, srcf, stails, True)
+                        place(own_ref[zz], zz * 2 + mine, srcf, stails, True)
+                        place(sib_ref[zz], zz * 2 + 1 - mine, srcf, stails, True)
 
     smask = stails[...]
 
@@ -230,12 +229,25 @@
     return jnp.stack(parts)
 
 
+def forwarded(x, axis, count):
+    chips = count // 2
+    up = [(j, j + 2) for j in range(count - 2)]
+    down = [(j + 2, j) for j in range(count - 2)]
+    left, right = [x], [x]
+    for _ in range(1, chips):
+        left.append(lax.ppermute(left[-1], axis, perm=up))
+        right.append(lax.ppermute(right[-1], axis, perm=down))
+    sequence = jnp.stack(left[:0:-1] + right)
+    chip = lax.axis_index(axis) // 2
+    return lax.dynamic_slice_in_dim(sequence, chips - 1 - chip, chips, axis=0)
+
+
 def local(spectra, valid, rcv_count, src_count):
     channels, windows, _, freqs = spectra.shape
     table = lag_table(freqs, LAGS)
     packed = whiten_pack(spectra, valid)
     rec_stack = shifted(packed, "rcv", rcv_count, 1)
-    own_stack = shifted(packed, "src", src_count, 2)
+    own_stack = forwarded(packed, "src", src_count)
     table, rec_stack, own_stack = lax.optimization_barrier((table, rec_stack, own_stack))
     sib_stack = lax.ppermute(own_stack, "src", perm=[(j, j ^ 1) for j in range(src_count)])
     src_index = lax.axis_index("src")

time: 35.9 us -> 49.4 us (1.38)
  starting transfers between devices: 9.66 us -> 21.5 us
  waiting for transfers between devices: 4.17 us -> 6.37 us
  Pallas kernels: 13.9 us -> 12.8 us
  local copies, waits for them, and re-layouts: 0.84 us -> 1.47 us
    ppermute x0 -> x6, starting transfers between devices: none -> 16.4 us  [the longest x3 12.6 us: forwarded(): left.append(lax.ppermute(left[-1], axis, perm=up))]
    ppermute x0 -> x6, waiting for transfers between devices: none -> 5.19 us  [the longest x3 5.18 us: forwarded(): right.append(lax.ppermute(right[-1], axis, perm=down))]
    ppermute x6 -> x3, starting transfers between devices: 9.66 us -> 4.99 us  [shifted(): parts.append(lax.ppermute(x, axis, perm=pairs))]
    ppermute x6 -> x3, waiting for transfers between devices: 2.98 us -> 0.01 us  [shifted(): parts.append(lax.ppermute(x, axis, perm=pairs))]
    pallas_call x1, Pallas kernels: 11.4 us -> 10.3 us  [correlate(): pl.pallas_call(kernel, grid_spec=pltpu.PrefetchScalarGridSpec(num_scalar_...]
    unnamed x6 -> x12, local copies, waits for them, and re-layouts: 0.84 us -> 1.21 us
  transfers between devices with their start and end apart: 7 -> 10, of which waited for: 3 -> 2; matrix products, arithmetic and copies ran while one was open for 15% -> 15% of each run, Pallas kernels for 0% -> 0%
where the time goes in v12:
time: 49.4 us; the launch traced here: 49.1 us
  starting transfers between devices  21.5 us (44%)
  Pallas kernels  12.8 us (26%)
  other arithmetic  6.77 us (14%)
  waiting for transfers between devices  6.37 us (13%)
  local copies, waits for them, and re-layouts  1.47 us (3%)
    ppermute x3, starting transfers between devices, forwarded(): left.append(lax.ppermute(left[-1], axis, perm=up))  12.6 us
    pallas_call x1, Pallas kernels, correlate(): pl.pallas_call(kernel, grid_spec=pltpu.PrefetchScalarGridSpec(num_scalar_...  10.3 us
    ppermute x3, waiting for transfers between devices, forwarded(): right.append(lax.ppermute(right[-1], axis, perm=down))  5.18 us
    ppermute x3, starting transfers between devices, shifted(): parts.append(lax.ppermute(x, axis, perm=pairs))  4.99 us
    ppermute x3, starting transfers between devices, forwarded(): right.append(lax.ppermute(right[-1], axis, perm=down))  3.85 us
    pallas_call x1, Pallas kernels, whiten_pack(): pl.pallas_call(kernel, out_shape=jax.ShapeDtypeStruct((channels, windows...  2.47 us
    another operation x1, other arithmetic, lag_table(): jnp.stack([cosines, sines], axis=0).reshape(2 * freq_count, lag_count)  2.32 us
    convert_element_type x1, other arithmetic, lag_table(): cosines = cosines.reshape(freq_count, lag_count).astype(jnp.bfloat16)  1.55 us
  transfers between devices with their start and end apart: 10, of which 2 were waited for; matrix products, arithmetic and copies ran while one was open for 15% of the time, Pallas kernels for 0%

profile of v12, /device:TPU:0, one launch (start us, length us, event | category | flops | bytes accessed | tf_op | source)
XLA Modules:
  0.0 49.1 jit_solution(10820093035129456232)
XLA Ops:
  0.0 2.5 %shard_map.28 = bf16[4,16512]{1,0:T(4,128)(2,1)} custom-call(bf16[4,4,2,2048]{3,2,1,0:T(2,128)(2,1)} %x_ref.1, s32[4,4]{1,0:T(4,128)} %v_ref.1), custom_call_target="tpu_custom_call" | custom-call | tf_op jit(solution)/shard_map/pallas_call | solution.py:70
  2.5 3.9 %collective-permute-start.2 = (bf16[4,16512]{1,0:T(4,128)(2,1)}, bf16[4,16512]{1,0:T(4,128)(2,1)S(1)}, u32[]{:S(2)}, u32[]{:S(2)}) collective-permute-start(bf16[4,16512]{1,0:T(4,128)(2,1)} %shard_map.28), channel_id=1, source_target_pairs={{0,3},{1,0},{2,1},{3,2},{4,7},{5,4},{6,5},{7,6},{8,11},{9,8},{10,9... | collective-permute-start | bytes 396296 | tf_op jit(solution)/shard_map/ppermute | solution.py:228
  6.4 0.5 %collective-permute-start.1 = (bf16[4,16512]{1,0:T(4,128)(2,1)}, bf16[4,16512]{1,0:T(4,128)(2,1)S(1)}, u32[]{:S(2)}, u32[]{:S(2)}) collective-permute-start(bf16[4,16512]{1,0:T(4,128)(2,1)} %shard_map.28), channel_id=1, source_target_pairs={{0,2},{1,3},{2,0},{3,1},{4,6},{5,7},{6,4},{7,5},{8,10},{9,11},{10,... | collective-permute-start | bytes 396296 | tf_op jit(solution)/shard_map/ppermute | solution.py:228
  6.9 0.6 %collective-permute-start = (bf16[4,16512]{1,0:T(4,128)(2,1)}, bf16[4,16512]{1,0:T(4,128)(2,1)S(1)}, u32[]{:S(2)}, u32[]{:S(2)}) collective-permute-start(bf16[4,16512]{1,0:T(4,128)(2,1)} %shard_map.28), channel_id=1, source_target_pairs={{0,1},{1,2},{2,3},{3,0},{4,5},{5,6},{6,7},{7,4},{8,9},{9,10},{10,1... | collective-permute-start | bytes 396296 | tf_op jit(solution)/shard_map/ppermute | solution.py:228
  7.5 3.5 %collective-permute-start.3 = (bf16[4,16512]{1,0:T(4,128)(2,1)}, bf16[4,16512]{1,0:T(4,128)(2,1)S(1)}, u32[]{:S(2)}, u32[]{:S(2)}) collective-permute-start(bf16[4,16512]{1,0:T(4,128)(2,1)} %shard_map.28), channel_id=1, source_target_pairs={{0,8},{4,12},{8,16},{12,20},{16,24},{20,28},{1,9},{5,13},{9,17},{1... | collective-permute-start | bytes 396296 | tf_op jit(solution)/shard_map/ppermute | solution.py:238
  10.9 1.3 %collective-permute-start.6 = (bf16[4,16512]{1,0:T(4,128)(2,1)}, bf16[4,16512]{1,0:T(4,128)(2,1)S(1)}, u32[]{:S(2)}, u32[]{:S(2)}) collective-permute-start(bf16[4,16512]{1,0:T(4,128)(2,1)} %shard_map.28), channel_id=1, source_target_pairs={{8,0},{12,4},{16,8},{20,12},{24,16},{28,20},{9,1},{13,5},{17,9},{2... | collective-permute-start | bytes 396296 | tf_op jit(solution)/shard_map/ppermute | solution.py:239
  12.3 0.5 %fusion.5 = (f32[64,512]{1,0:T(8,128)S(1)}, f32[64,512]{1,0:T(8,128)S(1)}) fusion(s32[512]{0:T(512)S(1)} %iota_add_fusion), kind=kLoop, calls=%fused_computation.17 | loop fusion | flops 294912 | bytes 264192 | tf_op jit(solution)/shard_map/cos | solution.py:86
  12.8 0.3 fusion.12
  13.2 1.5 %multiply_convert_fusion.1 = (bf16[32,64,512]{2,1,0:T(8,128)(2,1)S(1)}, bf16[32,64,512]{2,1,0:T(8,128)(2,1)S(1)}) fusion(f32[64,512]{1,0:T(8,128)S(1)} %get-tuple-element.16, f32[32,512]{1,0:T(8,128)S(1)} %get-tuple-element.14, f32[64,512]{1,0:T(8,128)S(1)} %get-tuple-element.15, f32[32,512]{1,0:T(8,128)S(1)} %get-tuple-element.13), kind=kLoop, calls=%fused_computation.2 | loop fusion | flops 10485760 | bytes 4587520 | tf_op jit(solution)/shard_map/convert_element_type | solution.py:90
  14.7 0.0 collective-permute-done.3
  14.7 4.6 %collective-permute-start.4 = (bf16[4,16512]{1,0:T(4,128)(2,1)S(1)}, bf16[4,16512]{1,0:T(4,128)(2,1)S(1)}, u32[]{:S(2)}, u32[]{:S(2)}) collective-permute-start(bf16[4,16512]{1,0:T(4,128)(2,1)S(1)} %collective-permute-done.3), channel_id=1, source_target_pairs={{0,8},{4,12},{8,16},{12,20},{16,24},{20,28},{1,9},{5,13},{9,17},{1... | collective-permute-start | bytes 396296 | tf_op jit(solution)/shard_map/ppermute | solution.py:238
  19.3 0.0 copy-start.1
  19.3 2.3 %pad_maximum_fusion = bf16[2,2048,512]{2,1,0:T(8,128)(2,1)} fusion(bf16[1,2048,512]{2,1,0:T(8,128)(2,1)S(1)} %bitcast.26, bf16[1,2048,512]{2,1,0:T(8,128)(2,1)S(1)} %bitcast.25), kind=kLoop, calls=%fused_computation | loop fusion | flops 2097152 | bytes 8388608 | tf_op jit(solution)/shard_map/stack | solution.py:92
  21.6 0.0 collective-permute-done.6
  21.6 1.3 %collective-permute-start.7 = (bf16[4,16512]{1,0:T(4,128)(2,1)S(1)}, bf16[4,16512]{1,0:T(4,128)(2,1)S(1)}, u32[]{:S(2)}, u32[]{:S(2)}) collective-permute-start(bf16[4,16512]{1,0:T(4,128)(2,1)S(1)} %collective-permute-done.6), channel_id=1, source_target_pairs={{8,0},{12,4},{16,8},{20,12},{24,16},{28,20},{9,1},{13,5},{17,9},{2... | collective-permute-start | bytes 396296 | tf_op jit(solution)/shard_map/ppermute | solution.py:239
  22.9 0.0 collective-permute-done.4
  22.9 4.6 %collective-permute-start.5 = (bf16[4,16512]{1,0:T(4,128)(2,1)S(1)}, bf16[4,16512]{1,0:T(4,128)(2,1)S(1)}, u32[]{:S(2)}, u32[]{:S(2)}) collective-permute-start(bf16[4,16512]{1,0:T(4,128)(2,1)S(1)} %collective-permute-done.4), channel_id=1, source_target_pairs={{0,8},{4,12},{8,16},{12,20},{16,24},{20,28},{1,9},{5,13},{9,17},{1... | collective-permute-start | bytes 396296 | tf_op jit(solution)/shard_map/ppermute | solution.py:238
  27.5 0.0 collective-permute-done.2
  27.5 0.0 collective-permute-done.1
  27.5 0.0 collective-permute-done
  27.5 0.0 copy-done.1
  27.5 1.3 %pad_maximum_fusion.1.rec_ref = bf16[4,4,16512]{2,1,0:T(4,128)(2,1)} fusion(bf16[1,4,16512]{2,1,0:T(4,128)(2,1)S(1)} %bitcast.28, bf16[1,4,16512]{2,1,0:T(4,128)(2,1)S(1)} %bitcast.29, bf16[1,4,16512]{2,1,0:T(4,128)(2,1)S(1)} %bitcast.30, bf16[1,4,16512]{2,1,0:T(4,128)(2,1)S(1)} %bitcast.27), kind=kLoop, calls=%fused_computation.3 | loop fusion | flops 792576 | bytes 1056768 | tf_op jit(solution)/shard_map/stack | solution.py:229
  28.8 0.0 collective-permute-done.7
  28.8 1.3 %collective-permute-start.8 = (bf16[4,16512]{1,0:T(4,128)(2,1)S(1)}, bf16[4,16512]{1,0:T(4,128)(2,1)S(1)}, u32[]{:S(2)}, u32[]{:S(2)}) collective-permute-start(bf16[4,16512]{1,0:T(4,128)(2,1)S(1)} %collective-permute-done.7), channel_id=1, source_target_pairs={{8,0},{12,4},{16,8},{20,12},{24,16},{28,20},{9,1},{13,5},{17,9},{2... | collective-permute-start | bytes 396296 | tf_op jit(solution)/shard_map/ppermute | solution.py:239
  30.1 0.0 collective-permute-done.5
  30.2 0.1 bitcast_dynamic-update-slice_fusion.4
  30.2 0.1 bitcast_dynamic-update-slice_fusion.3
  30.3 0.1 constant_dynamic-update-slice_fusion
  30.4 0.1 bitcast_dynamic-update-slice_fusion.2
  30.4 0.1 bitcast_dynamic-update-slice_fusion.1
  30.5 5.2 %collective-permute-done.8 = bf16[4,16512]{1,0:T(4,128)(2,1)S(1)} collective-permute-done((bf16[4,16512]{1,0:T(4,128)(2,1)S(1)}, bf16[4,16512]{1,0:T(4,128)(2,1)S(1)}, u32[]{:S(2)}, u32[]{:S(2)}) %collective-permute-start.8) | collective-permute-done | bytes 132128 | tf_op jit(solution)/shard_map/ppermute | solution.py:239
  35.7 0.1 bitcast_dynamic-update-slice_fusion
  35.7 0.2 constant_dynamic-slice_fusion.own_ref
  35.9 0.0 copy-start
  36.0 0.1 collective-permute-start.9
  36.0 0.7 %pad_add_fusion.place_ref = s32[3]{0:T(128)} fusion(s32[1]{0:T(128)} %bitcast.2, s32[1]{0:T(128)} %bitcast.1, s32[1]{0:T(128)} %bitcast), kind=kLoop, calls=%fused_computation.30 | loop fusion | flops 6 | bytes 24 | tf_op jit(solution)/shard_map/stack | solution.py:254
  36.8 1.2 %collective-permute-done.9.sib_ref = bf16[4,4,16512]{2,1,0:T(4,128)(2,1)S(1)} collective-permute-done((bf16[4,4,16512]{2,1,0:T(4,128)(2,1)S(1)}, bf16[4,4,16512]{2,1,0:T(4,128)(2,1)S(1)}, u32[]{:S(2)}, u32[]{:S(2)}) %collective-permute-start.9) | collective-permute-done | bytes 528416 | tf_op jit(solution)/shard_map/ppermute | solution.py:252
  37.9 0.0 copy-done
  37.9 0.0 copy-start.2
  37.9 0.8 %copy-done.2 = bf16[4,4,16512]{2,1,0:T(4,128)(2,1)} copy-done((bf16[4,4,16512]{2,1,0:T(4,128)(2,1)}, bf16[4,4,16512]{2,1,0:T(4,128)(2,1)S(1)}, u32[]{:S(2)}) %copy-start.2) | copy-done | bytes 528408
  38.8 10.3 %shard_map.29 = bf16[512,512]{1,0:T(8,128)(2,1)} custom-call(s32[3]{0:T(128)} %pad_add_fusion.place_ref, bf16[4,4,16512]{2,1,0:T(4,128)(2,1)} %pad_maximum_fusion.1.rec_ref, bf16[4,4,16512]{2,1,0:T(4,128)(2,1)} %copy-done, bf16[4,4,16512]{2,1,0:T(4,128)(2,1)} %copy-done.2, bf16[4096,512]{1,0:T(8,128)(2,1)} %bitcast.24), custom_call_target="tpu_custom_call" | custom-call | tf_op jit(solution)/shard_map/pallas_call | solution.py:196
  (3 shorter events, 0.1 us)
Async XLA Ops:
  2.5 25.0 %collective-permute-start.2 = (bf16[4,16512]{1,0:T(4,128)(2,1)}, bf16[4,16512]{1,0:T(4,128)(2,1)S(1)}, u32[]{:S(2)}, u32[]{:S(2)}) collective-permute-start(bf16[4,16512]{1,0:T(4,128)(2,1)} %shard_map.28), channel_id=1, source_target_pairs={{0,3},{1,0},{2,1},{3,2},{4,7},{5,4},{6,5},{7,6},{8,11},{9,8},{10,9... | collective-permute-start | bytes 396296 | tf_op jit(solution)/shard_map/ppermute | solution.py:228
  6.4 21.1 %collective-permute-start.1 = (bf16[4,16512]{1,0:T(4,128)(2,1)}, bf16[4,16512]{1,0:T(4,128)(2,1)S(1)}, u32[]{:S(2)}, u32[]{:S(2)}) collective-permute-start(bf16[4,16512]{1,0:T(4,128)(2,1)} %shard_map.28), channel_id=1, source_target_pairs={{0,2},{1,3},{2,0},{3,1},{4,6},{5,7},{6,4},{7,5},{8,10},{9,11},{10,... | collective-permute-start | bytes 396296 | tf_op jit(solution)/shard_map/ppermute | solution.py:228
  6.9 20.6 %collective-permute-start = (bf16[4,16512]{1,0:T(4,128)(2,1)}, bf16[4,16512]{1,0:T(4,128)(2,1)S(1)}, u32[]{:S(2)}, u32[]{:S(2)}) collective-permute-start(bf16[4,16512]{1,0:T(4,128)(2,1)} %shard_map.28), channel_id=1, source_target_pairs={{0,1},{1,2},{2,3},{3,0},{4,5},{5,6},{6,7},{7,4},{8,9},{9,10},{10,1... | collective-permute-start | bytes 396296 | tf_op jit(solution)/shard_map/ppermute | solution.py:228
  7.5 7.3 %collective-permute-start.3 = (bf16[4,16512]{1,0:T(4,128)(2,1)}, bf16[4,16512]{1,0:T(4,128)(2,1)S(1)}, u32[]{:S(2)}, u32[]{:S(2)}) collective-permute-start(bf16[4,16512]{1,0:T(4,128)(2,1)} %shard_map.28), channel_id=1, source_target_pairs={{0,8},{4,12},{8,16},{12,20},{16,24},{20,28},{1,9},{5,13},{9,17},{1... | collective-permute-start | bytes 396296 | tf_op jit(solution)/shard_map/ppermute | solution.py:238
  10.9 10.7 %collective-permute-start.6 = (bf16[4,16512]{1,0:T(4,128)(2,1)}, bf16[4,16512]{1,0:T(4,128)(2,1)S(1)}, u32[]{:S(2)}, u32[]{:S(2)}) collective-permute-start(bf16[4,16512]{1,0:T(4,128)(2,1)} %shard_map.28), channel_id=1, source_target_pairs={{8,0},{12,4},{16,8},{20,12},{24,16},{28,20},{9,1},{13,5},{17,9},{2... | collective-permute-start | bytes 396296 | tf_op jit(solution)/shard_map/ppermute | solution.py:239
  14.7 8.2 %collective-permute-start.4 = (bf16[4,16512]{1,0:T(4,128)(2,1)S(1)}, bf16[4,16512]{1,0:T(4,128)(2,1)S(1)}, u32[]{:S(2)}, u32[]{:S(2)}) collective-permute-start(bf16[4,16512]{1,0:T(4,128)(2,1)S(1)} %collective-permute-done.3), channel_id=1, source_target_pairs={{0,8},{4,12},{8,16},{12,20},{16,24},{20,28},{1,9},{5,13},{9,17},{1... | collective-permute-start | bytes 396296 | tf_op jit(solution)/shard_map/ppermute | solution.py:238
  19.3 8.2 %copy-start.1 = (bf16[4,16512]{1,0:T(4,128)(2,1)S(1)}, bf16[4,16512]{1,0:T(4,128)(2,1)}, u32[]{:S(2)}) copy-start(bf16[4,16512]{1,0:T(4,128)(2,1)} %shard_map.28) | copy-start | bytes 396292
  21.6 7.2 %collective-permute-start.7 = (bf16[4,16512]{1,0:T(4,128)(2,1)S(1)}, bf16[4,16512]{1,0:T(4,128)(2,1)S(1)}, u32[]{:S(2)}, u32[]{:S(2)}) collective-permute-start(bf16[4,16512]{1,0:T(4,128)(2,1)S(1)} %collective-permute-done.6), channel_id=1, source_target_pairs={{8,0},{12,4},{16,8},{20,12},{24,16},{28,20},{9,1},{13,5},{17,9},{2... | collective-permute-start | bytes 396296 | tf_op jit(solution)/shard_map/ppermute | solution.py:239
  22.9 7.2 %collective-permute-start.5 = (bf16[4,16512]{1,0:T(4,128)(2,1)S(1)}, bf16[4,16512]{1,0:T(4,128)(2,1)S(1)}, u32[]{:S(2)}, u32[]{:S(2)}) collective-permute-start(bf16[4,16512]{1,0:T(4,128)(2,1)S(1)} %collective-permute-done.4), channel_id=1, source_target_pairs={{0,8},{4,12},{8,16},{12,20},{16,24},{20,28},{1,9},{5,13},{9,17},{1... | collective-permute-start | bytes 396296 | tf_op jit(solution)/shard_map/ppermute | solution.py:238
  28.8 6.9 %collective-permute-start.8 = (bf16[4,16512]{1,0:T(4,128)(2,1)S(1)}, bf16[4,16512]{1,0:T(4,128)(2,1)S(1)}, u32[]{:S(2)}, u32[]{:S(2)}) collective-permute-start(bf16[4,16512]{1,0:T(4,128)(2,1)S(1)} %collective-permute-done.7), channel_id=1, source_target_pairs={{8,0},{12,4},{16,8},{20,12},{24,16},{28,20},{9,1},{13,5},{17,9},{2... | collective-permute-start | bytes 396296 | tf_op jit(solution)/shard_map/ppermute | solution.py:239
  35.9 2.0 %copy-start = (bf16[4,4,16512]{2,1,0:T(4,128)(2,1)}, bf16[4,4,16512]{2,1,0:T(4,128)(2,1)S(1)}, u32[]{:S(2)}) copy-start(bf16[4,4,16512]{2,1,0:T(4,128)(2,1)S(1)} %constant_dynamic-slice_fusion.own_ref) | copy-start | bytes 1585156
  36.0 2.0 %collective-permute-start.9 = (bf16[4,4,16512]{2,1,0:T(4,128)(2,1)S(1)}, bf16[4,4,16512]{2,1,0:T(4,128)(2,1)S(1)}, u32[]{:S(2)}, u32[]{:S(2)}) collective-permute-start(bf16[4,4,16512]{2,1,0:T(4,128)(2,1)S(1)} %constant_dynamic-slice_fusion.own_ref), channel_id=1, source_target_pairs={{0,4},{4,0},{8,12},{12,8},{16,20},{20,16},{24,28},{28,24},{1,5},{5... | collective-permute-start | bytes 1585160 | tf_op jit(solution)/shard_map/ppermute | solution.py:252
  37.9 0.8 %copy-start.2 = (bf16[4,4,16512]{2,1,0:T(4,128)(2,1)}, bf16[4,4,16512]{2,1,0:T(4,128)(2,1)S(1)}, u32[]{:S(2)}) copy-start(bf16[4,4,16512]{2,1,0:T(4,128)(2,1)S(1)} %collective-permute-done.9.sib_ref) | copy-start | bytes 1585156

commit v13 on v11

--- a/solution.py
+++ b/solution.py
@@ -126,12 +126,8 @@
     @pl.when(step == 0)
     def _():
         rcv_index, chip, core = place_ref[0], place_ref[1], place_ref[2]
-        for rot in range(rcv_count):
-
-            @pl.when(rcv_index == rot)
-            def _():
-                for dst in range(rcv_count):
-                    place(rec_ref[(rot - dst) % rcv_count], dst, recf, rtails, False)
+        for dst in range(rcv_count):
+            place(rec_ref[dst], dst, recf, rtails, False)
 
         for rot in range(chips):
             for mine in range(2):
@@ -234,7 +230,8 @@
     channels, windows, _, freqs = spectra.shape
     table = lag_table(freqs, LAGS)
     packed = whiten_pack(spectra, valid)
-    rec_stack = shifted(packed, "rcv", rcv_count, 1)
+    copies = jnp.broadcast_to(packed[None], (rcv_count,) + packed.shape)
+    rec_stack = lax.all_to_all(copies, "rcv", 0, 0, tiled=True)
     own_stack = shifted(packed, "src", src_count, 2)
     table, rec_stack, own_stack = lax.optimization_barrier((table, rec_stack, own_stack))
     sib_stack = lax.ppermute(own_stack, "src", perm=[(j, j ^ 1) for j in range(src_count)])

time: 35.9 us -> 36.8 us (1.025)
  local copies, waits for them, and re-layouts: 0.84 us -> 2.73 us
  other arithmetic: 7.15 us -> 5.92 us
  starting transfers between devices: 9.66 us -> 10.7 us
  waiting for transfers between devices: 4.17 us -> 3.17 us
    all_to_all x0 -> x1, starting transfers between devices: none -> 3.72 us  [local(): rec_stack = lax.all_to_all(copies, 'rcv', 0, 0, tiled=True)]
    ppermute x6 -> x3, waiting for transfers between devices: 2.98 us -> 0.01 us  [shifted(): parts.append(lax.ppermute(x, axis, perm=pairs))]
    ppermute x6 -> x3, starting transfers between devices: 9.66 us -> 6.96 us  [shifted(): parts.append(lax.ppermute(x, axis, perm=pairs))]
    all_to_all x0 -> x1, waiting for transfers between devices: none -> 1.93 us  [local(): rec_stack = lax.all_to_all(copies, 'rcv', 0, 0, tiled=True)]
    broadcast_in_dim x0 -> x1, local copies, waits for them, and re-layouts: none -> 1.88 us  [local(): copies = jnp.broadcast_to(packed[None], (rcv_count,) + packed.shape)]
    another operation x1, other arithmetic: 1.69 us -> 0.48 us  [shifted(): return jnp.stack(parts)]
    unnamed x6 -> x8, local copies, waits for them, and re-layouts: 0.84 us -> 0.85 us
  transfers between devices with their start and end apart: 7 -> 5, of which waited for: 3 -> 2; matrix products, arithmetic and copies ran while one was open for 15% -> 21% of each run, Pallas kernels for 0% -> 0%
where the time goes in v13:
time: 36.8 us; the launch traced here: 36.6 us
  Pallas kernels  14 us (38%)
  starting transfers between devices  10.7 us (29%)
  other arithmetic  5.92 us (16%)
  waiting for transfers between devices  3.17 us (9%)
  local copies, waits for them, and re-layouts  2.73 us (7%)
    pallas_call x1, Pallas kernels, correlate(): pl.pallas_call(kernel, grid_spec=pltpu.PrefetchScalarGridSpec(num_scalar_...  11.6 us
    ppermute x3, starting transfers between devices, shifted(): parts.append(lax.ppermute(x, axis, perm=pairs))  6.96 us
    all_to_all x1, starting transfers between devices, local(): rec_stack = lax.all_to_all(copies, 'rcv', 0, 0, tiled=True)  3.72 us
    pallas_call x1, Pallas kernels, whiten_pack(): pl.pallas_call(kernel, out_shape=jax.ShapeDtypeStruct((channels, windows...  2.47 us
    another operation x1, other arithmetic, lag_table(): jnp.stack([cosines, sines], axis=0).reshape(2 * freq_count, lag_count)  2.31 us
    all_to_all x1, waiting for transfers between devices, local(): rec_stack = lax.all_to_all(copies, 'rcv', 0, 0, tiled=True)  1.93 us
    broadcast_in_dim x1, local copies, waits for them, and re-layouts, local(): copies = jnp.broadcast_to(packed[None], (rcv_count,) + packed.shape)  1.88 us
    convert_element_type x1, other arithmetic, lag_table(): cosines = cosines.reshape(freq_count, lag_count).astype(jnp.bfloat16)  1.55 us
  transfers between devices with their start and end apart: 5, of which 2 were waited for; matrix products, arithmetic and copies ran while one was open for 21% of the time, Pallas kernels for 0%

profile of v13, /device:TPU:0, one launch (start us, length us, event | category | flops | bytes accessed | tf_op | source)
XLA Modules:
  0.0 36.6 jit_solution(17206991560301451205)
XLA Ops:
  0.0 2.5 %shard_map.28 = bf16[4,16512]{1,0:T(4,128)(2,1)} custom-call(bf16[4,4,2,2048]{3,2,1,0:T(2,128)(2,1)} %x_ref.1, s32[4,4]{1,0:T(4,128)} %v_ref.1), custom_call_target="tpu_custom_call" | custom-call | tf_op jit(solution)/shard_map/pallas_call | solution.py:70
  2.5 3.0 %collective-permute-start = (bf16[4,16512]{1,0:T(4,128)(2,1)}, bf16[4,16512]{1,0:T(4,128)(2,1)S(1)}, u32[]{:S(2)}, u32[]{:S(2)}) collective-permute-start(bf16[4,16512]{1,0:T(4,128)(2,1)} %shard_map.28), channel_id=1, source_target_pairs={{0,8},{4,12},{8,16},{12,20},{16,24},{20,28},{24,0},{28,4},{1,9},{5... | collective-permute-start | bytes 396296 | tf_op jit(solution)/shard_map/ppermute | solution.py:225
  5.5 2.6 %collective-permute-start.1 = (bf16[4,16512]{1,0:T(4,128)(2,1)}, bf16[4,16512]{1,0:T(4,128)(2,1)S(1)}, u32[]{:S(2)}, u32[]{:S(2)}) collective-permute-start(bf16[4,16512]{1,0:T(4,128)(2,1)} %shard_map.28), channel_id=1, source_target_pairs={{0,16},{4,20},{8,24},{12,28},{16,0},{20,4},{24,8},{28,12},{1,17},{... | collective-permute-start | bytes 396296 | tf_op jit(solution)/shard_map/ppermute | solution.py:225
  8.1 1.3 %collective-permute-start.2 = (bf16[4,16512]{1,0:T(4,128)(2,1)}, bf16[4,16512]{1,0:T(4,128)(2,1)S(1)}, u32[]{:S(2)}, u32[]{:S(2)}) collective-permute-start(bf16[4,16512]{1,0:T(4,128)(2,1)} %shard_map.28), channel_id=1, source_target_pairs={{0,24},{4,28},{8,0},{12,4},{16,8},{20,12},{24,16},{28,20},{1,25},{... | collective-permute-start | bytes 396296 | tf_op jit(solution)/shard_map/ppermute | solution.py:225
  9.4 1.9 %broadcast_in_dim.4 = bf16[4,4,16512]{2,1,0:T(4,128)(2,1)} broadcast(bf16[4,16512]{1,0:T(4,128)(2,1)} %shard_map.28), dimensions={1,2} | broadcast | bytes 660480 | tf_op jit(solution)/shard_map/broadcast_in_dim | solution.py:233
  11.3 3.7 %all-to-all-start = ((bf16[4,4,16512]{2,1,0:T(4,128)(2,1)}), bf16[4,4,16512]{2,1,0:T(4,128)(2,1)S(1)}, u32[]{:S(2)}, u32[]{:S(2)}) async-start(bf16[4,4,16512]{2,1,0:T(4,128)(2,1)} %broadcast_in_dim.4), calls=%async_computation | async-start | bytes 1056768 | tf_op jit(solution)/shard_map/all_to_all | solution.py:234
  15.0 0.5 %fusion.5 = (f32[64,512]{1,0:T(8,128)S(1)}, f32[64,512]{1,0:T(8,128)S(1)}) fusion(s32[512]{0:T(512)S(1)} %iota_add_fusion), kind=kLoop, calls=%fused_computation.11 | loop fusion | flops 294912 | bytes 264192 | tf_op jit(solution)/shard_map/cos | solution.py:86
  15.6 0.3 fusion.12
  15.9 1.5 %multiply_convert_fusion.1 = (bf16[32,64,512]{2,1,0:T(8,128)(2,1)S(1)}, bf16[32,64,512]{2,1,0:T(8,128)(2,1)S(1)}) fusion(f32[64,512]{1,0:T(8,128)S(1)} %get-tuple-element.16, f32[32,512]{1,0:T(8,128)S(1)} %get-tuple-element.14, f32[64,512]{1,0:T(8,128)S(1)} %get-tuple-element.15, f32[32,512]{1,0:T(8,128)S(1)} %get-tuple-element.13), kind=kLoop, calls=%fused_computation.2 | loop fusion | flops 10485760 | bytes 4587520 | tf_op jit(solution)/shard_map/convert_element_type | solution.py:90
  17.5 0.0 copy-start.2
  17.5 2.3 %pad_maximum_fusion = bf16[2,2048,512]{2,1,0:T(8,128)(2,1)} fusion(bf16[1,2048,512]{2,1,0:T(8,128)(2,1)S(1)} %bitcast.13, bf16[1,2048,512]{2,1,0:T(8,128)(2,1)S(1)} %bitcast.12), kind=kLoop, calls=%fused_computation | loop fusion | flops 2097152 | bytes 8388608 | tf_op jit(solution)/shard_map/stack | solution.py:92
  19.8 0.0 collective-permute-done
  19.8 0.0 collective-permute-done.1
  19.8 0.0 collective-permute-done.2
  19.8 0.0 copy-done.2
  19.8 0.5 %pad_maximum_fusion.1.own_ref = bf16[4,4,16512]{2,1,0:T(4,128)(2,1)S(1)} fusion(bf16[1,4,16512]{2,1,0:T(4,128)(2,1)S(1)} %bitcast.17, bf16[1,4,16512]{2,1,0:T(4,128)(2,1)S(1)} %bitcast.16, bf16[1,4,16512]{2,1,0:T(4,128)(2,1)S(1)} %bitcast.15, bf16[1,4,16512]{2,1,0:T(4,128)(2,1)S(1)} %bitcast.14), kind=kLoop, calls=%fused_computation.3 | loop fusion | flops 792576 | bytes 1056768 | tf_op jit(solution)/shard_map/stack | solution.py:226
  20.3 0.0 copy-start.1
  20.3 1.9 %all-to-all-done.rec_ref = bf16[4,4,16512]{2,1,0:T(4,128)(2,1)S(1)} async-done(((bf16[4,4,16512]{2,1,0:T(4,128)(2,1)}), bf16[4,4,16512]{2,1,0:T(4,128)(2,1)S(1)}, u32[]{:S(2)}, u32[]{:S(2)}) %all-to-all-start) | async-done | bytes 528416 | tf_op jit(solution)/shard_map/all_to_all | solution.py:234
  22.3 0.0 copy-start
  22.3 0.0 collective-permute-start.3
  22.3 0.7 %pad_add_fusion.place_ref = s32[3]{0:T(128)} fusion(s32[1]{0:T(128)} %bitcast.2, s32[1]{0:T(128)} %bitcast.1, s32[1]{0:T(128)} %bitcast), kind=kLoop, calls=%fused_computation.23 | loop fusion | flops 6 | bytes 24 | tf_op jit(solution)/shard_map/stack | solution.py:239
  22.9 1.2 %collective-permute-done.3.sib_ref = bf16[4,4,16512]{2,1,0:T(4,128)(2,1)S(1)} collective-permute-done((bf16[4,4,16512]{2,1,0:T(4,128)(2,1)S(1)}, bf16[4,4,16512]{2,1,0:T(4,128)(2,1)S(1)}, u32[]{:S(2)}, u32[]{:S(2)}) %collective-permute-start.3) | collective-permute-done | bytes 528416 | tf_op jit(solution)/shard_map/ppermute | solution.py:237
  24.2 0.0 copy-done.1
  24.2 0.0 copy-done
  24.2 0.0 copy-start.3
  24.2 0.8 %copy-done.3 = bf16[4,4,16512]{2,1,0:T(4,128)(2,1)} copy-done((bf16[4,4,16512]{2,1,0:T(4,128)(2,1)}, bf16[4,4,16512]{2,1,0:T(4,128)(2,1)S(1)}, u32[]{:S(2)}) %copy-start.3) | copy-done | bytes 528408
  25.0 11.6 %shard_map.29 = bf16[512,512]{1,0:T(8,128)(2,1)} custom-call(s32[3]{0:T(128)} %pad_add_fusion.place_ref, bf16[4,4,16512]{2,1,0:T(4,128)(2,1)} %copy-done, bf16[4,4,16512]{2,1,0:T(4,128)(2,1)} %copy-done.1, bf16[4,4,16512]{2,1,0:T(4,128)(2,1)} %copy-done.3, bf16[4096,512]{1,0:T(8,128)(2,1)} %bitcast.11), custom_call_target="tpu_custom_call" | custom-call | tf_op jit(solution)/shard_map/pallas_call | solution.py:193
  (2 shorter events, 0.0 us)
Async XLA Ops:
  2.5 17.3 %collective-permute-start = (bf16[4,16512]{1,0:T(4,128)(2,1)}, bf16[4,16512]{1,0:T(4,128)(2,1)S(1)}, u32[]{:S(2)}, u32[]{:S(2)}) collective-permute-start(bf16[4,16512]{1,0:T(4,128)(2,1)} %shard_map.28), channel_id=1, source_target_pairs={{0,8},{4,12},{8,16},{12,20},{16,24},{20,28},{24,0},{28,4},{1,9},{5... | collective-permute-start | bytes 396296 | tf_op jit(solution)/shard_map/ppermute | solution.py:225
  5.5 14.3 %collective-permute-start.1 = (bf16[4,16512]{1,0:T(4,128)(2,1)}, bf16[4,16512]{1,0:T(4,128)(2,1)S(1)}, u32[]{:S(2)}, u32[]{:S(2)}) collective-permute-start(bf16[4,16512]{1,0:T(4,128)(2,1)} %shard_map.28), channel_id=1, source_target_pairs={{0,16},{4,20},{8,24},{12,28},{16,0},{20,4},{24,8},{28,12},{1,17},{... | collective-permute-start | bytes 396296 | tf_op jit(solution)/shard_map/ppermute | solution.py:225
  8.1 11.7 %collective-permute-start.2 = (bf16[4,16512]{1,0:T(4,128)(2,1)}, bf16[4,16512]{1,0:T(4,128)(2,1)S(1)}, u32[]{:S(2)}, u32[]{:S(2)}) collective-permute-start(bf16[4,16512]{1,0:T(4,128)(2,1)} %shard_map.28), channel_id=1, source_target_pairs={{0,24},{4,28},{8,0},{12,4},{16,8},{20,12},{24,16},{28,20},{1,25},{... | collective-permute-start | bytes 396296 | tf_op jit(solution)/shard_map/ppermute | solution.py:225
  11.3 10.9 %all-to-all-start = ((bf16[4,4,16512]{2,1,0:T(4,128)(2,1)}), bf16[4,4,16512]{2,1,0:T(4,128)(2,1)S(1)}, u32[]{:S(2)}, u32[]{:S(2)}) async-start(bf16[4,4,16512]{2,1,0:T(4,128)(2,1)} %broadcast_in_dim.4), calls=%async_computation | async-start | bytes 1056768 | tf_op jit(solution)/shard_map/all_to_all | solution.py:234
  17.5 2.3 %copy-start.2 = (bf16[4,16512]{1,0:T(4,128)(2,1)S(1)}, bf16[4,16512]{1,0:T(4,128)(2,1)}, u32[]{:S(2)}) copy-start(bf16[4,16512]{1,0:T(4,128)(2,1)} %shard_map.28) | copy-start | bytes 396292
  20.3 3.9 %copy-start.1 = (bf16[4,4,16512]{2,1,0:T(4,128)(2,1)}, bf16[4,4,16512]{2,1,0:T(4,128)(2,1)S(1)}, u32[]{:S(2)}) copy-start(bf16[4,4,16512]{2,1,0:T(4,128)(2,1)S(1)} %pad_maximum_fusion.1.own_ref) | copy-start | bytes 1585156
  22.3 1.9 %copy-start = (bf16[4,4,16512]{2,1,0:T(4,128)(2,1)}, bf16[4,4,16512]{2,1,0:T(4,128)(2,1)S(1)}, u32[]{:S(2)}) copy-start(bf16[4,4,16512]{2,1,0:T(4,128)(2,1)S(1)} %all-to-all-done.rec_ref) | copy-start | bytes 1585156
  22.3 1.9 %collective-permute-start.3 = (bf16[4,4,16512]{2,1,0:T(4,128)(2,1)S(1)}, bf16[4,4,16512]{2,1,0:T(4,128)(2,1)S(1)}, u32[]{:S(2)}, u32[]{:S(2)}) collective-permute-start(bf16[4,4,16512]{2,1,0:T(4,128)(2,1)S(1)} %pad_maximum_fusion.1.own_ref), channel_id=1, source_target_pairs={{0,4},{4,0},{8,12},{12,8},{16,20},{20,16},{24,28},{28,24},{1,5},{5... | collective-permute-start | bytes 1585160 | tf_op jit(solution)/shard_map/ppermute | solution.py:237
  24.2 0.8 %copy-start.3 = (bf16[4,4,16512]{2,1,0:T(4,128)(2,1)}, bf16[4,4,16512]{2,1,0:T(4,128)(2,1)S(1)}, u32[]{:S(2)}) copy-start(bf16[4,4,16512]{2,1,0:T(4,128)(2,1)S(1)} %collective-permute-done.3.sib_ref) | copy-start | bytes 1585156

commit v14 on v11

--- a/solution.py
+++ b/solution.py
@@ -227,7 +227,10 @@
     for shift in range(1, count // stride):
         pairs = [(j, (j + stride * shift) % count) for j in range(count)]
         parts.append(lax.ppermute(x, axis, perm=pairs))
-    return jnp.stack(parts)
+    stack = jnp.zeros((len(parts),) + x.shape, x.dtype)
+    for k, part in enumerate(parts):
+        stack = lax.dynamic_update_slice_in_dim(stack, part[None], k, axis=0)
+    return stack
 
 
 def local(spectra, valid, rcv_count, src_count):

time: 35.9 us -> 37.8 us (1.053)
  starting transfers between devices: 9.66 us -> 11.5 us
  other arithmetic: 7.15 us -> 5.37 us
  waiting for transfers between devices: 4.17 us -> 5.22 us
  local copies, waits for them, and re-layouts: 0.84 us -> 1.56 us
    ppermute x6, starting transfers between devices: 9.66 us -> 11.5 us  [shifted(): parts.append(lax.ppermute(x, axis, perm=pairs))]
    another operation x1 -> x0, other arithmetic: 1.69 us -> none  [shifted(): return jnp.stack(parts)]
    ppermute x6, waiting for transfers between devices: 2.98 us -> 3.99 us  [shifted(): parts.append(lax.ppermute(x, axis, perm=pairs))]
    dynamic_update_slice x0 -> x7, local copies, waits for them, and re-layouts: none -> 0.53 us  [shifted(): stack = lax.dynamic_update_slice_in_dim(stack, part[None], k, axis=0)]
    unnamed x6 -> x9, local copies, waits for them, and re-layouts: 0.84 us -> 1.03 us
  transfers between devices with their start and end apart: 7 -> 7, of which waited for: 3 -> 3; matrix products, arithmetic and copies ran while one was open for 15% -> 16% of each run, Pallas kernels for 0% -> 0%
where the time goes in v14:
time: 37.8 us; the launch traced here: 37.7 us
  Pallas kernels  13.9 us (37%)
  starting transfers between devices  11.5 us (30%)
  other arithmetic  5.37 us (14%)
  waiting for transfers between devices  5.22 us (14%)
  local copies, waits for them, and re-layouts  1.56 us (4%)
    ppermute x6, starting transfers between devices, shifted(): parts.append(lax.ppermute(x, axis, perm=pairs))  11.5 us
    pallas_call x1, Pallas kernels, correlate(): pl.pallas_call(kernel, grid_spec=pltpu.PrefetchScalarGridSpec(num_scalar_...  11.4 us
    ppermute x6, waiting for transfers between devices, shifted(): parts.append(lax.ppermute(x, axis, perm=pairs))  3.99 us
    pallas_call x1, Pallas kernels, whiten_pack(): pl.pallas_call(kernel, out_shape=jax.ShapeDtypeStruct((channels, windows...  2.47 us
    another operation x1, other arithmetic, lag_table(): jnp.stack([cosines, sines], axis=0).reshape(2 * freq_count, lag_count)  2.31 us
    convert_element_type x1, other arithmetic, lag_table(): cosines = cosines.reshape(freq_count, lag_count).astype(jnp.bfloat16)  1.51 us
    ppermute x1, waiting for transfers between devices, local(): lax.ppermute(own_stack, 'src', perm=[(j, j ^ 1) for j in range(src_count)])  1.23 us
    unnamed x9, local copies, waits for them, and re-layouts  1.03 us
  transfers between devices with their start and end apart: 7, of which 3 were waited for; matrix products, arithmetic and copies ran while one was open for 16% of the time, Pallas kernels for 0%

profile of v14, /device:TPU:0, one launch (start us, length us, event | category | flops | bytes accessed | tf_op | source)
XLA Modules:
  0.0 37.7 jit_solution(15055404251184556600)
XLA Ops:
  0.0 2.5 %shard_map.28 = bf16[4,16512]{1,0:T(4,128)(2,1)} custom-call(bf16[4,4,2,2048]{3,2,1,0:T(2,128)(2,1)} %x_ref.1, s32[4,4]{1,0:T(4,128)} %v_ref.1), custom_call_target="tpu_custom_call" | custom-call | tf_op jit(solution)/shard_map/pallas_call | solution.py:70
  2.5 2.9 %collective-permute-start = (bf16[4,16512]{1,0:T(4,128)(2,1)}, bf16[4,16512]{1,0:T(4,128)(2,1)S(1)}, u32[]{:S(2)}, u32[]{:S(2)}) collective-permute-start(bf16[4,16512]{1,0:T(4,128)(2,1)} %shard_map.28), channel_id=1, source_target_pairs={{0,1},{1,2},{2,3},{3,0},{4,5},{5,6},{6,7},{7,4},{8,9},{9,10},{10,1... | collective-permute-start | bytes 396296 | tf_op jit(solution)/shard_map/ppermute | solution.py:229
  5.4 1.5 %collective-permute-start.1 = (bf16[4,16512]{1,0:T(4,128)(2,1)}, bf16[4,16512]{1,0:T(4,128)(2,1)S(1)}, u32[]{:S(2)}, u32[]{:S(2)}) collective-permute-start(bf16[4,16512]{1,0:T(4,128)(2,1)} %shard_map.28), channel_id=1, source_target_pairs={{0,2},{1,3},{2,0},{3,1},{4,6},{5,7},{6,4},{7,5},{8,10},{9,11},{10,... | collective-permute-start | bytes 396296 | tf_op jit(solution)/shard_map/ppermute | solution.py:229
  6.9 1.4 %collective-permute-start.2 = (bf16[4,16512]{1,0:T(4,128)(2,1)}, bf16[4,16512]{1,0:T(4,128)(2,1)S(1)}, u32[]{:S(2)}, u32[]{:S(2)}) collective-permute-start(bf16[4,16512]{1,0:T(4,128)(2,1)} %shard_map.28), channel_id=1, source_target_pairs={{0,3},{1,0},{2,1},{3,2},{4,7},{5,4},{6,5},{7,6},{8,11},{9,8},{10,9... | collective-permute-start | bytes 396296 | tf_op jit(solution)/shard_map/ppermute | solution.py:229
  8.4 1.6 %collective-permute-start.3 = (bf16[4,16512]{1,0:T(4,128)(2,1)}, bf16[4,16512]{1,0:T(4,128)(2,1)S(1)}, u32[]{:S(2)}, u32[]{:S(2)}) collective-permute-start(bf16[4,16512]{1,0:T(4,128)(2,1)} %shard_map.28), channel_id=1, source_target_pairs={{0,8},{4,12},{8,16},{12,20},{16,24},{20,28},{24,0},{28,4},{1,9},{5... | collective-permute-start | bytes 396296 | tf_op jit(solution)/shard_map/ppermute | solution.py:229
  9.9 2.6 %collective-permute-start.4 = (bf16[4,16512]{1,0:T(4,128)(2,1)}, bf16[4,16512]{1,0:T(4,128)(2,1)S(1)}, u32[]{:S(2)}, u32[]{:S(2)}) collective-permute-start(bf16[4,16512]{1,0:T(4,128)(2,1)} %shard_map.28), channel_id=1, source_target_pairs={{0,16},{4,20},{8,24},{12,28},{16,0},{20,4},{24,8},{28,12},{1,17},{... | collective-permute-start | bytes 396296 | tf_op jit(solution)/shard_map/ppermute | solution.py:229
  12.5 0.5 %fusion.5 = (f32[64,512]{1,0:T(8,128)S(1)}, f32[64,512]{1,0:T(8,128)S(1)}) fusion(s32[512]{0:T(512)S(1)} %iota_add_fusion), kind=kLoop, calls=%fused_computation.16 | loop fusion | flops 294912 | bytes 264192 | tf_op jit(solution)/shard_map/cos | solution.py:86
  13.1 0.3 fusion.12
  13.4 1.5 %multiply_convert_fusion.1 = (bf16[32,64,512]{2,1,0:T(8,128)(2,1)S(1)}, bf16[32,64,512]{2,1,0:T(8,128)(2,1)S(1)}) fusion(f32[64,512]{1,0:T(8,128)S(1)} %get-tuple-element.16, f32[32,512]{1,0:T(8,128)S(1)} %get-tuple-element.14, f32[64,512]{1,0:T(8,128)S(1)} %get-tuple-element.15, f32[32,512]{1,0:T(8,128)S(1)} %get-tuple-element.13), kind=kLoop, calls=%fused_computation.2 | loop fusion | flops 10485760 | bytes 4587520 | tf_op jit(solution)/shard_map/convert_element_type | solution.py:90
  14.9 0.0 copy-start.3
  15.0 2.3 %pad_maximum_fusion = bf16[2,2048,512]{2,1,0:T(8,128)(2,1)} fusion(bf16[1,2048,512]{2,1,0:T(8,128)(2,1)S(1)} %bitcast.22, bf16[1,2048,512]{2,1,0:T(8,128)(2,1)S(1)} %bitcast.21), kind=kLoop, calls=%fused_computation | loop fusion | flops 2097152 | bytes 8388608 | tf_op jit(solution)/shard_map/stack | solution.py:92
  17.3 0.0 copy-done.3
  17.3 0.1 dynamic_update_slice.22
  17.4 0.2 copy.6
  17.6 0.0 collective-permute-done
  17.6 1.4 %collective-permute-start.5 = (bf16[4,16512]{1,0:T(4,128)(2,1)S(1)}, bf16[4,16512]{1,0:T(4,128)(2,1)S(1)}, u32[]{:S(2)}, u32[]{:S(2)}) collective-permute-start(bf16[4,16512]{1,0:T(4,128)(2,1)S(1)} %copy-done.3), channel_id=1, source_target_pairs={{0,24},{4,28},{8,0},{12,4},{16,8},{20,12},{24,16},{28,20},{1,25},{... | collective-permute-start | bytes 396296 | tf_op jit(solution)/shard_map/ppermute | solution.py:229
  19.0 0.1 bitcast_dynamic-update-slice_fusion.5
  19.1 0.0 collective-permute-done.3
  19.1 0.1 bitcast_dynamic-update-slice_fusion.2
  19.2 0.0 collective-permute-done.1
  19.2 0.1 bitcast_dynamic-update-slice_fusion.4
  19.2 0.0 collective-permute-done.2
  19.3 0.1 bitcast_dynamic-update-slice_fusion.3.rec_ref
  19.3 0.0 copy-start
  19.3 1.3 %collective-permute-done.4 = bf16[4,16512]{1,0:T(4,128)(2,1)S(1)} collective-permute-done((bf16[4,16512]{1,0:T(4,128)(2,1)}, bf16[4,16512]{1,0:T(4,128)(2,1)S(1)}, u32[]{:S(2)}, u32[]{:S(2)}) %collective-permute-start.4) | collective-permute-done | bytes 132128 | tf_op jit(solution)/shard_map/ppermute | solution.py:229
  20.7 0.1 bitcast_dynamic-update-slice_fusion.1
  20.7 2.6 %collective-permute-done.5 = bf16[4,16512]{1,0:T(4,128)(2,1)S(1)} collective-permute-done((bf16[4,16512]{1,0:T(4,128)(2,1)S(1)}, bf16[4,16512]{1,0:T(4,128)(2,1)S(1)}, u32[]{:S(2)}, u32[]{:S(2)}) %collective-permute-start.5) | collective-permute-done | bytes 132128 | tf_op jit(solution)/shard_map/ppermute | solution.py:229
  23.4 0.1 bitcast_dynamic-update-slice_fusion.own_ref
  23.4 0.0 copy-start.1
  23.4 0.1 collective-permute-start.6
  23.5 0.7 %pad_add_fusion.place_ref = s32[3]{0:T(128)} fusion(s32[1]{0:T(128)} %bitcast.2, s32[1]{0:T(128)} %bitcast.1, s32[1]{0:T(128)} %bitcast), kind=kLoop, calls=%fused_computation.28 | loop fusion | flops 6 | bytes 24 | tf_op jit(solution)/shard_map/stack | solution.py:245
  24.2 1.2 %collective-permute-done.6.sib_ref = bf16[4,4,16512]{2,1,0:T(4,128)(2,1)S(1)} collective-permute-done((bf16[4,4,16512]{2,1,0:T(4,128)(2,1)S(1)}, bf16[4,4,16512]{2,1,0:T(4,128)(2,1)S(1)}, u32[]{:S(2)}, u32[]{:S(2)}) %collective-permute-start.6) | collective-permute-done | bytes 528416 | tf_op jit(solution)/shard_map/ppermute | solution.py:243
  25.4 0.0 copy-done
  25.4 0.0 copy-done.1
  25.4 0.0 copy-start.2
  25.4 0.8 %copy-done.2 = bf16[4,4,16512]{2,1,0:T(4,128)(2,1)} copy-done((bf16[4,4,16512]{2,1,0:T(4,128)(2,1)}, bf16[4,4,16512]{2,1,0:T(4,128)(2,1)S(1)}, u32[]{:S(2)}) %copy-start.2) | copy-done | bytes 528408
  26.3 11.4 %shard_map.29 = bf16[512,512]{1,0:T(8,128)(2,1)} custom-call(s32[3]{0:T(128)} %pad_add_fusion.place_ref, bf16[4,4,16512]{2,1,0:T(4,128)(2,1)} %copy-done, bf16[4,4,16512]{2,1,0:T(4,128)(2,1)} %copy-done.1, bf16[4,4,16512]{2,1,0:T(4,128)(2,1)} %copy-done.2, bf16[4096,512]{1,0:T(8,128)(2,1)} %bitcast.20), custom_call_target="tpu_custom_call" | custom-call | tf_op jit(solution)/shard_map/pallas_call | solution.py:197
  (2 shorter events, 0.0 us)
Async XLA Ops:
  2.5 15.2 %collective-permute-start = (bf16[4,16512]{1,0:T(4,128)(2,1)}, bf16[4,16512]{1,0:T(4,128)(2,1)S(1)}, u32[]{:S(2)}, u32[]{:S(2)}) collective-permute-start(bf16[4,16512]{1,0:T(4,128)(2,1)} %shard_map.28), channel_id=1, source_target_pairs={{0,1},{1,2},{2,3},{3,0},{4,5},{5,6},{6,7},{7,4},{8,9},{9,10},{10,1... | collective-permute-start | bytes 396296 | tf_op jit(solution)/shard_map/ppermute | solution.py:229
  5.4 13.8 %collective-permute-start.1 = (bf16[4,16512]{1,0:T(4,128)(2,1)}, bf16[4,16512]{1,0:T(4,128)(2,1)S(1)}, u32[]{:S(2)}, u32[]{:S(2)}) collective-permute-start(bf16[4,16512]{1,0:T(4,128)(2,1)} %shard_map.28), channel_id=1, source_target_pairs={{0,2},{1,3},{2,0},{3,1},{4,6},{5,7},{6,4},{7,5},{8,10},{9,11},{10,... | collective-permute-start | bytes 396296 | tf_op jit(solution)/shard_map/ppermute | solution.py:229
  6.9 12.3 %collective-permute-start.2 = (bf16[4,16512]{1,0:T(4,128)(2,1)}, bf16[4,16512]{1,0:T(4,128)(2,1)S(1)}, u32[]{:S(2)}, u32[]{:S(2)}) collective-permute-start(bf16[4,16512]{1,0:T(4,128)(2,1)} %shard_map.28), channel_id=1, source_target_pairs={{0,3},{1,0},{2,1},{3,2},{4,7},{5,4},{6,5},{7,6},{8,11},{9,8},{10,9... | collective-permute-start | bytes 396296 | tf_op jit(solution)/shard_map/ppermute | solution.py:229
  8.4 10.7 %collective-permute-start.3 = (bf16[4,16512]{1,0:T(4,128)(2,1)}, bf16[4,16512]{1,0:T(4,128)(2,1)S(1)}, u32[]{:S(2)}, u32[]{:S(2)}) collective-permute-start(bf16[4,16512]{1,0:T(4,128)(2,1)} %shard_map.28), channel_id=1, source_target_pairs={{0,8},{4,12},{8,16},{12,20},{16,24},{20,28},{24,0},{28,4},{1,9},{5... | collective-permute-start | bytes 396296 | tf_op jit(solution)/shard_map/ppermute | solution.py:229
  9.9 10.7 %collective-permute-start.4 = (bf16[4,16512]{1,0:T(4,128)(2,1)}, bf16[4,16512]{1,0:T(4,128)(2,1)S(1)}, u32[]{:S(2)}, u32[]{:S(2)}) collective-permute-start(bf16[4,16512]{1,0:T(4,128)(2,1)} %shard_map.28), channel_id=1, source_target_pairs={{0,16},{4,20},{8,24},{12,28},{16,0},{20,4},{24,8},{28,12},{1,17},{... | collective-permute-start | bytes 396296 | tf_op jit(solution)/shard_map/ppermute | solution.py:229
  14.9 2.3 %copy-start.3 = (bf16[4,16512]{1,0:T(4,128)(2,1)S(1)}, bf16[4,16512]{1,0:T(4,128)(2,1)}, u32[]{:S(2)}) copy-start(bf16[4,16512]{1,0:T(4,128)(2,1)} %shard_map.28) | copy-start | bytes 396292
  17.6 5.7 %collective-permute-start.5 = (bf16[4,16512]{1,0:T(4,128)(2,1)S(1)}, bf16[4,16512]{1,0:T(4,128)(2,1)S(1)}, u32[]{:S(2)}, u32[]{:S(2)}) collective-permute-start(bf16[4,16512]{1,0:T(4,128)(2,1)S(1)} %copy-done.3), channel_id=1, source_target_pairs={{0,24},{4,28},{8,0},{12,4},{16,8},{20,12},{24,16},{28,20},{1,25},{... | collective-permute-start | bytes 396296 | tf_op jit(solution)/shard_map/ppermute | solution.py:229
  19.3 6.1 %copy-start = (bf16[4,4,16512]{2,1,0:T(4,128)(2,1)}, bf16[4,4,16512]{2,1,0:T(4,128)(2,1)S(1)}, u32[]{:S(2)}) copy-start(bf16[4,4,16512]{2,1,0:T(4,128)(2,1)S(1)} %bitcast_dynamic-update-slice_fusion.3.rec_ref) | copy-start | bytes 1585156
  23.4 2.0 %copy-start.1 = (bf16[4,4,16512]{2,1,0:T(4,128)(2,1)}, bf16[4,4,16512]{2,1,0:T(4,128)(2,1)S(1)}, u32[]{:S(2)}) copy-start(bf16[4,4,16512]{2,1,0:T(4,128)(2,1)S(1)} %bitcast_dynamic-update-slice_fusion.own_ref) | copy-start | bytes 1585156
  23.4 2.0 %collective-permute-start.6 = (bf16[4,4,16512]{2,1,0:T(4,128)(2,1)S(1)}, bf16[4,4,16512]{2,1,0:T(4,128)(2,1)S(1)}, u32[]{:S(2)}, u32[]{:S(2)}) collective-permute-start(bf16[4,4,16512]{2,1,0:T(4,128)(2,1)S(1)} %bitcast_dynamic-update-slice_fusion.own_ref), channel_id=1, source_target_pairs={{0,4},{4,0},{8,12},{12,8},{16,20},{20,16},{24,28},{28,24},{1,5},{5... | collective-permute-start | bytes 1585160 | tf_op jit(solution)/shard_map/ppermute | solution.py:243
  25.4 0.8 %copy-start.2 = (bf16[4,4,16512]{2,1,0:T(4,128)(2,1)}, bf16[4,4,16512]{2,1,0:T(4,128)(2,1)S(1)}, u32[]{:S(2)}) copy-start(bf16[4,4,16512]{2,1,0:T(4,128)(2,1)S(1)} %collective-permute-done.6.sib_ref) | copy-start | bytes 1585156

commit v15 on v14

--- a/solution.py
+++ b/solution.py
@@ -227,7 +227,11 @@
     for shift in range(1, count // stride):
         pairs = [(j, (j + stride * shift) % count) for j in range(count)]
         parts.append(lax.ppermute(x, axis, perm=pairs))
-    stack = jnp.zeros((len(parts),) + x.shape, x.dtype)
+    return parts
+
+
+def in_place_stack(parts):
+    stack = jnp.zeros((len(parts),) + parts[0].shape, parts[0].dtype)
     for k, part in enumerate(parts):
         stack = lax.dynamic_update_slice_in_dim(stack, part[None], k, axis=0)
     return stack
@@ -240,6 +244,8 @@
     rec_stack = shifted(packed, "rcv", rcv_count, 1)
     own_stack = shifted(packed, "src", src_count, 2)
     table, rec_stack, own_stack = lax.optimization_barrier((table, rec_stack, own_stack))
+    rec_stack = in_place_stack(rec_stack)
+    own_stack = in_place_stack(own_stack)
     sib_stack = lax.ppermute(own_stack, "src", perm=[(j, j ^ 1) for j in range(src_count)])
     src_index = lax.axis_index("src")
     place = jnp.stack(

time: 37.8 us -> 35.9 us (0.950)
  Pallas kernels: 13.9 us -> 12.8 us
  waiting for transfers between devices: 5.22 us -> 4.43 us
    ppermute x6, waiting for transfers between devices: 3.99 us -> 2.67 us  [shifted(): parts.append(lax.ppermute(x, axis, perm=pairs))]
    pallas_call x1, Pallas kernels: 11.4 us -> 10.4 us  [correlate(): pl.pallas_call(kernel, grid_spec=pltpu.PrefetchScalarGridSpec(num_scalar_...]
    ppermute x1, waiting for transfers between devices: 1.23 us -> 1.76 us  [local(): lax.ppermute(own_stack, 'src', perm=[(j, j ^ 1) for j in range(src_count)])]
    unnamed x9 -> x8, local copies, waits for them, and re-layouts: 1.03 us -> 0.84 us
  transfers between devices with their start and end apart: 7 -> 7, of which waited for: 3 -> 3; matrix products, arithmetic and copies ran while one was open for 16% -> 15% of each run, Pallas kernels for 0% -> 0%
where the time goes in v15:
time: 35.9 us; the launch traced here: 35.7 us
  Pallas kernels  12.8 us (36%)
  starting transfers between devices  11.5 us (32%)
  other arithmetic  5.33 us (15%)
  waiting for transfers between devices  4.43 us (12%)
  local copies, waits for them, and re-layouts  1.52 us (4%)
    ppermute x6, starting transfers between devices, shifted(): parts.append(lax.ppermute(x, axis, perm=pairs))  11.5 us
    pallas_call x1, Pallas kernels, correlate(): pl.pallas_call(kernel, grid_spec=pltpu.PrefetchScalarGridSpec(num_scalar_...  10.4 us
    ppermute x6, waiting for transfers between devices, shifted(): parts.append(lax.ppermute(x, axis, perm=pairs))  2.67 us
    pallas_call x1, Pallas kernels, whiten_pack(): pl.pallas_call(kernel, out_shape=jax.ShapeDtypeStruct((channels, windows...  2.47 us
    another operation x1, other arithmetic, lag_table(): jnp.stack([cosines, sines], axis=0).reshape(2 * freq_count, lag_count)  2.31 us
    ppermute x1, waiting for transfers between devices, local(): lax.ppermute(own_stack, 'src', perm=[(j, j ^ 1) for j in range(src_count)])  1.76 us
    convert_element_type x1, other arithmetic, lag_table(): cosines = cosines.reshape(freq_count, lag_count).astype(jnp.bfloat16)  1.55 us
    unnamed x8, local copies, waits for them, and re-layouts  0.84 us
  transfers between devices with their start and end apart: 7, of which 3 were waited for; matrix products, arithmetic and copies ran while one was open for 15% of the time, Pallas kernels for 0%

profile of v15, /device:TPU:0, one launch (start us, length us, event | category | flops | bytes accessed | tf_op | source)
XLA Modules:
  0.0 35.7 jit_solution(4534674987312105457)
XLA Ops:
  0.0 2.5 %shard_map.28 = bf16[4,16512]{1,0:T(4,128)(2,1)} custom-call(bf16[4,4,2,2048]{3,2,1,0:T(2,128)(2,1)} %x_ref.1, s32[4,4]{1,0:T(4,128)} %v_ref.1), custom_call_target="tpu_custom_call" | custom-call | tf_op jit(solution)/shard_map/pallas_call | solution.py:70
  2.5 0.0 copy-start.2
  2.5 2.9 %collective-permute-start = (bf16[4,16512]{1,0:T(4,128)(2,1)}, bf16[4,16512]{1,0:T(4,128)(2,1)S(1)}, u32[]{:S(2)}, u32[]{:S(2)}) collective-permute-start(bf16[4,16512]{1,0:T(4,128)(2,1)} %shard_map.28), channel_id=1, source_target_pairs={{0,1},{1,2},{2,3},{3,0},{4,5},{5,6},{6,7},{7,4},{8,9},{9,10},{10,1... | collective-permute-start | bytes 396296 | tf_op jit(solution)/shard_map/ppermute | solution.py:229
  5.4 1.5 %collective-permute-start.1 = (bf16[4,16512]{1,0:T(4,128)(2,1)}, bf16[4,16512]{1,0:T(4,128)(2,1)S(1)}, u32[]{:S(2)}, u32[]{:S(2)}) collective-permute-start(bf16[4,16512]{1,0:T(4,128)(2,1)} %shard_map.28), channel_id=1, source_target_pairs={{0,2},{1,3},{2,0},{3,1},{4,6},{5,7},{6,4},{7,5},{8,10},{9,11},{10,... | collective-permute-start | bytes 396296 | tf_op jit(solution)/shard_map/ppermute | solution.py:229
  6.9 1.4 %collective-permute-start.2 = (bf16[4,16512]{1,0:T(4,128)(2,1)}, bf16[4,16512]{1,0:T(4,128)(2,1)S(1)}, u32[]{:S(2)}, u32[]{:S(2)}) collective-permute-start(bf16[4,16512]{1,0:T(4,128)(2,1)} %shard_map.28), channel_id=1, source_target_pairs={{0,3},{1,0},{2,1},{3,2},{4,7},{5,4},{6,5},{7,6},{8,11},{9,8},{10,9... | collective-permute-start | bytes 396296 | tf_op jit(solution)/shard_map/ppermute | solution.py:229
  8.4 1.6 %collective-permute-start.3 = (bf16[4,16512]{1,0:T(4,128)(2,1)}, bf16[4,16512]{1,0:T(4,128)(2,1)S(1)}, u32[]{:S(2)}, u32[]{:S(2)}) collective-permute-start(bf16[4,16512]{1,0:T(4,128)(2,1)} %shard_map.28), channel_id=1, source_target_pairs={{0,8},{4,12},{8,16},{12,20},{16,24},{20,28},{24,0},{28,4},{1,9},{5... | collective-permute-start | bytes 396296 | tf_op jit(solution)/shard_map/ppermute | solution.py:229
  9.9 2.6 %collective-permute-start.4 = (bf16[4,16512]{1,0:T(4,128)(2,1)}, bf16[4,16512]{1,0:T(4,128)(2,1)S(1)}, u32[]{:S(2)}, u32[]{:S(2)}) collective-permute-start(bf16[4,16512]{1,0:T(4,128)(2,1)} %shard_map.28), channel_id=1, source_target_pairs={{0,16},{4,20},{8,24},{12,28},{16,0},{20,4},{24,8},{28,12},{1,17},{... | collective-permute-start | bytes 396296 | tf_op jit(solution)/shard_map/ppermute | solution.py:229
  12.5 0.5 %fusion.5 = (f32[64,512]{1,0:T(8,128)S(1)}, f32[64,512]{1,0:T(8,128)S(1)}) fusion(s32[512]{0:T(512)S(1)} %iota_add_fusion), kind=kLoop, calls=%fused_computation.16 | loop fusion | flops 294912 | bytes 264192 | tf_op jit(solution)/shard_map/cos | solution.py:86
  13.1 0.3 fusion.12
  13.4 1.5 %multiply_convert_fusion.1 = (bf16[32,64,512]{2,1,0:T(8,128)(2,1)S(1)}, bf16[32,64,512]{2,1,0:T(8,128)(2,1)S(1)}) fusion(f32[64,512]{1,0:T(8,128)S(1)} %get-tuple-element.28, f32[32,512]{1,0:T(8,128)S(1)} %get-tuple-element.26, f32[64,512]{1,0:T(8,128)S(1)} %get-tuple-element.27, f32[32,512]{1,0:T(8,128)S(1)} %get-tuple-element.25), kind=kLoop, calls=%fused_computation.2 | loop fusion | flops 10485760 | bytes 4587520 | tf_op jit(solution)/shard_map/convert_element_type | solution.py:90
  15.0 0.0 collective-permute-done
  15.0 0.0 copy-done.2
  15.0 1.4 %collective-permute-start.5 = (bf16[4,16512]{1,0:T(4,128)(2,1)S(1)}, bf16[4,16512]{1,0:T(4,128)(2,1)S(1)}, u32[]{:S(2)}, u32[]{:S(2)}) collective-permute-start(bf16[4,16512]{1,0:T(4,128)(2,1)S(1)} %copy-done.2), channel_id=1, source_target_pairs={{0,24},{4,28},{8,0},{12,4},{16,8},{20,12},{24,16},{28,20},{1,25},{... | collective-permute-start | bytes 396296 | tf_op jit(solution)/shard_map/ppermute | solution.py:229
  16.4 2.3 %pad_maximum_fusion = bf16[2,2048,512]{2,1,0:T(8,128)(2,1)} fusion(bf16[1,2048,512]{2,1,0:T(8,128)(2,1)S(1)} %bitcast.23, bf16[1,2048,512]{2,1,0:T(8,128)(2,1)S(1)} %bitcast.22), kind=kLoop, calls=%fused_computation | loop fusion | flops 2097152 | bytes 8388608 | tf_op jit(solution)/shard_map/stack | solution.py:92
  18.7 0.6 %pad_add_fusion.place_ref = s32[3]{0:T(128)} fusion(s32[1]{0:T(128)} %bitcast.2, s32[1]{0:T(128)} %bitcast.1, s32[1]{0:T(128)} %bitcast), kind=kLoop, calls=%fused_computation.28 | loop fusion | flops 6 | bytes 24 | tf_op jit(solution)/shard_map/stack | solution.py:251
  19.3 0.0 collective-permute-done.1
  19.3 0.0 collective-permute-done.2
  19.3 0.0 collective-permute-done.3
  19.3 1.3 %collective-permute-done.4 = bf16[4,16512]{1,0:T(4,128)(2,1)S(1)} collective-permute-done((bf16[4,16512]{1,0:T(4,128)(2,1)}, bf16[4,16512]{1,0:T(4,128)(2,1)S(1)}, u32[]{:S(2)}, u32[]{:S(2)}) %collective-permute-start.4) | collective-permute-done | bytes 132128 | tf_op jit(solution)/shard_map/ppermute | solution.py:229
  20.6 1.3 %collective-permute-done.5 = bf16[4,16512]{1,0:T(4,128)(2,1)S(1)} collective-permute-done((bf16[4,16512]{1,0:T(4,128)(2,1)S(1)}, bf16[4,16512]{1,0:T(4,128)(2,1)S(1)}, u32[]{:S(2)}, u32[]{:S(2)}) %collective-permute-start.5) | collective-permute-done | bytes 132128 | tf_op jit(solution)/shard_map/ppermute | solution.py:229
  22.0 0.1 dynamic_update_slice.28
  22.1 0.1 dynamic_update_slice.24
  22.3 0.1 bitcast_dynamic-update-slice_fusion.2
  22.3 0.1 bitcast_dynamic-update-slice_fusion.1
  22.4 0.1 bitcast_dynamic-update-slice_fusion
  22.5 0.0 copy-start.1
  22.5 0.1 collective-permute-start.6
  22.6 0.1 bitcast_dynamic-update-slice_fusion.4
  22.7 0.1 bitcast_dynamic-update-slice_fusion.3.rec_ref
  22.7 0.0 copy-start
  22.8 1.8 %collective-permute-done.6.sib_ref = bf16[4,4,16512]{2,1,0:T(4,128)(2,1)S(1)} collective-permute-done((bf16[4,4,16512]{2,1,0:T(4,128)(2,1)S(1)}, bf16[4,4,16512]{2,1,0:T(4,128)(2,1)S(1)}, u32[]{:S(2)}, u32[]{:S(2)}) %collective-permute-start.6) | collective-permute-done | bytes 528416 | tf_op jit(solution)/shard_map/ppermute | solution.py:249
  24.5 0.0 copy-done.1
  24.5 0.0 copy-done
  24.5 0.0 copy-start.3
  24.5 0.8 %copy-done.3 = bf16[4,4,16512]{2,1,0:T(4,128)(2,1)} copy-done((bf16[4,4,16512]{2,1,0:T(4,128)(2,1)}, bf16[4,4,16512]{2,1,0:T(4,128)(2,1)S(1)}, u32[]{:S(2)}) %copy-start.3) | copy-done | bytes 528408
  25.4 10.4 %shard_map.29 = bf16[512,512]{1,0:T(8,128)(2,1)} custom-call(s32[3]{0:T(128)} %pad_add_fusion.place_ref, bf16[4,4,16512]{2,1,0:T(4,128)(2,1)} %copy-done, bf16[4,4,16512]{2,1,0:T(4,128)(2,1)} %copy-done.1, bf16[4,4,16512]{2,1,0:T(4,128)(2,1)} %copy-done.3, bf16[4096,512]{1,0:T(8,128)(2,1)} %bitcast.21), custom_call_target="tpu_custom_call" | custom-call | tf_op jit(solution)/shard_map/pallas_call | solution.py:197
  (2 shorter events, 0.0 us)
Async XLA Ops:
  2.5 12.5 %copy-start.2 = (bf16[4,16512]{1,0:T(4,128)(2,1)S(1)}, bf16[4,16512]{1,0:T(4,128)(2,1)}, u32[]{:S(2)}) copy-start(bf16[4,16512]{1,0:T(4,128)(2,1)} %shard_map.28) | copy-start | bytes 396292
  2.5 12.5 %collective-permute-start = (bf16[4,16512]{1,0:T(4,128)(2,1)}, bf16[4,16512]{1,0:T(4,128)(2,1)S(1)}, u32[]{:S(2)}, u32[]{:S(2)}) collective-permute-start(bf16[4,16512]{1,0:T(4,128)(2,1)} %shard_map.28), channel_id=1, source_target_pairs={{0,1},{1,2},{2,3},{3,0},{4,5},{5,6},{6,7},{7,4},{8,9},{9,10},{10,1... | collective-permute-start | bytes 396296 | tf_op jit(solution)/shard_map/ppermute | solution.py:229
  5.4 13.9 %collective-permute-start.1 = (bf16[4,16512]{1,0:T(4,128)(2,1)}, bf16[4,16512]{1,0:T(4,128)(2,1)S(1)}, u32[]{:S(2)}, u32[]{:S(2)}) collective-permute-start(bf16[4,16512]{1,0:T(4,128)(2,1)} %shard_map.28), channel_id=1, source_target_pairs={{0,2},{1,3},{2,0},{3,1},{4,6},{5,7},{6,4},{7,5},{8,10},{9,11},{10,... | collective-permute-start | bytes 396296 | tf_op jit(solution)/shard_map/ppermute | solution.py:229
  6.9 12.4 %collective-permute-start.2 = (bf16[4,16512]{1,0:T(4,128)(2,1)}, bf16[4,16512]{1,0:T(4,128)(2,1)S(1)}, u32[]{:S(2)}, u32[]{:S(2)}) collective-permute-start(bf16[4,16512]{1,0:T(4,128)(2,1)} %shard_map.28), channel_id=1, source_target_pairs={{0,3},{1,0},{2,1},{3,2},{4,7},{5,4},{6,5},{7,6},{8,11},{9,8},{10,9... | collective-permute-start | bytes 396296 | tf_op jit(solution)/shard_map/ppermute | solution.py:229
  8.4 10.9 %collective-permute-start.3 = (bf16[4,16512]{1,0:T(4,128)(2,1)}, bf16[4,16512]{1,0:T(4,128)(2,1)S(1)}, u32[]{:S(2)}, u32[]{:S(2)}) collective-permute-start(bf16[4,16512]{1,0:T(4,128)(2,1)} %shard_map.28), channel_id=1, source_target_pairs={{0,8},{4,12},{8,16},{12,20},{16,24},{20,28},{24,0},{28,4},{1,9},{5... | collective-permute-start | bytes 396296 | tf_op jit(solution)/shard_map/ppermute | solution.py:229
  9.9 10.7 %collective-permute-start.4 = (bf16[4,16512]{1,0:T(4,128)(2,1)}, bf16[4,16512]{1,0:T(4,128)(2,1)S(1)}, u32[]{:S(2)}, u32[]{:S(2)}) collective-permute-start(bf16[4,16512]{1,0:T(4,128)(2,1)} %shard_map.28), channel_id=1, source_target_pairs={{0,16},{4,20},{8,24},{12,28},{16,0},{20,4},{24,8},{28,12},{1,17},{... | collective-permute-start | bytes 396296 | tf_op jit(solution)/shard_map/ppermute | solution.py:229
  15.0 7.0 %collective-permute-start.5 = (bf16[4,16512]{1,0:T(4,128)(2,1)S(1)}, bf16[4,16512]{1,0:T(4,128)(2,1)S(1)}, u32[]{:S(2)}, u32[]{:S(2)}) collective-permute-start(bf16[4,16512]{1,0:T(4,128)(2,1)S(1)} %copy-done.2), channel_id=1, source_target_pairs={{0,24},{4,28},{8,0},{12,4},{16,8},{20,12},{24,16},{28,20},{1,25},{... | collective-permute-start | bytes 396296 | tf_op jit(solution)/shard_map/ppermute | solution.py:229
  22.5 2.0 %copy-start.1 = (bf16[4,4,16512]{2,1,0:T(4,128)(2,1)}, bf16[4,4,16512]{2,1,0:T(4,128)(2,1)S(1)}, u32[]{:S(2)}) copy-start(bf16[4,4,16512]{2,1,0:T(4,128)(2,1)S(1)} %get-tuple-element.29.own_ref) | copy-start | bytes 1585156
  22.5 2.0 %collective-permute-start.6 = (bf16[4,4,16512]{2,1,0:T(4,128)(2,1)S(1)}, bf16[4,4,16512]{2,1,0:T(4,128)(2,1)S(1)}, u32[]{:S(2)}, u32[]{:S(2)}) collective-permute-start(bf16[4,4,16512]{2,1,0:T(4,128)(2,1)S(1)} %get-tuple-element.29.own_ref), channel_id=1, source_target_pairs={{0,4},{4,0},{8,12},{12,8},{16,20},{20,16},{24,28},{28,24},{1,5},{5... | collective-permute-start | bytes 1585160 | tf_op jit(solution)/shard_map/ppermute | solution.py:249
  22.7 1.8 %copy-start = (bf16[4,4,16512]{2,1,0:T(4,128)(2,1)}, bf16[4,4,16512]{2,1,0:T(4,128)(2,1)S(1)}, u32[]{:S(2)}) copy-start(bf16[4,4,16512]{2,1,0:T(4,128)(2,1)S(1)} %bitcast_dynamic-update-slice_fusion.3.rec_ref) | copy-start | bytes 1585156
  24.5 0.8 %copy-start.3 = (bf16[4,4,16512]{2,1,0:T(4,128)(2,1)}, bf16[4,4,16512]{2,1,0:T(4,128)(2,1)S(1)}, u32[]{:S(2)}) copy-start(bf16[4,4,16512]{2,1,0:T(4,128)(2,1)S(1)} %collective-permute-done.6.sib_ref) | copy-start | bytes 1585156

commit v16 on v15

--- a/solution.py
+++ b/solution.py
@@ -243,10 +243,14 @@
     packed = whiten_pack(spectra, valid)
     rec_stack = shifted(packed, "rcv", rcv_count, 1)
     own_stack = shifted(packed, "src", src_count, 2)
-    table, rec_stack, own_stack = lax.optimization_barrier((table, rec_stack, own_stack))
+    sibling = [(j, j ^ 1) for j in range(src_count)]
+    sib_stack = [lax.ppermute(part, "src", perm=sibling) for part in own_stack]
+    table, rec_stack, own_stack, sib_stack = lax.optimization_barrier(
+        (table, rec_stack, own_stack, sib_stack)
+    )
     rec_stack = in_place_stack(rec_stack)
     own_stack = in_place_stack(own_stack)
-    sib_stack = lax.ppermute(own_stack, "src", perm=[(j, j ^ 1) for j in range(src_count)])
+    sib_stack = in_place_stack(sib_stack)
     src_index = lax.axis_index("src")
     place = jnp.stack(
         [lax.axis_index("rcv"), src_index // 2, src_index % 2]

time: 35.9 us -> 34.2 us (0.953); the launches traced: 35.7 us -> 33.6 us
  waiting for transfers between devices: 4.43 us -> 0.82 us
  starting transfers between devices: 11.5 us -> 12.3 us
  local copies, waits for them, and re-layouts: 1.52 us -> 2.09 us
    ppermute x6, waiting for transfers between devices: 2.67 us -> 0.81 us  [shifted(): parts.append(lax.ppermute(x, axis, perm=pairs))]
    ppermute x1 -> x4, waiting for transfers between devices: 1.76 us -> 0.01 us  [local(): sib_stack = [lax.ppermute(part, 'src', perm=sibling) for part in own_stack]]
    ppermute x1 -> x4, starting transfers between devices: 0.07 us -> 0.89 us  [local(): sib_stack = [lax.ppermute(part, 'src', perm=sibling) for part in own_stack]]
    dynamic_update_slice x7 -> x11, local copies, waits for them, and re-layouts: 0.68 us -> 1.02 us  [in_place_stack(): stack = lax.dynamic_update_slice_in_dim(stack, part[None], k, axis=0)]
  transfers between devices with their start and end apart: 7 -> 10, of which waited for: 3 -> 2; matrix products, arithmetic and copies ran while one was open for 15% -> 16% of each run, Pallas kernels for 0% -> 0%
where the time goes in v16:
time: 34.2 us; the launch traced here: 33.6 us
  Pallas kernels  12.8 us (37%)
  starting transfers between devices  12.3 us (36%)
  other arithmetic  5.38 us (16%)
  local copies, waits for them, and re-layouts  2.09 us (6%)
  waiting for transfers between devices  0.82 us (2%)
    ppermute x6, starting transfers between devices, shifted(): parts.append(lax.ppermute(x, axis, perm=pairs))  11.5 us
    pallas_call x1, Pallas kernels, correlate(): pl.pallas_call(kernel, grid_spec=pltpu.PrefetchScalarGridSpec(num_scalar_...  10.4 us
    pallas_call x1, Pallas kernels, whiten_pack(): pl.pallas_call(kernel, out_shape=jax.ShapeDtypeStruct((channels, windows...  2.47 us
    another operation x1, other arithmetic, lag_table(): jnp.stack([cosines, sines], axis=0).reshape(2 * freq_count, lag_count)  2.32 us
    convert_element_type x1, other arithmetic, lag_table(): cosines = cosines.reshape(freq_count, lag_count).astype(jnp.bfloat16)  1.55 us
    unnamed x8, local copies, waits for them, and re-layouts  1.07 us
    dynamic_update_slice x11, local copies, waits for them, and re-layouts, in_place_stack(): stack = lax.dynamic_update_slice_in_dim(stack, part[None], k, axis=0)  1.02 us
    ppermute x4, starting transfers between devices, local(): sib_stack = [lax.ppermute(part, 'src', perm=sibling) for part in own_stack]  0.89 us
  transfers between devices with their start and end apart: 10, of which 2 were waited for; matrix products, arithmetic and copies ran while one was open for 16% of the time, Pallas kernels for 0%

profile of v16, /device:TPU:0, one launch (start us, length us, event | category | flops | bytes accessed | tf_op | source)
XLA Modules:
  0.0 33.6 jit_solution(5449470233832181688)
XLA Ops:
  0.0 2.5 %shard_map.28 = bf16[4,16512]{1,0:T(4,128)(2,1)} custom-call(bf16[4,4,2,2048]{3,2,1,0:T(2,128)(2,1)} %x_ref.1, s32[4,4]{1,0:T(4,128)} %v_ref.1), custom_call_target="tpu_custom_call" | custom-call | tf_op jit(solution)/shard_map/pallas_call | solution.py:70
  2.5 0.0 copy-start.3
  2.5 3.0 %collective-permute-start.3 = (bf16[4,16512]{1,0:T(4,128)(2,1)}, bf16[4,16512]{1,0:T(4,128)(2,1)S(1)}, u32[]{:S(2)}, u32[]{:S(2)}) collective-permute-start(bf16[4,16512]{1,0:T(4,128)(2,1)} %shard_map.28), channel_id=1, source_target_pairs={{0,8},{4,12},{8,16},{12,20},{16,24},{20,28},{24,0},{28,4},{1,9},{5... | collective-permute-start | bytes 396296 | tf_op jit(solution)/shard_map/ppermute | solution.py:229
  5.5 2.6 %collective-permute-start.4 = (bf16[4,16512]{1,0:T(4,128)(2,1)}, bf16[4,16512]{1,0:T(4,128)(2,1)S(1)}, u32[]{:S(2)}, u32[]{:S(2)}) collective-permute-start(bf16[4,16512]{1,0:T(4,128)(2,1)} %shard_map.28), channel_id=1, source_target_pairs={{0,16},{4,20},{8,24},{12,28},{16,0},{20,4},{24,8},{28,12},{1,17},{... | collective-permute-start | bytes 396296 | tf_op jit(solution)/shard_map/ppermute | solution.py:229
  8.1 1.3 %collective-permute-start.5 = (bf16[4,16512]{1,0:T(4,128)(2,1)}, bf16[4,16512]{1,0:T(4,128)(2,1)S(1)}, u32[]{:S(2)}, u32[]{:S(2)}) collective-permute-start(bf16[4,16512]{1,0:T(4,128)(2,1)} %shard_map.28), channel_id=1, source_target_pairs={{0,24},{4,28},{8,0},{12,4},{16,8},{20,12},{24,16},{28,20},{1,25},{... | collective-permute-start | bytes 396296 | tf_op jit(solution)/shard_map/ppermute | solution.py:229
  9.4 1.5 %collective-permute-start = (bf16[4,16512]{1,0:T(4,128)(2,1)}, bf16[4,16512]{1,0:T(4,128)(2,1)S(1)}, u32[]{:S(2)}, u32[]{:S(2)}) collective-permute-start(bf16[4,16512]{1,0:T(4,128)(2,1)} %shard_map.28), channel_id=1, source_target_pairs={{0,1},{1,2},{2,3},{3,0},{4,5},{5,6},{6,7},{7,4},{8,9},{9,10},{10,1... | collective-permute-start | bytes 396296 | tf_op jit(solution)/shard_map/ppermute | solution.py:229
  10.9 1.5 %collective-permute-start.1 = (bf16[4,16512]{1,0:T(4,128)(2,1)}, bf16[4,16512]{1,0:T(4,128)(2,1)S(1)}, u32[]{:S(2)}, u32[]{:S(2)}) collective-permute-start(bf16[4,16512]{1,0:T(4,128)(2,1)} %shard_map.28), channel_id=1, source_target_pairs={{0,2},{1,3},{2,0},{3,1},{4,6},{5,7},{6,4},{7,5},{8,10},{9,11},{10,... | collective-permute-start | bytes 396296 | tf_op jit(solution)/shard_map/ppermute | solution.py:229
  12.5 0.5 %fusion.5 = (f32[64,512]{1,0:T(8,128)S(1)}, f32[64,512]{1,0:T(8,128)S(1)}) fusion(s32[512]{0:T(512)S(1)} %iota_add_fusion), kind=kLoop, calls=%fused_computation.19 | loop fusion | flops 294912 | bytes 264192 | tf_op jit(solution)/shard_map/cos | solution.py:86
  13.0 0.3 %fusion.12 = (f32[32,512]{1,0:T(8,128)S(1)}, f32[32,512]{1,0:T(8,128)S(1)}) fusion(s32[512]{0:T(512)S(1)} %iota_add_fusion, s32[32]{0:T(128)S(1)} %iota_multiply_fusion), kind=kLoop, calls=%fused_computation.28 | loop fusion | flops 147456 | bytes 133248 | tf_op jit(solution)/shard_map/cos | solution.py:85
  13.3 1.5 %multiply_convert_fusion.1 = (bf16[32,64,512]{2,1,0:T(8,128)(2,1)S(1)}, bf16[32,64,512]{2,1,0:T(8,128)(2,1)S(1)}) fusion(f32[64,512]{1,0:T(8,128)S(1)} %get-tuple-element.36, f32[32,512]{1,0:T(8,128)S(1)} %get-tuple-element.34, f32[64,512]{1,0:T(8,128)S(1)} %get-tuple-element.35, f32[32,512]{1,0:T(8,128)S(1)} %get-tuple-element.33), kind=kLoop, calls=%fused_computation.2 | loop fusion | flops 10485760 | bytes 4587520 | tf_op jit(solution)/shard_map/convert_element_type | solution.py:90
  14.9 0.0 collective-permute-done.3
  14.9 0.0 copy-done.3
  14.9 1.5 %collective-permute-start.2 = (bf16[4,16512]{1,0:T(4,128)(2,1)S(1)}, bf16[4,16512]{1,0:T(4,128)(2,1)S(1)}, u32[]{:S(2)}, u32[]{:S(2)}) collective-permute-start(bf16[4,16512]{1,0:T(4,128)(2,1)S(1)} %copy-done.3), channel_id=1, source_target_pairs={{0,3},{1,0},{2,1},{3,2},{4,7},{5,4},{6,5},{7,6},{8,11},{9,8},{10,9... | collective-permute-start | bytes 396296 | tf_op jit(solution)/shard_map/ppermute | solution.py:229
  16.4 0.7 %collective-permute-done.4 = bf16[4,16512]{1,0:T(4,128)(2,1)S(1)} collective-permute-done((bf16[4,16512]{1,0:T(4,128)(2,1)}, bf16[4,16512]{1,0:T(4,128)(2,1)S(1)}, u32[]{:S(2)}, u32[]{:S(2)}) %collective-permute-start.4) | collective-permute-done | bytes 132128 | tf_op jit(solution)/shard_map/ppermute | solution.py:229
  17.1 0.0 collective-permute-start.6
  17.1 0.0 collective-permute-done.5
  17.1 0.5 %collective-permute-start.7 = (bf16[4,16512]{1,0:T(4,128)(2,1)S(1)}, bf16[4,16512]{1,0:T(4,128)(2,1)S(1)}, u32[]{:S(2)}, u32[]{:S(2)}) collective-permute-start(bf16[4,16512]{1,0:T(4,128)(2,1)S(1)} %collective-permute-done.3), channel_id=1, source_target_pairs={{0,4},{4,0},{8,12},{12,8},{16,20},{20,16},{24,28},{28,24},{1,5},{5... | collective-permute-start | bytes 396296 | tf_op jit(solution)/shard_map/ppermute | solution.py:247
  17.6 0.0 collective-permute-done
  17.6 0.1 collective-permute-start.8
  17.7 0.1 collective-permute-done.1
  17.8 0.3 collective-permute-start.9
  18.1 2.3 %pad_maximum_fusion = bf16[2,2048,512]{2,1,0:T(8,128)(2,1)} fusion(bf16[1,2048,512]{2,1,0:T(8,128)(2,1)S(1)} %bitcast.30, bf16[1,2048,512]{2,1,0:T(8,128)(2,1)S(1)} %bitcast.29), kind=kLoop, calls=%fused_computation | loop fusion | flops 2097152 | bytes 8388608 | tf_op jit(solution)/shard_map/stack | solution.py:92
  20.4 0.6 %pad_add_fusion.place_ref = s32[3]{0:T(128)} fusion(s32[1]{0:T(128)} %bitcast.2, s32[1]{0:T(128)} %bitcast.1, s32[1]{0:T(128)} %bitcast), kind=kLoop, calls=%fused_computation.31 | loop fusion | flops 6 | bytes 24 | tf_op jit(solution)/shard_map/stack | solution.py:255
  21.0 0.0 collective-permute-done.2
  21.1 0.0 collective-permute-done.6
  21.1 0.0 collective-permute-done.7
  21.1 0.0 collective-permute-done.8
  21.1 0.0 collective-permute-done.9
  21.1 0.1 dynamic_update_slice.40
  21.2 0.1 dynamic_update_slice.44
  21.4 0.1 dynamic_update_slice.36
  21.6 0.1 bitcast_dynamic-update-slice_fusion.5
  21.6 0.1 bitcast_dynamic-update-slice_fusion.4
  21.7 0.1 bitcast_dynamic-update-slice_fusion.2
  21.8 0.1 bitcast_dynamic-update-slice_fusion.1
  21.8 0.1 bitcast_dynamic-update-slice_fusion.8
  21.9 0.1 bitcast_dynamic-update-slice_fusion.7
  22.0 0.1 bitcast_dynamic-update-slice_fusion.6.rec_ref
  22.0 0.0 copy-start
  22.0 0.1 bitcast_dynamic-update-slice_fusion
  22.1 0.0 copy-start.1
  22.2 0.0 copy-start.2
  22.2 0.7 %copy-done = bf16[4,4,16512]{2,1,0:T(4,128)(2,1)} copy-done((bf16[4,4,16512]{2,1,0:T(4,128)(2,1)}, bf16[4,4,16512]{2,1,0:T(4,128)(2,1)S(1)}, u32[]{:S(2)}) %copy-start) | copy-done | bytes 528408
  22.8 0.2 copy-done.1
  23.0 0.2 copy-done.2
  23.2 10.4 %shard_map.29 = bf16[512,512]{1,0:T(8,128)(2,1)} custom-call(s32[3]{0:T(128)} %pad_add_fusion.place_ref, bf16[4,4,16512]{2,1,0:T(4,128)(2,1)} %copy-done, bf16[4,4,16512]{2,1,0:T(4,128)(2,1)} %copy-done.2, bf16[4,4,16512]{2,1,0:T(4,128)(2,1)} %copy-done.1, bf16[4096,512]{1,0:T(8,128)(2,1)} %bitcast.28), custom_call_target="tpu_custom_call" | custom-call | tf_op jit(solution)/shard_map/pallas_call | solution.py:197
  (2 shorter events, 0.0 us)
Async XLA Ops:
  2.5 12.4 %copy-start.3 = (bf16[4,16512]{1,0:T(4,128)(2,1)S(1)}, bf16[4,16512]{1,0:T(4,128)(2,1)}, u32[]{:S(2)}) copy-start(bf16[4,16512]{1,0:T(4,128)(2,1)} %shard_map.28) | copy-start | bytes 396292
  2.5 12.4 %collective-permute-start.3 = (bf16[4,16512]{1,0:T(4,128)(2,1)}, bf16[4,16512]{1,0:T(4,128)(2,1)S(1)}, u32[]{:S(2)}, u32[]{:S(2)}) collective-permute-start(bf16[4,16512]{1,0:T(4,128)(2,1)} %shard_map.28), channel_id=1, source_target_pairs={{0,8},{4,12},{8,16},{12,20},{16,24},{20,28},{24,0},{28,4},{1,9},{5... | collective-permute-start | bytes 396296 | tf_op jit(solution)/shard_map/ppermute | solution.py:229
  5.5 11.6 %collective-permute-start.4 = (bf16[4,16512]{1,0:T(4,128)(2,1)}, bf16[4,16512]{1,0:T(4,128)(2,1)S(1)}, u32[]{:S(2)}, u32[]{:S(2)}) collective-permute-start(bf16[4,16512]{1,0:T(4,128)(2,1)} %shard_map.28), channel_id=1, source_target_pairs={{0,16},{4,20},{8,24},{12,28},{16,0},{20,4},{24,8},{28,12},{1,17},{... | collective-permute-start | bytes 396296 | tf_op jit(solution)/shard_map/ppermute | solution.py:229
  8.1 9.0 %collective-permute-start.5 = (bf16[4,16512]{1,0:T(4,128)(2,1)}, bf16[4,16512]{1,0:T(4,128)(2,1)S(1)}, u32[]{:S(2)}, u32[]{:S(2)}) collective-permute-start(bf16[4,16512]{1,0:T(4,128)(2,1)} %shard_map.28), channel_id=1, source_target_pairs={{0,24},{4,28},{8,0},{12,4},{16,8},{20,12},{24,16},{28,20},{1,25},{... | collective-permute-start | bytes 396296 | tf_op jit(solution)/shard_map/ppermute | solution.py:229
  9.4 8.2 %collective-permute-start = (bf16[4,16512]{1,0:T(4,128)(2,1)}, bf16[4,16512]{1,0:T(4,128)(2,1)S(1)}, u32[]{:S(2)}, u32[]{:S(2)}) collective-permute-start(bf16[4,16512]{1,0:T(4,128)(2,1)} %shard_map.28), channel_id=1, source_target_pairs={{0,1},{1,2},{2,3},{3,0},{4,5},{5,6},{6,7},{7,4},{8,9},{9,10},{10,1... | collective-permute-start | bytes 396296 | tf_op jit(solution)/shard_map/ppermute | solution.py:229
  10.9 6.9 %collective-permute-start.1 = (bf16[4,16512]{1,0:T(4,128)(2,1)}, bf16[4,16512]{1,0:T(4,128)(2,1)S(1)}, u32[]{:S(2)}, u32[]{:S(2)}) collective-permute-start(bf16[4,16512]{1,0:T(4,128)(2,1)} %shard_map.28), channel_id=1, source_target_pairs={{0,2},{1,3},{2,0},{3,1},{4,6},{5,7},{6,4},{7,5},{8,10},{9,11},{10,... | collective-permute-start | bytes 396296 | tf_op jit(solution)/shard_map/ppermute | solution.py:229
  14.9 6.1 %collective-permute-start.2 = (bf16[4,16512]{1,0:T(4,128)(2,1)S(1)}, bf16[4,16512]{1,0:T(4,128)(2,1)S(1)}, u32[]{:S(2)}, u32[]{:S(2)}) collective-permute-start(bf16[4,16512]{1,0:T(4,128)(2,1)S(1)} %copy-done.3), channel_id=1, source_target_pairs={{0,3},{1,0},{2,1},{3,2},{4,7},{5,4},{6,5},{7,6},{8,11},{9,8},{10,9... | collective-permute-start | bytes 396296 | tf_op jit(solution)/shard_map/ppermute | solution.py:229
  17.1 4.0 %collective-permute-start.6 = (bf16[4,16512]{1,0:T(4,128)(2,1)S(1)}, bf16[4,16512]{1,0:T(4,128)(2,1)S(1)}, u32[]{:S(2)}, u32[]{:S(2)}) collective-permute-start(bf16[4,16512]{1,0:T(4,128)(2,1)S(1)} %copy-done.3), channel_id=1, source_target_pairs={{0,4},{4,0},{8,12},{12,8},{16,20},{20,16},{24,28},{28,24},{1,5},{5... | collective-permute-start | bytes 396296 | tf_op jit(solution)/shard_map/ppermute | solution.py:247
  17.1 4.0 %collective-permute-start.7 = (bf16[4,16512]{1,0:T(4,128)(2,1)S(1)}, bf16[4,16512]{1,0:T(4,128)(2,1)S(1)}, u32[]{:S(2)}, u32[]{:S(2)}) collective-permute-start(bf16[4,16512]{1,0:T(4,128)(2,1)S(1)} %collective-permute-done.3), channel_id=1, source_target_pairs={{0,4},{4,0},{8,12},{12,8},{16,20},{20,16},{24,28},{28,24},{1,5},{5... | collective-permute-start | bytes 396296 | tf_op jit(solution)/shard_map/ppermute | solution.py:247
  17.6 3.5 %collective-permute-start.8 = (bf16[4,16512]{1,0:T(4,128)(2,1)S(1)}, bf16[4,16512]{1,0:T(4,128)(2,1)S(1)}, u32[]{:S(2)}, u32[]{:S(2)}) collective-permute-start(bf16[4,16512]{1,0:T(4,128)(2,1)S(1)} %collective-permute-done.4), channel_id=1, source_target_pairs={{0,4},{4,0},{8,12},{12,8},{16,20},{20,16},{24,28},{28,24},{1,5},{5... | collective-permute-start | bytes 396296 | tf_op jit(solution)/shard_map/ppermute | solution.py:247
  17.8 3.3 %collective-permute-start.9 = (bf16[4,16512]{1,0:T(4,128)(2,1)S(1)}, bf16[4,16512]{1,0:T(4,128)(2,1)S(1)}, u32[]{:S(2)}, u32[]{:S(2)}) collective-permute-start(bf16[4,16512]{1,0:T(4,128)(2,1)S(1)} %collective-permute-done.5), channel_id=1, source_target_pairs={{0,4},{4,0},{8,12},{12,8},{16,20},{20,16},{24,28},{28,24},{1,5},{5... | collective-permute-start | bytes 396296 | tf_op jit(solution)/shard_map/ppermute | solution.py:247
  22.0 0.8 %copy-start = (bf16[4,4,16512]{2,1,0:T(4,128)(2,1)}, bf16[4,4,16512]{2,1,0:T(4,128)(2,1)S(1)}, u32[]{:S(2)}) copy-start(bf16[4,4,16512]{2,1,0:T(4,128)(2,1)S(1)} %bitcast_dynamic-update-slice_fusion.6.rec_ref) | copy-start | bytes 1585156
  22.1 0.9 %copy-start.1 = (bf16[4,4,16512]{2,1,0:T(4,128)(2,1)}, bf16[4,4,16512]{2,1,0:T(4,128)(2,1)S(1)}, u32[]{:S(2)}) copy-start(bf16[4,4,16512]{2,1,0:T(4,128)(2,1)S(1)} %get-tuple-element.37.sib_ref) | copy-start | bytes 1585156
  22.2 1.1 %copy-start.2 = (bf16[4,4,16512]{2,1,0:T(4,128)(2,1)}, bf16[4,4,16512]{2,1,0:T(4,128)(2,1)S(1)}, u32[]{:S(2)}) copy-start(bf16[4,4,16512]{2,1,0:T(4,128)(2,1)S(1)} %get-tuple-element.38.own_ref) | copy-start | bytes 1585156

commit v17 on v16

--- a/solution.py
+++ b/solution.py
@@ -89,12 +89,12 @@
     sines = (sin_hi * cos_lo + cos_hi * sin_lo) * (-factor)
     cosines = cosines.reshape(freq_count, lag_count).astype(jnp.bfloat16)
     sines = sines.reshape(freq_count, lag_count).astype(jnp.bfloat16)
-    return jnp.stack([cosines, sines], axis=0).reshape(2 * freq_count, lag_count)
+    return cosines, sines
 
 
 def cross_kernel(
-    place_ref, rec_ref, own_ref, sib_ref, tab_hbm, out_ref, srcf, recf, rtails, stails, cross,
-    tab_ref, tab_sem, *, windows, freqs, group, chunk
+    place_ref, rec_ref, own_ref, sib_ref, cos_hbm, sin_hbm, out_ref, srcf, recf, rtails, stails,
+    cross, cos_ref, sin_ref, cos_sem, sin_sem, *, windows, freqs, group, chunk
 ):
     step = pl.program_id(0)
     rcv_count, per = rec_ref.shape[0], rec_ref.shape[1]
@@ -121,7 +121,8 @@
 
     @pl.when(step == 0)
     def _():
-        pltpu.make_async_copy(tab_hbm, tab_ref, tab_sem).start()
+        pltpu.make_async_copy(cos_hbm, cos_ref, cos_sem).start()
+        pltpu.make_async_copy(sin_hbm, sin_ref, sin_sem).start()
 
     @pl.when(step == 0)
     def _():
@@ -176,19 +177,20 @@
 
     @pl.when(step == 0)
     def _():
-        pltpu.make_async_copy(tab_hbm, tab_ref, tab_sem).wait()
-
-    out_ref[...] = jnp.dot(
-        cross[...], tab_ref[...], preferred_element_type=jnp.float32
-    ).astype(jnp.bfloat16)
-
-
-def correlate(place, rec_stack, own_stack, sib_stack, table, windows, freqs):
+        pltpu.make_async_copy(cos_hbm, cos_ref, cos_sem).wait()
+        pltpu.make_async_copy(sin_hbm, sin_ref, sin_sem).wait()
+
+    real = jnp.dot(cross[:, :freqs], cos_ref[...], preferred_element_type=jnp.float32)
+    imag = jnp.dot(cross[:, freqs:], sin_ref[...], preferred_element_type=jnp.float32)
+    out_ref[...] = (real + imag).astype(jnp.bfloat16)
+
+
+def correlate(place, rec_stack, own_stack, sib_stack, tables, windows, freqs):
     rcv_count, per, width = rec_stack.shape
     chips = own_stack.shape[0]
     nrec = rcv_count * per
     nsrc = 2 * chips * per
-    lags = table.shape[1]
+    lags = tables[0].shape[1]
     group = 8
     kernel = functools.partial(
         cross_kernel, windows=windows, freqs=freqs, group=group, chunk=256
@@ -204,6 +206,7 @@
                 pl.BlockSpec(own_stack.shape, full3),
                 pl.BlockSpec(sib_stack.shape, full3),
                 pl.BlockSpec(memory_space=pl.ANY),
+                pl.BlockSpec(memory_space=pl.ANY),
             ],
             out_specs=pl.BlockSpec((group * nsrc, lags), lambda g, p: (g, 0)),
             scratch_shapes=[
@@ -212,13 +215,15 @@
                 pltpu.VMEM((nrec, PAD), jnp.float32),
                 pltpu.VMEM((nsrc, PAD), jnp.float32),
                 pltpu.VMEM((group * nsrc, 2 * freqs), jnp.bfloat16),
-                pltpu.VMEM(table.shape, jnp.bfloat16),
+                pltpu.VMEM(tables[0].shape, jnp.bfloat16),
+                pltpu.VMEM(tables[1].shape, jnp.bfloat16),
+                pltpu.SemaphoreType.DMA(()),
                 pltpu.SemaphoreType.DMA(()),
             ],
         ),
         out_shape=jax.ShapeDtypeStruct((nrec * nsrc, lags), jnp.bfloat16),
         compiler_params=pltpu.CompilerParams(dimension_semantics=("arbitrary",)),
-    )(place, rec_stack, own_stack, sib_stack, table)
+    )(place, rec_stack, own_stack, sib_stack, *tables)
     return out.reshape(nrec, nsrc, lags)
 
 

time: 34.2 us -> 35.3 us (1.032)
  waiting for transfers between devices: 0.82 us -> 2.36 us
  other arithmetic: 5.38 us -> 4.97 us
    another operation x1 -> x0, other arithmetic: 2.32 us -> none  [lag_table(): jnp.stack([cosines, sines], axis=0).reshape(2 * freq_count, lag_count)]
    convert_element_type x1, other arithmetic: 1.55 us -> 3.45 us  [lag_table(): sines = sines.reshape(freq_count, lag_count).astype(jnp.bfloat16)]
    ppermute x6, waiting for transfers between devices: 0.81 us -> 2.35 us  [shifted(): parts.append(lax.ppermute(x, axis, perm=pairs))]
  transfers between devices with their start and end apart: 10 -> 10, of which waited for: 2 -> 2; matrix products, arithmetic and copies ran while one was open for 16% -> 14% of each run, Pallas kernels for 0% -> 0%
where the time goes in v17:
time: 35.3 us; the launch traced here: 34.7 us
  Pallas kernels  12.8 us (36%)
  starting transfers between devices  12.3 us (35%)
  other arithmetic  4.97 us (14%)
  waiting for transfers between devices  2.36 us (7%)
  local copies, waits for them, and re-layouts  2.09 us (6%)
    ppermute x6, starting transfers between devices, shifted(): parts.append(lax.ppermute(x, axis, perm=pairs))  11.5 us
    pallas_call x1, Pallas kernels, correlate(): pl.pallas_call(kernel, grid_spec=pltpu.PrefetchScalarGridSpec(num_scalar_...  10.4 us
    convert_element_type x1, other arithmetic, lag_table(): sines = sines.reshape(freq_count, lag_count).astype(jnp.bfloat16)  3.45 us
    pallas_call x1, Pallas kernels, whiten_pack(): pl.pallas_call(kernel, out_shape=jax.ShapeDtypeStruct((channels, windows...  2.47 us
    ppermute x6, waiting for transfers between devices, shifted(): parts.append(lax.ppermute(x, axis, perm=pairs))  2.35 us
    unnamed x8, local copies, waits for them, and re-layouts  1.07 us
    dynamic_update_slice x11, local copies, waits for them, and re-layouts, in_place_stack(): stack = lax.dynamic_update_slice_in_dim(stack, part[None], k, axis=0)  1.02 us
    ppermute x4, starting transfers between devices, local(): sib_stack = [lax.ppermute(part, 'src', perm=sibling) for part in own_stack]  0.82 us
  transfers between devices with their start and end apart: 10, of which 2 were waited for; matrix products, arithmetic and copies ran while one was open for 14% of the time, Pallas kernels for 0%

profile of v17, /device:TPU:0, one launch (start us, length us, event | category | flops | bytes accessed | tf_op | source)
XLA Modules:
  0.0 34.7 jit_solution(1660293565464899660)
XLA Ops:
  0.0 2.5 %shard_map.28 = bf16[4,16512]{1,0:T(4,128)(2,1)} custom-call(bf16[4,4,2,2048]{3,2,1,0:T(2,128)(2,1)} %x_ref.1, s32[4,4]{1,0:T(4,128)} %v_ref.1), custom_call_target="tpu_custom_call" | custom-call | tf_op jit(solution)/shard_map/pallas_call | solution.py:70
  2.5 3.0 %collective-permute-start.3 = (bf16[4,16512]{1,0:T(4,128)(2,1)}, bf16[4,16512]{1,0:T(4,128)(2,1)S(1)}, u32[]{:S(2)}, u32[]{:S(2)}) collective-permute-start(bf16[4,16512]{1,0:T(4,128)(2,1)} %shard_map.28), channel_id=1, source_target_pairs={{0,8},{4,12},{8,16},{12,20},{16,24},{20,28},{24,0},{28,4},{1,9},{5... | collective-permute-start | bytes 396296 | tf_op jit(solution)/shard_map/ppermute | solution.py:234
  5.5 2.6 %collective-permute-start.4 = (bf16[4,16512]{1,0:T(4,128)(2,1)}, bf16[4,16512]{1,0:T(4,128)(2,1)S(1)}, u32[]{:S(2)}, u32[]{:S(2)}) collective-permute-start(bf16[4,16512]{1,0:T(4,128)(2,1)} %shard_map.28), channel_id=1, source_target_pairs={{0,16},{4,20},{8,24},{12,28},{16,0},{20,4},{24,8},{28,12},{1,17},{... | collective-permute-start | bytes 396296 | tf_op jit(solution)/shard_map/ppermute | solution.py:234
  8.1 1.3 %collective-permute-start.5 = (bf16[4,16512]{1,0:T(4,128)(2,1)}, bf16[4,16512]{1,0:T(4,128)(2,1)S(1)}, u32[]{:S(2)}, u32[]{:S(2)}) collective-permute-start(bf16[4,16512]{1,0:T(4,128)(2,1)} %shard_map.28), channel_id=1, source_target_pairs={{0,24},{4,28},{8,0},{12,4},{16,8},{20,12},{24,16},{28,20},{1,25},{... | collective-permute-start | bytes 396296 | tf_op jit(solution)/shard_map/ppermute | solution.py:234
  9.4 1.5 %collective-permute-start = (bf16[4,16512]{1,0:T(4,128)(2,1)}, bf16[4,16512]{1,0:T(4,128)(2,1)S(1)}, u32[]{:S(2)}, u32[]{:S(2)}) collective-permute-start(bf16[4,16512]{1,0:T(4,128)(2,1)} %shard_map.28), channel_id=1, source_target_pairs={{0,1},{1,2},{2,3},{3,0},{4,5},{5,6},{6,7},{7,4},{8,9},{9,10},{10,1... | collective-permute-start | bytes 396296 | tf_op jit(solution)/shard_map/ppermute | solution.py:234
  10.9 1.5 %collective-permute-start.1 = (bf16[4,16512]{1,0:T(4,128)(2,1)}, bf16[4,16512]{1,0:T(4,128)(2,1)S(1)}, u32[]{:S(2)}, u32[]{:S(2)}) collective-permute-start(bf16[4,16512]{1,0:T(4,128)(2,1)} %shard_map.28), channel_id=1, source_target_pairs={{0,2},{1,3},{2,0},{3,1},{4,6},{5,7},{6,4},{7,5},{8,10},{9,11},{10,... | collective-permute-start | bytes 396296 | tf_op jit(solution)/shard_map/ppermute | solution.py:234
  12.4 0.5 %fusion.5 = (f32[64,512]{1,0:T(8,128)S(1)}, f32[64,512]{1,0:T(8,128)S(1)}) fusion(s32[512]{0:T(512)S(1)} %iota_add_fusion), kind=kLoop, calls=%fused_computation.18 | loop fusion | flops 294912 | bytes 264192 | tf_op jit(solution)/shard_map/cos | solution.py:86
  13.0 0.3 %fusion.12 = (f32[32,512]{1,0:T(8,128)S(1)}, f32[32,512]{1,0:T(8,128)S(1)}) fusion(s32[512]{0:T(512)S(1)} %iota_add_fusion, s32[32]{0:T(128)S(1)} %iota_multiply_fusion), kind=kLoop, calls=%fused_computation.27 | loop fusion | flops 147456 | bytes 133248 | tf_op jit(solution)/shard_map/cos | solution.py:85
  13.3 0.0 collective-permute-done.3
  13.4 1.5 %collective-permute-start.2 = (bf16[4,16512]{1,0:T(4,128)(2,1)}, bf16[4,16512]{1,0:T(4,128)(2,1)S(1)}, u32[]{:S(2)}, u32[]{:S(2)}) collective-permute-start(bf16[4,16512]{1,0:T(4,128)(2,1)} %shard_map.28), channel_id=1, source_target_pairs={{0,3},{1,0},{2,1},{3,2},{4,7},{5,4},{6,5},{7,6},{8,11},{9,8},{10,9... | collective-permute-start | bytes 396296 | tf_op jit(solution)/shard_map/ppermute | solution.py:234
  14.9 2.1 %collective-permute-done.4 = bf16[4,16512]{1,0:T(4,128)(2,1)S(1)} collective-permute-done((bf16[4,16512]{1,0:T(4,128)(2,1)}, bf16[4,16512]{1,0:T(4,128)(2,1)S(1)}, u32[]{:S(2)}, u32[]{:S(2)}) %collective-permute-start.4) | collective-permute-done | bytes 132128 | tf_op jit(solution)/shard_map/ppermute | solution.py:234
  17.0 0.0 collective-permute-start.6
  17.0 0.0 collective-permute-done.5
  17.0 0.5 %collective-permute-start.7 = (bf16[4,16512]{1,0:T(4,128)(2,1)S(1)}, bf16[4,16512]{1,0:T(4,128)(2,1)S(1)}, u32[]{:S(2)}, u32[]{:S(2)}) collective-permute-start(bf16[4,16512]{1,0:T(4,128)(2,1)S(1)} %collective-permute-done.3), channel_id=1, source_target_pairs={{0,4},{4,0},{8,12},{12,8},{16,20},{20,16},{24,28},{28,24},{1,5},{5... | collective-permute-start | bytes 396296 | tf_op jit(solution)/shard_map/ppermute | solution.py:252
  17.5 0.0 collective-permute-done
  17.5 0.1 collective-permute-start.8
  17.6 0.2 collective-permute-done.1
  17.8 0.2 collective-permute-start.9
  18.0 0.0 copy-start.3
  18.0 3.5 %multiply_convert_fusion = (bf16[32,64,512]{2,1,0:T(8,128)(2,1)}, bf16[32,64,512]{2,1,0:T(8,128)(2,1)}) fusion(f32[64,512]{1,0:T(8,128)S(1)} %get-tuple-element.38, f32[32,512]{1,0:T(8,128)S(1)} %get-tuple-element.36, f32[64,512]{1,0:T(8,128)S(1)} %get-tuple-element.37, f32[32,512]{1,0:T(8,128)S(1)} %get-tuple-element.35), kind=kLoop, calls=%fused_computation | loop fusion | flops 10485760 | bytes 4587520 | tf_op jit(solution)/shard_map/convert_element_type | solution.py:91
  21.5 0.6 %pad_add_fusion.place_ref = s32[3]{0:T(128)} fusion(s32[1]{0:T(128)} %bitcast.2, s32[1]{0:T(128)} %bitcast.1, s32[1]{0:T(128)} %bitcast), kind=kLoop, calls=%fused_computation.30 | loop fusion | flops 6 | bytes 24 | tf_op jit(solution)/shard_map/stack | solution.py:260
  22.1 0.0 collective-permute-done.2
  22.1 0.0 collective-permute-done.6
  22.1 0.0 collective-permute-done.7
  22.1 0.0 collective-permute-done.8
  22.1 0.0 collective-permute-done.9
  22.1 0.0 copy-done.3
  22.2 0.1 dynamic_update_slice.40
  22.3 0.1 dynamic_update_slice.44
  22.5 0.1 dynamic_update_slice.36
  22.6 0.1 bitcast_dynamic-update-slice_fusion.5
  22.7 0.1 bitcast_dynamic-update-slice_fusion.4
  22.8 0.1 bitcast_dynamic-update-slice_fusion.2
  22.8 0.1 bitcast_dynamic-update-slice_fusion.1
  22.9 0.1 bitcast_dynamic-update-slice_fusion.8
  23.0 0.1 bitcast_dynamic-update-slice_fusion.7
  23.0 0.1 bitcast_dynamic-update-slice_fusion.6.rec_ref
  23.1 0.0 copy-start
  23.1 0.1 bitcast_dynamic-update-slice_fusion
  23.2 0.0 copy-start.1
  23.2 0.0 copy-start.2
  23.2 0.7 %copy-done = bf16[4,4,16512]{2,1,0:T(4,128)(2,1)} copy-done((bf16[4,4,16512]{2,1,0:T(4,128)(2,1)}, bf16[4,4,16512]{2,1,0:T(4,128)(2,1)S(1)}, u32[]{:S(2)}) %copy-start) | copy-done | bytes 528408
  23.9 0.2 copy-done.1
  24.1 0.2 copy-done.2
  24.3 10.4 %shard_map.29 = bf16[512,512]{1,0:T(8,128)(2,1)} custom-call(s32[3]{0:T(128)} %pad_add_fusion.place_ref, bf16[4,4,16512]{2,1,0:T(4,128)(2,1)} %copy-done, bf16[4,4,16512]{2,1,0:T(4,128)(2,1)} %copy-done.2, bf16[4,4,16512]{2,1,0:T(4,128)(2,1)} %copy-done.1, bf16[2048,512]{1,0:T(8,128)(2,1)} %bitcast.28, bf16[2048,512]{1,0:T(8,128)(2,1)} %bitcast.27), custom_call_target="tpu_custom_call" | custom-call | tf_op jit(solution)/shard_map/pallas_call | solution.py:199
  (2 shorter events, 0.0 us)
Async XLA Ops:
  2.5 10.9 %collective-permute-start.3 = (bf16[4,16512]{1,0:T(4,128)(2,1)}, bf16[4,16512]{1,0:T(4,128)(2,1)S(1)}, u32[]{:S(2)}, u32[]{:S(2)}) collective-permute-start(bf16[4,16512]{1,0:T(4,128)(2,1)} %shard_map.28), channel_id=1, source_target_pairs={{0,8},{4,12},{8,16},{12,20},{16,24},{20,28},{24,0},{28,4},{1,9},{5... | collective-permute-start | bytes 396296 | tf_op jit(solution)/shard_map/ppermute | solution.py:234
  5.5 11.5 %collective-permute-start.4 = (bf16[4,16512]{1,0:T(4,128)(2,1)}, bf16[4,16512]{1,0:T(4,128)(2,1)S(1)}, u32[]{:S(2)}, u32[]{:S(2)}) collective-permute-start(bf16[4,16512]{1,0:T(4,128)(2,1)} %shard_map.28), channel_id=1, source_target_pairs={{0,16},{4,20},{8,24},{12,28},{16,0},{20,4},{24,8},{28,12},{1,17},{... | collective-permute-start | bytes 396296 | tf_op jit(solution)/shard_map/ppermute | solution.py:234
  8.1 8.9 %collective-permute-start.5 = (bf16[4,16512]{1,0:T(4,128)(2,1)}, bf16[4,16512]{1,0:T(4,128)(2,1)S(1)}, u32[]{:S(2)}, u32[]{:S(2)}) collective-permute-start(bf16[4,16512]{1,0:T(4,128)(2,1)} %shard_map.28), channel_id=1, source_target_pairs={{0,24},{4,28},{8,0},{12,4},{16,8},{20,12},{24,16},{28,20},{1,25},{... | collective-permute-start | bytes 396296 | tf_op jit(solution)/shard_map/ppermute | solution.py:234
  9.4 8.1 %collective-permute-start = (bf16[4,16512]{1,0:T(4,128)(2,1)}, bf16[4,16512]{1,0:T(4,128)(2,1)S(1)}, u32[]{:S(2)}, u32[]{:S(2)}) collective-permute-start(bf16[4,16512]{1,0:T(4,128)(2,1)} %shard_map.28), channel_id=1, source_target_pairs={{0,1},{1,2},{2,3},{3,0},{4,5},{5,6},{6,7},{7,4},{8,9},{9,10},{10,1... | collective-permute-start | bytes 396296 | tf_op jit(solution)/shard_map/ppermute | solution.py:234
  10.9 6.9 %collective-permute-start.1 = (bf16[4,16512]{1,0:T(4,128)(2,1)}, bf16[4,16512]{1,0:T(4,128)(2,1)S(1)}, u32[]{:S(2)}, u32[]{:S(2)}) collective-permute-start(bf16[4,16512]{1,0:T(4,128)(2,1)} %shard_map.28), channel_id=1, source_target_pairs={{0,2},{1,3},{2,0},{3,1},{4,6},{5,7},{6,4},{7,5},{8,10},{9,11},{10,... | collective-permute-start | bytes 396296 | tf_op jit(solution)/shard_map/ppermute | solution.py:234
  13.4 8.8 %collective-permute-start.2 = (bf16[4,16512]{1,0:T(4,128)(2,1)}, bf16[4,16512]{1,0:T(4,128)(2,1)S(1)}, u32[]{:S(2)}, u32[]{:S(2)}) collective-permute-start(bf16[4,16512]{1,0:T(4,128)(2,1)} %shard_map.28), channel_id=1, source_target_pairs={{0,3},{1,0},{2,1},{3,2},{4,7},{5,4},{6,5},{7,6},{8,11},{9,8},{10,9... | collective-permute-start | bytes 396296 | tf_op jit(solution)/shard_map/ppermute | solution.py:234
  17.0 5.1 %collective-permute-start.6 = (bf16[4,16512]{1,0:T(4,128)(2,1)}, bf16[4,16512]{1,0:T(4,128)(2,1)S(1)}, u32[]{:S(2)}, u32[]{:S(2)}) collective-permute-start(bf16[4,16512]{1,0:T(4,128)(2,1)} %shard_map.28), channel_id=1, source_target_pairs={{0,4},{4,0},{8,12},{12,8},{16,20},{20,16},{24,28},{28,24},{1,5},{5... | collective-permute-start | bytes 396296 | tf_op jit(solution)/shard_map/ppermute | solution.py:252
  17.0 5.1 %collective-permute-start.7 = (bf16[4,16512]{1,0:T(4,128)(2,1)S(1)}, bf16[4,16512]{1,0:T(4,128)(2,1)S(1)}, u32[]{:S(2)}, u32[]{:S(2)}) collective-permute-start(bf16[4,16512]{1,0:T(4,128)(2,1)S(1)} %collective-permute-done.3), channel_id=1, source_target_pairs={{0,4},{4,0},{8,12},{12,8},{16,20},{20,16},{24,28},{28,24},{1,5},{5... | collective-permute-start | bytes 396296 | tf_op jit(solution)/shard_map/ppermute | solution.py:252
  17.5 4.6 %collective-permute-start.8 = (bf16[4,16512]{1,0:T(4,128)(2,1)S(1)}, bf16[4,16512]{1,0:T(4,128)(2,1)S(1)}, u32[]{:S(2)}, u32[]{:S(2)}) collective-permute-start(bf16[4,16512]{1,0:T(4,128)(2,1)S(1)} %collective-permute-done.4), channel_id=1, source_target_pairs={{0,4},{4,0},{8,12},{12,8},{16,20},{20,16},{24,28},{28,24},{1,5},{5... | collective-permute-start | bytes 396296 | tf_op jit(solution)/shard_map/ppermute | solution.py:252
  17.8 4.3 %collective-permute-start.9 = (bf16[4,16512]{1,0:T(4,128)(2,1)S(1)}, bf16[4,16512]{1,0:T(4,128)(2,1)S(1)}, u32[]{:S(2)}, u32[]{:S(2)}) collective-permute-start(bf16[4,16512]{1,0:T(4,128)(2,1)S(1)} %collective-permute-done.5), channel_id=1, source_target_pairs={{0,4},{4,0},{8,12},{12,8},{16,20},{20,16},{24,28},{28,24},{1,5},{5... | collective-permute-start | bytes 396296 | tf_op jit(solution)/shard_map/ppermute | solution.py:252
  18.0 4.1 %copy-start.3 = (bf16[4,16512]{1,0:T(4,128)(2,1)S(1)}, bf16[4,16512]{1,0:T(4,128)(2,1)}, u32[]{:S(2)}) copy-start(bf16[4,16512]{1,0:T(4,128)(2,1)} %shard_map.28) | copy-start | bytes 396292
  23.1 0.8 %copy-start = (bf16[4,4,16512]{2,1,0:T(4,128)(2,1)}, bf16[4,4,16512]{2,1,0:T(4,128)(2,1)S(1)}, u32[]{:S(2)}) copy-start(bf16[4,4,16512]{2,1,0:T(4,128)(2,1)S(1)} %bitcast_dynamic-update-slice_fusion.6.rec_ref) | copy-start | bytes 1585156
  23.2 0.9 %copy-start.1 = (bf16[4,4,16512]{2,1,0:T(4,128)(2,1)}, bf16[4,4,16512]{2,1,0:T(4,128)(2,1)S(1)}, u32[]{:S(2)}) copy-start(bf16[4,4,16512]{2,1,0:T(4,128)(2,1)S(1)} %get-tuple-element.39.sib_ref) | copy-start | bytes 1585156
  23.2 1.1 %copy-start.2 = (bf16[4,4,16512]{2,1,0:T(4,128)(2,1)}, bf16[4,4,16512]{2,1,0:T(4,128)(2,1)S(1)}, u32[]{:S(2)}) copy-start(bf16[4,4,16512]{2,1,0:T(4,128)(2,1)S(1)} %get-tuple-element.40.own_ref) | copy-start | bytes 1585156

commit v18 on v16

--- a/solution.py
+++ b/solution.py
@@ -93,7 +93,7 @@
 
 
 def cross_kernel(
-    place_ref, rec_ref, own_ref, sib_ref, tab_hbm, out_ref, srcf, recf, rtails, stails, cross,
+    rec_ref, own_ref, sib_ref, tab_hbm, out_ref, srcf, recf, rtails, stails, cross,
     tab_ref, tab_sem, *, windows, freqs, group, chunk
 ):
     step = pl.program_id(0)
@@ -125,7 +125,8 @@
 
     @pl.when(step == 0)
     def _():
-        rcv_index, chip, core = place_ref[0], place_ref[1], place_ref[2]
+        src_index = lax.axis_index("src")
+        rcv_index, chip, core = lax.axis_index("rcv"), src_index // 2, src_index % 2
         for rot in range(rcv_count):
 
             @pl.when(rcv_index == rot)
@@ -183,7 +184,7 @@
     ).astype(jnp.bfloat16)
 
 
-def correlate(place, rec_stack, own_stack, sib_stack, table, windows, freqs):
+def correlate(rec_stack, own_stack, sib_stack, table, windows, freqs):
     rcv_count, per, width = rec_stack.shape
     chips = own_stack.shape[0]
     nrec = rcv_count * per
@@ -193,11 +194,10 @@
     kernel = functools.partial(
         cross_kernel, windows=windows, freqs=freqs, group=group, chunk=256
     )
-    full3 = lambda g, p: (0, 0, 0)
+    full3 = lambda g: (0, 0, 0)
     out = pl.pallas_call(
         kernel,
-        grid_spec=pltpu.PrefetchScalarGridSpec(
-            num_scalar_prefetch=1,
+        grid_spec=pl.GridSpec(
             grid=(nrec // group,),
             in_specs=[
                 pl.BlockSpec(rec_stack.shape, full3),
@@ -205,7 +205,7 @@
                 pl.BlockSpec(sib_stack.shape, full3),
                 pl.BlockSpec(memory_space=pl.ANY),
             ],
-            out_specs=pl.BlockSpec((group * nsrc, lags), lambda g, p: (g, 0)),
+            out_specs=pl.BlockSpec((group * nsrc, lags), lambda g: (g, 0)),
             scratch_shapes=[
                 pltpu.VMEM((nsrc, windows * 3 * freqs), jnp.float32),
                 pltpu.VMEM((nrec, windows * 3 * freqs), jnp.float32),
@@ -218,7 +218,7 @@
         ),
         out_shape=jax.ShapeDtypeStruct((nrec * nsrc, lags), jnp.bfloat16),
         compiler_params=pltpu.CompilerParams(dimension_semantics=("arbitrary",)),
-    )(place, rec_stack, own_stack, sib_stack, table)
+    )(rec_stack, own_stack, sib_stack, table)
     return out.reshape(nrec, nsrc, lags)
 
 
@@ -251,11 +251,7 @@
     rec_stack = in_place_stack(rec_stack)
     own_stack = in_place_stack(own_stack)
     sib_stack = in_place_stack(sib_stack)
-    src_index = lax.axis_index("src")
-    place = jnp.stack(
-        [lax.axis_index("rcv"), src_index // 2, src_index % 2]
-    ).astype(jnp.int32)
-    return correlate(place, rec_stack, own_stack, sib_stack, table, windows, freqs)
+    return correlate(rec_stack, own_stack, sib_stack, table, windows, freqs)
 
 
 def solution(mesh):

time: 34.2 us -> 32.9 us (0.962)
  other arithmetic: 5.38 us -> 4.76 us
  Pallas kernels: 12.8 us -> 12.2 us
    pallas_call x1, Pallas kernels: 10.4 us -> 9.69 us  [correlate(): pl.pallas_call(kernel, grid_spec=pl.GridSpec(grid=(nrec // group,), in_sp...]
    another operation x1 -> x0, other arithmetic: 0.62 us -> none  [local(): jnp.stack([lax.axis_index('rcv'), src_index // 2, src_index % 2])]
  transfers between devices with their start and end apart: 10 -> 10, of which waited for: 2 -> 2; matrix products, arithmetic and copies ran while one was open for 16% -> 15% of each run, Pallas kernels for 0% -> 0%
where the time goes in v18:
time: 32.9 us; the launch traced here: 32.3 us
  starting transfers between devices  12.3 us (37%)
  Pallas kernels  12.2 us (37%)
  other arithmetic  4.76 us (14%)
  local copies, waits for them, and re-layouts  2.09 us (6%)
  waiting for transfers between devices  0.82 us (2%)
    ppermute x6, starting transfers between devices, shifted(): parts.append(lax.ppermute(x, axis, perm=pairs))  11.5 us
    pallas_call x1, Pallas kernels, correlate(): pl.pallas_call(kernel, grid_spec=pl.GridSpec(grid=(nrec // group,), in_sp...  9.69 us
    pallas_call x1, Pallas kernels, whiten_pack(): pl.pallas_call(kernel, out_shape=jax.ShapeDtypeStruct((channels, windows...  2.47 us
    another operation x1, other arithmetic, lag_table(): jnp.stack([cosines, sines], axis=0).reshape(2 * freq_count, lag_count)  2.32 us
    convert_element_type x1, other arithmetic, lag_table(): cosines = cosines.reshape(freq_count, lag_count).astype(jnp.bfloat16)  1.55 us
    unnamed x8, local copies, waits for them, and re-layouts  1.07 us
    dynamic_update_slice x11, local copies, waits for them, and re-layouts, in_place_stack(): stack = lax.dynamic_update_slice_in_dim(stack, part[None], k, axis=0)  1.02 us
    ppermute x4, starting transfers between devices, local(): sib_stack = [lax.ppermute(part, 'src', perm=sibling) for part in own_stack]  0.89 us
  transfers between devices with their start and end apart: 10, of which 2 were waited for; matrix products, arithmetic and copies ran while one was open for 15% of the time, Pallas kernels for 0%

profile of v18, /device:TPU:0, one launch (start us, length us, event | category | flops | bytes accessed | tf_op | source)
XLA Modules:
  0.0 32.3 jit_solution(17094749322159217060)
XLA Ops:
  0.0 2.5 %shard_map.28 = bf16[4,16512]{1,0:T(4,128)(2,1)} custom-call(bf16[4,4,2,2048]{3,2,1,0:T(2,128)(2,1)} %x_ref.1, s32[4,4]{1,0:T(4,128)} %v_ref.1), custom_call_target="tpu_custom_call" | custom-call | tf_op jit(solution)/shard_map/pallas_call | solution.py:70
  2.5 0.0 copy-start.3
  2.5 3.0 %collective-permute-start.3 = (bf16[4,16512]{1,0:T(4,128)(2,1)}, bf16[4,16512]{1,0:T(4,128)(2,1)S(1)}, u32[]{:S(2)}, u32[]{:S(2)}) collective-permute-start(bf16[4,16512]{1,0:T(4,128)(2,1)} %shard_map.28), channel_id=1, source_target_pairs={{0,8},{4,12},{8,16},{12,20},{16,24},{20,28},{24,0},{28,4},{1,9},{5... | collective-permute-start | bytes 396296 | tf_op jit(solution)/shard_map/ppermute | solution.py:229
  5.5 2.6 %collective-permute-start.4 = (bf16[4,16512]{1,0:T(4,128)(2,1)}, bf16[4,16512]{1,0:T(4,128)(2,1)S(1)}, u32[]{:S(2)}, u32[]{:S(2)}) collective-permute-start(bf16[4,16512]{1,0:T(4,128)(2,1)} %shard_map.28), channel_id=1, source_target_pairs={{0,16},{4,20},{8,24},{12,28},{16,0},{20,4},{24,8},{28,12},{1,17},{... | collective-permute-start | bytes 396296 | tf_op jit(solution)/shard_map/ppermute | solution.py:229
  8.1 1.3 %collective-permute-start.5 = (bf16[4,16512]{1,0:T(4,128)(2,1)}, bf16[4,16512]{1,0:T(4,128)(2,1)S(1)}, u32[]{:S(2)}, u32[]{:S(2)}) collective-permute-start(bf16[4,16512]{1,0:T(4,128)(2,1)} %shard_map.28), channel_id=1, source_target_pairs={{0,24},{4,28},{8,0},{12,4},{16,8},{20,12},{24,16},{28,20},{1,25},{... | collective-permute-start | bytes 396296 | tf_op jit(solution)/shard_map/ppermute | solution.py:229
  9.4 1.5 %collective-permute-start = (bf16[4,16512]{1,0:T(4,128)(2,1)}, bf16[4,16512]{1,0:T(4,128)(2,1)S(1)}, u32[]{:S(2)}, u32[]{:S(2)}) collective-permute-start(bf16[4,16512]{1,0:T(4,128)(2,1)} %shard_map.28), channel_id=1, source_target_pairs={{0,1},{1,2},{2,3},{3,0},{4,5},{5,6},{6,7},{7,4},{8,9},{9,10},{10,1... | collective-permute-start | bytes 396296 | tf_op jit(solution)/shard_map/ppermute | solution.py:229
  10.9 1.5 %collective-permute-start.1 = (bf16[4,16512]{1,0:T(4,128)(2,1)}, bf16[4,16512]{1,0:T(4,128)(2,1)S(1)}, u32[]{:S(2)}, u32[]{:S(2)}) collective-permute-start(bf16[4,16512]{1,0:T(4,128)(2,1)} %shard_map.28), channel_id=1, source_target_pairs={{0,2},{1,3},{2,0},{3,1},{4,6},{5,7},{6,4},{7,5},{8,10},{9,11},{10,... | collective-permute-start | bytes 396296 | tf_op jit(solution)/shard_map/ppermute | solution.py:229
  12.5 0.5 %fusion.5 = (f32[64,512]{1,0:T(8,128)S(1)}, f32[64,512]{1,0:T(8,128)S(1)}) fusion(s32[512]{0:T(512)S(1)} %iota_add_fusion), kind=kLoop, calls=%fused_computation.19 | loop fusion | flops 294912 | bytes 264192 | tf_op jit(solution)/shard_map/cos | solution.py:86
  13.0 0.3 %fusion.12 = (f32[32,512]{1,0:T(8,128)S(1)}, f32[32,512]{1,0:T(8,128)S(1)}) fusion(s32[512]{0:T(512)S(1)} %iota_add_fusion, s32[32]{0:T(128)S(1)} %iota_multiply_fusion), kind=kLoop, calls=%fused_computation.28 | loop fusion | flops 147456 | bytes 133248 | tf_op jit(solution)/shard_map/cos | solution.py:85
  13.3 1.5 %multiply_convert_fusion.1 = (bf16[32,64,512]{2,1,0:T(8,128)(2,1)S(1)}, bf16[32,64,512]{2,1,0:T(8,128)(2,1)S(1)}) fusion(f32[64,512]{1,0:T(8,128)S(1)} %get-tuple-element.36, f32[32,512]{1,0:T(8,128)S(1)} %get-tuple-element.34, f32[64,512]{1,0:T(8,128)S(1)} %get-tuple-element.35, f32[32,512]{1,0:T(8,128)S(1)} %get-tuple-element.33), kind=kLoop, calls=%fused_computation.2 | loop fusion | flops 10485760 | bytes 4587520 | tf_op jit(solution)/shard_map/convert_element_type | solution.py:90
  14.9 0.0 collective-permute-done.3
  14.9 0.0 copy-done.3
  14.9 1.5 %collective-permute-start.2 = (bf16[4,16512]{1,0:T(4,128)(2,1)S(1)}, bf16[4,16512]{1,0:T(4,128)(2,1)S(1)}, u32[]{:S(2)}, u32[]{:S(2)}) collective-permute-start(bf16[4,16512]{1,0:T(4,128)(2,1)S(1)} %copy-done.3), channel_id=1, source_target_pairs={{0,3},{1,0},{2,1},{3,2},{4,7},{5,4},{6,5},{7,6},{8,11},{9,8},{10,9... | collective-permute-start | bytes 396296 | tf_op jit(solution)/shard_map/ppermute | solution.py:229
  16.4 0.7 %collective-permute-done.4 = bf16[4,16512]{1,0:T(4,128)(2,1)S(1)} collective-permute-done((bf16[4,16512]{1,0:T(4,128)(2,1)}, bf16[4,16512]{1,0:T(4,128)(2,1)S(1)}, u32[]{:S(2)}, u32[]{:S(2)}) %collective-permute-start.4) | collective-permute-done | bytes 132128 | tf_op jit(solution)/shard_map/ppermute | solution.py:229
  17.1 0.0 collective-permute-start.6
  17.1 0.0 collective-permute-done.5
  17.1 0.5 %collective-permute-start.7 = (bf16[4,16512]{1,0:T(4,128)(2,1)S(1)}, bf16[4,16512]{1,0:T(4,128)(2,1)S(1)}, u32[]{:S(2)}, u32[]{:S(2)}) collective-permute-start(bf16[4,16512]{1,0:T(4,128)(2,1)S(1)} %collective-permute-done.3), channel_id=1, source_target_pairs={{0,4},{4,0},{8,12},{12,8},{16,20},{20,16},{24,28},{28,24},{1,5},{5... | collective-permute-start | bytes 396296 | tf_op jit(solution)/shard_map/ppermute | solution.py:247
  17.6 0.0 collective-permute-done
  17.6 0.1 collective-permute-start.8
  17.7 0.1 collective-permute-done.1
  17.8 0.3 collective-permute-start.9
  18.1 2.3 %pad_maximum_fusion = bf16[2,2048,512]{2,1,0:T(8,128)(2,1)} fusion(bf16[1,2048,512]{2,1,0:T(8,128)(2,1)S(1)} %bitcast.27, bf16[1,2048,512]{2,1,0:T(8,128)(2,1)S(1)} %bitcast.26), kind=kLoop, calls=%fused_computation | loop fusion | flops 2097152 | bytes 8388608 | tf_op jit(solution)/shard_map/stack | solution.py:92
  20.4 0.0 collective-permute-done.2
  20.4 0.0 collective-permute-done.6
  20.4 0.0 collective-permute-done.7
  20.4 0.0 collective-permute-done.8
  20.5 0.0 collective-permute-done.9
  20.5 0.1 dynamic_update_slice.40
  20.6 0.1 dynamic_update_slice.44
  20.8 0.1 dynamic_update_slice.36
  20.9 0.1 bitcast_dynamic-update-slice_fusion.5
  21.0 0.1 bitcast_dynamic-update-slice_fusion.4
  21.1 0.1 bitcast_dynamic-update-slice_fusion.2
  21.1 0.1 bitcast_dynamic-update-slice_fusion.1
  21.2 0.1 bitcast_dynamic-update-slice_fusion.8
  21.3 0.1 bitcast_dynamic-update-slice_fusion.7
  21.3 0.1 bitcast_dynamic-update-slice_fusion.6.rec_ref
  21.4 0.0 copy-start
  21.4 0.1 bitcast_dynamic-update-slice_fusion
  21.5 0.0 copy-start.1
  21.5 0.0 copy-start.2
  21.6 0.7 %copy-done = bf16[4,4,16512]{2,1,0:T(4,128)(2,1)} copy-done((bf16[4,4,16512]{2,1,0:T(4,128)(2,1)}, bf16[4,4,16512]{2,1,0:T(4,128)(2,1)S(1)}, u32[]{:S(2)}) %copy-start) | copy-done | bytes 528408
  22.2 0.2 copy-done.1
  22.4 0.2 copy-done.2
  22.6 9.7 %shard_map.29 = bf16[512,512]{1,0:T(8,128)(2,1)} custom-call(bf16[4,4,16512]{2,1,0:T(4,128)(2,1)} %copy-done, bf16[4,4,16512]{2,1,0:T(4,128)(2,1)} %copy-done.2, bf16[4,4,16512]{2,1,0:T(4,128)(2,1)} %copy-done.1, bf16[4096,512]{1,0:T(8,128)(2,1)} %bitcast.25), custom_call_target="tpu_custom_call" | custom-call | tf_op jit(solution)/shard_map/pallas_call | solution.py:198
  (2 shorter events, 0.0 us)
Async XLA Ops:
  2.5 12.4 %copy-start.3 = (bf16[4,16512]{1,0:T(4,128)(2,1)S(1)}, bf16[4,16512]{1,0:T(4,128)(2,1)}, u32[]{:S(2)}) copy-start(bf16[4,16512]{1,0:T(4,128)(2,1)} %shard_map.28) | copy-start | bytes 396292
  2.5 12.4 %collective-permute-start.3 = (bf16[4,16512]{1,0:T(4,128)(2,1)}, bf16[4,16512]{1,0:T(4,128)(2,1)S(1)}, u32[]{:S(2)}, u32[]{:S(2)}) collective-permute-start(bf16[4,16512]{1,0:T(4,128)(2,1)} %shard_map.28), channel_id=1, source_target_pairs={{0,8},{4,12},{8,16},{12,20},{16,24},{20,28},{24,0},{28,4},{1,9},{5... | collective-permute-start | bytes 396296 | tf_op jit(solution)/shard_map/ppermute | solution.py:229
  5.5 11.6 %collective-permute-start.4 = (bf16[4,16512]{1,0:T(4,128)(2,1)}, bf16[4,16512]{1,0:T(4,128)(2,1)S(1)}, u32[]{:S(2)}, u32[]{:S(2)}) collective-permute-start(bf16[4,16512]{1,0:T(4,128)(2,1)} %shard_map.28), channel_id=1, source_target_pairs={{0,16},{4,20},{8,24},{12,28},{16,0},{20,4},{24,8},{28,12},{1,17},{... | collective-permute-start | bytes 396296 | tf_op jit(solution)/shard_map/ppermute | solution.py:229
  8.1 9.0 %collective-permute-start.5 = (bf16[4,16512]{1,0:T(4,128)(2,1)}, bf16[4,16512]{1,0:T(4,128)(2,1)S(1)}, u32[]{:S(2)}, u32[]{:S(2)}) collective-permute-start(bf16[4,16512]{1,0:T(4,128)(2,1)} %shard_map.28), channel_id=1, source_target_pairs={{0,24},{4,28},{8,0},{12,4},{16,8},{20,12},{24,16},{28,20},{1,25},{... | collective-permute-start | bytes 396296 | tf_op jit(solution)/shard_map/ppermute | solution.py:229
  9.4 8.2 %collective-permute-start = (bf16[4,16512]{1,0:T(4,128)(2,1)}, bf16[4,16512]{1,0:T(4,128)(2,1)S(1)}, u32[]{:S(2)}, u32[]{:S(2)}) collective-permute-start(bf16[4,16512]{1,0:T(4,128)(2,1)} %shard_map.28), channel_id=1, source_target_pairs={{0,1},{1,2},{2,3},{3,0},{4,5},{5,6},{6,7},{7,4},{8,9},{9,10},{10,1... | collective-permute-start | bytes 396296 | tf_op jit(solution)/shard_map/ppermute | solution.py:229
  10.9 6.9 %collective-permute-start.1 = (bf16[4,16512]{1,0:T(4,128)(2,1)}, bf16[4,16512]{1,0:T(4,128)(2,1)S(1)}, u32[]{:S(2)}, u32[]{:S(2)}) collective-permute-start(bf16[4,16512]{1,0:T(4,128)(2,1)} %shard_map.28), channel_id=1, source_target_pairs={{0,2},{1,3},{2,0},{3,1},{4,6},{5,7},{6,4},{7,5},{8,10},{9,11},{10,... | collective-permute-start | bytes 396296 | tf_op jit(solution)/shard_map/ppermute | solution.py:229
  14.9 5.5 %collective-permute-start.2 = (bf16[4,16512]{1,0:T(4,128)(2,1)S(1)}, bf16[4,16512]{1,0:T(4,128)(2,1)S(1)}, u32[]{:S(2)}, u32[]{:S(2)}) collective-permute-start(bf16[4,16512]{1,0:T(4,128)(2,1)S(1)} %copy-done.3), channel_id=1, source_target_pairs={{0,3},{1,0},{2,1},{3,2},{4,7},{5,4},{6,5},{7,6},{8,11},{9,8},{10,9... | collective-permute-start | bytes 396296 | tf_op jit(solution)/shard_map/ppermute | solution.py:229
  17.1 3.4 %collective-permute-start.6 = (bf16[4,16512]{1,0:T(4,128)(2,1)S(1)}, bf16[4,16512]{1,0:T(4,128)(2,1)S(1)}, u32[]{:S(2)}, u32[]{:S(2)}) collective-permute-start(bf16[4,16512]{1,0:T(4,128)(2,1)S(1)} %copy-done.3), channel_id=1, source_target_pairs={{0,4},{4,0},{8,12},{12,8},{16,20},{20,16},{24,28},{28,24},{1,5},{5... | collective-permute-start | bytes 396296 | tf_op jit(solution)/shard_map/ppermute | solution.py:247
  17.1 3.4 %collective-permute-start.7 = (bf16[4,16512]{1,0:T(4,128)(2,1)S(1)}, bf16[4,16512]{1,0:T(4,128)(2,1)S(1)}, u32[]{:S(2)}, u32[]{:S(2)}) collective-permute-start(bf16[4,16512]{1,0:T(4,128)(2,1)S(1)} %collective-permute-done.3), channel_id=1, source_target_pairs={{0,4},{4,0},{8,12},{12,8},{16,20},{20,16},{24,28},{28,24},{1,5},{5... | collective-permute-start | bytes 396296 | tf_op jit(solution)/shard_map/ppermute | solution.py:247
  17.6 2.9 %collective-permute-start.8 = (bf16[4,16512]{1,0:T(4,128)(2,1)S(1)}, bf16[4,16512]{1,0:T(4,128)(2,1)S(1)}, u32[]{:S(2)}, u32[]{:S(2)}) collective-permute-start(bf16[4,16512]{1,0:T(4,128)(2,1)S(1)} %collective-permute-done.4), channel_id=1, source_target_pairs={{0,4},{4,0},{8,12},{12,8},{16,20},{20,16},{24,28},{28,24},{1,5},{5... | collective-permute-start | bytes 396296 | tf_op jit(solution)/shard_map/ppermute | solution.py:247
  17.8 2.7 %collective-permute-start.9 = (bf16[4,16512]{1,0:T(4,128)(2,1)S(1)}, bf16[4,16512]{1,0:T(4,128)(2,1)S(1)}, u32[]{:S(2)}, u32[]{:S(2)}) collective-permute-start(bf16[4,16512]{1,0:T(4,128)(2,1)S(1)} %collective-permute-done.5), channel_id=1, source_target_pairs={{0,4},{4,0},{8,12},{12,8},{16,20},{20,16},{24,28},{28,24},{1,5},{5... | collective-permute-start | bytes 396296 | tf_op jit(solution)/shard_map/ppermute | solution.py:247
  21.4 0.8 %copy-start = (bf16[4,4,16512]{2,1,0:T(4,128)(2,1)}, bf16[4,4,16512]{2,1,0:T(4,128)(2,1)S(1)}, u32[]{:S(2)}) copy-start(bf16[4,4,16512]{2,1,0:T(4,128)(2,1)S(1)} %bitcast_dynamic-update-slice_fusion.6.rec_ref) | copy-start | bytes 1585156
  21.5 0.9 %copy-start.1 = (bf16[4,4,16512]{2,1,0:T(4,128)(2,1)}, bf16[4,4,16512]{2,1,0:T(4,128)(2,1)S(1)}, u32[]{:S(2)}) copy-start(bf16[4,4,16512]{2,1,0:T(4,128)(2,1)S(1)} %get-tuple-element.37.sib_ref) | copy-start | bytes 1585156
  21.5 1.1 %copy-start.2 = (bf16[4,4,16512]{2,1,0:T(4,128)(2,1)}, bf16[4,4,16512]{2,1,0:T(4,128)(2,1)S(1)}, u32[]{:S(2)}) copy-start(bf16[4,4,16512]{2,1,0:T(4,128)(2,1)S(1)} %get-tuple-element.38.own_ref) | copy-start | bytes 1585156

commit v19 on v17

--- a/solution.py
+++ b/solution.py
@@ -93,7 +93,7 @@
 
 
 def cross_kernel(
-    place_ref, rec_ref, own_ref, sib_ref, cos_hbm, sin_hbm, out_ref, srcf, recf, rtails, stails,
+    rec_ref, own_ref, sib_ref, cos_hbm, sin_hbm, out_ref, srcf, recf, rtails, stails,
     cross, cos_ref, sin_ref, cos_sem, sin_sem, *, windows, freqs, group, chunk
 ):
     step = pl.program_id(0)
@@ -126,7 +126,8 @@
 
     @pl.when(step == 0)
     def _():
-        rcv_index, chip, core = place_ref[0], place_ref[1], place_ref[2]
+        src_index = lax.axis_index("src")
+        rcv_index, chip, core = lax.axis_index("rcv"), src_index // 2, src_index % 2
         for rot in range(rcv_count):
 
             @pl.when(rcv_index == rot)
@@ -185,7 +186,7 @@
     out_ref[...] = (real + imag).astype(jnp.bfloat16)
 
 
-def correlate(place, rec_stack, own_stack, sib_stack, tables, windows, freqs):
+def correlate(rec_stack, own_stack, sib_stack, tables, windows, freqs):
     rcv_count, per, width = rec_stack.shape
     chips = own_stack.shape[0]
     nrec = rcv_count * per
@@ -195,11 +196,10 @@
     kernel = functools.partial(
         cross_kernel, windows=windows, freqs=freqs, group=group, chunk=256
     )
-    full3 = lambda g, p: (0, 0, 0)
+    full3 = lambda g: (0, 0, 0)
     out = pl.pallas_call(
         kernel,
-        grid_spec=pltpu.PrefetchScalarGridSpec(
-            num_scalar_prefetch=1,
+        grid_spec=pl.GridSpec(
             grid=(nrec // group,),
             in_specs=[
                 pl.BlockSpec(rec_stack.shape, full3),
@@ -208,7 +208,7 @@
                 pl.BlockSpec(memory_space=pl.ANY),
                 pl.BlockSpec(memory_space=pl.ANY),
             ],
-            out_specs=pl.BlockSpec((group * nsrc, lags), lambda g, p: (g, 0)),
+            out_specs=pl.BlockSpec((group * nsrc, lags), lambda g: (g, 0)),
             scratch_shapes=[
                 pltpu.VMEM((nsrc, windows * 3 * freqs), jnp.float32),
                 pltpu.VMEM((nrec, windows * 3 * freqs), jnp.float32),
@@ -223,7 +223,7 @@
         ),
         out_shape=jax.ShapeDtypeStruct((nrec * nsrc, lags), jnp.bfloat16),
         compiler_params=pltpu.CompilerParams(dimension_semantics=("arbitrary",)),
-    )(place, rec_stack, own_stack, sib_stack, *tables)
+    )(rec_stack, own_stack, sib_stack, *tables)
     return out.reshape(nrec, nsrc, lags)
 
 
@@ -256,11 +256,7 @@
     rec_stack = in_place_stack(rec_stack)
     own_stack = in_place_stack(own_stack)
     sib_stack = in_place_stack(sib_stack)
-    src_index = lax.axis_index("src")
-    place = jnp.stack(
-        [lax.axis_index("rcv"), src_index // 2, src_index % 2]
-    ).astype(jnp.int32)
-    return correlate(place, rec_stack, own_stack, sib_stack, table, windows, freqs)
+    return correlate(rec_stack, own_stack, sib_stack, table, windows, freqs)
 
 
 def solution(mesh):

time: 35.3 us -> 36 us (1.020); the launches traced: 34.7 us -> 35.8 us
  waiting for transfers between devices: 2.36 us -> 6.72 us
  starting transfers between devices: 12.3 us -> 10.4 us
  other arithmetic: 4.97 us -> 4.35 us
  Pallas kernels: 12.8 us -> 12.2 us
    ppermute x6, waiting for transfers between devices: 2.35 us -> 6.71 us  [shifted(): parts.append(lax.ppermute(x, axis, perm=pairs))]
    ppermute x6, starting transfers between devices: 11.5 us -> 9.41 us  [shifted(): parts.append(lax.ppermute(x, axis, perm=pairs))]
    pallas_call x1, Pallas kernels: 10.4 us -> 9.7 us  [correlate(): pl.pallas_call(kernel, grid_spec=pl.GridSpec(grid=(nrec // group,), in_sp...]
    another operation x1 -> x0, other arithmetic: 0.62 us -> none  [local(): jnp.stack([lax.axis_index('rcv'), src_index // 2, src_index % 2])]
  transfers between devices with their start and end apart: 10 -> 10, of which waited for: 2 -> 1; matrix products, arithmetic and copies ran while one was open for 14% -> 12% of each run, Pallas kernels for 0% -> 0%
where the time goes in v19:
time: 36 us; the launch traced here: 35.8 us
  Pallas kernels  12.2 us (34%)
  starting transfers between devices  10.4 us (29%)
  waiting for transfers between devices  6.72 us (19%)
  other arithmetic  4.35 us (12%)
  local copies, waits for them, and re-layouts  2.03 us (6%)
    pallas_call x1, Pallas kernels, correlate(): pl.pallas_call(kernel, grid_spec=pl.GridSpec(grid=(nrec // group,), in_sp...  9.7 us
    ppermute x6, starting transfers between devices, shifted(): parts.append(lax.ppermute(x, axis, perm=pairs))  9.41 us
    ppermute x6, waiting for transfers between devices, shifted(): parts.append(lax.ppermute(x, axis, perm=pairs))  6.71 us
    convert_element_type x1, other arithmetic, lag_table(): sines = sines.reshape(freq_count, lag_count).astype(jnp.bfloat16)  3.45 us
    pallas_call x1, Pallas kernels, whiten_pack(): pl.pallas_call(kernel, out_shape=jax.ShapeDtypeStruct((channels, windows...  2.47 us
    ppermute x4, starting transfers between devices, local(): sib_stack = [lax.ppermute(part, 'src', perm=sibling) for part in own_stack]  1.03 us
    dynamic_update_slice x11, local copies, waits for them, and re-layouts, in_place_stack(): stack = lax.dynamic_update_slice_in_dim(stack, part[None], k, axis=0)  1.02 us
    unnamed x8, local copies, waits for them, and re-layouts  1 us
  transfers between devices with their start and end apart: 10, of which 1 were waited for; matrix products, arithmetic and copies ran while one was open for 12% of the time, Pallas kernels for 0%

profile of v19, /device:TPU:0, one launch (start us, length us, event | category | flops | bytes accessed | tf_op | source)
XLA Modules:
  0.0 35.8 jit_solution(8070976907470917392)
XLA Ops:
  0.0 2.5 %shard_map.28 = bf16[4,16512]{1,0:T(4,128)(2,1)} custom-call(bf16[4,4,2,2048]{3,2,1,0:T(2,128)(2,1)} %x_ref.1, s32[4,4]{1,0:T(4,128)} %v_ref.1), custom_call_target="tpu_custom_call" | custom-call | tf_op jit(solution)/shard_map/pallas_call | solution.py:70
  2.5 0.5 %collective-permute-start.6 = (bf16[4,16512]{1,0:T(4,128)(2,1)}, bf16[4,16512]{1,0:T(4,128)(2,1)S(1)}, u32[]{:S(2)}, u32[]{:S(2)}) collective-permute-start(bf16[4,16512]{1,0:T(4,128)(2,1)} %shard_map.28), channel_id=1, source_target_pairs={{0,4},{4,0},{8,12},{12,8},{16,20},{20,16},{24,28},{28,24},{1,5},{5... | collective-permute-start | bytes 396296 | tf_op jit(solution)/shard_map/ppermute | solution.py:252
  2.9 4.6 %collective-permute-start.5 = (bf16[4,16512]{1,0:T(4,128)(2,1)}, bf16[4,16512]{1,0:T(4,128)(2,1)S(1)}, u32[]{:S(2)}, u32[]{:S(2)}) collective-permute-start(bf16[4,16512]{1,0:T(4,128)(2,1)} %shard_map.28), channel_id=1, source_target_pairs={{0,24},{4,28},{8,0},{12,4},{16,8},{20,12},{24,16},{28,20},{1,25},{... | collective-permute-start | bytes 396296 | tf_op jit(solution)/shard_map/ppermute | solution.py:234
  7.5 0.0 collective-permute-start.4
  7.5 1.0 %collective-permute-start.3 = (bf16[4,16512]{1,0:T(4,128)(2,1)}, bf16[4,16512]{1,0:T(4,128)(2,1)S(1)}, u32[]{:S(2)}, u32[]{:S(2)}) collective-permute-start(bf16[4,16512]{1,0:T(4,128)(2,1)} %shard_map.28), channel_id=1, source_target_pairs={{0,8},{4,12},{8,16},{12,20},{16,24},{20,28},{24,0},{28,4},{1,9},{5... | collective-permute-start | bytes 396296 | tf_op jit(solution)/shard_map/ppermute | solution.py:234
  8.5 2.4 %collective-permute-start.2 = (bf16[4,16512]{1,0:T(4,128)(2,1)}, bf16[4,16512]{1,0:T(4,128)(2,1)S(1)}, u32[]{:S(2)}, u32[]{:S(2)}) collective-permute-start(bf16[4,16512]{1,0:T(4,128)(2,1)} %shard_map.28), channel_id=1, source_target_pairs={{0,3},{1,0},{2,1},{3,2},{4,7},{5,4},{6,5},{7,6},{8,11},{9,8},{10,9... | collective-permute-start | bytes 396296 | tf_op jit(solution)/shard_map/ppermute | solution.py:234
  11.0 0.5 %fusion.5 = (f32[64,512]{1,0:T(8,128)S(1)}, f32[64,512]{1,0:T(8,128)S(1)}) fusion(s32[512]{0:T(512)S(1)} %iota_add_fusion), kind=kLoop, calls=%fused_computation.18 | loop fusion | flops 294912 | bytes 264192 | tf_op jit(solution)/shard_map/cos | solution.py:86
  11.5 0.3 fusion.12
  11.9 0.0 collective-permute-done.6
  11.9 0.6 %collective-permute-start.1 = (bf16[4,16512]{1,0:T(4,128)(2,1)}, bf16[4,16512]{1,0:T(4,128)(2,1)S(1)}, u32[]{:S(2)}, u32[]{:S(2)}) collective-permute-start(bf16[4,16512]{1,0:T(4,128)(2,1)} %shard_map.28), channel_id=1, source_target_pairs={{0,2},{1,3},{2,0},{3,1},{4,6},{5,7},{6,4},{7,5},{8,10},{9,11},{10,... | collective-permute-start | bytes 396296 | tf_op jit(solution)/shard_map/ppermute | solution.py:234
  12.5 0.0 collective-permute-done.5
  12.5 0.8 %collective-permute-start = (bf16[4,16512]{1,0:T(4,128)(2,1)}, bf16[4,16512]{1,0:T(4,128)(2,1)S(1)}, u32[]{:S(2)}, u32[]{:S(2)}) collective-permute-start(bf16[4,16512]{1,0:T(4,128)(2,1)} %shard_map.28), channel_id=1, source_target_pairs={{0,1},{1,2},{2,3},{3,0},{4,5},{5,6},{6,7},{7,4},{8,9},{9,10},{10,1... | collective-permute-start | bytes 396296 | tf_op jit(solution)/shard_map/ppermute | solution.py:234
  13.2 6.7 %collective-permute-done.4 = bf16[4,16512]{1,0:T(4,128)(2,1)S(1)} collective-permute-done((bf16[4,16512]{1,0:T(4,128)(2,1)}, bf16[4,16512]{1,0:T(4,128)(2,1)S(1)}, u32[]{:S(2)}, u32[]{:S(2)}) %collective-permute-start.4) | collective-permute-done | bytes 132128 | tf_op jit(solution)/shard_map/ppermute | solution.py:234
  19.9 0.0 collective-permute-start.9
  19.9 0.0 collective-permute-done.3
  20.0 0.5 %collective-permute-start.8 = (bf16[4,16512]{1,0:T(4,128)(2,1)S(1)}, bf16[4,16512]{1,0:T(4,128)(2,1)S(1)}, u32[]{:S(2)}, u32[]{:S(2)}) collective-permute-start(bf16[4,16512]{1,0:T(4,128)(2,1)S(1)} %collective-permute-done.4), channel_id=1, source_target_pairs={{0,4},{4,0},{8,12},{12,8},{16,20},{20,16},{24,28},{28,24},{1,5},{5... | collective-permute-start | bytes 396296 | tf_op jit(solution)/shard_map/ppermute | solution.py:252
  20.5 0.0 collective-permute-done.2
  20.5 0.1 collective-permute-start.7
  20.5 0.0 copy-start.3
  20.5 3.5 %multiply_convert_fusion = (bf16[32,64,512]{2,1,0:T(8,128)(2,1)}, bf16[32,64,512]{2,1,0:T(8,128)(2,1)}) fusion(f32[64,512]{1,0:T(8,128)S(1)} %get-tuple-element.38, f32[32,512]{1,0:T(8,128)S(1)} %get-tuple-element.36, f32[64,512]{1,0:T(8,128)S(1)} %get-tuple-element.37, f32[32,512]{1,0:T(8,128)S(1)} %get-tuple-element.35), kind=kLoop, calls=%fused_computation | loop fusion | flops 10485760 | bytes 4587520 | tf_op jit(solution)/shard_map/convert_element_type | solution.py:91
  24.0 0.0 collective-permute-done.1
  24.0 0.0 collective-permute-done
  24.0 0.0 collective-permute-done.9
  24.0 0.0 collective-permute-done.8
  24.0 0.0 collective-permute-done.7
  24.0 0.0 copy-done.3
  24.0 0.1 dynamic_update_slice.36
  24.2 0.1 dynamic_update_slice.44
  24.3 0.1 dynamic_update_slice.40
  24.5 0.1 bitcast_dynamic-update-slice_fusion.8
  24.6 0.1 bitcast_dynamic-update-slice_fusion.7
  24.6 0.1 bitcast_dynamic-update-slice_fusion.6.rec_ref
  24.7 0.0 copy-start.2
  24.7 0.1 bitcast_dynamic-update-slice_fusion.2
  24.8 0.1 bitcast_dynamic-update-slice_fusion.1
  24.8 0.1 bitcast_dynamic-update-slice_fusion.5
  24.9 0.1 bitcast_dynamic-update-slice_fusion.4
  25.0 0.1 bitcast_dynamic-update-slice_fusion
  25.1 0.0 copy-start
  25.1 0.0 copy-start.1
  25.1 0.4 %copy-done.2 = bf16[4,4,16512]{2,1,0:T(4,128)(2,1)} copy-done((bf16[4,4,16512]{2,1,0:T(4,128)(2,1)}, bf16[4,4,16512]{2,1,0:T(4,128)(2,1)S(1)}, u32[]{:S(2)}) %copy-start.2) | copy-done | bytes 528408
  25.5 0.4 %copy-done = bf16[4,4,16512]{2,1,0:T(4,128)(2,1)} copy-done((bf16[4,4,16512]{2,1,0:T(4,128)(2,1)}, bf16[4,4,16512]{2,1,0:T(4,128)(2,1)S(1)}, u32[]{:S(2)}) %copy-start) | copy-done | bytes 528408
  25.9 0.2 copy-done.1
  26.1 9.7 %shard_map.29 = bf16[512,512]{1,0:T(8,128)(2,1)} custom-call(bf16[4,4,16512]{2,1,0:T(4,128)(2,1)} %copy-done.2, bf16[4,4,16512]{2,1,0:T(4,128)(2,1)} %copy-done, bf16[4,4,16512]{2,1,0:T(4,128)(2,1)} %copy-done.1, bf16[2048,512]{1,0:T(8,128)(2,1)} %bitcast.25, bf16[2048,512]{1,0:T(8,128)(2,1)} %bitcast.24), custom_call_target="tpu_custom_call" | custom-call | tf_op jit(solution)/shard_map/pallas_call | solution.py:200
  (2 shorter events, 0.0 us)
Async XLA Ops:
  2.5 9.4 %collective-permute-start.6 = (bf16[4,16512]{1,0:T(4,128)(2,1)}, bf16[4,16512]{1,0:T(4,128)(2,1)S(1)}, u32[]{:S(2)}, u32[]{:S(2)}) collective-permute-start(bf16[4,16512]{1,0:T(4,128)(2,1)} %shard_map.28), channel_id=1, source_target_pairs={{0,4},{4,0},{8,12},{12,8},{16,20},{20,16},{24,28},{28,24},{1,5},{5... | collective-permute-start | bytes 396296 | tf_op jit(solution)/shard_map/ppermute | solution.py:252
  2.9 9.6 %collective-permute-start.5 = (bf16[4,16512]{1,0:T(4,128)(2,1)}, bf16[4,16512]{1,0:T(4,128)(2,1)S(1)}, u32[]{:S(2)}, u32[]{:S(2)}) collective-permute-start(bf16[4,16512]{1,0:T(4,128)(2,1)} %shard_map.28), channel_id=1, source_target_pairs={{0,24},{4,28},{8,0},{12,4},{16,8},{20,12},{24,16},{28,20},{1,25},{... | collective-permute-start | bytes 396296 | tf_op jit(solution)/shard_map/ppermute | solution.py:234
  7.5 12.4 %collective-permute-start.4 = (bf16[4,16512]{1,0:T(4,128)(2,1)}, bf16[4,16512]{1,0:T(4,128)(2,1)S(1)}, u32[]{:S(2)}, u32[]{:S(2)}) collective-permute-start(bf16[4,16512]{1,0:T(4,128)(2,1)} %shard_map.28), channel_id=1, source_target_pairs={{0,16},{4,20},{8,24},{12,28},{16,0},{20,4},{24,8},{28,12},{1,17},{... | collective-permute-start | bytes 396296 | tf_op jit(solution)/shard_map/ppermute | solution.py:234
  7.5 12.4 %collective-permute-start.3 = (bf16[4,16512]{1,0:T(4,128)(2,1)}, bf16[4,16512]{1,0:T(4,128)(2,1)S(1)}, u32[]{:S(2)}, u32[]{:S(2)}) collective-permute-start(bf16[4,16512]{1,0:T(4,128)(2,1)} %shard_map.28), channel_id=1, source_target_pairs={{0,8},{4,12},{8,16},{12,20},{16,24},{20,28},{24,0},{28,4},{1,9},{5... | collective-permute-start | bytes 396296 | tf_op jit(solution)/shard_map/ppermute | solution.py:234
  8.5 11.9 %collective-permute-start.2 = (bf16[4,16512]{1,0:T(4,128)(2,1)}, bf16[4,16512]{1,0:T(4,128)(2,1)S(1)}, u32[]{:S(2)}, u32[]{:S(2)}) collective-permute-start(bf16[4,16512]{1,0:T(4,128)(2,1)} %shard_map.28), channel_id=1, source_target_pairs={{0,3},{1,0},{2,1},{3,2},{4,7},{5,4},{6,5},{7,6},{8,11},{9,8},{10,9... | collective-permute-start | bytes 396296 | tf_op jit(solution)/shard_map/ppermute | solution.py:234
  11.9 12.1 %collective-permute-start.1 = (bf16[4,16512]{1,0:T(4,128)(2,1)}, bf16[4,16512]{1,0:T(4,128)(2,1)S(1)}, u32[]{:S(2)}, u32[]{:S(2)}) collective-permute-start(bf16[4,16512]{1,0:T(4,128)(2,1)} %shard_map.28), channel_id=1, source_target_pairs={{0,2},{1,3},{2,0},{3,1},{4,6},{5,7},{6,4},{7,5},{8,10},{9,11},{10,... | collective-permute-start | bytes 396296 | tf_op jit(solution)/shard_map/ppermute | solution.py:234
  12.5 11.5 %collective-permute-start = (bf16[4,16512]{1,0:T(4,128)(2,1)}, bf16[4,16512]{1,0:T(4,128)(2,1)S(1)}, u32[]{:S(2)}, u32[]{:S(2)}) collective-permute-start(bf16[4,16512]{1,0:T(4,128)(2,1)} %shard_map.28), channel_id=1, source_target_pairs={{0,1},{1,2},{2,3},{3,0},{4,5},{5,6},{6,7},{7,4},{8,9},{9,10},{10,1... | collective-permute-start | bytes 396296 | tf_op jit(solution)/shard_map/ppermute | solution.py:234
  19.9 4.1 %collective-permute-start.9 = (bf16[4,16512]{1,0:T(4,128)(2,1)S(1)}, bf16[4,16512]{1,0:T(4,128)(2,1)S(1)}, u32[]{:S(2)}, u32[]{:S(2)}) collective-permute-start(bf16[4,16512]{1,0:T(4,128)(2,1)S(1)} %collective-permute-done.5), channel_id=1, source_target_pairs={{0,4},{4,0},{8,12},{12,8},{16,20},{20,16},{24,28},{28,24},{1,5},{5... | collective-permute-start | bytes 396296 | tf_op jit(solution)/shard_map/ppermute | solution.py:252
  20.0 4.1 %collective-permute-start.8 = (bf16[4,16512]{1,0:T(4,128)(2,1)S(1)}, bf16[4,16512]{1,0:T(4,128)(2,1)S(1)}, u32[]{:S(2)}, u32[]{:S(2)}) collective-permute-start(bf16[4,16512]{1,0:T(4,128)(2,1)S(1)} %collective-permute-done.4), channel_id=1, source_target_pairs={{0,4},{4,0},{8,12},{12,8},{16,20},{20,16},{24,28},{28,24},{1,5},{5... | collective-permute-start | bytes 396296 | tf_op jit(solution)/shard_map/ppermute | solution.py:252
  20.5 3.6 %collective-permute-start.7 = (bf16[4,16512]{1,0:T(4,128)(2,1)S(1)}, bf16[4,16512]{1,0:T(4,128)(2,1)S(1)}, u32[]{:S(2)}, u32[]{:S(2)}) collective-permute-start(bf16[4,16512]{1,0:T(4,128)(2,1)S(1)} %collective-permute-done.3), channel_id=1, source_target_pairs={{0,4},{4,0},{8,12},{12,8},{16,20},{20,16},{24,28},{28,24},{1,5},{5... | collective-permute-start | bytes 396296 | tf_op jit(solution)/shard_map/ppermute | solution.py:252
  20.5 3.5 %copy-start.3 = (bf16[4,16512]{1,0:T(4,128)(2,1)S(1)}, bf16[4,16512]{1,0:T(4,128)(2,1)}, u32[]{:S(2)}) copy-start(bf16[4,16512]{1,0:T(4,128)(2,1)} %shard_map.28) | copy-start | bytes 396292
  24.7 0.8 %copy-start.2 = (bf16[4,4,16512]{2,1,0:T(4,128)(2,1)}, bf16[4,4,16512]{2,1,0:T(4,128)(2,1)S(1)}, u32[]{:S(2)}) copy-start(bf16[4,4,16512]{2,1,0:T(4,128)(2,1)S(1)} %bitcast_dynamic-update-slice_fusion.6.rec_ref) | copy-start | bytes 1585156
  25.1 0.8 %copy-start = (bf16[4,4,16512]{2,1,0:T(4,128)(2,1)}, bf16[4,4,16512]{2,1,0:T(4,128)(2,1)S(1)}, u32[]{:S(2)}) copy-start(bf16[4,4,16512]{2,1,0:T(4,128)(2,1)S(1)} %get-tuple-element.40.own_ref) | copy-start | bytes 1585156
  25.1 1.0 %copy-start.1 = (bf16[4,4,16512]{2,1,0:T(4,128)(2,1)}, bf16[4,4,16512]{2,1,0:T(4,128)(2,1)S(1)}, u32[]{:S(2)}) copy-start(bf16[4,4,16512]{2,1,0:T(4,128)(2,1)S(1)} %get-tuple-element.39.sib_ref) | copy-start | bytes 1585156

commit v20 on v18

--- a/solution.py
+++ b/solution.py
@@ -84,17 +84,12 @@
     angle_lo = jnp.mod(lo[:, None] * shifts[None, :], NSAMP).astype(jnp.float32) * scale
     cos_hi, sin_hi = jnp.cos(angle_hi)[:, None, :], jnp.sin(angle_hi)[:, None, :]
     cos_lo, sin_lo = jnp.cos(angle_lo)[None, :, :], jnp.sin(angle_lo)[None, :, :]
-    factor = 1.0 / math.sqrt(2.0 * freq_count)
-    cosines = (cos_hi * cos_lo - sin_hi * sin_lo) * factor
-    sines = (sin_hi * cos_lo + cos_hi * sin_lo) * (-factor)
-    cosines = cosines.reshape(freq_count, lag_count).astype(jnp.bfloat16)
-    sines = sines.reshape(freq_count, lag_count).astype(jnp.bfloat16)
-    return jnp.stack([cosines, sines], axis=0).reshape(2 * freq_count, lag_count)
+    return cos_hi[:, 0], sin_hi[:, 0], cos_lo[0], sin_lo[0]
 
 
 def cross_kernel(
-    rec_ref, own_ref, sib_ref, tab_hbm, out_ref, srcf, recf, rtails, stails, cross,
-    tab_ref, tab_sem, *, windows, freqs, group, chunk
+    rec_ref, own_ref, sib_ref, chi_ref, shi_ref, clo_ref, slo_ref, out_ref, srcf, recf, rtails,
+    stails, cross, tab_ref, *, windows, freqs, group, chunk
 ):
     step = pl.program_id(0)
     rcv_count, per = rec_ref.shape[0], rec_ref.shape[1]
@@ -121,7 +116,21 @@
 
     @pl.when(step == 0)
     def _():
-        pltpu.make_async_copy(tab_hbm, tab_ref, tab_sem).start()
+        factor = 1.0 / math.sqrt(2.0 * freqs)
+        span = clo_ref.shape[0]
+        clo = clo_ref[...]
+        slo = slo_ref[...]
+
+        def fill(h, carry):
+            ch = chi_ref[pl.ds(h, 1), :]
+            sh = shi_ref[pl.ds(h, 1), :]
+            rows = pl.ds(pl.multiple_of(h * span, span), span)
+            tab_ref[rows, :] = ((ch * clo - sh * slo) * factor).astype(jnp.bfloat16)
+            rows = pl.ds(pl.multiple_of(freqs + h * span, span), span)
+            tab_ref[rows, :] = ((sh * clo + ch * slo) * (-factor)).astype(jnp.bfloat16)
+            return carry
+
+        lax.fori_loop(0, chi_ref.shape[0], fill, 0)
 
     @pl.when(step == 0)
     def _():
@@ -175,21 +184,17 @@
 
     lax.fori_loop(0, group, per_receiver, 0)
 
-    @pl.when(step == 0)
-    def _():
-        pltpu.make_async_copy(tab_hbm, tab_ref, tab_sem).wait()
-
     out_ref[...] = jnp.dot(
         cross[...], tab_ref[...], preferred_element_type=jnp.float32
     ).astype(jnp.bfloat16)
 
 
-def correlate(rec_stack, own_stack, sib_stack, table, windows, freqs):
+def correlate(rec_stack, own_stack, sib_stack, angles, windows, freqs):
     rcv_count, per, width = rec_stack.shape
     chips = own_stack.shape[0]
     nrec = rcv_count * per
     nsrc = 2 * chips * per
-    lags = table.shape[1]
+    lags = angles[0].shape[1]
     group = 8
     kernel = functools.partial(
         cross_kernel, windows=windows, freqs=freqs, group=group, chunk=256
@@ -203,8 +208,8 @@
                 pl.BlockSpec(rec_stack.shape, full3),
                 pl.BlockSpec(own_stack.shape, full3),
                 pl.BlockSpec(sib_stack.shape, full3),
-                pl.BlockSpec(memory_space=pl.ANY),
-            ],
+            ]
+            + [pl.BlockSpec(a.shape, lambda g: (0, 0)) for a in angles],
             out_specs=pl.BlockSpec((group * nsrc, lags), lambda g: (g, 0)),
             scratch_shapes=[
                 pltpu.VMEM((nsrc, windows * 3 * freqs), jnp.float32),
@@ -212,13 +217,12 @@
                 pltpu.VMEM((nrec, PAD), jnp.float32),
                 pltpu.VMEM((nsrc, PAD), jnp.float32),
                 pltpu.VMEM((group * nsrc, 2 * freqs), jnp.bfloat16),
-                pltpu.VMEM(table.shape, jnp.bfloat16),
-                pltpu.SemaphoreType.DMA(()),
+                pltpu.VMEM((2 * freqs, lags), jnp.bfloat16),
             ],
         ),
         out_shape=jax.ShapeDtypeStruct((nrec * nsrc, lags), jnp.bfloat16),
         compiler_params=pltpu.CompilerParams(dimension_semantics=("arbitrary",)),
-    )(rec_stack, own_stack, sib_stack, table)
+    )(rec_stack, own_stack, sib_stack, *angles)
     return out.reshape(nrec, nsrc, lags)
 
 

time: 32.9 us -> 35.6 us (1.082); the launches traced: 32.3 us -> 35.5 us
  waiting for transfers between devices: 0.82 us -> 6.81 us
  other arithmetic: 4.76 us -> 2.25 us
  starting transfers between devices: 12.3 us -> 10.3 us
  Pallas kernels: 12.2 us -> 13.7 us
    ppermute x6, waiting for transfers between devices: 0.81 us -> 6.54 us  [shifted(): parts.append(lax.ppermute(x, axis, perm=pairs))]
    another operation x1 -> x0, other arithmetic: 2.32 us -> none  [lag_table(): jnp.stack([cosines, sines], axis=0).reshape(2 * freq_count, lag_count)]
    sin x0 -> x2, other arithmetic: none -> 2.25 us  [the longest x1 1.25 us: lag_table(): jnp.sin(angle_lo)[None, :, :]]
    ppermute x6, starting transfers between devices: 11.5 us -> 9.22 us  [shifted(): parts.append(lax.ppermute(x, axis, perm=pairs))]
    convert_element_type x1 -> x0, other arithmetic: 1.55 us -> none  [lag_table(): cosines = cosines.reshape(freq_count, lag_count).astype(jnp.bfloat16)]
    pallas_call x1, Pallas kernels: 9.69 us -> 11.2 us  [correlate(): pl.pallas_call(kernel, grid_spec=pl.GridSpec(grid=(nrec // group,), in_sp...]
    cos x2 -> x0, other arithmetic: 0.89 us -> none  [the longest x1 0.54 us: lag_table(): jnp.cos(angle_lo)[None, :, :]]
  transfers between devices with their start and end apart: 10 -> 10, of which waited for: 2 -> 2; matrix products, arithmetic and copies ran while one was open for 15% -> 6% of each run, Pallas kernels for 0% -> 0%
where the time goes in v20:
time: 35.6 us; the launch traced here: 35.5 us
  Pallas kernels  13.7 us (38%)
  starting transfers between devices  10.3 us (29%)
  waiting for transfers between devices  6.81 us (19%)
  local copies, waits for them, and re-layouts  2.42 us (7%)
  other arithmetic  2.25 us (6%)
    pallas_call x1, Pallas kernels, correlate(): pl.pallas_call(kernel, grid_spec=pl.GridSpec(grid=(nrec // group,), in_sp...  11.2 us
    ppermute x6, starting transfers between devices, shifted(): parts.append(lax.ppermute(x, axis, perm=pairs))  9.22 us
    ppermute x6, waiting for transfers between devices, shifted(): parts.append(lax.ppermute(x, axis, perm=pairs))  6.54 us
    pallas_call x1, Pallas kernels, whiten_pack(): pl.pallas_call(kernel, out_shape=jax.ShapeDtypeStruct((channels, windows...  2.47 us
    unnamed x8, local copies, waits for them, and re-layouts  1.4 us
    sin x1, other arithmetic, lag_table(): jnp.sin(angle_lo)[None, :, :]  1.25 us
    ppermute x4, starting transfers between devices, local(): sib_stack = [lax.ppermute(part, 'src', perm=sibling) for part in own_stack]  1.03 us
    dynamic_update_slice x11, local copies, waits for them, and re-layouts, in_place_stack(): stack = lax.dynamic_update_slice_in_dim(stack, part[None], k, axis=0)  1.02 us
  transfers between devices with their start and end apart: 10, of which 2 were waited for; matrix products, arithmetic and copies ran while one was open for 6% of the time, Pallas kernels for 0%

profile of v20, /device:TPU:0, one launch (start us, length us, event | category | flops | bytes accessed | tf_op | source)
XLA Modules:
  0.0 35.5 jit_solution(13241708277509330843)
XLA Ops:
  0.0 2.5 %shard_map.28 = bf16[4,16512]{1,0:T(4,128)(2,1)} custom-call(bf16[4,4,2,2048]{3,2,1,0:T(2,128)(2,1)} %x_ref.1, s32[4,4]{1,0:T(4,128)} %v_ref.1), custom_call_target="tpu_custom_call" | custom-call | tf_op jit(solution)/shard_map/pallas_call | solution.py:70
  2.5 0.5 %collective-permute-start.6 = (bf16[4,16512]{1,0:T(4,128)(2,1)}, bf16[4,16512]{1,0:T(4,128)(2,1)S(1)}, u32[]{:S(2)}, u32[]{:S(2)}) collective-permute-start(bf16[4,16512]{1,0:T(4,128)(2,1)} %shard_map.28), channel_id=1, source_target_pairs={{0,4},{4,0},{8,12},{12,8},{16,20},{20,16},{24,28},{28,24},{1,5},{5... | collective-permute-start | bytes 396296 | tf_op jit(solution)/shard_map/ppermute | solution.py:251
  2.9 4.6 %collective-permute-start.5 = (bf16[4,16512]{1,0:T(4,128)(2,1)}, bf16[4,16512]{1,0:T(4,128)(2,1)S(1)}, u32[]{:S(2)}, u32[]{:S(2)}) collective-permute-start(bf16[4,16512]{1,0:T(4,128)(2,1)} %shard_map.28), channel_id=1, source_target_pairs={{0,24},{4,28},{8,0},{12,4},{16,8},{20,12},{24,16},{28,20},{1,25},{... | collective-permute-start | bytes 396296 | tf_op jit(solution)/shard_map/ppermute | solution.py:233
  7.5 0.0 collective-permute-start.4
  7.5 1.0 %collective-permute-start.3 = (bf16[4,16512]{1,0:T(4,128)(2,1)}, bf16[4,16512]{1,0:T(4,128)(2,1)S(1)}, u32[]{:S(2)}, u32[]{:S(2)}) collective-permute-start(bf16[4,16512]{1,0:T(4,128)(2,1)} %shard_map.28), channel_id=1, source_target_pairs={{0,8},{4,12},{8,16},{12,20},{16,24},{20,28},{24,0},{28,4},{1,9},{5... | collective-permute-start | bytes 396296 | tf_op jit(solution)/shard_map/ppermute | solution.py:233
  8.5 2.4 %collective-permute-start.2 = (bf16[4,16512]{1,0:T(4,128)(2,1)}, bf16[4,16512]{1,0:T(4,128)(2,1)S(1)}, u32[]{:S(2)}, u32[]{:S(2)}) collective-permute-start(bf16[4,16512]{1,0:T(4,128)(2,1)} %shard_map.28), channel_id=1, source_target_pairs={{0,3},{1,0},{2,1},{3,2},{4,7},{5,4},{6,5},{7,6},{8,11},{9,8},{10,9... | collective-permute-start | bytes 396296 | tf_op jit(solution)/shard_map/ppermute | solution.py:233
  11.0 0.0 copy-start.3
  11.0 1.3 %fusion.4 = (f32[64,512]{1,0:T(8,128)}, f32[64,512]{1,0:T(8,128)}) fusion(s32[512]{0:T(512)S(1)} %iota_add_fusion), kind=kLoop, calls=%fused_computation.15 | loop fusion | flops 294912 | bytes 264192 | tf_op jit(solution)/shard_map/sin | solution.py:86
  12.2 0.0 collective-permute-done.6
  12.2 0.0 copy-done.3
  12.3 0.6 %collective-permute-start.1 = (bf16[4,16512]{1,0:T(4,128)(2,1)S(1)}, bf16[4,16512]{1,0:T(4,128)(2,1)S(1)}, u32[]{:S(2)}, u32[]{:S(2)}) collective-permute-start(bf16[4,16512]{1,0:T(4,128)(2,1)S(1)} %copy-done.3), channel_id=1, source_target_pairs={{0,2},{1,3},{2,0},{3,1},{4,6},{5,7},{6,4},{7,5},{8,10},{9,11},{10,... | collective-permute-start | bytes 396296 | tf_op jit(solution)/shard_map/ppermute | solution.py:233
  12.8 0.0 collective-permute-done.5
  12.8 0.6 %collective-permute-start = (bf16[4,16512]{1,0:T(4,128)(2,1)S(1)}, bf16[4,16512]{1,0:T(4,128)(2,1)S(1)}, u32[]{:S(2)}, u32[]{:S(2)}) collective-permute-start(bf16[4,16512]{1,0:T(4,128)(2,1)S(1)} %copy-done.3), channel_id=1, source_target_pairs={{0,1},{1,2},{2,3},{3,0},{4,5},{5,6},{6,7},{7,4},{8,9},{9,10},{10,1... | collective-permute-start | bytes 396296 | tf_op jit(solution)/shard_map/ppermute | solution.py:233
  13.4 6.5 %collective-permute-done.4 = bf16[4,16512]{1,0:T(4,128)(2,1)S(1)} collective-permute-done((bf16[4,16512]{1,0:T(4,128)(2,1)}, bf16[4,16512]{1,0:T(4,128)(2,1)S(1)}, u32[]{:S(2)}, u32[]{:S(2)}) %collective-permute-start.4) | collective-permute-done | bytes 132128 | tf_op jit(solution)/shard_map/ppermute | solution.py:233
  19.9 0.0 collective-permute-start.9
  19.9 0.0 collective-permute-done.3
  20.0 0.5 %collective-permute-start.8 = (bf16[4,16512]{1,0:T(4,128)(2,1)S(1)}, bf16[4,16512]{1,0:T(4,128)(2,1)S(1)}, u32[]{:S(2)}, u32[]{:S(2)}) collective-permute-start(bf16[4,16512]{1,0:T(4,128)(2,1)S(1)} %collective-permute-done.4), channel_id=1, source_target_pairs={{0,4},{4,0},{8,12},{12,8},{16,20},{20,16},{24,28},{28,24},{1,5},{5... | collective-permute-start | bytes 396296 | tf_op jit(solution)/shard_map/ppermute | solution.py:251
  20.5 0.0 collective-permute-done.2
  20.5 0.1 collective-permute-start.7
  20.5 1.0 %fusion.11 = (f32[32,512]{1,0:T(8,128)}, f32[32,512]{1,0:T(8,128)}) fusion(s32[512]{0:T(512)S(1)} %iota_add_fusion, s32[32]{0:T(128)S(1)} %iota_multiply_fusion), kind=kLoop, calls=%fused_computation.24 | loop fusion | flops 147456 | bytes 133248 | tf_op jit(solution)/shard_map/sin | solution.py:85
  21.5 0.0 collective-permute-done.1
  21.5 0.0 collective-permute-done
  21.5 0.0 collective-permute-done.9
  21.5 0.0 collective-permute-done.8
  21.5 0.3 collective-permute-done.7
  21.8 0.1 dynamic_update_slice.36
  22.0 0.1 dynamic_update_slice.44
  22.1 0.1 dynamic_update_slice.40
  22.3 0.1 bitcast_dynamic-update-slice_fusion.8
  22.3 0.1 bitcast_dynamic-update-slice_fusion.7
  22.4 0.1 bitcast_dynamic-update-slice_fusion.6.rec_ref
  22.5 0.0 copy-start.2
  22.5 0.1 bitcast_dynamic-update-slice_fusion.2
  22.6 0.1 bitcast_dynamic-update-slice_fusion.1
  22.6 0.1 bitcast_dynamic-update-slice_fusion.5
  22.7 0.1 bitcast_dynamic-update-slice_fusion.4
  22.8 0.1 bitcast_dynamic-update-slice_fusion
  22.9 0.4 %copy-done.2 = bf16[4,4,16512]{2,1,0:T(4,128)(2,1)} copy-done((bf16[4,4,16512]{2,1,0:T(4,128)(2,1)}, bf16[4,4,16512]{2,1,0:T(4,128)(2,1)S(1)}, u32[]{:S(2)}) %copy-start.2) | copy-done | bytes 528408
  23.3 0.0 copy-start
  23.3 0.0 copy-start.1
  23.3 0.8 %copy-done = bf16[4,4,16512]{2,1,0:T(4,128)(2,1)} copy-done((bf16[4,4,16512]{2,1,0:T(4,128)(2,1)}, bf16[4,4,16512]{2,1,0:T(4,128)(2,1)S(1)}, u32[]{:S(2)}) %copy-start) | copy-done | bytes 528408
  24.1 0.2 copy-done.1
  24.3 11.2 %shard_map.29 = bf16[512,512]{1,0:T(8,128)(2,1)} custom-call(bf16[4,4,16512]{2,1,0:T(4,128)(2,1)} %copy-done.2, bf16[4,4,16512]{2,1,0:T(4,128)(2,1)} %copy-done, bf16[4,4,16512]{2,1,0:T(4,128)(2,1)} %copy-done.1, f32[32,512]{1,0:T(8,128)} %get-tuple-element.33.chi_ref, f32[32,512]{1,0:T(8,128)} %get-tuple-element.34.shi_ref, ...), custom_call_target="tpu_custom_call" | custom-call | tf_op jit(solution)/shard_map/pallas_call | solution.py:203
  (2 shorter events, 0.0 us)
Async XLA Ops:
  2.5 9.8 %collective-permute-start.6 = (bf16[4,16512]{1,0:T(4,128)(2,1)}, bf16[4,16512]{1,0:T(4,128)(2,1)S(1)}, u32[]{:S(2)}, u32[]{:S(2)}) collective-permute-start(bf16[4,16512]{1,0:T(4,128)(2,1)} %shard_map.28), channel_id=1, source_target_pairs={{0,4},{4,0},{8,12},{12,8},{16,20},{20,16},{24,28},{28,24},{1,5},{5... | collective-permute-start | bytes 396296 | tf_op jit(solution)/shard_map/ppermute | solution.py:251
  2.9 9.9 %collective-permute-start.5 = (bf16[4,16512]{1,0:T(4,128)(2,1)}, bf16[4,16512]{1,0:T(4,128)(2,1)S(1)}, u32[]{:S(2)}, u32[]{:S(2)}) collective-permute-start(bf16[4,16512]{1,0:T(4,128)(2,1)} %shard_map.28), channel_id=1, source_target_pairs={{0,24},{4,28},{8,0},{12,4},{16,8},{20,12},{24,16},{28,20},{1,25},{... | collective-permute-start | bytes 396296 | tf_op jit(solution)/shard_map/ppermute | solution.py:233
  7.5 12.4 %collective-permute-start.4 = (bf16[4,16512]{1,0:T(4,128)(2,1)}, bf16[4,16512]{1,0:T(4,128)(2,1)S(1)}, u32[]{:S(2)}, u32[]{:S(2)}) collective-permute-start(bf16[4,16512]{1,0:T(4,128)(2,1)} %shard_map.28), channel_id=1, source_target_pairs={{0,16},{4,20},{8,24},{12,28},{16,0},{20,4},{24,8},{28,12},{1,17},{... | collective-permute-start | bytes 396296 | tf_op jit(solution)/shard_map/ppermute | solution.py:233
  7.5 12.4 %collective-permute-start.3 = (bf16[4,16512]{1,0:T(4,128)(2,1)}, bf16[4,16512]{1,0:T(4,128)(2,1)S(1)}, u32[]{:S(2)}, u32[]{:S(2)}) collective-permute-start(bf16[4,16512]{1,0:T(4,128)(2,1)} %shard_map.28), channel_id=1, source_target_pairs={{0,8},{4,12},{8,16},{12,20},{16,24},{20,28},{24,0},{28,4},{1,9},{5... | collective-permute-start | bytes 396296 | tf_op jit(solution)/shard_map/ppermute | solution.py:233
  8.5 11.9 %collective-permute-start.2 = (bf16[4,16512]{1,0:T(4,128)(2,1)}, bf16[4,16512]{1,0:T(4,128)(2,1)S(1)}, u32[]{:S(2)}, u32[]{:S(2)}) collective-permute-start(bf16[4,16512]{1,0:T(4,128)(2,1)} %shard_map.28), channel_id=1, source_target_pairs={{0,3},{1,0},{2,1},{3,2},{4,7},{5,4},{6,5},{7,6},{8,11},{9,8},{10,9... | collective-permute-start | bytes 396296 | tf_op jit(solution)/shard_map/ppermute | solution.py:233
  11.0 1.3 %copy-start.3 = (bf16[4,16512]{1,0:T(4,128)(2,1)S(1)}, bf16[4,16512]{1,0:T(4,128)(2,1)}, u32[]{:S(2)}) copy-start(bf16[4,16512]{1,0:T(4,128)(2,1)} %shard_map.28) | copy-start | bytes 396292
  12.3 9.3 %collective-permute-start.1 = (bf16[4,16512]{1,0:T(4,128)(2,1)S(1)}, bf16[4,16512]{1,0:T(4,128)(2,1)S(1)}, u32[]{:S(2)}, u32[]{:S(2)}) collective-permute-start(bf16[4,16512]{1,0:T(4,128)(2,1)S(1)} %copy-done.3), channel_id=1, source_target_pairs={{0,2},{1,3},{2,0},{3,1},{4,6},{5,7},{6,4},{7,5},{8,10},{9,11},{10,... | collective-permute-start | bytes 396296 | tf_op jit(solution)/shard_map/ppermute | solution.py:233
  12.8 8.7 %collective-permute-start = (bf16[4,16512]{1,0:T(4,128)(2,1)S(1)}, bf16[4,16512]{1,0:T(4,128)(2,1)S(1)}, u32[]{:S(2)}, u32[]{:S(2)}) collective-permute-start(bf16[4,16512]{1,0:T(4,128)(2,1)S(1)} %copy-done.3), channel_id=1, source_target_pairs={{0,1},{1,2},{2,3},{3,0},{4,5},{5,6},{6,7},{7,4},{8,9},{9,10},{10,1... | collective-permute-start | bytes 396296 | tf_op jit(solution)/shard_map/ppermute | solution.py:233
  19.9 1.6 %collective-permute-start.9 = (bf16[4,16512]{1,0:T(4,128)(2,1)S(1)}, bf16[4,16512]{1,0:T(4,128)(2,1)S(1)}, u32[]{:S(2)}, u32[]{:S(2)}) collective-permute-start(bf16[4,16512]{1,0:T(4,128)(2,1)S(1)} %collective-permute-done.5), channel_id=1, source_target_pairs={{0,4},{4,0},{8,12},{12,8},{16,20},{20,16},{24,28},{28,24},{1,5},{5... | collective-permute-start | bytes 396296 | tf_op jit(solution)/shard_map/ppermute | solution.py:251
  20.0 1.6 %collective-permute-start.8 = (bf16[4,16512]{1,0:T(4,128)(2,1)S(1)}, bf16[4,16512]{1,0:T(4,128)(2,1)S(1)}, u32[]{:S(2)}, u32[]{:S(2)}) collective-permute-start(bf16[4,16512]{1,0:T(4,128)(2,1)S(1)} %collective-permute-done.4), channel_id=1, source_target_pairs={{0,4},{4,0},{8,12},{12,8},{16,20},{20,16},{24,28},{28,24},{1,5},{5... | collective-permute-start | bytes 396296 | tf_op jit(solution)/shard_map/ppermute | solution.py:251
  20.5 1.4 %collective-permute-start.7 = (bf16[4,16512]{1,0:T(4,128)(2,1)S(1)}, bf16[4,16512]{1,0:T(4,128)(2,1)S(1)}, u32[]{:S(2)}, u32[]{:S(2)}) collective-permute-start(bf16[4,16512]{1,0:T(4,128)(2,1)S(1)} %collective-permute-done.3), channel_id=1, source_target_pairs={{0,4},{4,0},{8,12},{12,8},{16,20},{20,16},{24,28},{28,24},{1,5},{5... | collective-permute-start | bytes 396296 | tf_op jit(solution)/shard_map/ppermute | solution.py:251
  22.5 0.8 %copy-start.2 = (bf16[4,4,16512]{2,1,0:T(4,128)(2,1)}, bf16[4,4,16512]{2,1,0:T(4,128)(2,1)S(1)}, u32[]{:S(2)}) copy-start(bf16[4,4,16512]{2,1,0:T(4,128)(2,1)S(1)} %bitcast_dynamic-update-slice_fusion.6.rec_ref) | copy-start | bytes 1585156
  23.3 0.8 %copy-start = (bf16[4,4,16512]{2,1,0:T(4,128)(2,1)}, bf16[4,4,16512]{2,1,0:T(4,128)(2,1)S(1)}, u32[]{:S(2)}) copy-start(bf16[4,4,16512]{2,1,0:T(4,128)(2,1)S(1)} %get-tuple-element.42.own_ref) | copy-start | bytes 1585156
  23.3 1.0 %copy-start.1 = (bf16[4,4,16512]{2,1,0:T(4,128)(2,1)}, bf16[4,4,16512]{2,1,0:T(4,128)(2,1)S(1)}, u32[]{:S(2)}) copy-start(bf16[4,4,16512]{2,1,0:T(4,128)(2,1)S(1)} %get-tuple-element.41.sib_ref) | copy-start | bytes 1585156

commit v21 on v18

--- a/solution.py
+++ b/solution.py
@@ -190,7 +190,7 @@
     nrec = rcv_count * per
     nsrc = 2 * chips * per
     lags = table.shape[1]
-    group = 8
+    group = nrec if nrec <= 16 else 8
     kernel = functools.partial(
         cross_kernel, windows=windows, freqs=freqs, group=group, chunk=256
     )

time: 32.9 us -> 32.8 us (level)
  no operation moved by 1% of the time
where the time goes in v21:
time: 32.8 us; the launch traced here: 32.2 us
  starting transfers between devices  12.3 us (38%)
  Pallas kernels  12.1 us (37%)
  other arithmetic  4.76 us (15%)
  local copies, waits for them, and re-layouts  2.09 us (6%)
  waiting for transfers between devices  0.82 us (2%)
    ppermute x6, starting transfers between devices, shifted(): parts.append(lax.ppermute(x, axis, perm=pairs))  11.5 us
    pallas_call x1, Pallas kernels, correlate(): pl.pallas_call(kernel, grid_spec=pl.GridSpec(grid=(nrec // group,), in_sp...  9.59 us
    pallas_call x1, Pallas kernels, whiten_pack(): pl.pallas_call(kernel, out_shape=jax.ShapeDtypeStruct((channels, windows...  2.47 us
    another operation x1, other arithmetic, lag_table(): jnp.stack([cosines, sines], axis=0).reshape(2 * freq_count, lag_count)  2.32 us
    convert_element_type x1, other arithmetic, lag_table(): cosines = cosines.reshape(freq_count, lag_count).astype(jnp.bfloat16)  1.55 us
    unnamed x8, local copies, waits for them, and re-layouts  1.07 us
    dynamic_update_slice x11, local copies, waits for them, and re-layouts, in_place_stack(): stack = lax.dynamic_update_slice_in_dim(stack, part[None], k, axis=0)  1.02 us
    ppermute x4, starting transfers between devices, local(): sib_stack = [lax.ppermute(part, 'src', perm=sibling) for part in own_stack]  0.89 us
  transfers between devices with their start and end apart: 10, of which 2 were waited for; matrix products, arithmetic and copies ran while one was open for 15% of the time, Pallas kernels for 0%

profile of v21, /device:TPU:0, one launch (start us, length us, event | category | flops | bytes accessed | tf_op | source)
XLA Modules:
  0.0 32.2 jit_solution(5483477215392202847)
XLA Ops:
  0.0 2.5 %shard_map.28 = bf16[4,16512]{1,0:T(4,128)(2,1)} custom-call(bf16[4,4,2,2048]{3,2,1,0:T(2,128)(2,1)} %x_ref.1, s32[4,4]{1,0:T(4,128)} %v_ref.1), custom_call_target="tpu_custom_call" | custom-call | tf_op jit(solution)/shard_map/pallas_call | solution.py:70
  2.5 0.0 copy-start.3
  2.5 3.0 %collective-permute-start.3 = (bf16[4,16512]{1,0:T(4,128)(2,1)}, bf16[4,16512]{1,0:T(4,128)(2,1)S(1)}, u32[]{:S(2)}, u32[]{:S(2)}) collective-permute-start(bf16[4,16512]{1,0:T(4,128)(2,1)} %shard_map.28), channel_id=1, source_target_pairs={{0,8},{4,12},{8,16},{12,20},{16,24},{20,28},{24,0},{28,4},{1,9},{5... | collective-permute-start | bytes 396296 | tf_op jit(solution)/shard_map/ppermute | solution.py:229
  5.5 2.6 %collective-permute-start.4 = (bf16[4,16512]{1,0:T(4,128)(2,1)}, bf16[4,16512]{1,0:T(4,128)(2,1)S(1)}, u32[]{:S(2)}, u32[]{:S(2)}) collective-permute-start(bf16[4,16512]{1,0:T(4,128)(2,1)} %shard_map.28), channel_id=1, source_target_pairs={{0,16},{4,20},{8,24},{12,28},{16,0},{20,4},{24,8},{28,12},{1,17},{... | collective-permute-start | bytes 396296 | tf_op jit(solution)/shard_map/ppermute | solution.py:229
  8.1 1.3 %collective-permute-start.5 = (bf16[4,16512]{1,0:T(4,128)(2,1)}, bf16[4,16512]{1,0:T(4,128)(2,1)S(1)}, u32[]{:S(2)}, u32[]{:S(2)}) collective-permute-start(bf16[4,16512]{1,0:T(4,128)(2,1)} %shard_map.28), channel_id=1, source_target_pairs={{0,24},{4,28},{8,0},{12,4},{16,8},{20,12},{24,16},{28,20},{1,25},{... | collective-permute-start | bytes 396296 | tf_op jit(solution)/shard_map/ppermute | solution.py:229
  9.4 1.5 %collective-permute-start = (bf16[4,16512]{1,0:T(4,128)(2,1)}, bf16[4,16512]{1,0:T(4,128)(2,1)S(1)}, u32[]{:S(2)}, u32[]{:S(2)}) collective-permute-start(bf16[4,16512]{1,0:T(4,128)(2,1)} %shard_map.28), channel_id=1, source_target_pairs={{0,1},{1,2},{2,3},{3,0},{4,5},{5,6},{6,7},{7,4},{8,9},{9,10},{10,1... | collective-permute-start | bytes 396296 | tf_op jit(solution)/shard_map/ppermute | solution.py:229
  10.9 1.5 %collective-permute-start.1 = (bf16[4,16512]{1,0:T(4,128)(2,1)}, bf16[4,16512]{1,0:T(4,128)(2,1)S(1)}, u32[]{:S(2)}, u32[]{:S(2)}) collective-permute-start(bf16[4,16512]{1,0:T(4,128)(2,1)} %shard_map.28), channel_id=1, source_target_pairs={{0,2},{1,3},{2,0},{3,1},{4,6},{5,7},{6,4},{7,5},{8,10},{9,11},{10,... | collective-permute-start | bytes 396296 | tf_op jit(solution)/shard_map/ppermute | solution.py:229
  12.5 0.5 %fusion.5 = (f32[64,512]{1,0:T(8,128)S(1)}, f32[64,512]{1,0:T(8,128)S(1)}) fusion(s32[512]{0:T(512)S(1)} %iota_add_fusion), kind=kLoop, calls=%fused_computation.19 | loop fusion | flops 294912 | bytes 264192 | tf_op jit(solution)/shard_map/cos | solution.py:86
  13.0 0.3 %fusion.12 = (f32[32,512]{1,0:T(8,128)S(1)}, f32[32,512]{1,0:T(8,128)S(1)}) fusion(s32[512]{0:T(512)S(1)} %iota_add_fusion, s32[32]{0:T(128)S(1)} %iota_multiply_fusion), kind=kLoop, calls=%fused_computation.28 | loop fusion | flops 147456 | bytes 133248 | tf_op jit(solution)/shard_map/cos | solution.py:85
  13.3 1.5 %multiply_convert_fusion.1 = (bf16[32,64,512]{2,1,0:T(8,128)(2,1)S(1)}, bf16[32,64,512]{2,1,0:T(8,128)(2,1)S(1)}) fusion(f32[64,512]{1,0:T(8,128)S(1)} %get-tuple-element.36, f32[32,512]{1,0:T(8,128)S(1)} %get-tuple-element.34, f32[64,512]{1,0:T(8,128)S(1)} %get-tuple-element.35, f32[32,512]{1,0:T(8,128)S(1)} %get-tuple-element.33), kind=kLoop, calls=%fused_computation.2 | loop fusion | flops 10485760 | bytes 4587520 | tf_op jit(solution)/shard_map/convert_element_type | solution.py:90
  14.9 0.0 collective-permute-done.3
  14.9 0.0 copy-done.3
  14.9 1.5 %collective-permute-start.2 = (bf16[4,16512]{1,0:T(4,128)(2,1)S(1)}, bf16[4,16512]{1,0:T(4,128)(2,1)S(1)}, u32[]{:S(2)}, u32[]{:S(2)}) collective-permute-start(bf16[4,16512]{1,0:T(4,128)(2,1)S(1)} %copy-done.3), channel_id=1, source_target_pairs={{0,3},{1,0},{2,1},{3,2},{4,7},{5,4},{6,5},{7,6},{8,11},{9,8},{10,9... | collective-permute-start | bytes 396296 | tf_op jit(solution)/shard_map/ppermute | solution.py:229
  16.4 0.7 %collective-permute-done.4 = bf16[4,16512]{1,0:T(4,128)(2,1)S(1)} collective-permute-done((bf16[4,16512]{1,0:T(4,128)(2,1)}, bf16[4,16512]{1,0:T(4,128)(2,1)S(1)}, u32[]{:S(2)}, u32[]{:S(2)}) %collective-permute-start.4) | collective-permute-done | bytes 132128 | tf_op jit(solution)/shard_map/ppermute | solution.py:229
  17.1 0.0 collective-permute-start.6
  17.1 0.0 collective-permute-done.5
  17.1 0.5 %collective-permute-start.7 = (bf16[4,16512]{1,0:T(4,128)(2,1)S(1)}, bf16[4,16512]{1,0:T(4,128)(2,1)S(1)}, u32[]{:S(2)}, u32[]{:S(2)}) collective-permute-start(bf16[4,16512]{1,0:T(4,128)(2,1)S(1)} %collective-permute-done.3), channel_id=1, source_target_pairs={{0,4},{4,0},{8,12},{12,8},{16,20},{20,16},{24,28},{28,24},{1,5},{5... | collective-permute-start | bytes 396296 | tf_op jit(solution)/shard_map/ppermute | solution.py:247
  17.6 0.0 collective-permute-done
  17.6 0.1 collective-permute-start.8
  17.7 0.1 collective-permute-done.1
  17.8 0.3 collective-permute-start.9
  18.1 2.3 %pad_maximum_fusion = bf16[2,2048,512]{2,1,0:T(8,128)(2,1)} fusion(bf16[1,2048,512]{2,1,0:T(8,128)(2,1)S(1)} %bitcast.27, bf16[1,2048,512]{2,1,0:T(8,128)(2,1)S(1)} %bitcast.26), kind=kLoop, calls=%fused_computation | loop fusion | flops 2097152 | bytes 8388608 | tf_op jit(solution)/shard_map/stack | solution.py:92
  20.4 0.0 collective-permute-done.2
  20.4 0.0 collective-permute-done.6
  20.4 0.0 collective-permute-done.7
  20.4 0.0 collective-permute-done.8
  20.5 0.0 collective-permute-done.9
  20.5 0.1 dynamic_update_slice.40
  20.6 0.1 dynamic_update_slice.44
  20.8 0.1 dynamic_update_slice.36
  20.9 0.1 bitcast_dynamic-update-slice_fusion.5
  21.0 0.1 bitcast_dynamic-update-slice_fusion.4
  21.1 0.1 bitcast_dynamic-update-slice_fusion.2
  21.1 0.1 bitcast_dynamic-update-slice_fusion.1
  21.2 0.1 bitcast_dynamic-update-slice_fusion.8
  21.3 0.1 bitcast_dynamic-update-slice_fusion.7
  21.3 0.1 bitcast_dynamic-update-slice_fusion.6.rec_ref
  21.4 0.0 copy-start
  21.4 0.1 bitcast_dynamic-update-slice_fusion
  21.5 0.0 copy-start.1
  21.5 0.0 copy-start.2
  21.6 0.7 %copy-done = bf16[4,4,16512]{2,1,0:T(4,128)(2,1)} copy-done((bf16[4,4,16512]{2,1,0:T(4,128)(2,1)}, bf16[4,4,16512]{2,1,0:T(4,128)(2,1)S(1)}, u32[]{:S(2)}) %copy-start) | copy-done | bytes 528408
  22.2 0.2 copy-done.1
  22.4 0.2 copy-done.2
  22.6 9.6 %shard_map.29 = bf16[512,512]{1,0:T(8,128)(2,1)} custom-call(bf16[4,4,16512]{2,1,0:T(4,128)(2,1)} %copy-done, bf16[4,4,16512]{2,1,0:T(4,128)(2,1)} %copy-done.2, bf16[4,4,16512]{2,1,0:T(4,128)(2,1)} %copy-done.1, bf16[4096,512]{1,0:T(8,128)(2,1)} %bitcast.25), custom_call_target="tpu_custom_call" | custom-call | tf_op jit(solution)/shard_map/pallas_call | solution.py:198
  (2 shorter events, 0.0 us)
Async XLA Ops:
  2.5 12.4 %copy-start.3 = (bf16[4,16512]{1,0:T(4,128)(2,1)S(1)}, bf16[4,16512]{1,0:T(4,128)(2,1)}, u32[]{:S(2)}) copy-start(bf16[4,16512]{1,0:T(4,128)(2,1)} %shard_map.28) | copy-start | bytes 396292
  2.5 12.4 %collective-permute-start.3 = (bf16[4,16512]{1,0:T(4,128)(2,1)}, bf16[4,16512]{1,0:T(4,128)(2,1)S(1)}, u32[]{:S(2)}, u32[]{:S(2)}) collective-permute-start(bf16[4,16512]{1,0:T(4,128)(2,1)} %shard_map.28), channel_id=1, source_target_pairs={{0,8},{4,12},{8,16},{12,20},{16,24},{20,28},{24,0},{28,4},{1,9},{5... | collective-permute-start | bytes 396296 | tf_op jit(solution)/shard_map/ppermute | solution.py:229
  5.5 11.6 %collective-permute-start.4 = (bf16[4,16512]{1,0:T(4,128)(2,1)}, bf16[4,16512]{1,0:T(4,128)(2,1)S(1)}, u32[]{:S(2)}, u32[]{:S(2)}) collective-permute-start(bf16[4,16512]{1,0:T(4,128)(2,1)} %shard_map.28), channel_id=1, source_target_pairs={{0,16},{4,20},{8,24},{12,28},{16,0},{20,4},{24,8},{28,12},{1,17},{... | collective-permute-start | bytes 396296 | tf_op jit(solution)/shard_map/ppermute | solution.py:229
  8.1 9.0 %collective-permute-start.5 = (bf16[4,16512]{1,0:T(4,128)(2,1)}, bf16[4,16512]{1,0:T(4,128)(2,1)S(1)}, u32[]{:S(2)}, u32[]{:S(2)}) collective-permute-start(bf16[4,16512]{1,0:T(4,128)(2,1)} %shard_map.28), channel_id=1, source_target_pairs={{0,24},{4,28},{8,0},{12,4},{16,8},{20,12},{24,16},{28,20},{1,25},{... | collective-permute-start | bytes 396296 | tf_op jit(solution)/shard_map/ppermute | solution.py:229
  9.4 8.2 %collective-permute-start = (bf16[4,16512]{1,0:T(4,128)(2,1)}, bf16[4,16512]{1,0:T(4,128)(2,1)S(1)}, u32[]{:S(2)}, u32[]{:S(2)}) collective-permute-start(bf16[4,16512]{1,0:T(4,128)(2,1)} %shard_map.28), channel_id=1, source_target_pairs={{0,1},{1,2},{2,3},{3,0},{4,5},{5,6},{6,7},{7,4},{8,9},{9,10},{10,1... | collective-permute-start | bytes 396296 | tf_op jit(solution)/shard_map/ppermute | solution.py:229
  10.9 6.9 %collective-permute-start.1 = (bf16[4,16512]{1,0:T(4,128)(2,1)}, bf16[4,16512]{1,0:T(4,128)(2,1)S(1)}, u32[]{:S(2)}, u32[]{:S(2)}) collective-permute-start(bf16[4,16512]{1,0:T(4,128)(2,1)} %shard_map.28), channel_id=1, source_target_pairs={{0,2},{1,3},{2,0},{3,1},{4,6},{5,7},{6,4},{7,5},{8,10},{9,11},{10,... | collective-permute-start | bytes 396296 | tf_op jit(solution)/shard_map/ppermute | solution.py:229
  14.9 5.5 %collective-permute-start.2 = (bf16[4,16512]{1,0:T(4,128)(2,1)S(1)}, bf16[4,16512]{1,0:T(4,128)(2,1)S(1)}, u32[]{:S(2)}, u32[]{:S(2)}) collective-permute-start(bf16[4,16512]{1,0:T(4,128)(2,1)S(1)} %copy-done.3), channel_id=1, source_target_pairs={{0,3},{1,0},{2,1},{3,2},{4,7},{5,4},{6,5},{7,6},{8,11},{9,8},{10,9... | collective-permute-start | bytes 396296 | tf_op jit(solution)/shard_map/ppermute | solution.py:229
  17.1 3.4 %collective-permute-start.6 = (bf16[4,16512]{1,0:T(4,128)(2,1)S(1)}, bf16[4,16512]{1,0:T(4,128)(2,1)S(1)}, u32[]{:S(2)}, u32[]{:S(2)}) collective-permute-start(bf16[4,16512]{1,0:T(4,128)(2,1)S(1)} %copy-done.3), channel_id=1, source_target_pairs={{0,4},{4,0},{8,12},{12,8},{16,20},{20,16},{24,28},{28,24},{1,5},{5... | collective-permute-start | bytes 396296 | tf_op jit(solution)/shard_map/ppermute | solution.py:247
  17.1 3.4 %collective-permute-start.7 = (bf16[4,16512]{1,0:T(4,128)(2,1)S(1)}, bf16[4,16512]{1,0:T(4,128)(2,1)S(1)}, u32[]{:S(2)}, u32[]{:S(2)}) collective-permute-start(bf16[4,16512]{1,0:T(4,128)(2,1)S(1)} %collective-permute-done.3), channel_id=1, source_target_pairs={{0,4},{4,0},{8,12},{12,8},{16,20},{20,16},{24,28},{28,24},{1,5},{5... | collective-permute-start | bytes 396296 | tf_op jit(solution)/shard_map/ppermute | solution.py:247
  17.6 2.9 %collective-permute-start.8 = (bf16[4,16512]{1,0:T(4,128)(2,1)S(1)}, bf16[4,16512]{1,0:T(4,128)(2,1)S(1)}, u32[]{:S(2)}, u32[]{:S(2)}) collective-permute-start(bf16[4,16512]{1,0:T(4,128)(2,1)S(1)} %collective-permute-done.4), channel_id=1, source_target_pairs={{0,4},{4,0},{8,12},{12,8},{16,20},{20,16},{24,28},{28,24},{1,5},{5... | collective-permute-start | bytes 396296 | tf_op jit(solution)/shard_map/ppermute | solution.py:247
  17.8 2.7 %collective-permute-start.9 = (bf16[4,16512]{1,0:T(4,128)(2,1)S(1)}, bf16[4,16512]{1,0:T(4,128)(2,1)S(1)}, u32[]{:S(2)}, u32[]{:S(2)}) collective-permute-start(bf16[4,16512]{1,0:T(4,128)(2,1)S(1)} %collective-permute-done.5), channel_id=1, source_target_pairs={{0,4},{4,0},{8,12},{12,8},{16,20},{20,16},{24,28},{28,24},{1,5},{5... | collective-permute-start | bytes 396296 | tf_op jit(solution)/shard_map/ppermute | solution.py:247
  21.4 0.8 %copy-start = (bf16[4,4,16512]{2,1,0:T(4,128)(2,1)}, bf16[4,4,16512]{2,1,0:T(4,128)(2,1)S(1)}, u32[]{:S(2)}) copy-start(bf16[4,4,16512]{2,1,0:T(4,128)(2,1)S(1)} %bitcast_dynamic-update-slice_fusion.6.rec_ref) | copy-start | bytes 1585156
  21.5 0.9 %copy-start.1 = (bf16[4,4,16512]{2,1,0:T(4,128)(2,1)}, bf16[4,4,16512]{2,1,0:T(4,128)(2,1)S(1)}, u32[]{:S(2)}) copy-start(bf16[4,4,16512]{2,1,0:T(4,128)(2,1)S(1)} %get-tuple-element.37.sib_ref) | copy-start | bytes 1585156
  21.5 1.1 %copy-start.2 = (bf16[4,4,16512]{2,1,0:T(4,128)(2,1)}, bf16[4,4,16512]{2,1,0:T(4,128)(2,1)S(1)}, u32[]{:S(2)}) copy-start(bf16[4,4,16512]{2,1,0:T(4,128)(2,1)S(1)} %get-tuple-element.38.own_ref) | copy-start | bytes 1585156
